TPU v7x, 32 devices: a whole 2x2x4 slice. The times are simulated.
32 devices in a mesh: row: 4 (over x, core), col: 8 (over z, y).
Axes of the slice: x: 2, y: 2, z: 4, core: 2. Of those that a mesh axis runs over, the one named last changes fastest.
Arguments:
- a_blocks: bfloat16 [16, 32, 9, 64, 64], P('row', 'col'), may hold values from -0.375 to 0.375
- a_cols: int32 [16, 32, 9], P('row', 'col'), may hold values from 0 to 511, as said below
- p_blocks: bfloat16 [16, 32, 4, 64, 64], P('row', 'col'), may hold values from -1.5 to 1.5
- p_cols: int32 [16, 32, 4], P('row', 'col'), may hold values from 0 to 127, as said below
- c_cols: int32 [8, 16, 25], P('row', 'col'), may hold values from 0 to 127, as said below
Outputs:
- galerkin: bfloat16 [8, 16, 25, 64, 64], P('row', 'col')
Inputs may be any that keep to these rules, and one draw needn't show every extreme that they name: a_cols of tile (y, x) names, in an order drawn per tile, the 9 tiles (y + dy, x + dx) with dy, dx in -1, 0, 1, where a row or column outside the grid is mirrored at the edge (-1 becomes 1, 16 becomes 16 - 2, likewise for columns). p_cols of tile (y, x) names, in an order drawn per tile, the 4 aggregates (Y, X) with Y in floor((y - 1) / 2) + 0 or 1 and X in floor((x - 1) / 2) + 0 or 1, an aggregate row or column outside the grid mirrored at the edge (-1 becomes 1, 8 becomes 8 - 2, likewise for columns). c_cols of aggregate (Y, X) names, in an order drawn per aggregate, the 25 aggregates (Y + dY, X + dX) with dY, dX in -2 to 2, mirrored at the edges as for p_cols (so some are named twice).
All inputs are finite; a program needn't handle non-finite values.
Results may differ from a plain program's by a relative error of at most 0.006.
Values may be sent and summed in bfloat16 or wider, within the bound.
No kernel may reach another device: no remote copies, remote signals or barrier semaphores. Data moves between devices by JAX's collectives and lax.ppermute only.
A program may use at most 128 MiB of HBM per device.

v0:
```python
import jax
import jax.numpy as jnp
from jax import lax
from jax.sharding import PartitionSpec as P


def extended(block, sides, width):
    for axis, dim in sides:
        count = lax.axis_size(axis)
        forward = [(i, i + 1) for i in range(count - 1)]
        backward = [(target, source) for source, target in forward]
        low = lax.ppermute(
            lax.slice_in_dim(block, block.shape[dim] - width, None, axis=dim), axis, forward
        )
        high = lax.ppermute(lax.slice_in_dim(block, 0, width, axis=dim), axis, backward)
        block = jnp.concatenate([low, block, high], axis=dim)
    return block


def from_behind(block, axis, distance):
    devices = range(lax.axis_size(axis))
    route = [(i - distance, i) for i in devices if i - distance in devices]
    return lax.ppermute(block, axis, route)


def form_products(
    blocks, cols, panels, panel_cols, panel_row0, panel_col0, tile_row0, tile_col0, grid_cols
):
    coarse_cols = grid_cols // 2
    ext_rows, ext_cols = (panels.shape[0], panels.shape[1])
    block_size = blocks.shape[-1]
    flat_panels = panels.reshape(ext_rows * ext_cols, 4, block_size, block_size)
    flat_cols = panel_cols.reshape(ext_rows * ext_cols, 4)
    across = tile_col0 + jnp.arange(blocks.shape[1], dtype=jnp.int32)
    slots = jnp.arange(9, dtype=jnp.int32)

    def form_one_row(carry, row_data):
        row_blocks, row_cols, tile_row = row_data
        local_row = jnp.clip(row_cols // grid_cols - panel_row0, 0, ext_rows - 1)
        local_col = jnp.clip(row_cols % grid_cols - panel_col0, 0, ext_cols - 1)
        index = local_row * ext_cols + local_col
        near = flat_panels[index]
        near_cols = flat_cols[index]
        base_y = tile_row // 2 - 1
        base_x = across // 2 - 1
        slot = (near_cols // coarse_cols - base_y) * 3 + (
            near_cols % coarse_cols - base_x[:, None, None]
        )
        hot = (slot[..., None] == slots).astype(jnp.float32)
        prod = jnp.einsum("xkab,xklbc->xklac", row_blocks, near, preferred_element_type=jnp.float32)
        summed = jnp.einsum("xkle,xklac->xeac", hot, prod, precision=lax.Precision.HIGHEST)
        return (carry, summed.astype(jnp.bfloat16))

    tile_rows = tile_row0 + jnp.arange(blocks.shape[0], dtype=jnp.int32)
    _, result = lax.scan(form_one_row, jnp.int32(0), (blocks, cols, tile_rows))
    return result


def add_terms(
    panels,
    panel_cols,
    products,
    tile_row0,
    tile_col0,
    grid_cols,
    coarse_row0,
    coarse_col0,
    coarse_rows_n,
    coarse_cols_n,
):
    block_size = panels.shape[-1]
    coarse_cols = grid_cols // 2
    across = tile_col0 + jnp.arange(panels.shape[1], dtype=jnp.int32)
    slots = jnp.arange(9, dtype=jnp.int32)
    part_y = slots // 3
    part_x = slots % 3
    segments = coarse_rows_n * coarse_cols_n * 25

    def add_one_row(total, row_data):
        row_panels, row_cols, row_products, tile_row = row_data
        terms = jnp.einsum(
            "xmbu,xebv->xmeuv", row_panels, row_products, preferred_element_type=jnp.float32
        )
        coarse_y = row_cols // coarse_cols
        coarse_x = row_cols % coarse_cols
        target_y = tile_row // 2 - 1 + part_y
        target_x = (across // 2 - 1)[:, None] + part_x[None, :]
        offset = (target_y[None, None, :] - coarse_y[:, :, None] + 2) * 5 + (
            target_x[:, None, :] - coarse_x[:, :, None] + 2
        )
        local_y = coarse_y - coarse_row0
        local_x = coarse_x - coarse_col0
        inside = (
            (local_y >= 0) & (local_y < coarse_rows_n) & (local_x >= 0) & (local_x < coarse_cols_n)
        )
        target = jnp.where(
            inside[:, :, None], (local_y * coarse_cols_n + local_x)[:, :, None] * 25 + offset, 0
        )
        kept = jnp.where(inside[:, :, None, None, None], terms, 0.0)
        added = jax.ops.segment_sum(
            kept.reshape(-1, block_size, block_size), target.reshape(-1), num_segments=segments
        )
        return (total + added, None)

    tile_rows = tile_row0 + jnp.arange(panels.shape[0], dtype=jnp.int32)
    start = jnp.zeros((segments, block_size, block_size), jnp.float32)
    total, _ = lax.scan(add_one_row, start, (panels, panel_cols, products, tile_rows))
    return total.reshape(coarse_rows_n, coarse_cols_n, 25, block_size, block_size)


def body(a_blocks, a_cols, p_blocks, p_cols, c_cols):
    tile_rows_n, tile_cols_n = (a_blocks.shape[0], a_blocks.shape[1])
    grid_cols = tile_cols_n * lax.axis_size("col")
    coarse_cols = grid_cols // 2
    coarse_rows_n, coarse_cols_n = (tile_rows_n // 2, tile_cols_n // 2)
    anchor_row = lax.axis_index("row") * tile_rows_n
    anchor_col = lax.axis_index("col") * tile_cols_n
    panels, panel_cols = (
        extended(p_blocks, (("row", 0), ("col", 1)), 1),
        extended(p_cols, (("row", 0), ("col", 1)), 1),
    )
    products = form_products(
        a_blocks,
        a_cols,
        panels,
        panel_cols,
        anchor_row - 1,
        anchor_col - 1,
        anchor_row,
        anchor_col,
        grid_cols,
    )
    total = add_terms(
        p_blocks,
        p_cols,
        products,
        anchor_row,
        anchor_col,
        grid_cols,
        anchor_row // 2 - 1,
        anchor_col // 2 - 1,
        coarse_rows_n + 2,
        coarse_cols_n + 2,
    )
    for direction in (1, -1):
        edge = total[:, -1] if direction == 1 else total[:, 0]
        arrived = from_behind(edge.astype(jnp.bfloat16), "col", direction).astype(edge.dtype)
        total = total.at[:, 1].add(arrived) if direction == 1 else total.at[:, -2].add(arrived)
    total = total[:, 1:-1]
    for direction in (1, -1):
        edge = total[-1] if direction == 1 else total[0]
        arrived = from_behind(edge.astype(jnp.bfloat16), "row", direction).astype(edge.dtype)
        total = total.at[1].add(arrived) if direction == 1 else total.at[-2].add(arrived)
    total = total[1:-1]
    own_y = anchor_row // 2 + jnp.arange(coarse_rows_n, dtype=jnp.int32)
    own_x = anchor_col // 2 + jnp.arange(coarse_cols_n, dtype=jnp.int32)
    offset = (c_cols // coarse_cols - own_y[:, None, None] + 2) * 5 + (
        c_cols % coarse_cols - own_x[None, :, None] + 2
    )
    picked = jnp.take_along_axis(total, offset[:, :, :, None, None], axis=2)
    return picked.astype(jnp.bfloat16)


def solution(mesh):
    return jax.shard_map(
        body,
        mesh=mesh,
        in_specs=(
            P("row", "col", None, None, None),
            P("row", "col", None),
            P("row", "col", None, None, None),
            P("row", "col", None),
            P("row", "col", None),
        ),
        out_specs=P("row", "col", None, None, None),
        check_vma=False,
    )
```

profile of v0, /device:TPU:9, one launch (start us, length us, event | category | flops | bytes accessed | tf_op | source)
XLA Modules:
  0.0 452.8 jit_solution(16793653393516041760)
XLA Ops:
  29.7 7.1 %collective-permute-done.2 = s32[6,1,4]{2,1,0:T(1,128)S(1)} collective-permute-done((s32[6,1,4]{2,1,0:T(1,128)S(1)}, s32[6,1,4]{2,1,0:T(1,128)S(1)}, u32[]{:S(2)}, u32[]{:S(2)}) %collective-permute-start.2) | collective-permute-done | bytes 128 | tf_op jit(solution)/shard_map/ppermute | solution.py:12
  40.4 125.2 %while.34 = (s32[]{:T(128)}, bf16[4,4,9,64,64]{3,4,2,1,0:T(8,128)(2,1)}, s32[4,4,9]{2,1,0:T(4,128)}, s32[]{:T(128)}, s32[]{:T(128)}, /*index=5*/s32[36,4]{1,0:T(...) while((s32[]{:T(128)}, ...), condition=%wide.region_1.2_spmd.clone.clone, body=%wide.region_0.1_spmd.clone.clone.sunk | while | flops 139352640 | bytes 15348239 | solution.py:55
  47.9 4.1 fusion.90
  52.1 10.5 %copy.40 = f32[4,9,4,64,64]{3,1,2,4,0:T(8,128)} copy(f32[4,9,4,64,64]{4,3,2,1,0:T(8,128)} %fusion.90) | data formatting | bytes 4718592 | tf_op jit(solution)/shard_map/while/body/eval_jaxpr/xkab,xklbc->xklac/dot_general | solution.py:50
  62.5 7.6 %fusion.93 = bf16[1,4,9,64,64]{4,2,3,1,0:T(8,128)(2,1)S(1)} fusion(f32[4,9,4,64,64]{3,1,2,4,0:T(8,128)} %copy.40, s32[4,9,4]{1,2,0:T(4,128)S(1)} %copy.42), kind=kOutput, calls=%fused_computation.16.clone.1 | convolution fusion | flops 63849744 | bytes 2654784 | tf_op jit(solution)/shard_map/while/body/eval_jaxpr/xkle,xklac->xeac/dot_general | solution.py:51
  79.2 4.1 fusion.90
  83.4 10.5 %copy.40 = f32[4,9,4,64,64]{3,1,2,4,0:T(8,128)} copy(f32[4,9,4,64,64]{4,3,2,1,0:T(8,128)} %fusion.90) | data formatting | bytes 4718592 | tf_op jit(solution)/shard_map/while/body/eval_jaxpr/xkab,xklbc->xklac/dot_general | solution.py:50
  93.8 7.6 %fusion.93 = bf16[1,4,9,64,64]{4,2,3,1,0:T(8,128)(2,1)S(1)} fusion(f32[4,9,4,64,64]{3,1,2,4,0:T(8,128)} %copy.40, s32[4,9,4]{1,2,0:T(4,128)S(1)} %copy.42), kind=kOutput, calls=%fused_computation.16.clone.1 | convolution fusion | flops 63849744 | bytes 2654784 | tf_op jit(solution)/shard_map/while/body/eval_jaxpr/xkle,xklac->xeac/dot_general | solution.py:51
  110.5 4.1 fusion.90
  114.6 10.5 %copy.40 = f32[4,9,4,64,64]{3,1,2,4,0:T(8,128)} copy(f32[4,9,4,64,64]{4,3,2,1,0:T(8,128)} %fusion.90) | data formatting | bytes 4718592 | tf_op jit(solution)/shard_map/while/body/eval_jaxpr/xkab,xklbc->xklac/dot_general | solution.py:50
  125.1 7.6 %fusion.93 = bf16[1,4,9,64,64]{4,2,3,1,0:T(8,128)(2,1)S(1)} fusion(f32[4,9,4,64,64]{3,1,2,4,0:T(8,128)} %copy.40, s32[4,9,4]{1,2,0:T(4,128)S(1)} %copy.42), kind=kOutput, calls=%fused_computation.16.clone.1 | convolution fusion | flops 63849744 | bytes 2654784 | tf_op jit(solution)/shard_map/while/body/eval_jaxpr/xkle,xklac->xeac/dot_general | solution.py:51
  141.8 4.1 fusion.90
  145.9 10.5 %copy.40 = f32[4,9,4,64,64]{3,1,2,4,0:T(8,128)} copy(f32[4,9,4,64,64]{4,3,2,1,0:T(8,128)} %fusion.90) | data formatting | bytes 4718592 | tf_op jit(solution)/shard_map/while/body/eval_jaxpr/xkab,xklbc->xklac/dot_general | solution.py:50
  156.4 7.6 %fusion.93 = bf16[1,4,9,64,64]{4,2,3,1,0:T(8,128)(2,1)S(1)} fusion(f32[4,9,4,64,64]{3,1,2,4,0:T(8,128)} %copy.40, s32[4,9,4]{1,2,0:T(4,128)S(1)} %copy.42), kind=kOutput, calls=%fused_computation.16.clone.1 | convolution fusion | flops 63849744 | bytes 2654784 | tf_op jit(solution)/shard_map/while/body/eval_jaxpr/xkle,xklac->xeac/dot_general | solution.py:51
  165.6 6.4 %broadcast.1146 = f32[400,64,64]{2,1,0:T(8,128)} broadcast(f32[]{:T(128)} %constant.485.clone.1), dimensions={} | broadcast | bytes 6553604 | tf_op jit(solution)/shard_map/broadcast.49
  172.0 148.1 %while.35 = (s32[]{:T(128)}, f32[400,64,64]{2,1,0:T(8,128)}, s32[4,4,4]{2,1,0:T(4,128)}, s32[]{:T(128)}, s32[]{:T(128)}, /*index=5*/s32[4]{0:T(128)S(1)}, bf16[4...) while((s32[]{:T(128)}, f32[400,64,64]{2,1,0:T(8,128)}, ...), condition=%wide.region_4.5_spmd.clone.clone, body=%wide.region_2.4_spmd.clone.clone.sunk | while | flops 76679040 | bytes 15012975 | solution.py:107
  180.2 6.1 %copy.44 = f32[4,4,9,64,64]{4,3,2,1,0:T(8,128)} copy(f32[4,4,9,64,64]{3,4,1,2,0:T(8,128)} %select_bitcast_fusion.2) | data formatting | bytes 4718592 | tf_op jit(solution)/shard_map/while/body/eval_jaxpr/jit(_where)/select_n | solution.py:99
  186.3 22.8 %scatter_fusion = f32[400,64,64]{2,1,0:T(8,128)} fusion(f32[400,64,64]{2,1,0:T(8,128)} %get-tuple-element.834, s32[144]{0:T(256)S(1)} %reshape.881, f32[144,64,64]{2,1,0:T(8,128)} %bitcast.175), kind=kCustom, calls=%fused_computation.3.clone.clone.clone.1 | custom fusion | flops 589824 | bytes 7078464 | tf_op jit(solution)/shard_map/while/body/eval_jaxpr/scatter-add | solution.py:100
  213.2 4.0 select_bitcast_fusion.2
  217.2 6.1 %copy.44 = f32[4,4,9,64,64]{4,3,2,1,0:T(8,128)} copy(f32[4,4,9,64,64]{3,4,1,2,0:T(8,128)} %select_bitcast_fusion.2) | data formatting | bytes 4718592 | tf_op jit(solution)/shard_map/while/body/eval_jaxpr/jit(_where)/select_n | solution.py:99
  223.3 22.9 %scatter_fusion = f32[400,64,64]{2,1,0:T(8,128)} fusion(f32[400,64,64]{2,1,0:T(8,128)} %get-tuple-element.834, s32[144]{0:T(256)S(1)} %reshape.881, f32[144,64,64]{2,1,0:T(8,128)} %bitcast.175), kind=kCustom, calls=%fused_computation.3.clone.clone.clone.1 | custom fusion | flops 589824 | bytes 7078464 | tf_op jit(solution)/shard_map/while/body/eval_jaxpr/scatter-add | solution.py:100
  250.4 4.0 select_bitcast_fusion.2
  254.4 6.1 %copy.44 = f32[4,4,9,64,64]{4,3,2,1,0:T(8,128)} copy(f32[4,4,9,64,64]{3,4,1,2,0:T(8,128)} %select_bitcast_fusion.2) | data formatting | bytes 4718592 | tf_op jit(solution)/shard_map/while/body/eval_jaxpr/jit(_where)/select_n | solution.py:99
  260.4 22.7 %scatter_fusion = f32[400,64,64]{2,1,0:T(8,128)} fusion(f32[400,64,64]{2,1,0:T(8,128)} %get-tuple-element.834, s32[144]{0:T(256)S(1)} %reshape.881, f32[144,64,64]{2,1,0:T(8,128)} %bitcast.175), kind=kCustom, calls=%fused_computation.3.clone.clone.clone.1 | custom fusion | flops 589824 | bytes 7078464 | tf_op jit(solution)/shard_map/while/body/eval_jaxpr/scatter-add | solution.py:100
  291.4 6.1 %copy.44 = f32[4,4,9,64,64]{4,3,2,1,0:T(8,128)} copy(f32[4,4,9,64,64]{3,4,1,2,0:T(8,128)} %select_bitcast_fusion.2) | data formatting | bytes 4718592 | tf_op jit(solution)/shard_map/while/body/eval_jaxpr/jit(_where)/select_n | solution.py:99
  297.4 22.7 %scatter_fusion = f32[400,64,64]{2,1,0:T(8,128)} fusion(f32[400,64,64]{2,1,0:T(8,128)} %get-tuple-element.834, s32[144]{0:T(256)S(1)} %reshape.881, f32[144,64,64]{2,1,0:T(8,128)} %bitcast.175), kind=kCustom, calls=%fused_computation.3.clone.clone.clone.1 | custom fusion | flops 589824 | bytes 7078464 | tf_op jit(solution)/shard_map/while/body/eval_jaxpr/scatter-add | solution.py:100
  324.8 37.5 %collective-permute-done.8 = bf16[4,25,64,64]{3,2,1,0:T(8,128)(2,1)S(1)} collective-permute-done((bf16[4,25,64,64]{3,2,1,0:T(8,128)(2,1)S(1)}, bf16[4,25,64,64]{3,2,1,0:T(8,128)(2,1)S(1)}, u32[]{:S(2)}, u32[]{:S(2)}) %collective-permute-start.8) | collective-permute-done | bytes 819232 | tf_op jit(solution)/shard_map/ppermute | solution.py:23
  362.3 4.5 %fusion.60 = f32[4,4,25,64,64]{4,3,2,1,0:T(8,128)} fusion(f32[4,4,25,64,64]{4,3,2,1,0:T(8,128)} %bitcast.178, bf16[4,25,64,64]{3,2,1,0:T(8,128)(2,1)S(1)} %collective-permute-done.8), kind=kLoop, calls=%fused_computation.102 | loop fusion | flops 819200 | bytes 7372800 | tf_op jit(solution)/shard_map/scatter-add | solution.py:148
  371.1 36.1 %collective-permute-done.9 = bf16[4,25,64,64]{3,2,1,0:T(8,128)(2,1)S(1)} collective-permute-done((bf16[4,25,64,64]{3,2,1,0:T(8,128)(2,1)S(1)}, bf16[4,25,64,64]{3,2,1,0:T(8,128)(2,1)S(1)}, u32[]{:S(2)}, u32[]{:S(2)}) %collective-permute-start.9) | collective-permute-done | bytes 819232 | tf_op jit(solution)/shard_map/ppermute | solution.py:23
  407.2 4.4 fusion.59
  420.0 5.5 %collective-permute-done.10 = bf16[2,25,64,64]{3,2,1,0:T(8,128)(2,1)S(1)} collective-permute-done((bf16[2,25,64,64]{3,2,1,0:T(8,128)(2,1)S(1)}, bf16[2,25,64,64]{3,2,1,0:T(8,128)(2,1)S(1)}, u32[]{:S(2)}, u32[]{:S(2)}) %collective-permute-start.10) | collective-permute-done | bytes 409632 | tf_op jit(solution)/shard_map/ppermute | solution.py:23
  432.2 12.3 %collective-permute-done.11 = bf16[2,25,64,64]{3,2,1,0:T(8,128)(2,1)S(1)} collective-permute-done((bf16[2,25,64,64]{3,2,1,0:T(8,128)(2,1)S(1)}, bf16[2,25,64,64]{3,2,1,0:T(8,128)(2,1)S(1)}, u32[]{:S(2)}, u32[]{:S(2)}) %collective-permute-start.11) | collective-permute-done | bytes 409632 | tf_op jit(solution)/shard_map/ppermute | solution.py:23
  (140 shorter events, 105.4 us)
Async XLA Ops:
  0.0 16.1 %copy-start.1 = (bf16[4,4,4,64,64]{4,3,2,1,0:T(8,128)(2,1)S(1)}, bf16[4,4,4,64,64]{4,3,2,1,0:T(8,128)(2,1)}, u32[]{:S(2)}) copy-start(bf16[4,4,4,64,64]{4,3,2,1,0:T(8,128)(2,1)} %param.19) | copy-start | bytes 1572868
  1.2 14.9 %collective-permute-start.4 = (bf16[1,4,4,64,64]{4,3,2,1,0:T(8,128)(2,1)S(1)}, bf16[1,4,4,64,64]{4,3,2,1,0:T(8,128)(2,1)S(1)}, u32[]{:S(2)}, u32[]{:S(2)}) collective-permute-start(bf16[1,4,4,64,64]{4,3,2,1,0:T(8,128)(2,1)S(1)} %get-tuple-element.649), channel_id=1, source_target_pairs={{0,8},{8,16},{16,24},{1,9},{9,17},{17,25},{2,10},{10,18},{18,26},{... | collective-permute-start | bytes 393224 | tf_op jit(solution)/shard_map/ppermute | solution.py:12
  4.9 11.4 %collective-permute-start.5 = (bf16[1,4,4,64,64]{4,3,2,1,0:T(8,128)(2,1)S(1)}, bf16[1,4,4,64,64]{4,3,2,1,0:T(8,128)(2,1)S(1)}, u32[]{:S(2)}, u32[]{:S(2)}) collective-permute-start(bf16[1,4,4,64,64]{4,3,2,1,0:T(8,128)(2,1)S(1)} %get-tuple-element.648), channel_id=1, source_target_pairs={{8,0},{16,8},{24,16},{9,1},{17,9},{25,17},{10,2},{18,10},{26,18},{... | collective-permute-start | bytes 393224 | tf_op jit(solution)/shard_map/ppermute | solution.py:15
  7.5 5.6 %collective-permute-start = (s32[1,4,4]{2,1,0:T(4,128)S(1)}, s32[1,4,4]{2,1,0:T(4,128)S(1)}, u32[]{:S(2)}, u32[]{:S(2)}) collective-permute-start(s32[1,4,4]{2,1,0:T(4,128)S(1)} %get-tuple-element.653), channel_id=1, source_target_pairs={{0,8},{8,16},{16,24},{1,9},{9,17},{17,25},{2,10},{10,18},{18,26},{... | collective-permute-start | bytes 200 | tf_op jit(solution)/shard_map/ppermute | solution.py:12
  11.1 4.9 %collective-permute-start.1 = (s32[1,4,4]{2,1,0:T(4,128)S(1)}, s32[1,4,4]{2,1,0:T(4,128)S(1)}, u32[]{:S(2)}, u32[]{:S(2)}) collective-permute-start(s32[1,4,4]{2,1,0:T(4,128)S(1)} %get-tuple-element.652), channel_id=1, source_target_pairs={{8,0},{16,8},{24,16},{9,1},{17,9},{25,17},{10,2},{18,10},{26,18},{... | collective-permute-start | bytes 200 | tf_op jit(solution)/shard_map/ppermute | solution.py:15
  17.3 21.2 %collective-permute-start.6 = (bf16[6,1,4,64,64]{4,3,2,1,0:T(8,128)(2,1)}, bf16[6,1,4,64,64]{4,3,2,1,0:T(8,128)(2,1)S(1)}, u32[]{:S(2)}, u32[]{:S(2)}) collective-permute-start(bf16[6,1,4,64,64]{4,3,2,1,0:T(8,128)(2,1)} %get-tuple-element.646), channel_id=1, source_target_pairs={{0,1},{1,2},{2,3},{3,4},{4,5},{5,6},{6,7},{8,9},{9,10},{10,11},{11... | collective-permute-start | bytes 589832 | tf_op jit(solution)/shard_map/ppermute | solution.py:12
  20.4 18.1 %collective-permute-start.7 = (bf16[6,1,4,64,64]{4,3,2,1,0:T(8,128)(2,1)}, bf16[6,1,4,64,64]{4,3,2,1,0:T(8,128)(2,1)S(1)}, u32[]{:S(2)}, u32[]{:S(2)}) collective-permute-start(bf16[6,1,4,64,64]{4,3,2,1,0:T(8,128)(2,1)} %get-tuple-element.647), channel_id=1, source_target_pairs={{1,0},{2,1},{3,2},{4,3},{5,4},{6,5},{7,6},{9,8},{10,9},{11,10},{12... | collective-permute-start | bytes 589832 | tf_op jit(solution)/shard_map/ppermute | solution.py:15
  23.5 13.3 %collective-permute-start.2 = (s32[6,1,4]{2,1,0:T(1,128)S(1)}, s32[6,1,4]{2,1,0:T(1,128)S(1)}, u32[]{:S(2)}, u32[]{:S(2)}) collective-permute-start(s32[6,1,4]{2,1,0:T(1,128)S(1)} %get-tuple-element.650), channel_id=1, source_target_pairs={{0,1},{1,2},{2,3},{3,4},{4,5},{5,6},{6,7},{8,9},{9,10},{10,11},{11... | collective-permute-start | bytes 296 | tf_op jit(solution)/shard_map/ppermute | solution.py:12
  25.7 12.7 %collective-permute-start.3 = (s32[6,1,4]{2,1,0:T(1,128)S(1)}, s32[6,1,4]{2,1,0:T(1,128)S(1)}, u32[]{:S(2)}, u32[]{:S(2)}) collective-permute-start(s32[6,1,4]{2,1,0:T(1,128)S(1)} %get-tuple-element.651), channel_id=1, source_target_pairs={{1,0},{2,1},{3,2},{4,3},{5,4},{6,5},{7,6},{9,8},{10,9},{11,10},{12... | collective-permute-start | bytes 296 | tf_op jit(solution)/shard_map/ppermute | solution.py:15
  322.5 39.9 %collective-permute-start.8 = (bf16[4,25,64,64]{3,2,1,0:T(8,128)(2,1)S(1)}, bf16[4,25,64,64]{3,2,1,0:T(8,128)(2,1)S(1)}, u32[]{:S(2)}, u32[]{:S(2)}) collective-permute-start(bf16[4,25,64,64]{3,2,1,0:T(8,128)(2,1)S(1)} %fusion.61), channel_id=1, source_target_pairs={{0,1},{1,2},{2,3},{3,4},{4,5},{5,6},{6,7},{8,9},{9,10},{10,11},{11... | collective-permute-start | bytes 2457608 | tf_op jit(solution)/shard_map/ppermute | solution.py:23
  369.2 38.1 %collective-permute-start.9 = (bf16[4,25,64,64]{3,2,1,0:T(8,128)(2,1)S(1)}, bf16[4,25,64,64]{3,2,1,0:T(8,128)(2,1)S(1)}, u32[]{:S(2)}, u32[]{:S(2)}) collective-permute-start(bf16[4,25,64,64]{3,2,1,0:T(8,128)(2,1)S(1)} %fusion.62), channel_id=1, source_target_pairs={{1,0},{2,1},{3,2},{4,3},{5,4},{6,5},{7,6},{9,8},{10,9},{11,10},{12... | collective-permute-start | bytes 2457608 | tf_op jit(solution)/shard_map/ppermute | solution.py:23
  413.2 12.3 %collective-permute-start.10 = (bf16[2,25,64,64]{3,2,1,0:T(8,128)(2,1)S(1)}, bf16[2,25,64,64]{3,2,1,0:T(8,128)(2,1)S(1)}, u32[]{:S(2)}, u32[]{:S(2)}) collective-permute-start(bf16[2,25,64,64]{3,2,1,0:T(8,128)(2,1)S(1)} %fusion.65), channel_id=1, source_target_pairs={{0,8},{8,16},{16,24},{1,9},{9,17},{17,25},{2,10},{10,18},{18,26},{... | collective-permute-start | bytes 1228808 | tf_op jit(solution)/shard_map/ppermute | solution.py:23
  420.0 12.0 %copy-start.2 = (s32[2,2,25]{2,1,0:T(2,128)S(1)}, s32[2,2,25]{2,1,0:T(2,128)}, u32[]{:S(2)}) copy-start(s32[2,2,25]{2,1,0:T(2,128)} %param.21) | copy-start | bytes 1204
  427.2 2.7 copy-start
  430.1 14.4 %collective-permute-start.11 = (bf16[2,25,64,64]{3,2,1,0:T(8,128)(2,1)S(1)}, bf16[2,25,64,64]{3,2,1,0:T(8,128)(2,1)S(1)}, u32[]{:S(2)}, u32[]{:S(2)}) collective-permute-start(bf16[2,25,64,64]{3,2,1,0:T(8,128)(2,1)S(1)} %fusion.66), channel_id=1, source_target_pairs={{8,0},{16,8},{24,16},{9,1},{17,9},{25,17},{10,2},{18,10},{26,18},{... | collective-permute-start | bytes 1228808 | tf_op jit(solution)/shard_map/ppermute | solution.py:23
where the time goes:
time: 457 us; the launch traced here: 453 us
  local copies, waits for them, and re-layouts  118 us (26%)
  other arithmetic  115 us (25%)
  waiting for transfers between devices  102 us (22%)
  matrix products  62.8 us (14%)
  starting transfers between devices  32.7 us (7%)
  loops' own time  21.1 us (5%)
    ppermute x4, waiting for transfers between devices, from_behind(): return lax.ppermute(block, axis, route)  91.5 us
    scatter-add x4, other arithmetic, add_one_row(): jax.ops.segment_sum(kept.reshape(-1, block_size, block_size), target.resh...  91.1 us
    dot_general x4, local copies, waits for them, and re-layouts, form_one_row(): jnp.einsum('xkab,xklbc->xklac', row_blocks, near, preferred_element_type=...  42 us
    dot_general x4, matrix products, form_one_row(): jnp.einsum('xkle,xklac->xeac', hot, prod, precision=lax.Precision.HIGHEST)  30.3 us
    select_n x4, local copies, waits for them, and re-layouts, add_one_row(): kept = jnp.where(inside[:, :, None, None, None], terms, 0.0)  24.2 us
    dot_general x4, matrix products, form_one_row(): jnp.einsum('xkab,xklbc->xklac', row_blocks, near, preferred_element_type=...  16.4 us
    dot_general x4, matrix products, add_one_row(): jnp.einsum('xmbu,xebv->xmeuv', row_panels, row_products, preferred_elemen...  16 us
    ppermute x4, starting transfers between devices, extended(): lax.ppermute(lax.slice_in_dim(block, block.shape[dim] - width, None, axis...  12.7 us
  transfers between devices with their start and end apart: 12, of which 7 were waited for; matrix products, arithmetic and copies ran while one was open for 1% of the time, Pallas kernels for 0%

commit v1 on v0

v1 whole, which is shorter than its diff:
```python
import jax
import jax.numpy as jnp
from jax import lax
from jax.experimental import pallas as pl
from jax.experimental.pallas import tpu as pltpu
from jax.sharding import PartitionSpec as P


def mirror(values, limit):
    values = jnp.where(values < 0, -values, values)
    return jnp.where(values >= limit, 2 * (limit - 1) - values, values)


def shifted(piece, down, right):
    rows, cols = lax.axis_size("row"), lax.axis_size("col")
    if right == 0:
        pairs = [(s, s + down) for s in range(rows) if 0 <= s + down < rows]
        return lax.ppermute(piece, "row", pairs)
    if down == 0:
        pairs = [(s, s + right) for s in range(cols) if 0 <= s + right < cols]
        return lax.ppermute(piece, "col", pairs)
    pairs = []
    for sr in range(rows):
        for sc in range(cols):
            tr, tc = sr + down, sc + right
            if 0 <= tr < rows and 0 <= tc < cols:
                pairs.append((sr * cols + sc, tr * cols + tc))
    return lax.ppermute(piece, ("row", "col"), pairs)


def with_halo(x):
    top = shifted(x[-1], 1, 0)
    bottom = shifted(x[0], -1, 0)
    left = shifted(x[:, -1], 0, 1)
    right = shifted(x[:, 0], 0, -1)
    top_left = shifted(x[-1, -1], 1, 1)
    top_right = shifted(x[-1, 0], 1, -1)
    bottom_left = shifted(x[0, -1], -1, 1)
    bottom_right = shifted(x[0, 0], -1, -1)
    first = jnp.concatenate([top_left[None], top, top_right[None]], axis=0)
    last = jnp.concatenate([bottom_left[None], bottom, bottom_right[None]], axis=0)
    middle = jnp.concatenate([left[:, None], x, right[:, None]], axis=1)
    return jnp.concatenate([first[None], middle, last[None]], axis=0)


def ap_kernel(near_ref, slot_ref, a_ref, p_ref, out_ref, acc_ref):
    tiles, terms = a_ref.shape[0], a_ref.shape[1]

    def one_tile(t, carry):
        acc_ref[...] = jnp.zeros(acc_ref.shape, jnp.float32)
        for k in range(terms):
            j = near_ref[t * terms + k]
            a = a_ref[t, k]
            for q in range(4):
                e = slot_ref[(t * terms + k) * 4 + q]

                @pl.when(e >= 0)
                def _():
                    acc_ref[e] += jnp.dot(a, p_ref[j, q], preferred_element_type=jnp.float32)

        out_ref[t] = acc_ref[...].astype(out_ref.dtype)
        return carry

    lax.fori_loop(0, tiles, one_tile, 0)


def coarse_kernel(target_ref, pick_ref, ap_ref, pt_ref, out_ref, acc_ref):
    tiles = ap_ref.shape[0]
    owned, stencil = out_ref.shape[0], out_ref.shape[1]
    acc_ref[...] = jnp.zeros(acc_ref.shape, jnp.float32)

    def one_tile(t, carry):
        for q in range(4):
            g = target_ref[t * 4 + q]

            @pl.when(g >= 0)
            def _():
                pt = pt_ref[t, q]
                for e in range(9):
                    acc_ref[g + (e // 3) * 5 + e % 3] += jnp.dot(
                        pt, ap_ref[t, e], preferred_element_type=jnp.float32
                    )

        return carry

    lax.fori_loop(0, tiles, one_tile, 0)

    def one_pick(i, carry):
        a = i // stencil
        s = i % stencil
        out_ref[a, s] = acc_ref[a * stencil + pick_ref[i]].astype(out_ref.dtype)
        return carry

    lax.fori_loop(0, owned * stencil, one_pick, 0)


def body(a_blocks, a_cols, p_blocks, p_cols, c_cols):
    n_r, n_c = a_blocks.shape[0], a_blocks.shape[1]
    bs = a_blocks.shape[-1]
    terms = a_blocks.shape[2]
    grid_rows = n_r * lax.axis_size("row")
    grid_cols = n_c * lax.axis_size("col")
    coarse_rows, coarse_cols = grid_rows // 2, grid_cols // 2
    y0 = lax.axis_index("row") * n_r
    x0 = lax.axis_index("col") * n_c
    ys = y0 + jnp.arange(n_r, dtype=jnp.int32)
    xs = x0 + jnp.arange(n_c, dtype=jnp.int32)
    two = jnp.arange(2, dtype=jnp.int32)

    agg_y = mirror((ys - 1)[:, None] // 2 + two, coarse_rows)
    agg_x = mirror((xs - 1)[:, None] // 2 + two, coarse_cols)
    wanted = (agg_y[:, None, :, None] * coarse_cols + agg_x[None, :, None, :]).reshape(n_r, n_c, 4)
    match = p_cols[:, :, None, :] == wanted[:, :, :, None]
    canon = jnp.sum(
        jnp.where(match[..., None, None], p_blocks[:, :, None], jnp.zeros((), p_blocks.dtype)),
        axis=3,
        dtype=p_blocks.dtype,
    )
    p_ext = with_halo(canon)
    ext_r, ext_c = n_r + 2, n_c + 2

    near_y = a_cols // grid_cols
    near_x = a_cols % grid_cols
    near = jnp.clip(near_y - (y0 - 1), 0, ext_r - 1) * ext_c + jnp.clip(near_x - (x0 - 1), 0, ext_c - 1)
    near_agg_y = mirror((near_y - 1)[..., None] // 2 + two, coarse_rows)
    near_agg_x = mirror((near_x - 1)[..., None] // 2 + two, coarse_cols)
    slot_y = near_agg_y - (ys // 2 - 1)[:, None, None, None]
    slot_x = near_agg_x - (xs // 2 - 1)[None, :, None, None]
    slot = (slot_y[..., :, None] * 3 + slot_x[..., None, :]).reshape(n_r, n_c, terms, 4)
    slot = jnp.where((slot >= 0) & (slot < 9), slot, -1)

    ap = pl.pallas_call(
        ap_kernel,
        out_shape=jax.ShapeDtypeStruct((n_r * n_c, 9, bs, bs), jnp.bfloat16),
        in_specs=[
            pl.BlockSpec(memory_space=pltpu.SMEM),
            pl.BlockSpec(memory_space=pltpu.SMEM),
            pl.BlockSpec(memory_space=pltpu.VMEM),
            pl.BlockSpec(memory_space=pltpu.VMEM),
        ],
        out_specs=pl.BlockSpec(memory_space=pltpu.VMEM),
        scratch_shapes=[pltpu.VMEM((9, bs, bs), jnp.float32)],
    )(
        near.reshape(-1),
        slot.reshape(-1),
        a_blocks.reshape(n_r * n_c, terms, bs, bs),
        p_ext.reshape(ext_r * ext_c, 4, bs, bs),
    )
    ap_ext = with_halo(ap.reshape(n_r, n_c, 9, bs, bs))

    o_r, o_c = n_r // 2, n_c // 2
    ey = y0 - 1 + jnp.arange(ext_r, dtype=jnp.int32)
    ex = x0 - 1 + jnp.arange(ext_c, dtype=jnp.int32)
    e_agg_y = mirror((ey - 1)[:, None] // 2 + two, coarse_rows)
    e_agg_x = mirror((ex - 1)[:, None] // 2 + two, coarse_cols)
    own_y = e_agg_y - y0 // 2
    own_x = e_agg_x - x0 // 2
    off_y = (ey // 2 - 1)[:, None] - e_agg_y + 2
    off_x = (ex // 2 - 1)[:, None] - e_agg_x + 2
    ok_y = (ey >= 0)[:, None] & (ey < grid_rows)[:, None] & (own_y >= 0) & (own_y < o_r) & (off_y >= 0) & (off_y <= 2)
    ok_x = (ex >= 0)[:, None] & (ex < grid_cols)[:, None] & (own_x >= 0) & (own_x < o_c) & (off_x >= 0) & (off_x <= 2)
    target = (own_y[:, None, :, None] * o_c + own_x[None, :, None, :]) * 25 + (
        off_y[:, None, :, None] * 5 + off_x[None, :, None, :]
    )
    target = jnp.where(ok_y[:, None, :, None] & ok_x[None, :, None, :], target, -1).reshape(-1)

    cy = ys[0] // 2 + jnp.arange(o_r, dtype=jnp.int32)
    cx = xs[0] // 2 + jnp.arange(o_c, dtype=jnp.int32)
    pick = (c_cols // coarse_cols - cy[:, None, None] + 2) * 5 + (c_cols % coarse_cols - cx[None, :, None] + 2)
    pick = jnp.clip(pick, 0, 24).reshape(-1)

    p_t = jnp.swapaxes(p_ext, -1, -2).reshape(ext_r * ext_c, 4, bs, bs)
    stencil = c_cols.shape[-1]
    out = pl.pallas_call(
        coarse_kernel,
        out_shape=jax.ShapeDtypeStruct((o_r * o_c, stencil, bs, bs), jnp.bfloat16),
        in_specs=[
            pl.BlockSpec(memory_space=pltpu.SMEM),
            pl.BlockSpec(memory_space=pltpu.SMEM),
            pl.BlockSpec(memory_space=pltpu.VMEM),
            pl.BlockSpec(memory_space=pltpu.VMEM),
        ],
        out_specs=pl.BlockSpec(memory_space=pltpu.VMEM),
        scratch_shapes=[pltpu.VMEM((o_r * o_c * 25, bs, bs), jnp.float32)],
    )(target, pick, ap_ext.reshape(ext_r * ext_c, 9, bs, bs), p_t)
    return out.reshape(o_r, o_c, stencil, bs, bs)


def solution(mesh):
    return jax.shard_map(
        body,
        mesh=mesh,
        in_specs=(
            P("row", "col", None, None, None),
            P("row", "col", None),
            P("row", "col", None, None, None),
            P("row", "col", None),
            P("row", "col", None),
        ),
        out_specs=P("row", "col", None, None, None),
        check_vma=False,
    )
```

time: 457 us -> 199 us (0.44)
  local copies, waits for them, and re-layouts: 118 us -> 11.7 us
  other arithmetic: 115 us -> 16.2 us
  Pallas kernels: 0 us -> 95.8 us
  waiting for transfers between devices: 102 us -> 24.2 us
  matrix products: 62.8 us -> 0 us
  loops' own time: 21.1 us -> 0 us
  starting transfers between devices: 32.7 us -> 48.4 us
    scatter-add x8 -> x0, other arithmetic: 105 us -> none  [the longest x4 91.1 us: add_one_row(): jax.ops.segment_sum(kept.reshape(-1, block_size, block_size), target.resh...]
    pallas_call x0 -> x2, Pallas kernels: none -> 95.8 us  [the longest x1 77.3 us: body(): pl.pallas_call(ap_kernel, out_shape=jax.ShapeDtypeStruct((n_r * n_c, 9, b...]
    ppermute x12 -> x16, waiting for transfers between devices: 102 us -> 24.2 us  [the longest x8 14.6 us: shifted(): return lax.ppermute(piece, ('row', 'col'), pairs)]
    dot_general x12 -> x0, matrix products: 62.8 us -> none  [the longest x4 30.3 us: form_one_row(): jnp.einsum('xkle,xklac->xeac', hot, prod, precision=lax.Precision.HIGHEST)]
    dot_general x4 -> x0, local copies, waits for them, and re-layouts: 42 us -> none  [form_one_row(): jnp.einsum('xkab,xklbc->xklac', row_blocks, near, preferred_element_type=...]
    select_n x12 -> x1, local copies, waits for them, and re-layouts: 24.9 us -> 0.66 us  [body(): jnp.where(ok_y[:, None, :, None] & ok_x[None, :, None, :], target, -1)]
    another operation x2 -> x0, loops' own time: 21.1 us -> none  [the longest x1 10.5 us: add_terms(): lax.scan(add_one_row, start, (panels, panel_cols, products, tile_rows))]
    ppermute x12 -> x16, starting transfers between devices: 32.7 us -> 48.4 us  [the longest x8 26 us: shifted(): return lax.ppermute(piece, ('row', 'col'), pairs)]
  transfers between devices with their start and end apart: 12 -> 16, of which waited for: 7 -> 3; matrix products, arithmetic and copies ran while one was open for 1% -> 7% of each run, Pallas kernels for 0% -> 0%
where the time goes in v1:
time: 199 us; the launch traced here: 197 us
  Pallas kernels  95.8 us (48%)
  starting transfers between devices  48.4 us (24%)
  waiting for transfers between devices  24.2 us (12%)
  other arithmetic  16.2 us (8%)
  local copies, waits for them, and re-layouts  11.7 us (6%)
    pallas_call x1, Pallas kernels, body(): pl.pallas_call(ap_kernel, out_shape=jax.ShapeDtypeStruct((n_r * n_c, 9, b...  77.3 us
    ppermute x8, starting transfers between devices, shifted(): return lax.ppermute(piece, ('row', 'col'), pairs)  26 us
    pallas_call x1, Pallas kernels, body(): pl.pallas_call(coarse_kernel, out_shape=jax.ShapeDtypeStruct((o_r * o_c,...  18.5 us
    ppermute x8, waiting for transfers between devices, shifted(): return lax.ppermute(piece, ('row', 'col'), pairs)  14.6 us
    ppermute x4, starting transfers between devices, shifted(): return lax.ppermute(piece, 'col', pairs)  12.4 us
    ppermute x4, starting transfers between devices, shifted(): return lax.ppermute(piece, 'row', pairs)  10 us
    ppermute x4, waiting for transfers between devices, shifted(): return lax.ppermute(piece, 'col', pairs)  9.54 us
    concatenate x2, other arithmetic, with_halo(): return jnp.concatenate([first[None], middle, last[None]], axis=0)  6.6 us
  transfers between devices with their start and end apart: 16, of which 3 were waited for; matrix products, arithmetic and copies ran while one was open for 7% of the time, Pallas kernels for 0%

profile of v1, /device:TPU:9, one launch (start us, length us, event | category | flops | bytes accessed | tf_op | source)
XLA Modules:
  0.0 197.1 jit_solution(1223917924873892137)
XLA Ops:
  0.3 0.8 broadcast_compare_fusion
  1.1 2.8 %select_reduce_fusion = bf16[4,4,4,64,64]{4,3,2,1,0:T(8,128)(2,1)S(1)} fusion(pred[4,4,4,4]{3,2,1,0:T(4,128)(4,1)S(1)} %broadcast_compare_fusion, bf16[4,4,4,64,64]{4,3,2,1,0:T(8,128)(2,1)} %param.7), kind=kLoop, calls=%fused_computation.1 | loop fusion | flops 1835008 | bytes 1048832 | tf_op jit(solution)/shard_map/reduce_sum | solution.py:114
  3.9 4.6 %collective-permute-start = (bf16[4,64,64]{2,1,0:T(8,128)(2,1)S(1)}, bf16[4,64,64]{2,1,0:T(8,128)(2,1)S(1)}, u32[]{:S(2)}, u32[]{:S(2)}) collective-permute-start(bf16[4,64,64]{2,1,0:T(8,128)(2,1)S(1)} %get-tuple-element.13), channel_id=1, source_target_pairs={{0,9},{1,10},{2,11},{3,12},{4,13},{5,14},{6,15},{8,17},{9,18},{10,... | collective-permute-start | bytes 98312 | tf_op jit(solution)/shard_map/ppermute | solution.py:28
  8.5 1.9 collective-permute-start.5
  10.5 5.4 %collective-permute-start.2 = (bf16[4,64,64]{2,1,0:T(8,128)(2,1)S(1)}, bf16[4,64,64]{2,1,0:T(8,128)(2,1)S(1)}, u32[]{:S(2)}, u32[]{:S(2)}) collective-permute-start(bf16[4,64,64]{2,1,0:T(8,128)(2,1)S(1)} %get-tuple-element.16), channel_id=1, source_target_pairs={{1,8},{2,9},{3,10},{4,11},{5,12},{6,13},{7,14},{9,16},{10,17},{11,... | collective-permute-start | bytes 98312 | tf_op jit(solution)/shard_map/ppermute | solution.py:28
  15.9 1.9 collective-permute-start.1
  17.9 2.4 %collective-permute-start.6 = (bf16[4,4,64,64]{3,2,1,0:T(8,128)(2,1)S(1)}, bf16[4,4,64,64]{3,2,1,0:T(8,128)(2,1)S(1)}, u32[]{:S(2)}, u32[]{:S(2)}) collective-permute-start(bf16[4,4,64,64]{3,2,1,0:T(8,128)(2,1)S(1)} %get-tuple-element.18), channel_id=1, source_target_pairs={{8,0},{16,8},{24,16},{9,1},{17,9},{25,17},{10,2},{18,10},{26,18},{... | collective-permute-start | bytes 393224 | tf_op jit(solution)/shard_map/ppermute | solution.py:18
  24.9 1.9 collective-permute-start.7
  26.8 2.6 %collective-permute-start.3 = (bf16[4,4,64,64]{3,2,1,0:T(8,128)(2,1)S(1)}, bf16[4,4,64,64]{3,2,1,0:T(8,128)(2,1)S(1)}, u32[]{:S(2)}, u32[]{:S(2)}) collective-permute-start(bf16[4,4,64,64]{3,2,1,0:T(8,128)(2,1)S(1)} %get-tuple-element.19), channel_id=1, source_target_pairs={{0,1},{1,2},{2,3},{3,4},{4,5},{5,6},{6,7},{8,9},{9,10},{10,11},{11... | collective-permute-start | bytes 393224 | tf_op jit(solution)/shard_map/ppermute | solution.py:21
  29.5 3.6 %collective-permute-start.4 = (bf16[4,4,64,64]{3,2,1,0:T(8,128)(2,1)S(1)}, bf16[4,4,64,64]{3,2,1,0:T(8,128)(2,1)S(1)}, u32[]{:S(2)}, u32[]{:S(2)}) collective-permute-start(bf16[4,4,64,64]{3,2,1,0:T(8,128)(2,1)S(1)} %get-tuple-element.20), channel_id=1, source_target_pairs={{1,0},{2,1},{3,2},{4,3},{5,4},{6,5},{7,6},{9,8},{10,9},{11,10},{12... | collective-permute-start | bytes 393224 | tf_op jit(solution)/shard_map/ppermute | solution.py:21
  33.3 7.7 %collective-permute-done.3 = bf16[4,4,64,64]{3,2,1,0:T(8,128)(2,1)S(1)} collective-permute-done((bf16[4,4,64,64]{3,2,1,0:T(8,128)(2,1)S(1)}, bf16[4,4,64,64]{3,2,1,0:T(8,128)(2,1)S(1)}, u32[]{:S(2)}, u32[]{:S(2)}) %collective-permute-start.3) | collective-permute-done | bytes 131104 | tf_op jit(solution)/shard_map/ppermute | solution.py:21
  41.0 1.9 collective-permute-done.4
  42.9 1.8 pad_maximum_fusion.1
  44.6 77.3 %shard_map.55 = bf16[16,9,64,64]{3,2,1,0:T(8,128)(2,1)} custom-call(s32[144]{0:T(256)} %reshape.636.near_ref, s32[576]{0:T(1024)} %and_select_fusion.1.slot_ref, bf16[16,9,64,64]{3,2,1,0:T(8,128)(2,1)} %bitcast.76, bf16[36,4,64,64]{3,2,1,0:T(8,128)(2,1)} %bitcast.75), custom_call_target="tpu_custom_call" | custom-call | tf_op jit(solution)/shard_map/pallas_call | solution.py:132
  121.9 2.5 %fusion.15 = (bf16[4,9,64,64]{3,2,1,0:T(8,128)(2,1)}, bf16[4,9,64,64]{3,2,1,0:T(8,128)(2,1)}) fusion(bf16[16,9,64,64]{3,2,1,0:T(8,128)(2,1)} %shard_map.55), kind=kLoop, calls=%fused_computation.123 | loop fusion | bytes 1179648 | tf_op jit(solution)/shard_map/slice | solution.py:32
  124.4 0.8 slice_bitcast_fusion.9
  125.2 4.4 %collective-permute-start.8 = (bf16[9,64,64]{2,1,0:T(8,128)(2,1)S(1)}, bf16[9,64,64]{2,1,0:T(8,128)(2,1)}, u32[]{:S(2)}, u32[]{:S(2)}) collective-permute-start(bf16[9,64,64]{2,1,0:T(8,128)(2,1)S(1)} %get-tuple-element.5), channel_id=1, source_target_pairs={{0,9},{1,10},{2,11},{3,12},{4,13},{5,14},{6,15},{8,17},{9,18},{10,... | collective-permute-start | bytes 221192 | tf_op jit(solution)/shard_map/ppermute | solution.py:28
  129.7 1.9 collective-permute-start.9
  131.6 1.1 slice_bitcast_fusion.1
  132.7 3.9 %collective-permute-start.10 = (bf16[9,64,64]{2,1,0:T(8,128)(2,1)}, bf16[9,64,64]{2,1,0:T(8,128)(2,1)}, u32[]{:S(2)}, u32[]{:S(2)}) collective-permute-start(bf16[9,64,64]{2,1,0:T(8,128)(2,1)} %get-tuple-element.8), channel_id=1, source_target_pairs={{1,8},{2,9},{3,10},{4,11},{5,12},{6,13},{7,14},{9,16},{10,17},{11,... | collective-permute-start | bytes 221192 | tf_op jit(solution)/shard_map/ppermute | solution.py:28
  136.6 2.3 %collective-permute-start.11 = (bf16[4,9,64,64]{3,2,1,0:T(8,128)(2,1)}, bf16[4,9,64,64]{3,2,1,0:T(8,128)(2,1)}, u32[]{:S(2)}, u32[]{:S(2)}) collective-permute-start(bf16[4,9,64,64]{3,2,1,0:T(8,128)(2,1)} %get-tuple-element.11), channel_id=1, source_target_pairs={{0,1},{1,2},{2,3},{3,4},{4,5},{5,6},{6,7},{8,9},{9,10},{10,11},{11... | collective-permute-start | bytes 884744 | tf_op jit(solution)/shard_map/ppermute | solution.py:21
  138.9 3.9 %collective-permute-start.12 = (bf16[4,9,64,64]{3,2,1,0:T(8,128)(2,1)}, bf16[4,9,64,64]{3,2,1,0:T(8,128)(2,1)}, u32[]{:S(2)}, u32[]{:S(2)}) collective-permute-start(bf16[4,9,64,64]{3,2,1,0:T(8,128)(2,1)} %get-tuple-element.12), channel_id=1, source_target_pairs={{1,0},{2,1},{3,2},{4,3},{5,4},{6,5},{7,6},{9,8},{10,9},{11,10},{12... | collective-permute-start | bytes 884744 | tf_op jit(solution)/shard_map/ppermute | solution.py:21
  142.8 3.8 %collective-permute-start.14 = (bf16[4,9,64,64]{3,2,1,0:T(8,128)(2,1)}, bf16[4,9,64,64]{3,2,1,0:T(8,128)(2,1)}, u32[]{:S(2)}, u32[]{:S(2)}) collective-permute-start(bf16[4,9,64,64]{3,2,1,0:T(8,128)(2,1)} %get-tuple-element.10), channel_id=1, source_target_pairs={{8,0},{16,8},{24,16},{9,1},{17,9},{25,17},{10,2},{18,10},{26,18},{... | collective-permute-start | bytes 884744 | tf_op jit(solution)/shard_map/ppermute | solution.py:18
  146.6 1.8 fusion.16
  148.4 4.3 %copy.39 = bf16[6,6,4,64,64]{4,3,2,1,0:T(8,128)(2,1)} copy(bf16[6,6,4,64,64]{3,4,2,1,0:T(8,128)(2,1)} %fusion.16) | data formatting | bytes 2359296 | tf_op jit(solution)/shard_map/transpose | solution.py:172
  152.7 1.9 collective-permute-start.13
  154.6 1.9 collective-permute-start.15
  156.6 1.4 maximum_bitcast_fusion
  157.9 14.6 %collective-permute-done.13 = bf16[9,64,64]{2,1,0:T(8,128)(2,1)S(1)} collective-permute-done((bf16[9,64,64]{2,1,0:T(8,128)(2,1)S(1)}, bf16[9,64,64]{2,1,0:T(8,128)(2,1)S(1)}, u32[]{:S(2)}, u32[]{:S(2)}) %collective-permute-start.13) | collective-permute-done | bytes 73760 | tf_op jit(solution)/shard_map/ppermute | solution.py:28
  172.5 1.3 maximum_bitcast_fusion.1
  173.8 4.8 %pad_maximum_fusion = bf16[6,6,9,64,64]{4,3,2,1,0:T(8,128)(2,1)} fusion(bf16[1,6,9,64,64]{4,3,2,1,0:T(8,128)(2,1)S(1)} %maximum_bitcast_fusion.1, bf16[4,1,9,64,64]{4,3,2,1,0:T(8,128)(2,1)} %bitcast.31, bf16[4,4,9,64,64]{4,3,2,1,0:T(8,128)(2,1)S(1)} %bitcast.72, bf16[4,1,9,64,64]{4,3,2,1,0:T(8,128)(2,1)} %bitcast.29, ...), kind=kLoop, calls=%fused_computation | loop fusion | flops 5308416 | bytes 5308416 | tf_op jit(solution)/shard_map/concatenate | solution.py:43
  178.7 18.5 %shard_map.56 = bf16[4,25,64,64]{3,2,1,0:T(8,128)(2,1)} custom-call(s32[144]{0:T(256)} %select_n.253.target_ref, s32[100]{0:T(128)} %reshape.635.pick_ref, bf16[36,9,64,64]{3,2,1,0:T(8,128)(2,1)} %bitcast.73, bf16[36,4,64,64]{3,2,1,0:T(8,128)(2,1)} %bitcast.74), custom_call_target="tpu_custom_call" | custom-call | tf_op jit(solution)/shard_map/pallas_call | solution.py:174
  (79 shorter events, 4.7 us)
Async XLA Ops:
  1.1 20.4 %copy-start.10 = (s32[4,4,9]{2,1,0:T(4,128)S(1)}, s32[4,4,9]{2,1,0:T(4,128)}, u32[]{:S(2)}) copy-start(s32[4,4,9]{2,1,0:T(4,128)} %param.6) | copy-start | bytes 1732
  3.8 19.0 %copy-start.11 = (s32[2,2,25]{2,1,0:T(2,128)S(1)}, s32[2,2,25]{2,1,0:T(2,128)}, u32[]{:S(2)}) copy-start(s32[2,2,25]{2,1,0:T(2,128)} %param.9) | copy-start | bytes 1204
  3.9 21.0 %collective-permute-start = (bf16[4,64,64]{2,1,0:T(8,128)(2,1)S(1)}, bf16[4,64,64]{2,1,0:T(8,128)(2,1)S(1)}, u32[]{:S(2)}, u32[]{:S(2)}) collective-permute-start(bf16[4,64,64]{2,1,0:T(8,128)(2,1)S(1)} %get-tuple-element.13), channel_id=1, source_target_pairs={{0,9},{1,10},{2,11},{3,12},{4,13},{5,14},{6,15},{8,17},{9,18},{10,... | collective-permute-start | bytes 98312 | tf_op jit(solution)/shard_map/ppermute | solution.py:28
  8.5 24.6 %collective-permute-start.5 = (bf16[4,64,64]{2,1,0:T(8,128)(2,1)S(1)}, bf16[4,64,64]{2,1,0:T(8,128)(2,1)S(1)}, u32[]{:S(2)}, u32[]{:S(2)}) collective-permute-start(bf16[4,64,64]{2,1,0:T(8,128)(2,1)S(1)} %get-tuple-element.14), channel_id=1, source_target_pairs={{8,1},{9,2},{10,3},{11,4},{12,5},{13,6},{14,7},{16,9},{17,10},{18,... | collective-permute-start | bytes 98312 | tf_op jit(solution)/shard_map/ppermute | solution.py:28
  10.5 16.4 %collective-permute-start.2 = (bf16[4,64,64]{2,1,0:T(8,128)(2,1)S(1)}, bf16[4,64,64]{2,1,0:T(8,128)(2,1)S(1)}, u32[]{:S(2)}, u32[]{:S(2)}) collective-permute-start(bf16[4,64,64]{2,1,0:T(8,128)(2,1)S(1)} %get-tuple-element.16), channel_id=1, source_target_pairs={{1,8},{2,9},{3,10},{4,11},{5,12},{6,13},{7,14},{9,16},{10,17},{11,... | collective-permute-start | bytes 98312 | tf_op jit(solution)/shard_map/ppermute | solution.py:28
  15.9 13.5 %collective-permute-start.1 = (bf16[4,4,64,64]{3,2,1,0:T(8,128)(2,1)S(1)}, bf16[4,4,64,64]{3,2,1,0:T(8,128)(2,1)S(1)}, u32[]{:S(2)}, u32[]{:S(2)}) collective-permute-start(bf16[4,4,64,64]{3,2,1,0:T(8,128)(2,1)S(1)} %get-tuple-element.17), channel_id=1, source_target_pairs={{0,8},{8,16},{16,24},{1,9},{9,17},{17,25},{2,10},{10,18},{18,26},{... | collective-permute-start | bytes 393224 | tf_op jit(solution)/shard_map/ppermute | solution.py:18
  17.9 15.3 %collective-permute-start.6 = (bf16[4,4,64,64]{3,2,1,0:T(8,128)(2,1)S(1)}, bf16[4,4,64,64]{3,2,1,0:T(8,128)(2,1)S(1)}, u32[]{:S(2)}, u32[]{:S(2)}) collective-permute-start(bf16[4,4,64,64]{3,2,1,0:T(8,128)(2,1)S(1)} %get-tuple-element.18), channel_id=1, source_target_pairs={{8,0},{16,8},{24,16},{9,1},{17,9},{25,17},{10,2},{18,10},{26,18},{... | collective-permute-start | bytes 393224 | tf_op jit(solution)/shard_map/ppermute | solution.py:18
  24.9 8.3 %collective-permute-start.7 = (bf16[4,64,64]{2,1,0:T(8,128)(2,1)S(1)}, bf16[4,64,64]{2,1,0:T(8,128)(2,1)S(1)}, u32[]{:S(2)}, u32[]{:S(2)}) collective-permute-start(bf16[4,64,64]{2,1,0:T(8,128)(2,1)S(1)} %get-tuple-element.15), channel_id=1, source_target_pairs={{9,0},{10,1},{11,2},{12,3},{13,4},{14,5},{15,6},{17,8},{18,9},{19,... | collective-permute-start | bytes 98312 | tf_op jit(solution)/shard_map/ppermute | solution.py:28
  26.8 14.1 %collective-permute-start.3 = (bf16[4,4,64,64]{3,2,1,0:T(8,128)(2,1)S(1)}, bf16[4,4,64,64]{3,2,1,0:T(8,128)(2,1)S(1)}, u32[]{:S(2)}, u32[]{:S(2)}) collective-permute-start(bf16[4,4,64,64]{3,2,1,0:T(8,128)(2,1)S(1)} %get-tuple-element.19), channel_id=1, source_target_pairs={{0,1},{1,2},{2,3},{3,4},{4,5},{5,6},{6,7},{8,9},{9,10},{10,11},{11... | collective-permute-start | bytes 393224 | tf_op jit(solution)/shard_map/ppermute | solution.py:21
  29.5 13.3 %collective-permute-start.4 = (bf16[4,4,64,64]{3,2,1,0:T(8,128)(2,1)S(1)}, bf16[4,4,64,64]{3,2,1,0:T(8,128)(2,1)S(1)}, u32[]{:S(2)}, u32[]{:S(2)}) collective-permute-start(bf16[4,4,64,64]{3,2,1,0:T(8,128)(2,1)S(1)} %get-tuple-element.20), channel_id=1, source_target_pairs={{1,0},{2,1},{3,2},{4,3},{5,4},{6,5},{7,6},{9,8},{10,9},{11,10},{12... | collective-permute-start | bytes 393224 | tf_op jit(solution)/shard_map/ppermute | solution.py:21
  33.2 11.5 %copy-start.1 = (bf16[1,6,4,64,64]{4,3,2,1,0:T(8,128)(2,1)}, bf16[1,6,4,64,64]{4,3,2,1,0:T(8,128)(2,1)S(1)}, u32[]{:S(2)}) copy-start(bf16[1,6,4,64,64]{4,3,2,1,0:T(8,128)(2,1)S(1)} %maximum_bitcast_fusion.2) | copy-start | bytes 589828
  33.3 11.3 %copy-start.3 = (bf16[1,6,4,64,64]{4,3,2,1,0:T(8,128)(2,1)}, bf16[1,6,4,64,64]{4,3,2,1,0:T(8,128)(2,1)S(1)}, u32[]{:S(2)}) copy-start(bf16[1,6,4,64,64]{4,3,2,1,0:T(8,128)(2,1)S(1)} %maximum_bitcast_fusion.3) | copy-start | bytes 589828
  41.0 3.7 %copy-start.5 = (bf16[4,4,64,64]{3,2,1,0:T(8,128)(2,1)}, bf16[4,4,64,64]{3,2,1,0:T(8,128)(2,1)S(1)}, u32[]{:S(2)}) copy-start(bf16[4,4,64,64]{3,2,1,0:T(8,128)(2,1)S(1)} %collective-permute-done.3) | copy-start | bytes 393220
  42.8 1.8 copy-start.7
  121.9 2.5 %copy-start = (bf16[16,9,64,64]{3,2,1,0:T(8,128)(2,1)S(1)}, bf16[16,9,64,64]{3,2,1,0:T(8,128)(2,1)}, u32[]{:S(2)}) copy-start(bf16[16,9,64,64]{3,2,1,0:T(8,128)(2,1)} %shard_map.55) | copy-start | bytes 3538948
  124.4 22.1 %copy-start.2 = (bf16[1,6,4,64,64]{4,3,2,1,0:T(8,128)(2,1)S(1)}, bf16[1,6,4,64,64]{4,3,2,1,0:T(8,128)(2,1)}, u32[]{:S(2)}) copy-start(bf16[1,6,4,64,64]{4,3,2,1,0:T(8,128)(2,1)} %copy-done.1) | copy-start | bytes 589828
  124.4 22.1 %copy-start.4 = (bf16[1,6,4,64,64]{4,3,2,1,0:T(8,128)(2,1)S(1)}, bf16[1,6,4,64,64]{4,3,2,1,0:T(8,128)(2,1)}, u32[]{:S(2)}) copy-start(bf16[1,6,4,64,64]{4,3,2,1,0:T(8,128)(2,1)} %copy-done.3) | copy-start | bytes 589828
  124.4 22.2 %copy-start.6 = (bf16[4,4,64,64]{3,2,1,0:T(8,128)(2,1)S(1)}, bf16[4,4,64,64]{3,2,1,0:T(8,128)(2,1)}, u32[]{:S(2)}) copy-start(bf16[4,4,64,64]{3,2,1,0:T(8,128)(2,1)} %copy-done.5) | copy-start | bytes 393220
  124.4 22.2 %copy-start.8 = (bf16[4,4,64,64]{3,2,1,0:T(8,128)(2,1)S(1)}, bf16[4,4,64,64]{3,2,1,0:T(8,128)(2,1)}, u32[]{:S(2)}) copy-start(bf16[4,4,64,64]{3,2,1,0:T(8,128)(2,1)} %copy-done.7) | copy-start | bytes 393220
  125.2 17.6 %collective-permute-start.8 = (bf16[9,64,64]{2,1,0:T(8,128)(2,1)S(1)}, bf16[9,64,64]{2,1,0:T(8,128)(2,1)}, u32[]{:S(2)}, u32[]{:S(2)}) collective-permute-start(bf16[9,64,64]{2,1,0:T(8,128)(2,1)S(1)} %get-tuple-element.5), channel_id=1, source_target_pairs={{0,9},{1,10},{2,11},{3,12},{4,13},{5,14},{6,15},{8,17},{9,18},{10,... | collective-permute-start | bytes 221192 | tf_op jit(solution)/shard_map/ppermute | solution.py:28
  129.7 25.0 %collective-permute-start.9 = (bf16[4,9,64,64]{3,2,1,0:T(8,128)(2,1)}, bf16[4,9,64,64]{3,2,1,0:T(8,128)(2,1)}, u32[]{:S(2)}, u32[]{:S(2)}) collective-permute-start(bf16[4,9,64,64]{3,2,1,0:T(8,128)(2,1)} %get-tuple-element.9), channel_id=1, source_target_pairs={{0,8},{8,16},{16,24},{1,9},{9,17},{17,25},{2,10},{10,18},{18,26},{... | collective-permute-start | bytes 884744 | tf_op jit(solution)/shard_map/ppermute | solution.py:18
  132.7 20.0 %collective-permute-start.10 = (bf16[9,64,64]{2,1,0:T(8,128)(2,1)}, bf16[9,64,64]{2,1,0:T(8,128)(2,1)}, u32[]{:S(2)}, u32[]{:S(2)}) collective-permute-start(bf16[9,64,64]{2,1,0:T(8,128)(2,1)} %get-tuple-element.8), channel_id=1, source_target_pairs={{1,8},{2,9},{3,10},{4,11},{5,12},{6,13},{7,14},{9,16},{10,17},{11,... | collective-permute-start | bytes 221192 | tf_op jit(solution)/shard_map/ppermute | solution.py:28
  136.6 37.2 %collective-permute-start.11 = (bf16[4,9,64,64]{3,2,1,0:T(8,128)(2,1)}, bf16[4,9,64,64]{3,2,1,0:T(8,128)(2,1)}, u32[]{:S(2)}, u32[]{:S(2)}) collective-permute-start(bf16[4,9,64,64]{3,2,1,0:T(8,128)(2,1)} %get-tuple-element.11), channel_id=1, source_target_pairs={{0,1},{1,2},{2,3},{3,4},{4,5},{5,6},{6,7},{8,9},{9,10},{10,11},{11... | collective-permute-start | bytes 884744 | tf_op jit(solution)/shard_map/ppermute | solution.py:21
  138.9 34.9 %collective-permute-start.12 = (bf16[4,9,64,64]{3,2,1,0:T(8,128)(2,1)}, bf16[4,9,64,64]{3,2,1,0:T(8,128)(2,1)}, u32[]{:S(2)}, u32[]{:S(2)}) collective-permute-start(bf16[4,9,64,64]{3,2,1,0:T(8,128)(2,1)} %get-tuple-element.12), channel_id=1, source_target_pairs={{1,0},{2,1},{3,2},{4,3},{5,4},{6,5},{7,6},{9,8},{10,9},{11,10},{12... | collective-permute-start | bytes 884744 | tf_op jit(solution)/shard_map/ppermute | solution.py:21
  142.8 29.7 %collective-permute-start.14 = (bf16[4,9,64,64]{3,2,1,0:T(8,128)(2,1)}, bf16[4,9,64,64]{3,2,1,0:T(8,128)(2,1)}, u32[]{:S(2)}, u32[]{:S(2)}) collective-permute-start(bf16[4,9,64,64]{3,2,1,0:T(8,128)(2,1)} %get-tuple-element.10), channel_id=1, source_target_pairs={{8,0},{16,8},{24,16},{9,1},{17,9},{25,17},{10,2},{18,10},{26,18},{... | collective-permute-start | bytes 884744 | tf_op jit(solution)/shard_map/ppermute | solution.py:18
  148.4 4.3 %copy-start.9 = (bf16[9,64,64]{2,1,0:T(8,128)(2,1)S(1)}, bf16[9,64,64]{2,1,0:T(8,128)(2,1)}, u32[]{:S(2)}) copy-start(bf16[9,64,64]{2,1,0:T(8,128)(2,1)} %get-tuple-element.6) | copy-start | bytes 221188
  152.7 19.8 %collective-permute-start.13 = (bf16[9,64,64]{2,1,0:T(8,128)(2,1)S(1)}, bf16[9,64,64]{2,1,0:T(8,128)(2,1)S(1)}, u32[]{:S(2)}, u32[]{:S(2)}) collective-permute-start(bf16[9,64,64]{2,1,0:T(8,128)(2,1)S(1)} %copy-done.9), channel_id=1, source_target_pairs={{8,1},{9,2},{10,3},{11,4},{12,5},{13,6},{14,7},{16,9},{17,10},{18,... | collective-permute-start | bytes 221192 | tf_op jit(solution)/shard_map/ppermute | solution.py:28
  154.6 17.9 %collective-permute-start.15 = (bf16[9,64,64]{2,1,0:T(8,128)(2,1)S(1)}, bf16[9,64,64]{2,1,0:T(8,128)(2,1)S(1)}, u32[]{:S(2)}, u32[]{:S(2)}) collective-permute-start(bf16[9,64,64]{2,1,0:T(8,128)(2,1)S(1)} %get-tuple-element.7), channel_id=1, source_target_pairs={{9,0},{10,1},{11,2},{12,3},{13,4},{14,5},{15,6},{17,8},{18,9},{19,... | collective-permute-start | bytes 221192 | tf_op jit(solution)/shard_map/ppermute | solution.py:28

commit v2 on v1

--- a/solution.py
+++ b/solution.py
@@ -53,10 +53,9 @@
             a = a_ref[t, k]
             for q in range(4):
                 e = slot_ref[(t * terms + k) * 4 + q]
-
-                @pl.when(e >= 0)
-                def _():
-                    acc_ref[e] += jnp.dot(a, p_ref[j, q], preferred_element_type=jnp.float32)
+                keep = jnp.where(e >= 0, 1.0, 0.0).astype(jnp.float32)
+                prod = jnp.dot(a, p_ref[j, q], preferred_element_type=jnp.float32)
+                acc_ref[jnp.clip(e, 0, 8)] += prod * keep
 
         out_ref[t] = acc_ref[...].astype(out_ref.dtype)
         return carry
@@ -64,18 +63,15 @@
     lax.fori_loop(0, tiles, one_tile, 0)
 
 
-def coarse_kernel(target_ref, pick_ref, ap_ref, pt_ref, out_ref, acc_ref):
-    tiles = ap_ref.shape[0]
-    owned, stencil = out_ref.shape[0], out_ref.shape[1]
-    acc_ref[...] = jnp.zeros(acc_ref.shape, jnp.float32)
-
+def add_terms(where_ref, target_ref, ap_ref, pt_ref, acc_ref):
     def one_tile(t, carry):
+        w = where_ref[t]
         for q in range(4):
             g = target_ref[t * 4 + q]
 
             @pl.when(g >= 0)
             def _():
-                pt = pt_ref[t, q]
+                pt = pt_ref[w * 4 + q]
                 for e in range(9):
                     acc_ref[g + (e // 3) * 5 + e % 3] += jnp.dot(
                         pt, ap_ref[t, e], preferred_element_type=jnp.float32
@@ -83,15 +79,29 @@
 
         return carry
 
-    lax.fori_loop(0, tiles, one_tile, 0)
+    lax.fori_loop(0, ap_ref.shape[0], one_tile, 0)
+
+
+def own_kernel(where_ref, target_ref, ap_ref, pt_ref, acc_ref):
+    acc_ref[...] = jnp.zeros(acc_ref.shape, jnp.float32)
+    add_terms(where_ref, target_ref, ap_ref, pt_ref, acc_ref)
+
+
+def ring_kernel(where_ref, target_ref, pick_ref, ap_ref, pt_ref, part_ref, out_ref, acc_ref):
+    acc_ref[...] = part_ref[...]
+    add_terms(where_ref, target_ref, ap_ref, pt_ref, acc_ref)
+    owned, stencil = out_ref.shape[0], out_ref.shape[1]
 
     def one_pick(i, carry):
         a = i // stencil
-        s = i % stencil
-        out_ref[a, s] = acc_ref[a * stencil + pick_ref[i]].astype(out_ref.dtype)
+        out_ref[a, i % stencil] = acc_ref[a * stencil + pick_ref[i]].astype(out_ref.dtype)
         return carry
 
     lax.fori_loop(0, owned * stencil, one_pick, 0)
+
+
+def ring_of(x):
+    return jnp.concatenate([x[0], x[-1], x[1:-1, 0], x[1:-1, -1]], axis=0)
 
 
 def body(a_blocks, a_cols, p_blocks, p_cols, c_cols):
@@ -146,7 +156,8 @@
         a_blocks.reshape(n_r * n_c, terms, bs, bs),
         p_ext.reshape(ext_r * ext_c, 4, bs, bs),
     )
-    ap_ext = with_halo(ap.reshape(n_r, n_c, 9, bs, bs))
+    ap = ap.reshape(n_r, n_c, 9, bs, bs)
+    ap_ext = with_halo(ap)
 
     o_r, o_c = n_r // 2, n_c // 2
     ey = y0 - 1 + jnp.arange(ext_r, dtype=jnp.int32)
@@ -162,27 +173,50 @@
     target = (own_y[:, None, :, None] * o_c + own_x[None, :, None, :]) * 25 + (
         off_y[:, None, :, None] * 5 + off_x[None, :, None, :]
     )
-    target = jnp.where(ok_y[:, None, :, None] & ok_x[None, :, None, :], target, -1).reshape(-1)
+    target = jnp.where(ok_y[:, None, :, None] & ok_x[None, :, None, :], target, -1).reshape(ext_r, ext_c, 4)
+    place = jnp.arange(ext_r * ext_c, dtype=jnp.int32).reshape(ext_r, ext_c)
 
     cy = ys[0] // 2 + jnp.arange(o_r, dtype=jnp.int32)
     cx = xs[0] // 2 + jnp.arange(o_c, dtype=jnp.int32)
     pick = (c_cols // coarse_cols - cy[:, None, None] + 2) * 5 + (c_cols % coarse_cols - cx[None, :, None] + 2)
     pick = jnp.clip(pick, 0, 24).reshape(-1)
 
-    p_t = jnp.swapaxes(p_ext, -1, -2).reshape(ext_r * ext_c, 4, bs, bs)
+    p_t = jnp.swapaxes(p_ext, -1, -2).reshape(ext_r * ext_c * 4, bs, bs)
     stencil = c_cols.shape[-1]
+    acc_shape = jax.ShapeDtypeStruct((o_r * o_c * 25, bs, bs), jnp.float32)
+    dot_cost = 2 * bs * bs * bs * 9
+    part = pl.pallas_call(
+        own_kernel,
+        out_shape=acc_shape,
+        in_specs=[pl.BlockSpec(memory_space=pltpu.SMEM)] * 2 + [pl.BlockSpec(memory_space=pltpu.VMEM)] * 2,
+        out_specs=pl.BlockSpec(memory_space=pltpu.VMEM),
+        cost_estimate=pl.CostEstimate(
+            flops=dot_cost * n_r * n_c * 4, bytes_accessed=4 * 1024 * 1024, transcendentals=0
+        ),
+    )(
+        place[1:-1, 1:-1].reshape(-1),
+        target[1:-1, 1:-1].reshape(-1),
+        ap.reshape(n_r * n_c, 9, bs, bs),
+        p_t,
+    )
+    ring_tiles = 2 * ext_c + 2 * n_r
     out = pl.pallas_call(
-        coarse_kernel,
+        ring_kernel,
         out_shape=jax.ShapeDtypeStruct((o_r * o_c, stencil, bs, bs), jnp.bfloat16),
-        in_specs=[
-            pl.BlockSpec(memory_space=pltpu.SMEM),
-            pl.BlockSpec(memory_space=pltpu.SMEM),
-            pl.BlockSpec(memory_space=pltpu.VMEM),
-            pl.BlockSpec(memory_space=pltpu.VMEM),
-        ],
+        in_specs=[pl.BlockSpec(memory_space=pltpu.SMEM)] * 3 + [pl.BlockSpec(memory_space=pltpu.VMEM)] * 3,
         out_specs=pl.BlockSpec(memory_space=pltpu.VMEM),
-        scratch_shapes=[pltpu.VMEM((o_r * o_c * 25, bs, bs), jnp.float32)],
-    )(target, pick, ap_ext.reshape(ext_r * ext_c, 9, bs, bs), p_t)
+        scratch_shapes=[pltpu.VMEM(acc_shape.shape, jnp.float32)],
+        cost_estimate=pl.CostEstimate(
+            flops=dot_cost * ring_tiles * 4, bytes_accessed=5 * 1024 * 1024, transcendentals=0
+        ),
+    )(
+        ring_of(place),
+        ring_of(target).reshape(-1),
+        pick,
+        ring_of(ap_ext),
+        p_t,
+        part,
+    )
     return out.reshape(o_r, o_c, stencil, bs, bs)
 
 

time: 199 us -> 149 us (0.75)
  Pallas kernels: 95.8 us -> 33 us
  local copies, waits for them, and re-layouts: 11.7 us -> 19.8 us
  waiting for transfers between devices: 24.2 us -> 31.3 us
  other arithmetic: 16.2 us -> 13.2 us
    pallas_call x1, Pallas kernels: 77.3 us -> 10 us  [body(): pl.pallas_call(ap_kernel, out_shape=jax.ShapeDtypeStruct((n_r * n_c, 9, b...]
    ppermute x4, waiting for transfers between devices: 9.54 us -> 31.3 us  [shifted(): return lax.ppermute(piece, 'col', pairs)]
    ppermute x8, waiting for transfers between devices: 14.6 us -> 0.02 us  [shifted(): return lax.ppermute(piece, ('row', 'col'), pairs)]
    unnamed x24 -> x29, local copies, waits for them, and re-layouts: 0.05 us -> 5.76 us
    concatenate x2 -> x1, other arithmetic: 6.6 us -> 1.78 us  [with_halo(): return jnp.concatenate([first[None], middle, last[None]], axis=0)]
    pallas_call x1 -> x2, Pallas kernels: 18.5 us -> 23 us  [the longest x1 12 us: body(): pl.pallas_call(ring_kernel, out_shape=jax.ShapeDtypeStruct((o_r * o_c, st...]
    squeeze x0 -> x5, local copies, waits for them, and re-layouts: none -> 3.88 us  [the longest x1 1.96 us: with_halo(): bottom_right = shifted(x[0, 0], -1, -1)]
    broadcast_in_dim x4 -> x2, other arithmetic: 2.82 us -> 0.18 us  [with_halo(): return jnp.concatenate([first[None], middle, last[None]], axis=0)]
  transfers between devices with their start and end apart: 16 -> 16, of which waited for: 3 -> 4; matrix products, arithmetic and copies ran while one was open for 7% -> 14% of each run, Pallas kernels for 0% -> 7%
where the time goes in v2:
time: 149 us; the launch traced here: 146 us
  starting transfers between devices  47.9 us (32%)
  Pallas kernels  33 us (22%)
  waiting for transfers between devices  31.3 us (21%)
  local copies, waits for them, and re-layouts  19.8 us (13%)
  other arithmetic  13.2 us (9%)
    ppermute x4, waiting for transfers between devices, shifted(): return lax.ppermute(piece, 'col', pairs)  31.3 us
    ppermute x8, starting transfers between devices, shifted(): return lax.ppermute(piece, ('row', 'col'), pairs)  26.9 us
    ppermute x4, starting transfers between devices, shifted(): return lax.ppermute(piece, 'col', pairs)  12.4 us
    pallas_call x1, Pallas kernels, body(): pl.pallas_call(ring_kernel, out_shape=jax.ShapeDtypeStruct((o_r * o_c, st...  12 us
    pallas_call x1, Pallas kernels, body(): pl.pallas_call(own_kernel, out_shape=acc_shape, in_specs=[pl.BlockSpec(me...  11 us
    pallas_call x1, Pallas kernels, body(): pl.pallas_call(ap_kernel, out_shape=jax.ShapeDtypeStruct((n_r * n_c, 9, b...  10 us
    ppermute x4, starting transfers between devices, shifted(): return lax.ppermute(piece, 'row', pairs)  8.61 us
    unnamed x29, local copies, waits for them, and re-layouts  5.76 us
  transfers between devices with their start and end apart: 16, of which 4 were waited for; matrix products, arithmetic and copies ran while one was open for 14% of the time, Pallas kernels for 7%

profile of v2, /device:TPU:9, one launch (start us, length us, event | category | flops | bytes accessed | tf_op | source)
XLA Modules:
  0.0 146.1 jit_solution(8001767877046198317)
XLA Ops:
  1.1 2.8 %select_reduce_fusion = bf16[4,4,4,64,64]{4,3,2,1,0:T(8,128)(2,1)S(1)} fusion(pred[4,4,4,4]{3,2,1,0:T(4,128)(4,1)S(1)} %broadcast_compare_fusion, bf16[4,4,4,64,64]{4,3,2,1,0:T(8,128)(2,1)} %param.7), kind=kLoop, calls=%fused_computation | loop fusion | flops 1835008 | bytes 1048832 | tf_op jit(solution)/shard_map/reduce_sum | solution.py:124
  3.9 4.6 %collective-permute-start = (bf16[4,64,64]{2,1,0:T(8,128)(2,1)S(1)}, bf16[4,64,64]{2,1,0:T(8,128)(2,1)S(1)}, u32[]{:S(2)}, u32[]{:S(2)}) collective-permute-start(bf16[4,64,64]{2,1,0:T(8,128)(2,1)S(1)} %get-tuple-element.15), channel_id=1, source_target_pairs={{0,9},{1,10},{2,11},{3,12},{4,13},{5,14},{6,15},{8,17},{9,18},{10,... | collective-permute-start | bytes 98312 | tf_op jit(solution)/shard_map/ppermute | solution.py:28
  8.5 2.8 %collective-permute-start.2 = (bf16[4,64,64]{2,1,0:T(8,128)(2,1)S(1)}, bf16[4,64,64]{2,1,0:T(8,128)(2,1)S(1)}, u32[]{:S(2)}, u32[]{:S(2)}) collective-permute-start(bf16[4,64,64]{2,1,0:T(8,128)(2,1)S(1)} %get-tuple-element.18), channel_id=1, source_target_pairs={{1,8},{2,9},{3,10},{4,11},{5,12},{6,13},{7,14},{9,16},{10,17},{11,... | collective-permute-start | bytes 98312 | tf_op jit(solution)/shard_map/ppermute | solution.py:28
  11.3 1.9 %collective-permute-start.1 = (bf16[4,4,64,64]{3,2,1,0:T(8,128)(2,1)S(1)}, bf16[4,4,64,64]{3,2,1,0:T(8,128)(2,1)S(1)}, u32[]{:S(2)}, u32[]{:S(2)}) collective-permute-start(bf16[4,4,64,64]{3,2,1,0:T(8,128)(2,1)S(1)} %get-tuple-element.19), channel_id=1, source_target_pairs={{0,8},{8,16},{16,24},{1,9},{9,17},{17,25},{2,10},{10,18},{18,26},{... | collective-permute-start | bytes 393224 | tf_op jit(solution)/shard_map/ppermute | solution.py:18
  13.2 2.7 %collective-permute-start.5 = (bf16[4,64,64]{2,1,0:T(8,128)(2,1)S(1)}, bf16[4,64,64]{2,1,0:T(8,128)(2,1)S(1)}, u32[]{:S(2)}, u32[]{:S(2)}) collective-permute-start(bf16[4,64,64]{2,1,0:T(8,128)(2,1)S(1)} %get-tuple-element.16), channel_id=1, source_target_pairs={{8,1},{9,2},{10,3},{11,4},{12,5},{13,6},{14,7},{16,9},{17,10},{18,... | collective-permute-start | bytes 98312 | tf_op jit(solution)/shard_map/ppermute | solution.py:28
  16.0 1.9 %collective-permute-start.6 = (bf16[4,4,64,64]{3,2,1,0:T(8,128)(2,1)S(1)}, bf16[4,4,64,64]{3,2,1,0:T(8,128)(2,1)S(1)}, u32[]{:S(2)}, u32[]{:S(2)}) collective-permute-start(bf16[4,4,64,64]{3,2,1,0:T(8,128)(2,1)S(1)} %get-tuple-element.20), channel_id=1, source_target_pairs={{8,0},{16,8},{24,16},{9,1},{17,9},{25,17},{10,2},{18,10},{26,18},{... | collective-permute-start | bytes 393224 | tf_op jit(solution)/shard_map/ppermute | solution.py:18
  26.1 1.2 pad_add_fusion.1.where_ref
  30.9 1.9 %collective-permute-start.7 = (bf16[4,64,64]{2,1,0:T(8,128)(2,1)S(1)}, bf16[4,64,64]{2,1,0:T(8,128)(2,1)S(1)}, u32[]{:S(2)}, u32[]{:S(2)}) collective-permute-start(bf16[4,64,64]{2,1,0:T(8,128)(2,1)S(1)} %get-tuple-element.17), channel_id=1, source_target_pairs={{9,0},{10,1},{11,2},{12,3},{13,4},{14,5},{15,6},{17,8},{18,9},{19,... | collective-permute-start | bytes 98312 | tf_op jit(solution)/shard_map/ppermute | solution.py:28
  32.8 4.0 %collective-permute-start.3 = (bf16[4,4,64,64]{3,2,1,0:T(8,128)(2,1)S(1)}, bf16[4,4,64,64]{3,2,1,0:T(8,128)(2,1)S(1)}, u32[]{:S(2)}, u32[]{:S(2)}) collective-permute-start(bf16[4,4,64,64]{3,2,1,0:T(8,128)(2,1)S(1)} %get-tuple-element.21), channel_id=1, source_target_pairs={{0,1},{1,2},{2,3},{3,4},{4,5},{5,6},{6,7},{8,9},{9,10},{10,11},{11... | collective-permute-start | bytes 393224 | tf_op jit(solution)/shard_map/ppermute | solution.py:21
  36.8 2.2 %collective-permute-start.4 = (bf16[4,4,64,64]{3,2,1,0:T(8,128)(2,1)S(1)}, bf16[4,4,64,64]{3,2,1,0:T(8,128)(2,1)S(1)}, u32[]{:S(2)}, u32[]{:S(2)}) collective-permute-start(bf16[4,4,64,64]{3,2,1,0:T(8,128)(2,1)S(1)} %get-tuple-element.22), channel_id=1, source_target_pairs={{1,0},{2,1},{3,2},{4,3},{5,4},{6,5},{7,6},{9,8},{10,9},{11,10},{12... | collective-permute-start | bytes 393224 | tf_op jit(solution)/shard_map/ppermute | solution.py:21
  39.2 7.3 %collective-permute-done.3 = bf16[4,4,64,64]{3,2,1,0:T(8,128)(2,1)S(1)} collective-permute-done((bf16[4,4,64,64]{3,2,1,0:T(8,128)(2,1)S(1)}, bf16[4,4,64,64]{3,2,1,0:T(8,128)(2,1)S(1)}, u32[]{:S(2)}, u32[]{:S(2)}) %collective-permute-start.3) | collective-permute-done | bytes 131104 | tf_op jit(solution)/shard_map/ppermute | solution.py:21
  46.5 2.1 %collective-permute-done.4 = bf16[4,4,64,64]{3,2,1,0:T(8,128)(2,1)S(1)} collective-permute-done((bf16[4,4,64,64]{3,2,1,0:T(8,128)(2,1)S(1)}, bf16[4,4,64,64]{3,2,1,0:T(8,128)(2,1)S(1)}, u32[]{:S(2)}, u32[]{:S(2)}) %collective-permute-start.4) | collective-permute-done | bytes 131104 | tf_op jit(solution)/shard_map/ppermute | solution.py:21
  48.7 1.8 %pad_maximum_fusion = bf16[6,6,4,64,64]{4,3,2,1,0:T(8,128)(2,1)} fusion(bf16[1,6,4,64,64]{4,3,2,1,0:T(8,128)(2,1)S(1)} %maximum_bitcast_fusion.1, bf16[4,1,4,64,64]{4,3,2,1,0:T(8,128)(2,1)S(1)} %bitcast.91, bf16[4,4,4,64,64]{4,3,2,1,0:T(8,128)(2,1)S(1)} %select_reduce_fusion, bf16[4,1,4,64,64]{4,3,2,1,0:T(8,128)(2,1)S(1)} %bitcast.89, ...), kind=kLoop, calls=%fused_computation.1 | loop fusion | flops 2359296 | bytes 2359296 | tf_op jit(solution)/shard_map/concatenate | solution.py:43
  50.5 10.0 %shard_map.55.ap_ref = bf16[16,9,64,64]{3,2,1,0:T(8,128)(2,1)} custom-call(s32[144]{0:T(256)} %reshape.665.near_ref, s32[576]{0:T(1024)} %and_select_fusion.1.slot_ref, bf16[16,9,64,64]{3,2,1,0:T(8,128)(2,1)} %bitcast.88, bf16[36,4,64,64]{3,2,1,0:T(8,128)(2,1)} %bitcast.87), custom_call_target="tpu_custom_call" | custom-call | tf_op jit(solution)/shard_map/pallas_call | solution.py:142
  60.5 2.5 %fusion.15 = (bf16[4,9,64,64]{3,2,1,0:T(8,128)(2,1)}, bf16[4,9,64,64]{3,2,1,0:T(8,128)(2,1)}) fusion(bf16[16,9,64,64]{3,2,1,0:T(8,128)(2,1)} %shard_map.55.ap_ref), kind=kLoop, calls=%fused_computation.136 | loop fusion | bytes 1179648 | tf_op jit(solution)/shard_map/slice | solution.py:33
  63.0 2.0 %slice_bitcast_fusion.6 = (bf16[9,64,64]{2,1,0:T(8,128)(2,1)}, bf16[9,64,64]{2,1,0:T(8,128)(2,1)}, bf16[9,64,64]{2,1,0:T(8,128)(2,1)}, bf16[9,64,64]{2,1,0:T(8,128)(2,1)}) fusion(bf16[4,4,9,64,64]{4,3,2,1,0:T(8,128)(2,1)} %bitcast.83), kind=kLoop, calls=%fused_computation.14 | loop fusion | bytes 589824 | tf_op jit(solution)/shard_map/squeeze | solution.py:39
  65.0 1.2 slice_bitcast_fusion
  66.1 5.8 %collective-permute-start.8 = (bf16[9,64,64]{2,1,0:T(8,128)(2,1)}, bf16[9,64,64]{2,1,0:T(8,128)(2,1)}, u32[]{:S(2)}, u32[]{:S(2)}) collective-permute-start(bf16[9,64,64]{2,1,0:T(8,128)(2,1)} %get-tuple-element.12), channel_id=1, source_target_pairs={{0,9},{1,10},{2,11},{3,12},{4,13},{5,14},{6,15},{8,17},{9,18},{10,... | collective-permute-start | bytes 221192 | tf_op jit(solution)/shard_map/ppermute | solution.py:28
  71.9 2.9 %collective-permute-start.9 = (bf16[4,9,64,64]{3,2,1,0:T(8,128)(2,1)}, bf16[4,9,64,64]{3,2,1,0:T(8,128)(2,1)}, u32[]{:S(2)}, u32[]{:S(2)}) collective-permute-start(bf16[4,9,64,64]{3,2,1,0:T(8,128)(2,1)} %get-tuple-element.14), channel_id=1, source_target_pairs={{0,8},{8,16},{16,24},{1,9},{9,17},{17,25},{2,10},{10,18},{18,26},{... | collective-permute-start | bytes 884744 | tf_op jit(solution)/shard_map/ppermute | solution.py:18
  75.5 4.0 %collective-permute-start.10 = (bf16[9,64,64]{2,1,0:T(8,128)(2,1)}, bf16[9,64,64]{2,1,0:T(8,128)(2,1)}, u32[]{:S(2)}, u32[]{:S(2)}) collective-permute-start(bf16[9,64,64]{2,1,0:T(8,128)(2,1)} %get-tuple-element.11), channel_id=1, source_target_pairs={{1,8},{2,9},{3,10},{4,11},{5,12},{6,13},{7,14},{9,16},{10,17},{11,... | collective-permute-start | bytes 221192 | tf_op jit(solution)/shard_map/ppermute | solution.py:28
  79.5 3.3 %collective-permute-start.11 = (bf16[9,64,64]{2,1,0:T(8,128)(2,1)}, bf16[9,64,64]{2,1,0:T(8,128)(2,1)}, u32[]{:S(2)}, u32[]{:S(2)}) collective-permute-start(bf16[9,64,64]{2,1,0:T(8,128)(2,1)} %get-tuple-element.10), channel_id=1, source_target_pairs={{8,1},{9,2},{10,3},{11,4},{12,5},{13,6},{14,7},{16,9},{17,10},{18,... | collective-permute-start | bytes 221192 | tf_op jit(solution)/shard_map/ppermute | solution.py:28
  82.8 1.9 %collective-permute-start.12 = (bf16[4,9,64,64]{3,2,1,0:T(8,128)(2,1)}, bf16[4,9,64,64]{3,2,1,0:T(8,128)(2,1)S(1)}, u32[]{:S(2)}, u32[]{:S(2)}) collective-permute-start(bf16[4,9,64,64]{3,2,1,0:T(8,128)(2,1)} %get-tuple-element.13), channel_id=1, source_target_pairs={{8,0},{16,8},{24,16},{9,1},{17,9},{25,17},{10,2},{18,10},{26,18},{... | collective-permute-start | bytes 884744 | tf_op jit(solution)/shard_map/ppermute | solution.py:18
  84.7 2.5 %copy.60 = bf16[6,6,4,64,64]{4,3,2,1,0:T(8,128)(2,1)} copy(bf16[6,6,4,64,64]{3,4,2,1,0:T(8,128)(2,1)S(1)} %fusion.18) | data formatting | bytes 2359296 | tf_op jit(solution)/shard_map/transpose | solution.py:184
  87.2 11.0 %shard_map.56.part_ref = f32[100,64,64]{2,1,0:T(8,128)} custom-call(s32[16]{0:T(128)} %reshape.670.where_ref, s32[64]{0:T(128)} %reshape.671.target_ref, bf16[16,9,64,64]{3,2,1,0:T(8,128)(2,1)} %shard_map.55.ap_ref, bf16[144,64,64]{2,1,0:T(8,128)(2,1)} %bitcast.85), custom_call_target="tpu_custom_call" | custom-call | flops 301989888 | bytes 4194304 | tf_op jit(solution)/shard_map/pallas_call | solution.py:188
  98.2 1.9 %collective-permute-start.13 = (bf16[9,64,64]{2,1,0:T(8,128)(2,1)}, bf16[9,64,64]{2,1,0:T(8,128)(2,1)S(1)}, u32[]{:S(2)}, u32[]{:S(2)}) collective-permute-start(bf16[9,64,64]{2,1,0:T(8,128)(2,1)} %get-tuple-element.9), channel_id=1, source_target_pairs={{9,0},{10,1},{11,2},{12,3},{13,4},{14,5},{15,6},{17,8},{18,9},{19,... | collective-permute-start | bytes 221192 | tf_op jit(solution)/shard_map/ppermute | solution.py:28
  101.0 4.2 %collective-permute-start.14 = (bf16[4,9,64,64]{3,2,1,0:T(8,128)(2,1)}, bf16[4,9,64,64]{3,2,1,0:T(8,128)(2,1)S(1)}, u32[]{:S(2)}, u32[]{:S(2)}) collective-permute-start(bf16[4,9,64,64]{3,2,1,0:T(8,128)(2,1)} %get-tuple-element.8), channel_id=1, source_target_pairs={{0,1},{1,2},{2,3},{3,4},{4,5},{5,6},{6,7},{8,9},{9,10},{10,11},{11... | collective-permute-start | bytes 884744 | tf_op jit(solution)/shard_map/ppermute | solution.py:21
  105.2 1.1 constant_dynamic-update-slice_fusion.3
  106.4 2.0 %collective-permute-start.15 = (bf16[4,9,64,64]{3,2,1,0:T(8,128)(2,1)}, bf16[4,9,64,64]{3,2,1,0:T(8,128)(2,1)S(1)}, u32[]{:S(2)}, u32[]{:S(2)}) collective-permute-start(bf16[4,9,64,64]{3,2,1,0:T(8,128)(2,1)} %get-tuple-element.7), channel_id=1, source_target_pairs={{1,0},{2,1},{3,2},{4,3},{5,4},{6,5},{7,6},{9,8},{10,9},{11,10},{12... | collective-permute-start | bytes 884744 | tf_op jit(solution)/shard_map/ppermute | solution.py:21
  110.4 20.0 %collective-permute-done.14 = bf16[4,9,64,64]{3,2,1,0:T(8,128)(2,1)S(1)} collective-permute-done((bf16[4,9,64,64]{3,2,1,0:T(8,128)(2,1)}, bf16[4,9,64,64]{3,2,1,0:T(8,128)(2,1)S(1)}, u32[]{:S(2)}, u32[]{:S(2)}) %collective-permute-start.14) | collective-permute-done | bytes 294944 | tf_op jit(solution)/shard_map/ppermute | solution.py:21
  130.4 1.9 %collective-permute-done.15 = bf16[4,9,64,64]{3,2,1,0:T(8,128)(2,1)S(1)} collective-permute-done((bf16[4,9,64,64]{3,2,1,0:T(8,128)(2,1)}, bf16[4,9,64,64]{3,2,1,0:T(8,128)(2,1)S(1)}, u32[]{:S(2)}, u32[]{:S(2)}) %collective-permute-start.15) | collective-permute-done | bytes 294944 | tf_op jit(solution)/shard_map/ppermute | solution.py:21
  132.4 1.6 %copy-done.5 = bf16[20,9,64,64]{3,2,1,0:T(8,128)(2,1)} copy-done((bf16[20,9,64,64]{3,2,1,0:T(8,128)(2,1)}, bf16[20,9,64,64]{3,2,1,0:T(8,128)(2,1)S(1)}, u32[]{:S(2)}) %copy-start.5) | copy-done | bytes 1474584
  134.0 12.0 %shard_map.57 = bf16[4,25,64,64]{3,2,1,0:T(8,128)(2,1)} custom-call(s32[20]{0:T(128)} %pad_add_fusion.1.where_ref, s32[80]{0:T(128)} %reshape.663.target_ref, s32[100]{0:T(128)} %reshape.664.pick_ref, bf16[20,9,64,64]{3,2,1,0:T(8,128)(2,1)} %copy-done.5, bf16[144,64,64]{2,1,0:T(8,128)(2,1)} %bitcast.86, f32[100,64,64]{2,1,0:T(8,128)} %shard_map.56.part_ref), custom_call_target="tpu_custom_call" | custom-call | flops 377487360 | bytes 5242880 | tf_op jit(solution)/shard_map/pallas_call | solution.py:203
  (109 shorter events, 16.4 us)
Async XLA Ops:
  0.0 20.7 %copy-start.10 = (s32[4,4,9]{2,1,0:T(4,128)S(1)}, s32[4,4,9]{2,1,0:T(4,128)}, u32[]{:S(2)}) copy-start(s32[4,4,9]{2,1,0:T(4,128)} %param.6) | copy-start | bytes 1732
  3.9 27.0 %collective-permute-start = (bf16[4,64,64]{2,1,0:T(8,128)(2,1)S(1)}, bf16[4,64,64]{2,1,0:T(8,128)(2,1)S(1)}, u32[]{:S(2)}, u32[]{:S(2)}) collective-permute-start(bf16[4,64,64]{2,1,0:T(8,128)(2,1)S(1)} %get-tuple-element.15), channel_id=1, source_target_pairs={{0,9},{1,10},{2,11},{3,12},{4,13},{5,14},{6,15},{8,17},{9,18},{10,... | collective-permute-start | bytes 98312 | tf_op jit(solution)/shard_map/ppermute | solution.py:28
  8.5 24.3 %collective-permute-start.2 = (bf16[4,64,64]{2,1,0:T(8,128)(2,1)S(1)}, bf16[4,64,64]{2,1,0:T(8,128)(2,1)S(1)}, u32[]{:S(2)}, u32[]{:S(2)}) collective-permute-start(bf16[4,64,64]{2,1,0:T(8,128)(2,1)S(1)} %get-tuple-element.18), channel_id=1, source_target_pairs={{1,8},{2,9},{3,10},{4,11},{5,12},{6,13},{7,14},{9,16},{10,17},{11,... | collective-permute-start | bytes 98312 | tf_op jit(solution)/shard_map/ppermute | solution.py:28
  11.3 25.5 %collective-permute-start.1 = (bf16[4,4,64,64]{3,2,1,0:T(8,128)(2,1)S(1)}, bf16[4,4,64,64]{3,2,1,0:T(8,128)(2,1)S(1)}, u32[]{:S(2)}, u32[]{:S(2)}) collective-permute-start(bf16[4,4,64,64]{3,2,1,0:T(8,128)(2,1)S(1)} %get-tuple-element.19), channel_id=1, source_target_pairs={{0,8},{8,16},{16,24},{1,9},{9,17},{17,25},{2,10},{10,18},{18,26},{... | collective-permute-start | bytes 393224 | tf_op jit(solution)/shard_map/ppermute | solution.py:18
  13.2 25.9 %collective-permute-start.5 = (bf16[4,64,64]{2,1,0:T(8,128)(2,1)S(1)}, bf16[4,64,64]{2,1,0:T(8,128)(2,1)S(1)}, u32[]{:S(2)}, u32[]{:S(2)}) collective-permute-start(bf16[4,64,64]{2,1,0:T(8,128)(2,1)S(1)} %get-tuple-element.16), channel_id=1, source_target_pairs={{8,1},{9,2},{10,3},{11,4},{12,5},{13,6},{14,7},{16,9},{17,10},{18,... | collective-permute-start | bytes 98312 | tf_op jit(solution)/shard_map/ppermute | solution.py:28
  16.0 23.2 %collective-permute-start.6 = (bf16[4,4,64,64]{3,2,1,0:T(8,128)(2,1)S(1)}, bf16[4,4,64,64]{3,2,1,0:T(8,128)(2,1)S(1)}, u32[]{:S(2)}, u32[]{:S(2)}) collective-permute-start(bf16[4,4,64,64]{3,2,1,0:T(8,128)(2,1)S(1)} %get-tuple-element.20), channel_id=1, source_target_pairs={{8,0},{16,8},{24,16},{9,1},{17,9},{25,17},{10,2},{18,10},{26,18},{... | collective-permute-start | bytes 393224 | tf_op jit(solution)/shard_map/ppermute | solution.py:18
  30.9 8.3 %collective-permute-start.7 = (bf16[4,64,64]{2,1,0:T(8,128)(2,1)S(1)}, bf16[4,64,64]{2,1,0:T(8,128)(2,1)S(1)}, u32[]{:S(2)}, u32[]{:S(2)}) collective-permute-start(bf16[4,64,64]{2,1,0:T(8,128)(2,1)S(1)} %get-tuple-element.17), channel_id=1, source_target_pairs={{9,0},{10,1},{11,2},{12,3},{13,4},{14,5},{15,6},{17,8},{18,9},{19,... | collective-permute-start | bytes 98312 | tf_op jit(solution)/shard_map/ppermute | solution.py:28
  32.8 13.7 %collective-permute-start.3 = (bf16[4,4,64,64]{3,2,1,0:T(8,128)(2,1)S(1)}, bf16[4,4,64,64]{3,2,1,0:T(8,128)(2,1)S(1)}, u32[]{:S(2)}, u32[]{:S(2)}) collective-permute-start(bf16[4,4,64,64]{3,2,1,0:T(8,128)(2,1)S(1)} %get-tuple-element.21), channel_id=1, source_target_pairs={{0,1},{1,2},{2,3},{3,4},{4,5},{5,6},{6,7},{8,9},{9,10},{10,11},{11... | collective-permute-start | bytes 393224 | tf_op jit(solution)/shard_map/ppermute | solution.py:21
  36.8 11.9 %collective-permute-start.4 = (bf16[4,4,64,64]{3,2,1,0:T(8,128)(2,1)S(1)}, bf16[4,4,64,64]{3,2,1,0:T(8,128)(2,1)S(1)}, u32[]{:S(2)}, u32[]{:S(2)}) collective-permute-start(bf16[4,4,64,64]{3,2,1,0:T(8,128)(2,1)S(1)} %get-tuple-element.22), channel_id=1, source_target_pairs={{1,0},{2,1},{3,2},{4,3},{5,4},{6,5},{7,6},{9,8},{10,9},{11,10},{12... | collective-permute-start | bytes 393224 | tf_op jit(solution)/shard_map/ppermute | solution.py:21
  39.1 9.6 %copy-start.1 = (bf16[1,6,4,64,64]{4,3,2,1,0:T(8,128)(2,1)}, bf16[1,6,4,64,64]{4,3,2,1,0:T(8,128)(2,1)S(1)}, u32[]{:S(2)}) copy-start(bf16[1,6,4,64,64]{4,3,2,1,0:T(8,128)(2,1)S(1)} %maximum_bitcast_fusion) | copy-start | bytes 589828
  39.2 11.2 %copy-start.3 = (bf16[1,6,4,64,64]{4,3,2,1,0:T(8,128)(2,1)}, bf16[1,6,4,64,64]{4,3,2,1,0:T(8,128)(2,1)S(1)}, u32[]{:S(2)}) copy-start(bf16[1,6,4,64,64]{4,3,2,1,0:T(8,128)(2,1)S(1)} %maximum_bitcast_fusion.1) | copy-start | bytes 589828
  46.5 3.9 %copy-start.6 = (bf16[4,4,64,64]{3,2,1,0:T(8,128)(2,1)}, bf16[4,4,64,64]{3,2,1,0:T(8,128)(2,1)S(1)}, u32[]{:S(2)}) copy-start(bf16[4,4,64,64]{3,2,1,0:T(8,128)(2,1)S(1)} %collective-permute-done.3) | copy-start | bytes 393220
  48.7 1.8 %copy-start.8 = (bf16[4,4,64,64]{3,2,1,0:T(8,128)(2,1)}, bf16[4,4,64,64]{3,2,1,0:T(8,128)(2,1)S(1)}, u32[]{:S(2)}) copy-start(bf16[4,4,64,64]{3,2,1,0:T(8,128)(2,1)S(1)} %collective-permute-done.4) | copy-start | bytes 393220
  60.5 4.5 %copy-start = (bf16[16,9,64,64]{3,2,1,0:T(8,128)(2,1)S(1)}, bf16[16,9,64,64]{3,2,1,0:T(8,128)(2,1)}, u32[]{:S(2)}) copy-start(bf16[16,9,64,64]{3,2,1,0:T(8,128)(2,1)} %shard_map.55.ap_ref) | copy-start | bytes 3538948
  60.5 14.3 %copy-start.2 = (bf16[1,6,4,64,64]{4,3,2,1,0:T(8,128)(2,1)S(1)}, bf16[1,6,4,64,64]{4,3,2,1,0:T(8,128)(2,1)}, u32[]{:S(2)}) copy-start(bf16[1,6,4,64,64]{4,3,2,1,0:T(8,128)(2,1)} %copy-done.1) | copy-start | bytes 589828
  60.5 14.3 %copy-start.4 = (bf16[1,6,4,64,64]{4,3,2,1,0:T(8,128)(2,1)S(1)}, bf16[1,6,4,64,64]{4,3,2,1,0:T(8,128)(2,1)}, u32[]{:S(2)}) copy-start(bf16[1,6,4,64,64]{4,3,2,1,0:T(8,128)(2,1)} %copy-done.3) | copy-start | bytes 589828
  60.5 14.3 %copy-start.7 = (bf16[4,4,64,64]{3,2,1,0:T(8,128)(2,1)S(1)}, bf16[4,4,64,64]{3,2,1,0:T(8,128)(2,1)}, u32[]{:S(2)}) copy-start(bf16[4,4,64,64]{3,2,1,0:T(8,128)(2,1)} %copy-done.6) | copy-start | bytes 393220
  60.5 14.3 %copy-start.9 = (bf16[4,4,64,64]{3,2,1,0:T(8,128)(2,1)S(1)}, bf16[4,4,64,64]{3,2,1,0:T(8,128)(2,1)}, u32[]{:S(2)}) copy-start(bf16[4,4,64,64]{3,2,1,0:T(8,128)(2,1)} %copy-done.8) | copy-start | bytes 393220
  66.1 32.0 %collective-permute-start.8 = (bf16[9,64,64]{2,1,0:T(8,128)(2,1)}, bf16[9,64,64]{2,1,0:T(8,128)(2,1)}, u32[]{:S(2)}, u32[]{:S(2)}) collective-permute-start(bf16[9,64,64]{2,1,0:T(8,128)(2,1)} %get-tuple-element.12), channel_id=1, source_target_pairs={{0,9},{1,10},{2,11},{3,12},{4,13},{5,14},{6,15},{8,17},{9,18},{10,... | collective-permute-start | bytes 221192 | tf_op jit(solution)/shard_map/ppermute | solution.py:28
  71.9 29.1 %collective-permute-start.9 = (bf16[4,9,64,64]{3,2,1,0:T(8,128)(2,1)}, bf16[4,9,64,64]{3,2,1,0:T(8,128)(2,1)}, u32[]{:S(2)}, u32[]{:S(2)}) collective-permute-start(bf16[4,9,64,64]{3,2,1,0:T(8,128)(2,1)} %get-tuple-element.14), channel_id=1, source_target_pairs={{0,8},{8,16},{16,24},{1,9},{9,17},{17,25},{2,10},{10,18},{18,26},{... | collective-permute-start | bytes 884744 | tf_op jit(solution)/shard_map/ppermute | solution.py:18
  75.5 30.9 %collective-permute-start.10 = (bf16[9,64,64]{2,1,0:T(8,128)(2,1)}, bf16[9,64,64]{2,1,0:T(8,128)(2,1)}, u32[]{:S(2)}, u32[]{:S(2)}) collective-permute-start(bf16[9,64,64]{2,1,0:T(8,128)(2,1)} %get-tuple-element.11), channel_id=1, source_target_pairs={{1,8},{2,9},{3,10},{4,11},{5,12},{6,13},{7,14},{9,16},{10,17},{11,... | collective-permute-start | bytes 221192 | tf_op jit(solution)/shard_map/ppermute | solution.py:28
  79.5 29.8 %collective-permute-start.11 = (bf16[9,64,64]{2,1,0:T(8,128)(2,1)}, bf16[9,64,64]{2,1,0:T(8,128)(2,1)}, u32[]{:S(2)}, u32[]{:S(2)}) collective-permute-start(bf16[9,64,64]{2,1,0:T(8,128)(2,1)} %get-tuple-element.10), channel_id=1, source_target_pairs={{8,1},{9,2},{10,3},{11,4},{12,5},{13,6},{14,7},{16,9},{17,10},{18,... | collective-permute-start | bytes 221192 | tf_op jit(solution)/shard_map/ppermute | solution.py:28
  82.8 27.5 %collective-permute-start.12 = (bf16[4,9,64,64]{3,2,1,0:T(8,128)(2,1)}, bf16[4,9,64,64]{3,2,1,0:T(8,128)(2,1)S(1)}, u32[]{:S(2)}, u32[]{:S(2)}) collective-permute-start(bf16[4,9,64,64]{3,2,1,0:T(8,128)(2,1)} %get-tuple-element.13), channel_id=1, source_target_pairs={{8,0},{16,8},{24,16},{9,1},{17,9},{25,17},{10,2},{18,10},{26,18},{... | collective-permute-start | bytes 884744 | tf_op jit(solution)/shard_map/ppermute | solution.py:18
  98.2 12.2 %collective-permute-start.13 = (bf16[9,64,64]{2,1,0:T(8,128)(2,1)}, bf16[9,64,64]{2,1,0:T(8,128)(2,1)S(1)}, u32[]{:S(2)}, u32[]{:S(2)}) collective-permute-start(bf16[9,64,64]{2,1,0:T(8,128)(2,1)} %get-tuple-element.9), channel_id=1, source_target_pairs={{9,0},{10,1},{11,2},{12,3},{13,4},{14,5},{15,6},{17,8},{18,9},{19,... | collective-permute-start | bytes 221192 | tf_op jit(solution)/shard_map/ppermute | solution.py:28
  101.0 29.3 %collective-permute-start.14 = (bf16[4,9,64,64]{3,2,1,0:T(8,128)(2,1)}, bf16[4,9,64,64]{3,2,1,0:T(8,128)(2,1)S(1)}, u32[]{:S(2)}, u32[]{:S(2)}) collective-permute-start(bf16[4,9,64,64]{3,2,1,0:T(8,128)(2,1)} %get-tuple-element.8), channel_id=1, source_target_pairs={{0,1},{1,2},{2,3},{3,4},{4,5},{5,6},{6,7},{8,9},{9,10},{10,11},{11... | collective-permute-start | bytes 884744 | tf_op jit(solution)/shard_map/ppermute | solution.py:21
  106.4 25.9 %collective-permute-start.15 = (bf16[4,9,64,64]{3,2,1,0:T(8,128)(2,1)}, bf16[4,9,64,64]{3,2,1,0:T(8,128)(2,1)S(1)}, u32[]{:S(2)}, u32[]{:S(2)}) collective-permute-start(bf16[4,9,64,64]{3,2,1,0:T(8,128)(2,1)} %get-tuple-element.7), channel_id=1, source_target_pairs={{1,0},{2,1},{3,2},{4,3},{5,4},{6,5},{7,6},{9,8},{10,9},{11,10},{12... | collective-permute-start | bytes 884744 | tf_op jit(solution)/shard_map/ppermute | solution.py:21
  132.4 1.6 %copy-start.5 = (bf16[20,9,64,64]{3,2,1,0:T(8,128)(2,1)}, bf16[20,9,64,64]{3,2,1,0:T(8,128)(2,1)S(1)}, u32[]{:S(2)}) copy-start(bf16[20,9,64,64]{3,2,1,0:T(8,128)(2,1)S(1)} %constant_dynamic-update-slice_fusion.ap_ref) | copy-start | bytes 4423684

commit v3 on v1

v3 whole, which is shorter than its diff:
```python
import math

import jax
import jax.numpy as jnp
from jax import lax
from jax.experimental import pallas as pl
from jax.experimental.pallas import tpu as pltpu
from jax.sharding import PartitionSpec as P


def mirror(values, limit):
    values = jnp.where(values < 0, -values, values)
    return jnp.where(values >= limit, 2 * (limit - 1) - values, values)


def shifted(piece, down, right):
    rows, cols = lax.axis_size("row"), lax.axis_size("col")
    if right == 0:
        pairs = [(s, s + down) for s in range(rows) if 0 <= s + down < rows]
        return lax.ppermute(piece, "row", pairs)
    if down == 0:
        pairs = [(s, s + right) for s in range(cols) if 0 <= s + right < cols]
        return lax.ppermute(piece, "col", pairs)
    pairs = []
    for sr in range(rows):
        for sc in range(cols):
            tr, tc = sr + down, sc + right
            if 0 <= tr < rows and 0 <= tc < cols:
                pairs.append((sr * cols + sc, tr * cols + tc))
    return lax.ppermute(piece, ("row", "col"), pairs)


def edge(x, step, width, axis):
    if step == 1:
        return lax.slice_in_dim(x, x.shape[axis] - width, None, axis=axis)
    if step == -1:
        return lax.slice_in_dim(x, 0, width, axis=axis)
    return x


def with_rings(arrays):
    got = {}
    for down in (1, 0, -1):
        for right in (1, 0, -1):
            if down == 0 and right == 0:
                continue
            pieces = [edge(edge(x, down, w, 0), right, w, 1) for x, w in arrays]
            packed = jnp.concatenate([p.reshape((-1,) + p.shape[-2:]) for p in pieces], axis=0)
            arrived = shifted(packed, down, right)
            parts, start = [], 0
            for p in pieces:
                count = math.prod(p.shape[:-2])
                parts.append(arrived[start : start + count].reshape(p.shape))
                start += count
            got[(down, right)] = parts
    out = []
    for i, (x, _) in enumerate(arrays):
        g = lambda d, r: got[(d, r)][i]
        top = jnp.concatenate([g(1, 1), g(1, 0), g(1, -1)], axis=1)
        middle = jnp.concatenate([g(0, 1), x, g(0, -1)], axis=1)
        bottom = jnp.concatenate([g(-1, 1), g(-1, 0), g(-1, -1)], axis=1)
        out.append(jnp.concatenate([top, middle, bottom], axis=0))
    return out


def galerkin_kernel(
    near_ref, slot_ref, target_ref, pick_ref, a_ref, p_ref, pt_ref, out_ref, ap_ref, sum_ref, acc_ref
):
    tiles, terms = a_ref.shape[0], a_ref.shape[1]

    def form(t, carry):
        sum_ref[...] = jnp.zeros(sum_ref.shape, jnp.float32)
        for k in range(terms):
            j = near_ref[t * terms + k]
            a = a_ref[t, k]
            for q in range(4):
                e = slot_ref[(t * terms + k) * 4 + q]
                keep = jnp.where(e >= 0, 1.0, 0.0).astype(jnp.float32)
                prod = jnp.dot(a, p_ref[j, q], preferred_element_type=jnp.float32)
                sum_ref[jnp.clip(e, 0, 8)] += prod * keep

        ap_ref[t] = sum_ref[...].astype(ap_ref.dtype)
        return carry

    lax.fori_loop(0, tiles, form, 0)
    acc_ref[...] = jnp.zeros(acc_ref.shape, jnp.float32)

    def add(t, carry):
        for q in range(4):
            g = target_ref[t * 4 + q]

            @pl.when(g >= 0)
            def _():
                pt = pt_ref[t * 4 + q]
                for e in range(9):
                    acc_ref[g + (e // 3) * 5 + e % 3] += jnp.dot(
                        pt, ap_ref[t, e], preferred_element_type=jnp.float32
                    )

        return carry

    lax.fori_loop(0, tiles, add, 0)
    owned, stencil = out_ref.shape[0], out_ref.shape[1]

    def one_pick(i, carry):
        a = i // stencil
        out_ref[a, i % stencil] = acc_ref[a * stencil + pick_ref[i]].astype(out_ref.dtype)
        return carry

    lax.fori_loop(0, owned * stencil, one_pick, 0)


def rank_among_equal(values):
    n = values.shape[-1]
    same = values[..., :, None] == values[..., None, :]
    earlier = jnp.arange(n)[None, :] < jnp.arange(n)[:, None]
    return jnp.sum(same & earlier, axis=-1, dtype=jnp.int32)


def body(a_blocks, a_cols, p_blocks, p_cols, c_cols):
    n_r, n_c = a_blocks.shape[0], a_blocks.shape[1]
    bs = a_blocks.shape[-1]
    terms = a_blocks.shape[2]
    grid_rows = n_r * lax.axis_size("row")
    grid_cols = n_c * lax.axis_size("col")
    coarse_rows, coarse_cols = grid_rows // 2, grid_cols // 2
    y0 = lax.axis_index("row") * n_r
    x0 = lax.axis_index("col") * n_c
    ys = y0 + jnp.arange(n_r, dtype=jnp.int32)
    xs = x0 + jnp.arange(n_c, dtype=jnp.int32)
    two = jnp.arange(2, dtype=jnp.int32)
    dirs = jnp.arange(terms, dtype=jnp.int32)
    dir_y, dir_x = dirs // 3 - 1, dirs % 3 - 1
    zero = jnp.zeros((), a_blocks.dtype)

    agg_y = mirror((ys - 1)[:, None] // 2 + two, coarse_rows)
    agg_x = mirror((xs - 1)[:, None] // 2 + two, coarse_cols)
    wanted = (agg_y[:, None, :, None] * coarse_cols + agg_x[None, :, None, :]).reshape(n_r, n_c, 4)
    match = p_cols[:, :, None, :] == wanted[:, :, :, None]
    p_canon = jnp.sum(jnp.where(match[..., None, None], p_blocks[:, :, None], zero), axis=3, dtype=zero.dtype)

    to_y = mirror(ys[:, None] + dir_y, grid_rows)
    to_x = mirror(xs[:, None] + dir_x, grid_cols)
    to = to_y[:, None, :] * grid_cols + to_x[None, :, :]
    match = (a_cols[:, :, None, :] == to[:, :, :, None]) & (
        rank_among_equal(a_cols)[:, :, None, :] == rank_among_equal(to)[:, :, :, None]
    )
    a_canon = jnp.sum(jnp.where(match[..., None, None], a_blocks[:, :, None], zero), axis=3, dtype=zero.dtype)

    a_ext, p_ext = with_rings([(a_canon, 1), (p_canon, 2)])
    ext_r, ext_c = n_r + 2, n_c + 2
    wide_r, wide_c = n_r + 4, n_c + 4

    ey = y0 - 1 + jnp.arange(ext_r, dtype=jnp.int32)
    ex = x0 - 1 + jnp.arange(ext_c, dtype=jnp.int32)
    real_y = (ey >= 0) & (ey < grid_rows)
    real_x = (ex >= 0) & (ex < grid_cols)
    ny = mirror(ey[:, None] + dir_y, grid_rows)
    nx = mirror(ex[:, None] + dir_x, grid_cols)
    near = (
        jnp.clip(ny - (y0 - 2), 0, wide_r - 1)[:, None, :] * wide_c
        + jnp.clip(nx - (x0 - 2), 0, wide_c - 1)[None, :, :]
    )
    slot_y = mirror((ny - 1)[..., None] // 2 + two, coarse_rows) - (ey // 2 - 1)[:, None, None]
    slot_x = mirror((nx - 1)[..., None] // 2 + two, coarse_cols) - (ex // 2 - 1)[:, None, None]
    slot = slot_y[:, None, :, :, None] * 3 + slot_x[None, :, :, None, :]
    real = real_y[:, None, None, None, None] & real_x[None, :, None, None, None]
    slot = jnp.where(real & (slot >= 0) & (slot < 9), slot, -1)

    o_r, o_c = n_r // 2, n_c // 2
    e_agg_y = mirror((ey - 1)[:, None] // 2 + two, coarse_rows)
    e_agg_x = mirror((ex - 1)[:, None] // 2 + two, coarse_cols)
    own_y = e_agg_y - y0 // 2
    own_x = e_agg_x - x0 // 2
    off_y = (ey // 2 - 1)[:, None] - e_agg_y + 2
    off_x = (ex // 2 - 1)[:, None] - e_agg_x + 2
    ok_y = real_y[:, None] & (own_y >= 0) & (own_y < o_r) & (off_y >= 0) & (off_y <= 2)
    ok_x = real_x[:, None] & (own_x >= 0) & (own_x < o_c) & (off_x >= 0) & (off_x <= 2)
    target = (own_y[:, None, :, None] * o_c + own_x[None, :, None, :]) * 25 + (
        off_y[:, None, :, None] * 5 + off_x[None, :, None, :]
    )
    target = jnp.where(ok_y[:, None, :, None] & ok_x[None, :, None, :], target, -1)

    cy = y0 // 2 + jnp.arange(o_r, dtype=jnp.int32)
    cx = x0 // 2 + jnp.arange(o_c, dtype=jnp.int32)
    pick = (c_cols // coarse_cols - cy[:, None, None] + 2) * 5 + (c_cols % coarse_cols - cx[None, :, None] + 2)
    pick = jnp.clip(pick, 0, 24)

    p_t = jnp.swapaxes(p_ext[1:-1, 1:-1], -1, -2).reshape(ext_r * ext_c * 4, bs, bs)
    stencil = c_cols.shape[-1]
    tiles = ext_r * ext_c
    smem = pl.BlockSpec(memory_space=pltpu.SMEM)
    vmem = pl.BlockSpec(memory_space=pltpu.VMEM)
    out = pl.pallas_call(
        galerkin_kernel,
        out_shape=jax.ShapeDtypeStruct((o_r * o_c, stencil, bs, bs), jnp.bfloat16),
        in_specs=[smem] * 4 + [vmem] * 3,
        out_specs=vmem,
        scratch_shapes=[
            pltpu.VMEM((tiles, 9, bs, bs), jnp.bfloat16),
            pltpu.VMEM((9, bs, bs), jnp.float32),
            pltpu.VMEM((o_r * o_c * 25, bs, bs), jnp.float32),
        ],
        compiler_params=pltpu.CompilerParams(vmem_limit_bytes=48 * 1024 * 1024),
    )(
        near.reshape(-1),
        slot.reshape(-1),
        target.reshape(-1),
        pick.reshape(-1),
        a_ext.reshape(tiles, terms, bs, bs),
        p_ext.reshape(wide_r * wide_c, 4, bs, bs),
        p_t,
    )
    return out.reshape(o_r, o_c, stencil, bs, bs)


def solution(mesh):
    return jax.shard_map(
        body,
        mesh=mesh,
        in_specs=(
            P("row", "col", None, None, None),
            P("row", "col", None),
            P("row", "col", None, None, None),
            P("row", "col", None),
            P("row", "col", None),
        ),
        out_specs=P("row", "col", None, None, None),
        check_vma=False,
    )
```

time: 199 us -> 167 us (0.84)
  Pallas kernels: 95.8 us -> 33 us
  local copies, waits for them, and re-layouts: 11.7 us -> 59.6 us
  starting transfers between devices: 48.4 us -> 25.3 us
  other arithmetic: 16.2 us -> 31.7 us
  waiting for transfers between devices: 24.2 us -> 15.5 us
    pallas_call x2 -> x1, Pallas kernels: 95.8 us -> 33 us  [body(): pl.pallas_call(galerkin_kernel, out_shape=jax.ShapeDtypeStruct((o_r * o_c...]
    unnamed x24 -> x29, local copies, waits for them, and re-layouts: 0.05 us -> 20.3 us
    slice x1 -> x13, local copies, waits for them, and re-layouts: 2.49 us -> 16 us  [the longest x8 11.9 us: with_rings(): parts.append(arrived[start:start + count].reshape(p.shape))]
    ppermute x8 -> x4, starting transfers between devices: 26 us -> 13.9 us  [shifted(): return lax.ppermute(piece, ('row', 'col'), pairs)]
    concatenate x2 -> x10, other arithmetic: 6.6 us -> 17.4 us  [the longest x8 8.82 us: with_rings(): jnp.concatenate([p.reshape((-1,) + p.shape[-2:]) for p in pieces], axis=0)]
    concatenate x0 -> x4, local copies, waits for them, and re-layouts: none -> 9.56 us  [with_rings(): jnp.concatenate([p.reshape((-1,) + p.shape[-2:]) for p in pieces], axis=0)]
    reduce_sum x1 -> x3, other arithmetic: 2.77 us -> 11.4 us  [the longest x1 6.57 us: body(): jnp.sum(jnp.where(match[..., None, None], a_blocks[:, :, None], zero), ax...]
    ppermute x4 -> x2, starting transfers between devices: 12.4 us -> 5.71 us  [shifted(): return lax.ppermute(piece, 'col', pairs)]
  transfers between devices with their start and end apart: 16 -> 8, of which waited for: 3 -> 2; matrix products, arithmetic and copies ran while one was open for 7% -> 34% of each run, Pallas kernels for 0% -> 0%
where the time goes in v3:
time: 167 us; the launch traced here: 166 us
  local copies, waits for them, and re-layouts  59.6 us (36%)
  Pallas kernels  33 us (20%)
  other arithmetic  31.7 us (19%)
  starting transfers between devices  25.3 us (15%)
  waiting for transfers between devices  15.5 us (9%)
    pallas_call x1, Pallas kernels, body(): pl.pallas_call(galerkin_kernel, out_shape=jax.ShapeDtypeStruct((o_r * o_c...  33 us
    unnamed x29, local copies, waits for them, and re-layouts  20.3 us
    ppermute x4, starting transfers between devices, shifted(): return lax.ppermute(piece, ('row', 'col'), pairs)  13.9 us
    slice x8, local copies, waits for them, and re-layouts, with_rings(): parts.append(arrived[start:start + count].reshape(p.shape))  11.9 us
    concatenate x4, local copies, waits for them, and re-layouts, with_rings(): jnp.concatenate([p.reshape((-1,) + p.shape[-2:]) for p in pieces], axis=0)  9.56 us
    concatenate x8, other arithmetic, with_rings(): jnp.concatenate([p.reshape((-1,) + p.shape[-2:]) for p in pieces], axis=0)  8.82 us
    ppermute x4, waiting for transfers between devices, shifted(): return lax.ppermute(piece, ('row', 'col'), pairs)  8.75 us
    concatenate x2, other arithmetic, with_rings(): out.append(jnp.concatenate([top, middle, bottom], axis=0))  8.6 us
  transfers between devices with their start and end apart: 8, of which 2 were waited for; matrix products, arithmetic and copies ran while one was open for 34% of the time, Pallas kernels for 0%

profile of v3, /device:TPU:9, one launch (start us, length us, event | category | flops | bytes accessed | tf_op | source)
XLA Modules:
  0.0 165.6 jit_solution(15231143376275904018)
XLA Ops:
  1.6 2.1 %convert_reduce_fusion.1 = (s32[4,4,9]{1,2,0:T(8,128)S(1)}, s32[4,4,9]{1,2,0:T(8,128)S(1)}) fusion(s32[4,4,9]{1,2,0:T(8,128)S(1)} %copy.117, s32[4,4,9]{2,1,0:T(4,128)} %param.6, pred[9,9]{1,0:T(8,128)(4,1)S(1)} %iota_compare_fusion, s32[4,4,9]{2,1,0:T(4,128)S(1)} %copy.119, s32[4,4,9]{1,2,0:T(8,128)S(1)} %broadcast_add_fusion.1), kind=kLoop, calls=%fused_computation.27 | loop fusion | flops 10080 | bytes 3537 | tf_op jit(solution)/shard_map/reduce_sum | solution.py:117
  5.6 2.8 %select_reduce_fusion.1 = bf16[4,4,4,64,64]{4,3,2,1,0:T(8,128)(2,1)S(1)} fusion(pred[4,4,4,4]{3,2,1,0:T(4,128)(4,1)S(1)} %broadcast_compare_fusion, bf16[4,4,4,64,64]{4,3,2,1,0:T(8,128)(2,1)} %param.7), kind=kLoop, calls=%fused_computation.3 | loop fusion | flops 1835008 | bytes 1048832 | tf_op jit(solution)/shard_map/reduce_sum | solution.py:140
  8.5 6.6 %select_reduce_fusion = bf16[4,4,9,64,64]{4,3,2,1,0:T(8,128)(2,1)S(1)} fusion(pred[4,4,9,9]{3,2,1,0:T(8,128)(4,1)S(1)} %copy.120, bf16[4,4,9,64,64]{4,3,2,1,0:T(8,128)(2,1)S(1)} %copy-done.2), kind=kLoop, calls=%fused_computation | loop fusion | flops 10027008 | bytes 2360592 | tf_op jit(solution)/shard_map/reduce_sum | solution.py:148
  16.1 4.5 %collective-permute-start.2 = (bf16[25,64,64]{2,1,0:T(8,128)(2,1)}, bf16[25,64,64]{2,1,0:T(8,128)(2,1)}, u32[]{:S(2)}, u32[]{:S(2)}) collective-permute-start(bf16[25,64,64]{2,1,0:T(8,128)(2,1)} %pad_maximum_fusion.5), channel_id=1, source_target_pairs={{1,8},{2,9},{3,10},{4,11},{5,12},{6,13},{7,14},{9,16},{10,17},{11,... | collective-permute-start | bytes 614408 | tf_op jit(solution)/shard_map/ppermute | solution.py:30
  21.5 1.9 %collective-permute-start.5 = (bf16[25,64,64]{2,1,0:T(8,128)(2,1)}, bf16[25,64,64]{2,1,0:T(8,128)(2,1)}, u32[]{:S(2)}, u32[]{:S(2)}) collective-permute-start(bf16[25,64,64]{2,1,0:T(8,128)(2,1)} %pad_maximum_fusion.6), channel_id=1, source_target_pairs={{8,1},{9,2},{10,3},{11,4},{12,5},{13,6},{14,7},{16,9},{17,10},{18,... | collective-permute-start | bytes 614408 | tf_op jit(solution)/shard_map/ppermute | solution.py:30
  24.3 1.9 %collective-permute-start.7 = (bf16[25,64,64]{2,1,0:T(8,128)(2,1)}, bf16[25,64,64]{2,1,0:T(8,128)(2,1)}, u32[]{:S(2)}, u32[]{:S(2)}) collective-permute-start(bf16[25,64,64]{2,1,0:T(8,128)(2,1)} %pad_maximum_fusion.7), channel_id=1, source_target_pairs={{9,0},{10,1},{11,2},{12,3},{13,4},{14,5},{15,6},{17,8},{18,9},{19,... | collective-permute-start | bytes 614408 | tf_op jit(solution)/shard_map/ppermute | solution.py:30
  27.0 5.5 %collective-permute-start = (bf16[25,64,64]{2,1,0:T(8,128)(2,1)}, bf16[25,64,64]{2,1,0:T(8,128)(2,1)}, u32[]{:S(2)}, u32[]{:S(2)}) collective-permute-start(bf16[25,64,64]{2,1,0:T(8,128)(2,1)} %pad_maximum_fusion.4), channel_id=1, source_target_pairs={{0,9},{1,10},{2,11},{3,12},{4,13},{5,14},{6,15},{8,17},{9,18},{10,... | collective-permute-start | bytes 614408 | tf_op jit(solution)/shard_map/ppermute | solution.py:30
  35.6 3.1 %copy.127 = bf16[68,64,64]{0,2,1:T(8,128)(2,1)} copy(bf16[68,64,64]{2,1,0:T(8,128)(2,1)} %pad_maximum_fusion.2) | data formatting | bytes 1114112 | tf_op jit(solution)/shard_map/concatenate | solution.py:48
  38.7 3.7 %collective-permute-start.4 = (bf16[68,64,64]{0,2,1:T(8,128)(2,1)}, bf16[68,64,64]{0,2,1:T(8,128)(2,1)}, u32[]{:S(2)}, u32[]{:S(2)}) collective-permute-start(bf16[68,64,64]{0,2,1:T(8,128)(2,1)} %copy.127), channel_id=1, source_target_pairs={{1,0},{2,1},{3,2},{4,3},{5,4},{6,5},{7,6},{9,8},{10,9},{11,10},{12... | collective-permute-start | bytes 1671176 | tf_op jit(solution)/shard_map/ppermute | solution.py:23
  48.8 2.2 %copy.125 = bf16[68,64,64]{0,2,1:T(8,128)(2,1)} copy(bf16[68,64,64]{2,1,0:T(8,128)(2,1)S(1)} %pad_maximum_fusion.1) | data formatting | bytes 1114112 | tf_op jit(solution)/shard_map/concatenate | solution.py:48
  52.2 2.2 %copy.123 = bf16[68,64,64]{0,2,1:T(8,128)(2,1)} copy(bf16[68,64,64]{2,1,0:T(8,128)(2,1)S(1)} %pad_maximum_fusion) | data formatting | bytes 1114112 | tf_op jit(solution)/shard_map/concatenate | solution.py:48
  55.6 2.1 %copy.131 = bf16[68,64,64]{0,2,1:T(8,128)(2,1)} copy(bf16[68,64,64]{2,1,0:T(8,128)(2,1)S(1)} %pad_maximum_fusion.3) | data formatting | bytes 1114112 | tf_op jit(solution)/shard_map/concatenate | solution.py:48
  57.8 2.0 %collective-permute-start.3 = (bf16[68,64,64]{0,2,1:T(8,128)(2,1)}, bf16[68,64,64]{0,2,1:T(8,128)(2,1)S(1)}, u32[]{:S(2)}, u32[]{:S(2)}) collective-permute-start(bf16[68,64,64]{0,2,1:T(8,128)(2,1)} %copy.125), channel_id=1, source_target_pairs={{0,1},{1,2},{2,3},{3,4},{4,5},{5,6},{6,7},{8,9},{9,10},{10,11},{11... | collective-permute-start | bytes 1671176 | tf_op jit(solution)/shard_map/ppermute | solution.py:23
  61.4 8.7 %collective-permute-done.5 = bf16[25,64,64]{2,1,0:T(8,128)(2,1)} collective-permute-done((bf16[25,64,64]{2,1,0:T(8,128)(2,1)}, bf16[25,64,64]{2,1,0:T(8,128)(2,1)}, u32[]{:S(2)}, u32[]{:S(2)}) %collective-permute-start.5) | collective-permute-done | bytes 204832 | tf_op jit(solution)/shard_map/ppermute | solution.py:30
  70.1 1.9 %collective-permute-start.6 = (bf16[68,64,64]{0,2,1:T(8,128)(2,1)}, bf16[68,64,64]{0,2,1:T(8,128)(2,1)}, u32[]{:S(2)}, u32[]{:S(2)}) collective-permute-start(bf16[68,64,64]{0,2,1:T(8,128)(2,1)} %copy.131), channel_id=1, source_target_pairs={{8,0},{16,8},{24,16},{9,1},{17,9},{25,17},{10,2},{18,10},{26,18},{... | collective-permute-start | bytes 1671176 | tf_op jit(solution)/shard_map/ppermute | solution.py:20
  72.1 3.8 %collective-permute-start.1 = (bf16[68,64,64]{0,2,1:T(8,128)(2,1)}, bf16[68,64,64]{0,2,1:T(8,128)(2,1)S(1)}, u32[]{:S(2)}, u32[]{:S(2)}) collective-permute-start(bf16[68,64,64]{0,2,1:T(8,128)(2,1)} %copy.123), channel_id=1, source_target_pairs={{0,8},{8,16},{16,24},{1,9},{9,17},{17,25},{2,10},{10,18},{18,26},{... | collective-permute-start | bytes 1671176 | tf_op jit(solution)/shard_map/ppermute | solution.py:20
  80.1 1.7 %slice.179 = bf16[16,64,64]{2,1,0:T(8,128)(2,1)} slice(bf16[25,64,64]{2,1,0:T(8,128)(2,1)} %collective-permute-done.7), slice={[9:25], [0:64], [0:64]} | slice | bytes 262144 | tf_op jit(solution)/shard_map/slice | solution.py:53
  86.6 6.8 %collective-permute-done.4 = bf16[68,64,64]{0,2,1:T(8,128)(2,1)} collective-permute-done((bf16[68,64,64]{0,2,1:T(8,128)(2,1)}, bf16[68,64,64]{0,2,1:T(8,128)(2,1)}, u32[]{:S(2)}, u32[]{:S(2)}) %collective-permute-start.4) | collective-permute-done | bytes 557088 | tf_op jit(solution)/shard_map/ppermute | solution.py:23
  93.4 2.8 %copy.140 = bf16[36,64,64]{2,1,0:T(8,128)(2,1)} copy(bf16[36,64,64]{0,2,1:T(8,128)(2,1)} %bitcast.53) | data formatting | bytes 589824
  96.2 2.6 %slice.176 = bf16[32,64,64]{0,2,1:T(8,128)(2,1)} slice(bf16[68,64,64]{0,2,1:T(8,128)(2,1)} %collective-permute-done.4), slice={[36:68], [0:64], [0:64]} | slice | bytes 524288 | tf_op jit(solution)/shard_map/slice | solution.py:53
  98.8 2.8 %copy.144 = bf16[32,64,64]{2,1,0:T(8,128)(2,1)} copy(bf16[32,64,64]{0,2,1:T(8,128)(2,1)} %slice.176) | data formatting | bytes 524288
  101.6 1.8 %copy.139 = bf16[36,64,64]{2,1,0:T(8,128)(2,1)} copy(bf16[36,64,64]{0,2,1:T(8,128)(2,1)S(1)} %bitcast.60) | data formatting | bytes 589824
  104.8 2.8 %copy.143 = bf16[32,64,64]{2,1,0:T(8,128)(2,1)} copy(bf16[32,64,64]{0,2,1:T(8,128)(2,1)} %slice.175) | data formatting | bytes 524288
  107.6 2.8 %copy.141 = bf16[36,64,64]{2,1,0:T(8,128)(2,1)} copy(bf16[36,64,64]{0,2,1:T(8,128)(2,1)} %bitcast.52) | data formatting | bytes 589824
  111.9 1.7 %copy.145 = bf16[32,64,64]{2,1,0:T(8,128)(2,1)} copy(bf16[32,64,64]{0,2,1:T(8,128)(2,1)S(1)} %slice.178) | data formatting | bytes 524288
  113.6 1.8 %copy.138 = bf16[36,64,64]{2,1,0:T(8,128)(2,1)} copy(bf16[36,64,64]{0,2,1:T(8,128)(2,1)S(1)} %bitcast.59) | data formatting | bytes 589824
  116.8 2.5 %maximum_maximum_fusion.1 = bf16[8,8,4,64,64]{4,3,2,1,0:T(8,128)(2,1)S(1)} fusion(bf16[2,2,4,64,64]{4,3,2,1,0:T(8,128)(2,1)} %bitcast.79, bf16[2,4,4,64,64]{4,3,2,1,0:T(8,128)(2,1)} %bitcast.71, bf16[2,2,4,64,64]{4,3,2,1,0:T(8,128)(2,1)} %bitcast.78, bf16[4,2,4,64,64]{4,3,2,1,0:T(8,128)(2,1)} %bitcast.69, ...), kind=kLoop, calls=%fused_computation.2 | loop fusion | flops 8388608 | bytes 4194304 | tf_op jit(solution)/shard_map/concatenate | solution.py:62
  119.3 2.0 %copy-done = bf16[8,8,4,64,64]{4,3,2,1,0:T(8,128)(2,1)} copy-done((bf16[8,8,4,64,64]{4,3,2,1,0:T(8,128)(2,1)}, bf16[8,8,4,64,64]{4,3,2,1,0:T(8,128)(2,1)S(1)}, u32[]{:S(2)}) %copy-start) | copy-done | bytes 2097176
  121.4 1.9 %slice_bitcast_fusion = bf16[6,6,4,64,64]{3,4,2,1,0:T(8,128)(2,1)} fusion(bf16[8,8,4,64,64]{4,3,2,1,0:T(8,128)(2,1)S(1)} %maximum_maximum_fusion.1), kind=kLoop, calls=%fused_computation.4 | loop fusion | bytes 2359296 | tf_op jit(solution)/shard_map/transpose | solution.py:189
  123.3 3.1 %copy.137 = bf16[6,6,4,64,64]{4,3,2,1,0:T(8,128)(2,1)S(1)} copy(bf16[6,6,4,64,64]{3,4,2,1,0:T(8,128)(2,1)} %slice_bitcast_fusion) | data formatting | bytes 2359296 | tf_op jit(solution)/shard_map/transpose | solution.py:189
  126.5 6.1 %maximum_maximum_fusion = bf16[6,6,9,64,64]{4,3,2,1,0:T(8,128)(2,1)} fusion(bf16[1,1,9,64,64]{4,3,2,1,0:T(8,128)(2,1)S(1)} %copy-done.8, bf16[1,4,9,64,64]{4,3,2,1,0:T(8,128)(2,1)} %bitcast.67, bf16[1,1,9,64,64]{4,3,2,1,0:T(8,128)(2,1)S(1)} %copy-done.7, bf16[4,1,9,64,64]{4,3,2,1,0:T(8,128)(2,1)S(1)} %bitcast.65, bf16[4,4,9,64,64]{4,3,2,1,0:T(8,128)(2,1)} %copy-done.1, ...), kind=kLoop, calls=%fused_computation.1 | loop fusion | flops 10616832 | bytes 5308416 | tf_op jit(solution)/shard_map/concatenate | solution.py:62
  132.6 33.0 %shard_map.55 = bf16[4,25,64,64]{3,2,1,0:T(8,128)(2,1)} custom-call(s32[324]{0:T(512)S(1)} %add.590.near_ref, s32[1296]{0:T(1024)S(1)} %and_select_fusion.1.slot_ref, s32[144]{0:T(256)S(1)} %select_n.354.target_ref, s32[100]{0:T(128)S(1)} %reshape.1043.pick_ref, bf16[36,9,64,64]{3,2,1,0:T(8,128)(2,1)} %bitcast.58, bf16[64,4,64,64]{3,2,1,0:T(8,128)(2,1)} %bitcast.57, ...), custom_call_target="tpu_custom_call" | custom-call | tf_op jit(solution)/shard_map/pallas_call | solution.py:194
  (103 shorter events, 33.8 us)
Async XLA Ops:
  3.8 4.7 %copy-start.2 = (bf16[4,4,9,64,64]{4,3,2,1,0:T(8,128)(2,1)S(1)}, bf16[4,4,9,64,64]{4,3,2,1,0:T(8,128)(2,1)}, u32[]{:S(2)}) copy-start(bf16[4,4,9,64,64]{4,3,2,1,0:T(8,128)(2,1)} %param.5) | copy-start | bytes 3538948
  15.0 28.7 %copy-start.1 = (bf16[4,4,9,64,64]{4,3,2,1,0:T(8,128)(2,1)}, bf16[4,4,9,64,64]{4,3,2,1,0:T(8,128)(2,1)S(1)}, u32[]{:S(2)}) copy-start(bf16[4,4,9,64,64]{4,3,2,1,0:T(8,128)(2,1)S(1)} %select_reduce_fusion) | copy-start | bytes 3538948
  16.1 41.7 %collective-permute-start.2 = (bf16[25,64,64]{2,1,0:T(8,128)(2,1)}, bf16[25,64,64]{2,1,0:T(8,128)(2,1)}, u32[]{:S(2)}, u32[]{:S(2)}) collective-permute-start(bf16[25,64,64]{2,1,0:T(8,128)(2,1)} %pad_maximum_fusion.5), channel_id=1, source_target_pairs={{1,8},{2,9},{3,10},{4,11},{5,12},{6,13},{7,14},{9,16},{10,17},{11,... | collective-permute-start | bytes 614408 | tf_op jit(solution)/shard_map/ppermute | solution.py:30
  21.5 48.7 %collective-permute-start.5 = (bf16[25,64,64]{2,1,0:T(8,128)(2,1)}, bf16[25,64,64]{2,1,0:T(8,128)(2,1)}, u32[]{:S(2)}, u32[]{:S(2)}) collective-permute-start(bf16[25,64,64]{2,1,0:T(8,128)(2,1)} %pad_maximum_fusion.6), channel_id=1, source_target_pairs={{8,1},{9,2},{10,3},{11,4},{12,5},{13,6},{14,7},{16,9},{17,10},{18,... | collective-permute-start | bytes 614408 | tf_op jit(solution)/shard_map/ppermute | solution.py:30
  24.3 47.8 %collective-permute-start.7 = (bf16[25,64,64]{2,1,0:T(8,128)(2,1)}, bf16[25,64,64]{2,1,0:T(8,128)(2,1)}, u32[]{:S(2)}, u32[]{:S(2)}) collective-permute-start(bf16[25,64,64]{2,1,0:T(8,128)(2,1)} %pad_maximum_fusion.7), channel_id=1, source_target_pairs={{9,0},{10,1},{11,2},{12,3},{13,4},{14,5},{15,6},{17,8},{18,9},{19,... | collective-permute-start | bytes 614408 | tf_op jit(solution)/shard_map/ppermute | solution.py:30
  27.0 54.8 %collective-permute-start = (bf16[25,64,64]{2,1,0:T(8,128)(2,1)}, bf16[25,64,64]{2,1,0:T(8,128)(2,1)}, u32[]{:S(2)}, u32[]{:S(2)}) collective-permute-start(bf16[25,64,64]{2,1,0:T(8,128)(2,1)} %pad_maximum_fusion.4), channel_id=1, source_target_pairs={{0,9},{1,10},{2,11},{3,12},{4,13},{5,14},{6,15},{8,17},{9,18},{10,... | collective-permute-start | bytes 614408 | tf_op jit(solution)/shard_map/ppermute | solution.py:30
  34.4 10.5 %copy-start.9 = (s32[2,2,25]{2,1,0:T(2,128)S(1)}, s32[2,2,25]{2,1,0:T(2,128)}, u32[]{:S(2)}) copy-start(s32[2,2,25]{2,1,0:T(2,128)} %param.9) | copy-start | bytes 1204
  38.7 54.7 %collective-permute-start.4 = (bf16[68,64,64]{0,2,1:T(8,128)(2,1)}, bf16[68,64,64]{0,2,1:T(8,128)(2,1)}, u32[]{:S(2)}, u32[]{:S(2)}) collective-permute-start(bf16[68,64,64]{0,2,1:T(8,128)(2,1)} %copy.127), channel_id=1, source_target_pairs={{1,0},{2,1},{3,2},{4,3},{5,4},{6,5},{7,6},{9,8},{10,9},{11,10},{12... | collective-permute-start | bytes 1671176 | tf_op jit(solution)/shard_map/ppermute | solution.py:23
  44.9 6.1 %copy-start.4 = (bf16[1,4,9,64,64]{4,3,2,1,0:T(8,128)(2,1)S(1)}, bf16[1,4,9,64,64]{4,3,2,1,0:T(8,128)(2,1)}, u32[]{:S(2)}) copy-start(bf16[1,4,9,64,64]{4,3,2,1,0:T(8,128)(2,1)} %get-tuple-element.11) | copy-start | bytes 884740
  47.3 7.1 %copy-start.3 = (bf16[1,4,9,64,64]{4,3,2,1,0:T(8,128)(2,1)S(1)}, bf16[1,4,9,64,64]{4,3,2,1,0:T(8,128)(2,1)}, u32[]{:S(2)}) copy-start(bf16[1,4,9,64,64]{4,3,2,1,0:T(8,128)(2,1)} %get-tuple-element.12) | copy-start | bytes 884740
  57.8 43.8 %collective-permute-start.3 = (bf16[68,64,64]{0,2,1:T(8,128)(2,1)}, bf16[68,64,64]{0,2,1:T(8,128)(2,1)S(1)}, u32[]{:S(2)}, u32[]{:S(2)}) collective-permute-start(bf16[68,64,64]{0,2,1:T(8,128)(2,1)} %copy.125), channel_id=1, source_target_pairs={{0,1},{1,2},{2,3},{3,4},{4,5},{5,6},{6,7},{8,9},{9,10},{10,11},{11... | collective-permute-start | bytes 1671176 | tf_op jit(solution)/shard_map/ppermute | solution.py:23
  70.1 37.4 %collective-permute-start.6 = (bf16[68,64,64]{0,2,1:T(8,128)(2,1)}, bf16[68,64,64]{0,2,1:T(8,128)(2,1)}, u32[]{:S(2)}, u32[]{:S(2)}) collective-permute-start(bf16[68,64,64]{0,2,1:T(8,128)(2,1)} %copy.131), channel_id=1, source_target_pairs={{8,0},{16,8},{24,16},{9,1},{17,9},{25,17},{10,2},{18,10},{26,18},{... | collective-permute-start | bytes 1671176 | tf_op jit(solution)/shard_map/ppermute | solution.py:20
  72.1 41.6 %collective-permute-start.1 = (bf16[68,64,64]{0,2,1:T(8,128)(2,1)}, bf16[68,64,64]{0,2,1:T(8,128)(2,1)S(1)}, u32[]{:S(2)}, u32[]{:S(2)}) collective-permute-start(bf16[68,64,64]{0,2,1:T(8,128)(2,1)} %copy.123), channel_id=1, source_target_pairs={{0,8},{8,16},{16,24},{1,9},{9,17},{17,25},{2,10},{10,18},{18,26},{... | collective-permute-start | bytes 1671176 | tf_op jit(solution)/shard_map/ppermute | solution.py:20
  119.3 2.0 %copy-start = (bf16[8,8,4,64,64]{4,3,2,1,0:T(8,128)(2,1)}, bf16[8,8,4,64,64]{4,3,2,1,0:T(8,128)(2,1)S(1)}, u32[]{:S(2)}) copy-start(bf16[8,8,4,64,64]{4,3,2,1,0:T(8,128)(2,1)S(1)} %maximum_maximum_fusion.1) | copy-start | bytes 6291460
  121.4 5.1 %copy-start.5 = (bf16[36,64,64]{2,1,0:T(8,128)(2,1)S(1)}, bf16[36,64,64]{2,1,0:T(8,128)(2,1)}, u32[]{:S(2)}) copy-start(bf16[36,64,64]{2,1,0:T(8,128)(2,1)} %copy.140) | copy-start | bytes 884740
  121.4 5.1 %copy-start.6 = (bf16[1,1,9,64,64]{4,3,2,1,0:T(8,128)(2,1)S(1)}, bf16[1,1,9,64,64]{4,3,2,1,0:T(8,128)(2,1)}, u32[]{:S(2)}) copy-start(bf16[1,1,9,64,64]{4,3,2,1,0:T(8,128)(2,1)} %slice_bitcast_fusion.5) | copy-start | bytes 221188
  121.4 5.1 %copy-start.7 = (bf16[1,1,9,64,64]{4,3,2,1,0:T(8,128)(2,1)S(1)}, bf16[1,1,9,64,64]{4,3,2,1,0:T(8,128)(2,1)}, u32[]{:S(2)}) copy-start(bf16[1,1,9,64,64]{4,3,2,1,0:T(8,128)(2,1)} %slice_bitcast_fusion.3) | copy-start | bytes 221188
  121.4 5.1 %copy-start.8 = (bf16[1,1,9,64,64]{4,3,2,1,0:T(8,128)(2,1)S(1)}, bf16[1,1,9,64,64]{4,3,2,1,0:T(8,128)(2,1)}, u32[]{:S(2)}) copy-start(bf16[1,1,9,64,64]{4,3,2,1,0:T(8,128)(2,1)} %slice_bitcast_fusion.1) | copy-start | bytes 221188

commit v4 on v2

--- a/solution.py
+++ b/solution.py
@@ -28,15 +28,22 @@
     return lax.ppermute(piece, ("row", "col"), pairs)
 
 
+def dense_shifted(piece, down, right):
+    rows, cols = piece.shape[-2], piece.shape[-1]
+    lanes = 128 if (rows * cols) % 128 == 0 and cols < 128 else cols
+    packed = piece.reshape(piece.shape[:-2] + (rows * cols // lanes, lanes))
+    return shifted(packed, down, right).reshape(piece.shape)
+
+
 def with_halo(x):
-    top = shifted(x[-1], 1, 0)
-    bottom = shifted(x[0], -1, 0)
-    left = shifted(x[:, -1], 0, 1)
-    right = shifted(x[:, 0], 0, -1)
-    top_left = shifted(x[-1, -1], 1, 1)
-    top_right = shifted(x[-1, 0], 1, -1)
-    bottom_left = shifted(x[0, -1], -1, 1)
-    bottom_right = shifted(x[0, 0], -1, -1)
+    top = dense_shifted(x[-1], 1, 0)
+    bottom = dense_shifted(x[0], -1, 0)
+    left = dense_shifted(x[:, -1], 0, 1)
+    right = dense_shifted(x[:, 0], 0, -1)
+    top_left = dense_shifted(x[-1, -1], 1, 1)
+    top_right = dense_shifted(x[-1, 0], 1, -1)
+    bottom_left = dense_shifted(x[0, -1], -1, 1)
+    bottom_right = dense_shifted(x[0, 0], -1, -1)
     first = jnp.concatenate([top_left[None], top, top_right[None]], axis=0)
     last = jnp.concatenate([bottom_left[None], bottom, bottom_right[None]], axis=0)
     middle = jnp.concatenate([left[:, None], x, right[:, None]], axis=1)

time: 149 us -> 138 us (0.926)
  the two profiles are of different devices: /device:TPU:9 before, /device:TPU:6 now
where the time goes in v4:
time: 138 us; the launch traced here: 137 us
  starting transfers between devices  46.2 us (33%)
  local copies, waits for them, and re-layouts  35.6 us (26%)
  Pallas kernels  33 us (24%)
  waiting for transfers between devices  11.8 us (9%)
  other arithmetic  9.58 us (7%)
    ppermute x8, starting transfers between devices, shifted(): return lax.ppermute(piece, ('row', 'col'), pairs)  25.1 us
    ppermute x4, starting transfers between devices, shifted(): return lax.ppermute(piece, 'col', pairs)  12.1 us
    pallas_call x1, Pallas kernels, body(): pl.pallas_call(ring_kernel, out_shape=jax.ShapeDtypeStruct((o_r * o_c, st...  12 us
    ppermute x4, waiting for transfers between devices, shifted(): return lax.ppermute(piece, 'col', pairs)  11.8 us
    another operation x16, local copies, waits for them, and re-layouts, dense_shifted(): packed = piece.reshape(piece.shape[:-2] + (rows * cols // lanes, lanes))  11.2 us
    pallas_call x1, Pallas kernels, body(): pl.pallas_call(own_kernel, out_shape=acc_shape, in_specs=[pl.BlockSpec(me...  10.9 us
    pallas_call x1, Pallas kernels, body(): pl.pallas_call(ap_kernel, out_shape=jax.ShapeDtypeStruct((n_r * n_c, 9, b...  10 us
    ppermute x4, starting transfers between devices, shifted(): return lax.ppermute(piece, 'row', pairs)  9.04 us
  transfers between devices with their start and end apart: 16, of which 2 were waited for; matrix products, arithmetic and copies ran while one was open for 23% of the time, Pallas kernels for 8%

profile of v4, /device:TPU:6, one launch (start us, length us, event | category | flops | bytes accessed | tf_op | source)
XLA Modules:
  0.0 137.2 jit_solution(10098069593336550331)
XLA Ops:
  1.1 2.8 %select_reduce_fusion = bf16[4,4,4,64,64]{4,3,2,1,0:T(8,128)(2,1)S(1)} fusion(pred[4,4,4,4]{3,2,1,0:T(4,128)(4,1)S(1)} %broadcast_compare_fusion, bf16[4,4,4,64,64]{4,3,2,1,0:T(8,128)(2,1)} %param.7), kind=kLoop, calls=%fused_computation | loop fusion | flops 1835008 | bytes 1048832 | tf_op jit(solution)/shard_map/reduce_sum | solution.py:131
  4.0 2.9 %collective-permute-start = (bf16[4,32,128]{2,1,0:T(8,128)(2,1)S(1)}, bf16[4,32,128]{2,1,0:T(8,128)(2,1)S(1)}, u32[]{:S(2)}, u32[]{:S(2)}) collective-permute-start(bf16[4,32,128]{2,1,0:T(8,128)(2,1)S(1)} %reshape_squeeze.48), channel_id=1, source_target_pairs={{0,9},{1,10},{2,11},{3,12},{4,13},{5,14},{6,15},{8,17},{9,18},{10,... | collective-permute-start | bytes 98312 | tf_op jit(solution)/shard_map/ppermute | solution.py:28
  6.9 1.9 %collective-permute-start.2 = (bf16[4,32,128]{2,1,0:T(8,128)(2,1)S(1)}, bf16[4,32,128]{2,1,0:T(8,128)(2,1)S(1)}, u32[]{:S(2)}, u32[]{:S(2)}) collective-permute-start(bf16[4,32,128]{2,1,0:T(8,128)(2,1)S(1)} %reshape_squeeze.50), channel_id=1, source_target_pairs={{1,8},{2,9},{3,10},{4,11},{5,12},{6,13},{7,14},{9,16},{10,17},{11,... | collective-permute-start | bytes 98312 | tf_op jit(solution)/shard_map/ppermute | solution.py:28
  9.1 1.9 %collective-permute-start.1 = (bf16[4,4,32,128]{3,2,1,0:T(8,128)(2,1)S(1)}, bf16[4,4,32,128]{3,2,1,0:T(8,128)(2,1)S(1)}, u32[]{:S(2)}, u32[]{:S(2)}) collective-permute-start(bf16[4,4,32,128]{3,2,1,0:T(8,128)(2,1)S(1)} %reshape_squeeze.49), channel_id=1, source_target_pairs={{0,8},{8,16},{16,24},{1,9},{9,17},{17,25},{2,10},{10,18},{18,26},{... | collective-permute-start | bytes 393224 | tf_op jit(solution)/shard_map/ppermute | solution.py:18
  11.1 5.4 %collective-permute-start.5 = (bf16[4,32,128]{2,1,0:T(8,128)(2,1)S(1)}, bf16[4,32,128]{2,1,0:T(8,128)(2,1)S(1)}, u32[]{:S(2)}, u32[]{:S(2)}) collective-permute-start(bf16[4,32,128]{2,1,0:T(8,128)(2,1)S(1)} %reshape_squeeze.53), channel_id=1, source_target_pairs={{8,1},{9,2},{10,3},{11,4},{12,5},{13,6},{14,7},{16,9},{17,10},{18,... | collective-permute-start | bytes 98312 | tf_op jit(solution)/shard_map/ppermute | solution.py:28
  16.7 1.9 %collective-permute-start.7 = (bf16[4,32,128]{2,1,0:T(8,128)(2,1)S(1)}, bf16[4,32,128]{2,1,0:T(8,128)(2,1)S(1)}, u32[]{:S(2)}, u32[]{:S(2)}) collective-permute-start(bf16[4,32,128]{2,1,0:T(8,128)(2,1)S(1)} %reshape_squeeze.55), channel_id=1, source_target_pairs={{9,0},{10,1},{11,2},{12,3},{13,4},{14,5},{15,6},{17,8},{18,9},{19,... | collective-permute-start | bytes 98312 | tf_op jit(solution)/shard_map/ppermute | solution.py:28
  22.4 2.6 %collective-permute-start.6 = (bf16[4,4,32,128]{3,2,1,0:T(8,128)(2,1)S(1)}, bf16[4,4,32,128]{3,2,1,0:T(8,128)(2,1)S(1)}, u32[]{:S(2)}, u32[]{:S(2)}) collective-permute-start(bf16[4,4,32,128]{3,2,1,0:T(8,128)(2,1)S(1)} %reshape_squeeze.54), channel_id=1, source_target_pairs={{8,0},{16,8},{24,16},{9,1},{17,9},{25,17},{10,2},{18,10},{26,18},{... | collective-permute-start | bytes 393224 | tf_op jit(solution)/shard_map/ppermute | solution.py:18
  25.0 4.3 %collective-permute-start.3 = (bf16[4,4,32,128]{3,2,1,0:T(8,128)(2,1)S(1)}, bf16[4,4,32,128]{3,2,1,0:T(8,128)(2,1)S(1)}, u32[]{:S(2)}, u32[]{:S(2)}) collective-permute-start(bf16[4,4,32,128]{3,2,1,0:T(8,128)(2,1)S(1)} %reshape_squeeze.51), channel_id=1, source_target_pairs={{0,1},{1,2},{2,3},{3,4},{4,5},{5,6},{6,7},{8,9},{9,10},{10,11},{11... | collective-permute-start | bytes 393224 | tf_op jit(solution)/shard_map/ppermute | solution.py:21
  33.7 1.9 %collective-permute-start.4 = (bf16[4,4,32,128]{3,2,1,0:T(8,128)(2,1)S(1)}, bf16[4,4,32,128]{3,2,1,0:T(8,128)(2,1)S(1)}, u32[]{:S(2)}, u32[]{:S(2)}) collective-permute-start(bf16[4,4,32,128]{3,2,1,0:T(8,128)(2,1)S(1)} %reshape_squeeze.52), channel_id=1, source_target_pairs={{1,0},{2,1},{3,2},{4,3},{5,4},{6,5},{7,6},{9,8},{10,9},{11,10},{12... | collective-permute-start | bytes 393224 | tf_op jit(solution)/shard_map/ppermute | solution.py:21
  36.5 5.6 %collective-permute-done.4 = bf16[4,4,32,128]{3,2,1,0:T(8,128)(2,1)S(1)} collective-permute-done((bf16[4,4,32,128]{3,2,1,0:T(8,128)(2,1)S(1)}, bf16[4,4,32,128]{3,2,1,0:T(8,128)(2,1)S(1)}, u32[]{:S(2)}, u32[]{:S(2)}) %collective-permute-start.4) | collective-permute-done | bytes 131104 | tf_op jit(solution)/shard_map/ppermute | solution.py:21
  42.3 1.8 %pad_maximum_fusion = bf16[6,6,4,64,64]{4,3,2,1,0:T(8,128)(2,1)} fusion(bf16[1,6,4,64,64]{4,3,2,1,0:T(8,128)(2,1)S(1)} %maximum_bitcast_fusion.1, bf16[4,1,4,64,64]{4,3,2,1,0:T(8,128)(2,1)S(1)} %bitcast.91, bf16[4,4,4,64,64]{4,3,2,1,0:T(8,128)(2,1)S(1)} %select_reduce_fusion, bf16[4,1,4,64,64]{4,3,2,1,0:T(8,128)(2,1)S(1)} %bitcast.89, ...), kind=kLoop, calls=%fused_computation.1 | loop fusion | flops 2359296 | bytes 2359296 | tf_op jit(solution)/shard_map/concatenate | solution.py:50
  44.1 10.0 %shard_map.55.ap_ref = bf16[16,9,64,64]{3,2,1,0:T(8,128)(2,1)} custom-call(s32[144]{0:T(256)} %reshape.677.near_ref, s32[576]{0:T(1024)} %and_select_fusion.1.slot_ref, bf16[16,9,64,64]{3,2,1,0:T(8,128)(2,1)} %bitcast.88, bf16[36,4,64,64]{3,2,1,0:T(8,128)(2,1)} %bitcast.87), custom_call_target="tpu_custom_call" | custom-call | tf_op jit(solution)/shard_map/pallas_call | solution.py:149
  54.1 2.3 %fusion.17 = (bf16[4,9,64,64]{3,2,1,0:T(8,128)(2,1)}, bf16[4,9,64,64]{3,2,1,0:T(8,128)(2,1)S(1)}) fusion(bf16[16,9,64,64]{3,2,1,0:T(8,128)(2,1)} %shard_map.55.ap_ref), kind=kLoop, calls=%fused_computation.124 | loop fusion | bytes 1179648 | tf_op jit(solution)/shard_map/slice | solution.py:40
  56.4 1.9 %fusion.16 = (bf16[1,1,9,64,64]{4,3,2,1,0:T(8,128)(2,1)S(1)}, bf16[1,1,9,64,64]{4,3,2,1,0:T(8,128)(2,1)}, bf16[1,1,9,64,64]{4,3,2,1,0:T(8,128)(2,1)}, bf16[1,1,9,64,64]{4,3,2,1,0:T(8,128)(2,1)S(1)}) fusion(bf16[4,4,9,64,64]{4,3,2,1,0:T(8,128)(2,1)} %bitcast.83), kind=kLoop, calls=%fused_computation.123 | loop fusion | bytes 589824 | tf_op jit(solution)/shard_map/slice | solution.py:46
  60.2 1.9 %collective-permute-start.8 = (bf16[9,32,128]{2,1,0:T(8,128)(2,1)}, bf16[9,32,128]{2,1,0:T(8,128)(2,1)}, u32[]{:S(2)}, u32[]{:S(2)}) collective-permute-start(bf16[9,32,128]{2,1,0:T(8,128)(2,1)} %reshape_squeeze.56), channel_id=1, source_target_pairs={{0,9},{1,10},{2,11},{3,12},{4,13},{5,14},{6,15},{8,17},{9,18},{10,... | collective-permute-start | bytes 221192 | tf_op jit(solution)/shard_map/ppermute | solution.py:28
  63.1 1.9 %collective-permute-start.9 = (bf16[4,9,32,128]{3,2,1,0:T(8,128)(2,1)}, bf16[4,9,32,128]{3,2,1,0:T(8,128)(2,1)}, u32[]{:S(2)}, u32[]{:S(2)}) collective-permute-start(bf16[4,9,32,128]{3,2,1,0:T(8,128)(2,1)} %reshape_squeeze.57), channel_id=1, source_target_pairs={{0,8},{8,16},{16,24},{1,9},{9,17},{17,25},{2,10},{10,18},{18,26},{... | collective-permute-start | bytes 884744 | tf_op jit(solution)/shard_map/ppermute | solution.py:18
  65.0 1.9 %fusion.23 = bf16[6,6,4,64,64]{3,4,2,1,0:T(8,128)(2,1)S(1)} fusion(bf16[1,6,4,64,64]{4,3,2,1,0:T(8,128)(2,1)} %copy-done.2, bf16[4,1,4,64,64]{4,3,2,1,0:T(8,128)(2,1)} %bitcast.92, bf16[4,4,4,64,64]{4,3,2,1,0:T(8,128)(2,1)S(1)} %select_reduce_fusion, bf16[4,1,4,64,64]{4,3,2,1,0:T(8,128)(2,1)} %bitcast.90, bf16[1,6,4,64,64]{4,3,2,1,0:T(8,128)(2,1)} %copy-done.1), kind=kLoop, calls=%fused_computation.130 | loop fusion | flops 2359296 | bytes 2359296 | tf_op jit(solution)/shard_map/transpose | solution.py:191
  67.9 1.9 %collective-permute-start.10 = (bf16[9,32,128]{2,1,0:T(8,128)(2,1)S(1)}, bf16[9,32,128]{2,1,0:T(8,128)(2,1)S(1)}, u32[]{:S(2)}, u32[]{:S(2)}) collective-permute-start(bf16[9,32,128]{2,1,0:T(8,128)(2,1)S(1)} %reshape_squeeze.58), channel_id=1, source_target_pairs={{1,8},{2,9},{3,10},{4,11},{5,12},{6,13},{7,14},{9,16},{10,17},{11,... | collective-permute-start | bytes 221192 | tf_op jit(solution)/shard_map/ppermute | solution.py:28
  70.9 5.6 %collective-permute-start.11 = (bf16[9,32,128]{2,1,0:T(8,128)(2,1)S(1)}, bf16[9,32,128]{2,1,0:T(8,128)(2,1)S(1)}, u32[]{:S(2)}, u32[]{:S(2)}) collective-permute-start(bf16[9,32,128]{2,1,0:T(8,128)(2,1)S(1)} %reshape_squeeze.59), channel_id=1, source_target_pairs={{8,1},{9,2},{10,3},{11,4},{12,5},{13,6},{14,7},{16,9},{17,10},{18,... | collective-permute-start | bytes 221192 | tf_op jit(solution)/shard_map/ppermute | solution.py:28
  76.4 2.1 %reshape_squeeze.60 = bf16[4,9,32,128]{3,2,1,0:T(8,128)(2,1)} reshape(bf16[4,9,64,64]{3,2,1,0:T(8,128)(2,1)} %get-tuple-element.13) | data formatting | bytes 589824 | tf_op jit(solution)/shard_map/reshape;squeeze | solution.py:34
  78.5 2.6 %collective-permute-start.12 = (bf16[4,9,32,128]{3,2,1,0:T(8,128)(2,1)}, bf16[4,9,32,128]{3,2,1,0:T(8,128)(2,1)}, u32[]{:S(2)}, u32[]{:S(2)}) collective-permute-start(bf16[4,9,32,128]{3,2,1,0:T(8,128)(2,1)} %reshape_squeeze.60), channel_id=1, source_target_pairs={{8,0},{16,8},{24,16},{9,1},{17,9},{25,17},{10,2},{18,10},{26,18},{... | collective-permute-start | bytes 884744 | tf_op jit(solution)/shard_map/ppermute | solution.py:18
  81.3 2.1 %reshape_squeeze.62 = bf16[4,9,32,128]{3,2,1,0:T(8,128)(2,1)} reshape(bf16[4,1,9,64,64]{4,3,2,1,0:T(8,128)(2,1)} %get-tuple-element.8) | data formatting | bytes 589824 | tf_op jit(solution)/shard_map/reshape;squeeze | solution.py:34
  83.4 2.1 %reshape_squeeze.63 = bf16[4,9,32,128]{3,2,1,0:T(8,128)(2,1)} reshape(bf16[4,1,9,64,64]{4,3,2,1,0:T(8,128)(2,1)} %get-tuple-element.7) | data formatting | bytes 589824 | tf_op jit(solution)/shard_map/reshape;squeeze | solution.py:34
  85.5 2.5 %copy.54 = bf16[6,6,4,64,64]{4,3,2,1,0:T(8,128)(2,1)} copy(bf16[6,6,4,64,64]{3,4,2,1,0:T(8,128)(2,1)S(1)} %fusion.23) | data formatting | bytes 2359296 | tf_op jit(solution)/shard_map/transpose | solution.py:191
  88.0 10.9 %shard_map.56.part_ref = f32[100,64,64]{2,1,0:T(8,128)} custom-call(s32[16]{0:T(128)} %reshape.686.where_ref, s32[64]{0:T(128)} %reshape.687.target_ref, bf16[16,9,64,64]{3,2,1,0:T(8,128)(2,1)} %shard_map.55.ap_ref, bf16[144,64,64]{2,1,0:T(8,128)(2,1)} %bitcast.85), custom_call_target="tpu_custom_call" | custom-call | flops 301989888 | bytes 4194304 | tf_op jit(solution)/shard_map/pallas_call | solution.py:195
  98.9 3.6 %collective-permute-start.13 = (bf16[9,32,128]{2,1,0:T(8,128)(2,1)S(1)}, bf16[9,32,128]{2,1,0:T(8,128)(2,1)S(1)}, u32[]{:S(2)}, u32[]{:S(2)}) collective-permute-start(bf16[9,32,128]{2,1,0:T(8,128)(2,1)S(1)} %reshape_squeeze.61), channel_id=1, source_target_pairs={{9,0},{10,1},{11,2},{12,3},{13,4},{14,5},{15,6},{17,8},{18,9},{19,... | collective-permute-start | bytes 221192 | tf_op jit(solution)/shard_map/ppermute | solution.py:28
  104.1 2.6 %collective-permute-start.14 = (bf16[4,9,32,128]{3,2,1,0:T(8,128)(2,1)}, bf16[4,9,32,128]{3,2,1,0:T(8,128)(2,1)S(1)}, u32[]{:S(2)}, u32[]{:S(2)}) collective-permute-start(bf16[4,9,32,128]{3,2,1,0:T(8,128)(2,1)} %reshape_squeeze.62), channel_id=1, source_target_pairs={{0,1},{1,2},{2,3},{3,4},{4,5},{5,6},{6,7},{8,9},{9,10},{10,11},{11... | collective-permute-start | bytes 884744 | tf_op jit(solution)/shard_map/ppermute | solution.py:21
  106.9 3.2 %collective-permute-start.15 = (bf16[4,9,32,128]{3,2,1,0:T(8,128)(2,1)}, bf16[4,9,32,128]{3,2,1,0:T(8,128)(2,1)S(1)}, u32[]{:S(2)}, u32[]{:S(2)}) collective-permute-start(bf16[4,9,32,128]{3,2,1,0:T(8,128)(2,1)} %reshape_squeeze.63), channel_id=1, source_target_pairs={{1,0},{2,1},{3,2},{4,3},{5,4},{6,5},{7,6},{9,8},{10,9},{11,10},{12... | collective-permute-start | bytes 884744 | tf_op jit(solution)/shard_map/ppermute | solution.py:21
  110.4 1.2 reshape.683
  113.2 1.2 reshape.684
  115.9 6.2 %collective-permute-done.14 = bf16[4,9,32,128]{3,2,1,0:T(8,128)(2,1)S(1)} collective-permute-done((bf16[4,9,32,128]{3,2,1,0:T(8,128)(2,1)}, bf16[4,9,32,128]{3,2,1,0:T(8,128)(2,1)S(1)}, u32[]{:S(2)}, u32[]{:S(2)}) %collective-permute-start.14) | collective-permute-done | bytes 294944 | tf_op jit(solution)/shard_map/ppermute | solution.py:21
  125.1 12.0 %shard_map.57 = bf16[4,25,64,64]{3,2,1,0:T(8,128)(2,1)} custom-call(s32[20]{0:T(128)} %pad_add_fusion.1.where_ref, s32[80]{0:T(128)} %reshape.675.target_ref, s32[100]{0:T(128)} %reshape.676.pick_ref, bf16[20,9,64,64]{3,2,1,0:T(8,128)(2,1)} %constant_dynamic-update-slice_fusion.ap_ref, bf16[144,64,64]{2,1,0:T(8,128)(2,1)} %bitcast.86, ...), custom_call_target="tpu_custom_call" | custom-call | flops 377487360 | bytes 5242880 | tf_op jit(solution)/shard_map/pallas_call | solution.py:210
  (133 shorter events, 23.3 us)
Async XLA Ops:
  0.0 19.2 %copy-start.5 = (s32[4,4,9]{2,1,0:T(4,128)S(1)}, s32[4,4,9]{2,1,0:T(4,128)}, u32[]{:S(2)}) copy-start(s32[4,4,9]{2,1,0:T(4,128)} %param.6) | copy-start | bytes 1732
  1.1 20.9 %copy-start.6 = (s32[2,2,25]{2,1,0:T(2,128)S(1)}, s32[2,2,25]{2,1,0:T(2,128)}, u32[]{:S(2)}) copy-start(s32[2,2,25]{2,1,0:T(2,128)} %param.9) | copy-start | bytes 1204
  4.0 18.4 %collective-permute-start = (bf16[4,32,128]{2,1,0:T(8,128)(2,1)S(1)}, bf16[4,32,128]{2,1,0:T(8,128)(2,1)S(1)}, u32[]{:S(2)}, u32[]{:S(2)}) collective-permute-start(bf16[4,32,128]{2,1,0:T(8,128)(2,1)S(1)} %reshape_squeeze.48), channel_id=1, source_target_pairs={{0,9},{1,10},{2,11},{3,12},{4,13},{5,14},{6,15},{8,17},{9,18},{10,... | collective-permute-start | bytes 98312 | tf_op jit(solution)/shard_map/ppermute | solution.py:28
  6.9 18.0 %collective-permute-start.2 = (bf16[4,32,128]{2,1,0:T(8,128)(2,1)S(1)}, bf16[4,32,128]{2,1,0:T(8,128)(2,1)S(1)}, u32[]{:S(2)}, u32[]{:S(2)}) collective-permute-start(bf16[4,32,128]{2,1,0:T(8,128)(2,1)S(1)} %reshape_squeeze.50), channel_id=1, source_target_pairs={{1,8},{2,9},{3,10},{4,11},{5,12},{6,13},{7,14},{9,16},{10,17},{11,... | collective-permute-start | bytes 98312 | tf_op jit(solution)/shard_map/ppermute | solution.py:28
  9.1 26.7 %collective-permute-start.1 = (bf16[4,4,32,128]{3,2,1,0:T(8,128)(2,1)S(1)}, bf16[4,4,32,128]{3,2,1,0:T(8,128)(2,1)S(1)}, u32[]{:S(2)}, u32[]{:S(2)}) collective-permute-start(bf16[4,4,32,128]{3,2,1,0:T(8,128)(2,1)S(1)} %reshape_squeeze.49), channel_id=1, source_target_pairs={{0,8},{8,16},{16,24},{1,9},{9,17},{17,25},{2,10},{10,18},{18,26},{... | collective-permute-start | bytes 393224 | tf_op jit(solution)/shard_map/ppermute | solution.py:18
  11.1 22.6 %collective-permute-start.5 = (bf16[4,32,128]{2,1,0:T(8,128)(2,1)S(1)}, bf16[4,32,128]{2,1,0:T(8,128)(2,1)S(1)}, u32[]{:S(2)}, u32[]{:S(2)}) collective-permute-start(bf16[4,32,128]{2,1,0:T(8,128)(2,1)S(1)} %reshape_squeeze.53), channel_id=1, source_target_pairs={{8,1},{9,2},{10,3},{11,4},{12,5},{13,6},{14,7},{16,9},{17,10},{18,... | collective-permute-start | bytes 98312 | tf_op jit(solution)/shard_map/ppermute | solution.py:28
  16.7 19.1 %collective-permute-start.7 = (bf16[4,32,128]{2,1,0:T(8,128)(2,1)S(1)}, bf16[4,32,128]{2,1,0:T(8,128)(2,1)S(1)}, u32[]{:S(2)}, u32[]{:S(2)}) collective-permute-start(bf16[4,32,128]{2,1,0:T(8,128)(2,1)S(1)} %reshape_squeeze.55), channel_id=1, source_target_pairs={{9,0},{10,1},{11,2},{12,3},{13,4},{14,5},{15,6},{17,8},{18,9},{19,... | collective-permute-start | bytes 98312 | tf_op jit(solution)/shard_map/ppermute | solution.py:28
  22.4 13.7 %collective-permute-start.6 = (bf16[4,4,32,128]{3,2,1,0:T(8,128)(2,1)S(1)}, bf16[4,4,32,128]{3,2,1,0:T(8,128)(2,1)S(1)}, u32[]{:S(2)}, u32[]{:S(2)}) collective-permute-start(bf16[4,4,32,128]{3,2,1,0:T(8,128)(2,1)S(1)} %reshape_squeeze.54), channel_id=1, source_target_pairs={{8,0},{16,8},{24,16},{9,1},{17,9},{25,17},{10,2},{18,10},{26,18},{... | collective-permute-start | bytes 393224 | tf_op jit(solution)/shard_map/ppermute | solution.py:18
  25.0 11.2 %collective-permute-start.3 = (bf16[4,4,32,128]{3,2,1,0:T(8,128)(2,1)S(1)}, bf16[4,4,32,128]{3,2,1,0:T(8,128)(2,1)S(1)}, u32[]{:S(2)}, u32[]{:S(2)}) collective-permute-start(bf16[4,4,32,128]{3,2,1,0:T(8,128)(2,1)S(1)} %reshape_squeeze.51), channel_id=1, source_target_pairs={{0,1},{1,2},{2,3},{3,4},{4,5},{5,6},{6,7},{8,9},{9,10},{10,11},{11... | collective-permute-start | bytes 393224 | tf_op jit(solution)/shard_map/ppermute | solution.py:21
  33.7 8.4 %collective-permute-start.4 = (bf16[4,4,32,128]{3,2,1,0:T(8,128)(2,1)S(1)}, bf16[4,4,32,128]{3,2,1,0:T(8,128)(2,1)S(1)}, u32[]{:S(2)}, u32[]{:S(2)}) collective-permute-start(bf16[4,4,32,128]{3,2,1,0:T(8,128)(2,1)S(1)} %reshape_squeeze.52), channel_id=1, source_target_pairs={{1,0},{2,1},{3,2},{4,3},{5,4},{6,5},{7,6},{9,8},{10,9},{11,10},{12... | collective-permute-start | bytes 393224 | tf_op jit(solution)/shard_map/ppermute | solution.py:21
  36.1 8.0 %copy-start.1 = (bf16[1,6,4,64,64]{4,3,2,1,0:T(8,128)(2,1)}, bf16[1,6,4,64,64]{4,3,2,1,0:T(8,128)(2,1)S(1)}, u32[]{:S(2)}) copy-start(bf16[1,6,4,64,64]{4,3,2,1,0:T(8,128)(2,1)S(1)} %maximum_bitcast_fusion) | copy-start | bytes 589828
  36.4 7.7 %copy-start.3 = (bf16[4,1,4,64,64]{4,3,2,0,1:T(8,128)(2,1)}, bf16[4,1,4,64,64]{4,3,2,0,1:T(8,128)(2,1)S(1)}, u32[]{:S(2)}) copy-start(bf16[4,1,4,64,64]{4,3,2,0,1:T(8,128)(2,1)S(1)} %broadcast_in_dim_reshape.33) | copy-start | bytes 393220
  36.5 17.6 %copy-start.2 = (bf16[1,6,4,64,64]{4,3,2,1,0:T(8,128)(2,1)}, bf16[1,6,4,64,64]{4,3,2,1,0:T(8,128)(2,1)S(1)}, u32[]{:S(2)}) copy-start(bf16[1,6,4,64,64]{4,3,2,1,0:T(8,128)(2,1)S(1)} %maximum_bitcast_fusion.1) | copy-start | bytes 589828
  42.2 11.8 %copy-start.4 = (bf16[4,1,4,64,64]{4,3,2,0,1:T(8,128)(2,1)}, bf16[4,1,4,64,64]{4,3,2,0,1:T(8,128)(2,1)S(1)}, u32[]{:S(2)}) copy-start(bf16[4,1,4,64,64]{4,3,2,0,1:T(8,128)(2,1)S(1)} %broadcast_in_dim_reshape.34) | copy-start | bytes 393220
  54.1 4.2 %copy-start = (bf16[16,9,64,64]{3,2,1,0:T(8,128)(2,1)S(1)}, bf16[16,9,64,64]{3,2,1,0:T(8,128)(2,1)}, u32[]{:S(2)}) copy-start(bf16[16,9,64,64]{3,2,1,0:T(8,128)(2,1)} %shard_map.55.ap_ref) | copy-start | bytes 3538948
  60.2 38.8 %collective-permute-start.8 = (bf16[9,32,128]{2,1,0:T(8,128)(2,1)}, bf16[9,32,128]{2,1,0:T(8,128)(2,1)}, u32[]{:S(2)}, u32[]{:S(2)}) collective-permute-start(bf16[9,32,128]{2,1,0:T(8,128)(2,1)} %reshape_squeeze.56), channel_id=1, source_target_pairs={{0,9},{1,10},{2,11},{3,12},{4,13},{5,14},{6,15},{8,17},{9,18},{10,... | collective-permute-start | bytes 221192 | tf_op jit(solution)/shard_map/ppermute | solution.py:28
  63.1 47.3 %collective-permute-start.9 = (bf16[4,9,32,128]{3,2,1,0:T(8,128)(2,1)}, bf16[4,9,32,128]{3,2,1,0:T(8,128)(2,1)}, u32[]{:S(2)}, u32[]{:S(2)}) collective-permute-start(bf16[4,9,32,128]{3,2,1,0:T(8,128)(2,1)} %reshape_squeeze.57), channel_id=1, source_target_pairs={{0,8},{8,16},{16,24},{1,9},{9,17},{17,25},{2,10},{10,18},{18,26},{... | collective-permute-start | bytes 884744 | tf_op jit(solution)/shard_map/ppermute | solution.py:18
  67.9 36.2 %collective-permute-start.10 = (bf16[9,32,128]{2,1,0:T(8,128)(2,1)S(1)}, bf16[9,32,128]{2,1,0:T(8,128)(2,1)S(1)}, u32[]{:S(2)}, u32[]{:S(2)}) collective-permute-start(bf16[9,32,128]{2,1,0:T(8,128)(2,1)S(1)} %reshape_squeeze.58), channel_id=1, source_target_pairs={{1,8},{2,9},{3,10},{4,11},{5,12},{6,13},{7,14},{9,16},{10,17},{11,... | collective-permute-start | bytes 221192 | tf_op jit(solution)/shard_map/ppermute | solution.py:28
  70.9 36.0 %collective-permute-start.11 = (bf16[9,32,128]{2,1,0:T(8,128)(2,1)S(1)}, bf16[9,32,128]{2,1,0:T(8,128)(2,1)S(1)}, u32[]{:S(2)}, u32[]{:S(2)}) collective-permute-start(bf16[9,32,128]{2,1,0:T(8,128)(2,1)S(1)} %reshape_squeeze.59), channel_id=1, source_target_pairs={{8,1},{9,2},{10,3},{11,4},{12,5},{13,6},{14,7},{16,9},{17,10},{18,... | collective-permute-start | bytes 221192 | tf_op jit(solution)/shard_map/ppermute | solution.py:28
  78.5 34.6 %collective-permute-start.12 = (bf16[4,9,32,128]{3,2,1,0:T(8,128)(2,1)}, bf16[4,9,32,128]{3,2,1,0:T(8,128)(2,1)}, u32[]{:S(2)}, u32[]{:S(2)}) collective-permute-start(bf16[4,9,32,128]{3,2,1,0:T(8,128)(2,1)} %reshape_squeeze.60), channel_id=1, source_target_pairs={{8,0},{16,8},{24,16},{9,1},{17,9},{25,17},{10,2},{18,10},{26,18},{... | collective-permute-start | bytes 884744 | tf_op jit(solution)/shard_map/ppermute | solution.py:18
  98.9 11.3 %collective-permute-start.13 = (bf16[9,32,128]{2,1,0:T(8,128)(2,1)S(1)}, bf16[9,32,128]{2,1,0:T(8,128)(2,1)S(1)}, u32[]{:S(2)}, u32[]{:S(2)}) collective-permute-start(bf16[9,32,128]{2,1,0:T(8,128)(2,1)S(1)} %reshape_squeeze.61), channel_id=1, source_target_pairs={{9,0},{10,1},{11,2},{12,3},{13,4},{14,5},{15,6},{17,8},{18,9},{19,... | collective-permute-start | bytes 221192 | tf_op jit(solution)/shard_map/ppermute | solution.py:28
  104.1 18.0 %collective-permute-start.14 = (bf16[4,9,32,128]{3,2,1,0:T(8,128)(2,1)}, bf16[4,9,32,128]{3,2,1,0:T(8,128)(2,1)S(1)}, u32[]{:S(2)}, u32[]{:S(2)}) collective-permute-start(bf16[4,9,32,128]{3,2,1,0:T(8,128)(2,1)} %reshape_squeeze.62), channel_id=1, source_target_pairs={{0,1},{1,2},{2,3},{3,4},{4,5},{5,6},{6,7},{8,9},{9,10},{10,11},{11... | collective-permute-start | bytes 884744 | tf_op jit(solution)/shard_map/ppermute | solution.py:21
  106.9 17.1 %collective-permute-start.15 = (bf16[4,9,32,128]{3,2,1,0:T(8,128)(2,1)}, bf16[4,9,32,128]{3,2,1,0:T(8,128)(2,1)S(1)}, u32[]{:S(2)}, u32[]{:S(2)}) collective-permute-start(bf16[4,9,32,128]{3,2,1,0:T(8,128)(2,1)} %reshape_squeeze.63), channel_id=1, source_target_pairs={{1,0},{2,1},{3,2},{4,3},{5,4},{6,5},{7,6},{9,8},{10,9},{11,10},{12... | collective-permute-start | bytes 884744 | tf_op jit(solution)/shard_map/ppermute | solution.py:21

commit v5 on v4

--- a/solution.py
+++ b/solution.py
@@ -35,19 +35,42 @@
     return shifted(packed, down, right).reshape(piece.shape)
 
 
+def halo_pieces(x):
+    return {
+        "left": dense_shifted(x[:, -1], 0, 1),
+        "right": dense_shifted(x[:, 0], 0, -1),
+        "top": dense_shifted(x[-1], 1, 0),
+        "bottom": dense_shifted(x[0], -1, 0),
+        "top_left": dense_shifted(x[-1, -1], 1, 1),
+        "top_right": dense_shifted(x[-1, 0], 1, -1),
+        "bottom_left": dense_shifted(x[0, -1], -1, 1),
+        "bottom_right": dense_shifted(x[0, 0], -1, -1),
+    }
+
+
 def with_halo(x):
-    top = dense_shifted(x[-1], 1, 0)
-    bottom = dense_shifted(x[0], -1, 0)
-    left = dense_shifted(x[:, -1], 0, 1)
-    right = dense_shifted(x[:, 0], 0, -1)
-    top_left = dense_shifted(x[-1, -1], 1, 1)
-    top_right = dense_shifted(x[-1, 0], 1, -1)
-    bottom_left = dense_shifted(x[0, -1], -1, 1)
-    bottom_right = dense_shifted(x[0, 0], -1, -1)
-    first = jnp.concatenate([top_left[None], top, top_right[None]], axis=0)
-    last = jnp.concatenate([bottom_left[None], bottom, bottom_right[None]], axis=0)
-    middle = jnp.concatenate([left[:, None], x, right[:, None]], axis=1)
+    h = halo_pieces(x)
+    first = jnp.concatenate([h["top_left"][None], h["top"], h["top_right"][None]], axis=0)
+    last = jnp.concatenate([h["bottom_left"][None], h["bottom"], h["bottom_right"][None]], axis=0)
+    middle = jnp.concatenate([h["left"][:, None], x, h["right"][:, None]], axis=1)
     return jnp.concatenate([first[None], middle, last[None]], axis=0)
+
+
+def halo_ring(x):
+    h = halo_pieces(x)
+    return jnp.concatenate(
+        [
+            h["top_left"][None],
+            h["top"],
+            h["top_right"][None],
+            h["bottom_left"][None],
+            h["bottom"],
+            h["bottom_right"][None],
+            h["left"],
+            h["right"],
+        ],
+        axis=0,
+    )
 
 
 def ap_kernel(near_ref, slot_ref, a_ref, p_ref, out_ref, acc_ref):
@@ -164,7 +187,6 @@
         p_ext.reshape(ext_r * ext_c, 4, bs, bs),
     )
     ap = ap.reshape(n_r, n_c, 9, bs, bs)
-    ap_ext = with_halo(ap)
 
     o_r, o_c = n_r // 2, n_c // 2
     ey = y0 - 1 + jnp.arange(ext_r, dtype=jnp.int32)
@@ -220,7 +242,7 @@
         ring_of(place),
         ring_of(target).reshape(-1),
         pick,
-        ring_of(ap_ext),
+        halo_ring(ap),
         p_t,
         part,
     )

time: 138 us -> 138 us (level)
    reshape x4 -> x6, local copies, waits for them, and re-layouts: 2.74 us -> 3.28 us  [dense_shifted(): return shifted(packed, down, right).reshape(piece.shape)]
where the time goes in v5:
time: 138 us; the launch traced here: 137 us
  starting transfers between devices  46.2 us (33%)
  local copies, waits for them, and re-layouts  35.6 us (26%)
  Pallas kernels  33 us (24%)
  waiting for transfers between devices  11.8 us (9%)
  other arithmetic  9.58 us (7%)
    ppermute x8, starting transfers between devices, shifted(): return lax.ppermute(piece, ('row', 'col'), pairs)  25.1 us
    ppermute x4, starting transfers between devices, shifted(): return lax.ppermute(piece, 'col', pairs)  12.1 us
    pallas_call x1, Pallas kernels, body(): pl.pallas_call(ring_kernel, out_shape=jax.ShapeDtypeStruct((o_r * o_c, st...  12 us
    ppermute x4, waiting for transfers between devices, shifted(): return lax.ppermute(piece, 'col', pairs)  11.8 us
    another operation x16, local copies, waits for them, and re-layouts, dense_shifted(): packed = piece.reshape(piece.shape[:-2] + (rows * cols // lanes, lanes))  11.2 us
    pallas_call x1, Pallas kernels, body(): pl.pallas_call(own_kernel, out_shape=acc_shape, in_specs=[pl.BlockSpec(me...  10.9 us
    pallas_call x1, Pallas kernels, body(): pl.pallas_call(ap_kernel, out_shape=jax.ShapeDtypeStruct((n_r * n_c, 9, b...  10 us
    ppermute x4, starting transfers between devices, shifted(): return lax.ppermute(piece, 'row', pairs)  9.04 us
  transfers between devices with their start and end apart: 16, of which 2 were waited for; matrix products, arithmetic and copies ran while one was open for 23% of the time, Pallas kernels for 8%

profile of v5, /device:TPU:6, one launch (start us, length us, event | category | flops | bytes accessed | tf_op | source)
XLA Modules:
  0.0 137.2 jit_solution(10098069593336550331)
XLA Ops:
  1.1 2.8 %select_reduce_fusion = bf16[4,4,4,64,64]{4,3,2,1,0:T(8,128)(2,1)S(1)} fusion(pred[4,4,4,4]{3,2,1,0:T(4,128)(4,1)S(1)} %broadcast_compare_fusion, bf16[4,4,4,64,64]{4,3,2,1,0:T(8,128)(2,1)} %param.7), kind=kLoop, calls=%fused_computation | loop fusion | flops 1835008 | bytes 1048832 | tf_op jit(solution)/shard_map/reduce_sum | solution.py:154
  4.0 2.9 %collective-permute-start = (bf16[4,32,128]{2,1,0:T(8,128)(2,1)S(1)}, bf16[4,32,128]{2,1,0:T(8,128)(2,1)S(1)}, u32[]{:S(2)}, u32[]{:S(2)}) collective-permute-start(bf16[4,32,128]{2,1,0:T(8,128)(2,1)S(1)} %reshape_squeeze.48), channel_id=1, source_target_pairs={{0,9},{1,10},{2,11},{3,12},{4,13},{5,14},{6,15},{8,17},{9,18},{10,... | collective-permute-start | bytes 98312 | tf_op jit(solution)/shard_map/ppermute | solution.py:28
  6.9 1.9 %collective-permute-start.2 = (bf16[4,32,128]{2,1,0:T(8,128)(2,1)S(1)}, bf16[4,32,128]{2,1,0:T(8,128)(2,1)S(1)}, u32[]{:S(2)}, u32[]{:S(2)}) collective-permute-start(bf16[4,32,128]{2,1,0:T(8,128)(2,1)S(1)} %reshape_squeeze.50), channel_id=1, source_target_pairs={{1,8},{2,9},{3,10},{4,11},{5,12},{6,13},{7,14},{9,16},{10,17},{11,... | collective-permute-start | bytes 98312 | tf_op jit(solution)/shard_map/ppermute | solution.py:28
  9.1 1.9 %collective-permute-start.1 = (bf16[4,4,32,128]{3,2,1,0:T(8,128)(2,1)S(1)}, bf16[4,4,32,128]{3,2,1,0:T(8,128)(2,1)S(1)}, u32[]{:S(2)}, u32[]{:S(2)}) collective-permute-start(bf16[4,4,32,128]{3,2,1,0:T(8,128)(2,1)S(1)} %reshape_squeeze.49), channel_id=1, source_target_pairs={{0,8},{8,16},{16,24},{1,9},{9,17},{17,25},{2,10},{10,18},{18,26},{... | collective-permute-start | bytes 393224 | tf_op jit(solution)/shard_map/ppermute | solution.py:18
  11.1 5.4 %collective-permute-start.5 = (bf16[4,32,128]{2,1,0:T(8,128)(2,1)S(1)}, bf16[4,32,128]{2,1,0:T(8,128)(2,1)S(1)}, u32[]{:S(2)}, u32[]{:S(2)}) collective-permute-start(bf16[4,32,128]{2,1,0:T(8,128)(2,1)S(1)} %reshape_squeeze.53), channel_id=1, source_target_pairs={{8,1},{9,2},{10,3},{11,4},{12,5},{13,6},{14,7},{16,9},{17,10},{18,... | collective-permute-start | bytes 98312 | tf_op jit(solution)/shard_map/ppermute | solution.py:28
  16.7 1.9 %collective-permute-start.7 = (bf16[4,32,128]{2,1,0:T(8,128)(2,1)S(1)}, bf16[4,32,128]{2,1,0:T(8,128)(2,1)S(1)}, u32[]{:S(2)}, u32[]{:S(2)}) collective-permute-start(bf16[4,32,128]{2,1,0:T(8,128)(2,1)S(1)} %reshape_squeeze.55), channel_id=1, source_target_pairs={{9,0},{10,1},{11,2},{12,3},{13,4},{14,5},{15,6},{17,8},{18,9},{19,... | collective-permute-start | bytes 98312 | tf_op jit(solution)/shard_map/ppermute | solution.py:28
  22.4 2.6 %collective-permute-start.6 = (bf16[4,4,32,128]{3,2,1,0:T(8,128)(2,1)S(1)}, bf16[4,4,32,128]{3,2,1,0:T(8,128)(2,1)S(1)}, u32[]{:S(2)}, u32[]{:S(2)}) collective-permute-start(bf16[4,4,32,128]{3,2,1,0:T(8,128)(2,1)S(1)} %reshape_squeeze.54), channel_id=1, source_target_pairs={{8,0},{16,8},{24,16},{9,1},{17,9},{25,17},{10,2},{18,10},{26,18},{... | collective-permute-start | bytes 393224 | tf_op jit(solution)/shard_map/ppermute | solution.py:18
  25.0 4.3 %collective-permute-start.3 = (bf16[4,4,32,128]{3,2,1,0:T(8,128)(2,1)S(1)}, bf16[4,4,32,128]{3,2,1,0:T(8,128)(2,1)S(1)}, u32[]{:S(2)}, u32[]{:S(2)}) collective-permute-start(bf16[4,4,32,128]{3,2,1,0:T(8,128)(2,1)S(1)} %reshape_squeeze.51), channel_id=1, source_target_pairs={{0,1},{1,2},{2,3},{3,4},{4,5},{5,6},{6,7},{8,9},{9,10},{10,11},{11... | collective-permute-start | bytes 393224 | tf_op jit(solution)/shard_map/ppermute | solution.py:21
  33.7 1.9 %collective-permute-start.4 = (bf16[4,4,32,128]{3,2,1,0:T(8,128)(2,1)S(1)}, bf16[4,4,32,128]{3,2,1,0:T(8,128)(2,1)S(1)}, u32[]{:S(2)}, u32[]{:S(2)}) collective-permute-start(bf16[4,4,32,128]{3,2,1,0:T(8,128)(2,1)S(1)} %reshape_squeeze.52), channel_id=1, source_target_pairs={{1,0},{2,1},{3,2},{4,3},{5,4},{6,5},{7,6},{9,8},{10,9},{11,10},{12... | collective-permute-start | bytes 393224 | tf_op jit(solution)/shard_map/ppermute | solution.py:21
  36.5 5.6 %collective-permute-done.4 = bf16[4,4,32,128]{3,2,1,0:T(8,128)(2,1)S(1)} collective-permute-done((bf16[4,4,32,128]{3,2,1,0:T(8,128)(2,1)S(1)}, bf16[4,4,32,128]{3,2,1,0:T(8,128)(2,1)S(1)}, u32[]{:S(2)}, u32[]{:S(2)}) %collective-permute-start.4) | collective-permute-done | bytes 131104 | tf_op jit(solution)/shard_map/ppermute | solution.py:21
  42.3 1.8 %pad_maximum_fusion = bf16[6,6,4,64,64]{4,3,2,1,0:T(8,128)(2,1)} fusion(bf16[1,6,4,64,64]{4,3,2,1,0:T(8,128)(2,1)S(1)} %maximum_bitcast_fusion.1, bf16[4,1,4,64,64]{4,3,2,1,0:T(8,128)(2,1)S(1)} %bitcast.91, bf16[4,4,4,64,64]{4,3,2,1,0:T(8,128)(2,1)S(1)} %select_reduce_fusion, bf16[4,1,4,64,64]{4,3,2,1,0:T(8,128)(2,1)S(1)} %bitcast.89, ...), kind=kLoop, calls=%fused_computation.1 | loop fusion | flops 2359296 | bytes 2359296 | tf_op jit(solution)/shard_map/concatenate | solution.py:56
  44.1 10.0 %shard_map.55.ap_ref = bf16[16,9,64,64]{3,2,1,0:T(8,128)(2,1)} custom-call(s32[144]{0:T(256)} %reshape.683.near_ref, s32[576]{0:T(1024)} %and_select_fusion.1.slot_ref, bf16[16,9,64,64]{3,2,1,0:T(8,128)(2,1)} %bitcast.88, bf16[36,4,64,64]{3,2,1,0:T(8,128)(2,1)} %bitcast.87), custom_call_target="tpu_custom_call" | custom-call | tf_op jit(solution)/shard_map/pallas_call | solution.py:172
  54.1 2.3 %fusion.17 = (bf16[4,9,64,64]{3,2,1,0:T(8,128)(2,1)}, bf16[4,9,64,64]{3,2,1,0:T(8,128)(2,1)S(1)}) fusion(bf16[16,9,64,64]{3,2,1,0:T(8,128)(2,1)} %shard_map.55.ap_ref), kind=kLoop, calls=%fused_computation.124 | loop fusion | bytes 1179648 | tf_op jit(solution)/shard_map/slice | solution.py:43
  56.4 1.9 %fusion.16 = (bf16[1,1,9,64,64]{4,3,2,1,0:T(8,128)(2,1)S(1)}, bf16[1,1,9,64,64]{4,3,2,1,0:T(8,128)(2,1)}, bf16[1,1,9,64,64]{4,3,2,1,0:T(8,128)(2,1)}, bf16[1,1,9,64,64]{4,3,2,1,0:T(8,128)(2,1)S(1)}) fusion(bf16[4,4,9,64,64]{4,3,2,1,0:T(8,128)(2,1)} %bitcast.83), kind=kLoop, calls=%fused_computation.123 | loop fusion | bytes 589824 | tf_op jit(solution)/shard_map/slice | solution.py:47
  60.2 1.9 %collective-permute-start.8 = (bf16[9,32,128]{2,1,0:T(8,128)(2,1)}, bf16[9,32,128]{2,1,0:T(8,128)(2,1)}, u32[]{:S(2)}, u32[]{:S(2)}) collective-permute-start(bf16[9,32,128]{2,1,0:T(8,128)(2,1)} %reshape_squeeze.56), channel_id=1, source_target_pairs={{0,9},{1,10},{2,11},{3,12},{4,13},{5,14},{6,15},{8,17},{9,18},{10,... | collective-permute-start | bytes 221192 | tf_op jit(solution)/shard_map/ppermute | solution.py:28
  63.1 1.9 %collective-permute-start.9 = (bf16[4,9,32,128]{3,2,1,0:T(8,128)(2,1)}, bf16[4,9,32,128]{3,2,1,0:T(8,128)(2,1)}, u32[]{:S(2)}, u32[]{:S(2)}) collective-permute-start(bf16[4,9,32,128]{3,2,1,0:T(8,128)(2,1)} %reshape_squeeze.57), channel_id=1, source_target_pairs={{0,8},{8,16},{16,24},{1,9},{9,17},{17,25},{2,10},{10,18},{18,26},{... | collective-permute-start | bytes 884744 | tf_op jit(solution)/shard_map/ppermute | solution.py:18
  65.0 1.9 %fusion.23 = bf16[6,6,4,64,64]{3,4,2,1,0:T(8,128)(2,1)S(1)} fusion(bf16[1,6,4,64,64]{4,3,2,1,0:T(8,128)(2,1)} %copy-done.2, bf16[4,1,4,64,64]{4,3,2,1,0:T(8,128)(2,1)} %bitcast.92, bf16[4,4,4,64,64]{4,3,2,1,0:T(8,128)(2,1)S(1)} %select_reduce_fusion, bf16[4,1,4,64,64]{4,3,2,1,0:T(8,128)(2,1)} %bitcast.90, bf16[1,6,4,64,64]{4,3,2,1,0:T(8,128)(2,1)} %copy-done.1), kind=kLoop, calls=%fused_computation.130 | loop fusion | flops 2359296 | bytes 2359296 | tf_op jit(solution)/shard_map/transpose | solution.py:213
  67.9 1.9 %collective-permute-start.10 = (bf16[9,32,128]{2,1,0:T(8,128)(2,1)S(1)}, bf16[9,32,128]{2,1,0:T(8,128)(2,1)S(1)}, u32[]{:S(2)}, u32[]{:S(2)}) collective-permute-start(bf16[9,32,128]{2,1,0:T(8,128)(2,1)S(1)} %reshape_squeeze.58), channel_id=1, source_target_pairs={{1,8},{2,9},{3,10},{4,11},{5,12},{6,13},{7,14},{9,16},{10,17},{11,... | collective-permute-start | bytes 221192 | tf_op jit(solution)/shard_map/ppermute | solution.py:28
  70.9 5.6 %collective-permute-start.11 = (bf16[9,32,128]{2,1,0:T(8,128)(2,1)S(1)}, bf16[9,32,128]{2,1,0:T(8,128)(2,1)S(1)}, u32[]{:S(2)}, u32[]{:S(2)}) collective-permute-start(bf16[9,32,128]{2,1,0:T(8,128)(2,1)S(1)} %reshape_squeeze.59), channel_id=1, source_target_pairs={{8,1},{9,2},{10,3},{11,4},{12,5},{13,6},{14,7},{16,9},{17,10},{18,... | collective-permute-start | bytes 221192 | tf_op jit(solution)/shard_map/ppermute | solution.py:28
  76.5 2.1 %reshape_squeeze.60 = bf16[4,9,32,128]{3,2,1,0:T(8,128)(2,1)} reshape(bf16[4,9,64,64]{3,2,1,0:T(8,128)(2,1)} %get-tuple-element.13) | data formatting | bytes 589824 | tf_op jit(solution)/shard_map/reshape;squeeze | solution.py:34
  78.5 2.6 %collective-permute-start.12 = (bf16[4,9,32,128]{3,2,1,0:T(8,128)(2,1)}, bf16[4,9,32,128]{3,2,1,0:T(8,128)(2,1)}, u32[]{:S(2)}, u32[]{:S(2)}) collective-permute-start(bf16[4,9,32,128]{3,2,1,0:T(8,128)(2,1)} %reshape_squeeze.60), channel_id=1, source_target_pairs={{8,0},{16,8},{24,16},{9,1},{17,9},{25,17},{10,2},{18,10},{26,18},{... | collective-permute-start | bytes 884744 | tf_op jit(solution)/shard_map/ppermute | solution.py:18
  81.3 2.1 %reshape_squeeze.62 = bf16[4,9,32,128]{3,2,1,0:T(8,128)(2,1)} reshape(bf16[4,1,9,64,64]{4,3,2,1,0:T(8,128)(2,1)} %get-tuple-element.8) | data formatting | bytes 589824 | tf_op jit(solution)/shard_map/reshape;squeeze | solution.py:34
  83.4 2.1 %reshape_squeeze.63 = bf16[4,9,32,128]{3,2,1,0:T(8,128)(2,1)} reshape(bf16[4,1,9,64,64]{4,3,2,1,0:T(8,128)(2,1)} %get-tuple-element.7) | data formatting | bytes 589824 | tf_op jit(solution)/shard_map/reshape;squeeze | solution.py:34
  85.5 2.5 %copy.54 = bf16[6,6,4,64,64]{4,3,2,1,0:T(8,128)(2,1)} copy(bf16[6,6,4,64,64]{3,4,2,1,0:T(8,128)(2,1)S(1)} %fusion.23) | data formatting | bytes 2359296 | tf_op jit(solution)/shard_map/transpose | solution.py:213
  88.0 10.9 %shard_map.56.part_ref = f32[100,64,64]{2,1,0:T(8,128)} custom-call(s32[16]{0:T(128)} %reshape.694.where_ref, s32[64]{0:T(128)} %reshape.695.target_ref, bf16[16,9,64,64]{3,2,1,0:T(8,128)(2,1)} %shard_map.55.ap_ref, bf16[144,64,64]{2,1,0:T(8,128)(2,1)} %bitcast.85), custom_call_target="tpu_custom_call" | custom-call | flops 301989888 | bytes 4194304 | tf_op jit(solution)/shard_map/pallas_call | solution.py:217
  98.9 3.5 %collective-permute-start.13 = (bf16[9,32,128]{2,1,0:T(8,128)(2,1)S(1)}, bf16[9,32,128]{2,1,0:T(8,128)(2,1)S(1)}, u32[]{:S(2)}, u32[]{:S(2)}) collective-permute-start(bf16[9,32,128]{2,1,0:T(8,128)(2,1)S(1)} %reshape_squeeze.61), channel_id=1, source_target_pairs={{9,0},{10,1},{11,2},{12,3},{13,4},{14,5},{15,6},{17,8},{18,9},{19,... | collective-permute-start | bytes 221192 | tf_op jit(solution)/shard_map/ppermute | solution.py:28
  104.1 2.6 %collective-permute-start.14 = (bf16[4,9,32,128]{3,2,1,0:T(8,128)(2,1)}, bf16[4,9,32,128]{3,2,1,0:T(8,128)(2,1)S(1)}, u32[]{:S(2)}, u32[]{:S(2)}) collective-permute-start(bf16[4,9,32,128]{3,2,1,0:T(8,128)(2,1)} %reshape_squeeze.62), channel_id=1, source_target_pairs={{0,1},{1,2},{2,3},{3,4},{4,5},{5,6},{6,7},{8,9},{9,10},{10,11},{11... | collective-permute-start | bytes 884744 | tf_op jit(solution)/shard_map/ppermute | solution.py:21
  106.9 3.2 %collective-permute-start.15 = (bf16[4,9,32,128]{3,2,1,0:T(8,128)(2,1)}, bf16[4,9,32,128]{3,2,1,0:T(8,128)(2,1)S(1)}, u32[]{:S(2)}, u32[]{:S(2)}) collective-permute-start(bf16[4,9,32,128]{3,2,1,0:T(8,128)(2,1)} %reshape_squeeze.63), channel_id=1, source_target_pairs={{1,0},{2,1},{3,2},{4,3},{5,4},{6,5},{7,6},{9,8},{10,9},{11,10},{12... | collective-permute-start | bytes 884744 | tf_op jit(solution)/shard_map/ppermute | solution.py:21
  110.4 1.2 reshape.689
  113.2 1.2 reshape.690
  116.0 6.2 %collective-permute-done.14 = bf16[4,9,32,128]{3,2,1,0:T(8,128)(2,1)S(1)} collective-permute-done((bf16[4,9,32,128]{3,2,1,0:T(8,128)(2,1)}, bf16[4,9,32,128]{3,2,1,0:T(8,128)(2,1)S(1)}, u32[]{:S(2)}, u32[]{:S(2)}) %collective-permute-start.14) | collective-permute-done | bytes 294944 | tf_op jit(solution)/shard_map/ppermute | solution.py:21
  125.1 12.0 %shard_map.57 = bf16[4,25,64,64]{3,2,1,0:T(8,128)(2,1)} custom-call(s32[20]{0:T(128)} %pad_add_fusion.1.where_ref, s32[80]{0:T(128)} %reshape.681.target_ref, s32[100]{0:T(128)} %reshape.682.pick_ref, bf16[20,9,64,64]{3,2,1,0:T(8,128)(2,1)} %constant_dynamic-update-slice_fusion.ap_ref, bf16[144,64,64]{2,1,0:T(8,128)(2,1)} %bitcast.86, ...), custom_call_target="tpu_custom_call" | custom-call | flops 377487360 | bytes 5242880 | tf_op jit(solution)/shard_map/pallas_call | solution.py:232
  (133 shorter events, 23.3 us)
Async XLA Ops:
  0.0 19.2 %copy-start.5 = (s32[4,4,9]{2,1,0:T(4,128)S(1)}, s32[4,4,9]{2,1,0:T(4,128)}, u32[]{:S(2)}) copy-start(s32[4,4,9]{2,1,0:T(4,128)} %param.6) | copy-start | bytes 1732
  1.1 20.9 %copy-start.6 = (s32[2,2,25]{2,1,0:T(2,128)S(1)}, s32[2,2,25]{2,1,0:T(2,128)}, u32[]{:S(2)}) copy-start(s32[2,2,25]{2,1,0:T(2,128)} %param.9) | copy-start | bytes 1204
  4.0 18.4 %collective-permute-start = (bf16[4,32,128]{2,1,0:T(8,128)(2,1)S(1)}, bf16[4,32,128]{2,1,0:T(8,128)(2,1)S(1)}, u32[]{:S(2)}, u32[]{:S(2)}) collective-permute-start(bf16[4,32,128]{2,1,0:T(8,128)(2,1)S(1)} %reshape_squeeze.48), channel_id=1, source_target_pairs={{0,9},{1,10},{2,11},{3,12},{4,13},{5,14},{6,15},{8,17},{9,18},{10,... | collective-permute-start | bytes 98312 | tf_op jit(solution)/shard_map/ppermute | solution.py:28
  6.9 18.0 %collective-permute-start.2 = (bf16[4,32,128]{2,1,0:T(8,128)(2,1)S(1)}, bf16[4,32,128]{2,1,0:T(8,128)(2,1)S(1)}, u32[]{:S(2)}, u32[]{:S(2)}) collective-permute-start(bf16[4,32,128]{2,1,0:T(8,128)(2,1)S(1)} %reshape_squeeze.50), channel_id=1, source_target_pairs={{1,8},{2,9},{3,10},{4,11},{5,12},{6,13},{7,14},{9,16},{10,17},{11,... | collective-permute-start | bytes 98312 | tf_op jit(solution)/shard_map/ppermute | solution.py:28
  9.1 26.7 %collective-permute-start.1 = (bf16[4,4,32,128]{3,2,1,0:T(8,128)(2,1)S(1)}, bf16[4,4,32,128]{3,2,1,0:T(8,128)(2,1)S(1)}, u32[]{:S(2)}, u32[]{:S(2)}) collective-permute-start(bf16[4,4,32,128]{3,2,1,0:T(8,128)(2,1)S(1)} %reshape_squeeze.49), channel_id=1, source_target_pairs={{0,8},{8,16},{16,24},{1,9},{9,17},{17,25},{2,10},{10,18},{18,26},{... | collective-permute-start | bytes 393224 | tf_op jit(solution)/shard_map/ppermute | solution.py:18
  11.1 22.6 %collective-permute-start.5 = (bf16[4,32,128]{2,1,0:T(8,128)(2,1)S(1)}, bf16[4,32,128]{2,1,0:T(8,128)(2,1)S(1)}, u32[]{:S(2)}, u32[]{:S(2)}) collective-permute-start(bf16[4,32,128]{2,1,0:T(8,128)(2,1)S(1)} %reshape_squeeze.53), channel_id=1, source_target_pairs={{8,1},{9,2},{10,3},{11,4},{12,5},{13,6},{14,7},{16,9},{17,10},{18,... | collective-permute-start | bytes 98312 | tf_op jit(solution)/shard_map/ppermute | solution.py:28
  16.7 19.1 %collective-permute-start.7 = (bf16[4,32,128]{2,1,0:T(8,128)(2,1)S(1)}, bf16[4,32,128]{2,1,0:T(8,128)(2,1)S(1)}, u32[]{:S(2)}, u32[]{:S(2)}) collective-permute-start(bf16[4,32,128]{2,1,0:T(8,128)(2,1)S(1)} %reshape_squeeze.55), channel_id=1, source_target_pairs={{9,0},{10,1},{11,2},{12,3},{13,4},{14,5},{15,6},{17,8},{18,9},{19,... | collective-permute-start | bytes 98312 | tf_op jit(solution)/shard_map/ppermute | solution.py:28
  22.4 13.7 %collective-permute-start.6 = (bf16[4,4,32,128]{3,2,1,0:T(8,128)(2,1)S(1)}, bf16[4,4,32,128]{3,2,1,0:T(8,128)(2,1)S(1)}, u32[]{:S(2)}, u32[]{:S(2)}) collective-permute-start(bf16[4,4,32,128]{3,2,1,0:T(8,128)(2,1)S(1)} %reshape_squeeze.54), channel_id=1, source_target_pairs={{8,0},{16,8},{24,16},{9,1},{17,9},{25,17},{10,2},{18,10},{26,18},{... | collective-permute-start | bytes 393224 | tf_op jit(solution)/shard_map/ppermute | solution.py:18
  25.0 11.2 %collective-permute-start.3 = (bf16[4,4,32,128]{3,2,1,0:T(8,128)(2,1)S(1)}, bf16[4,4,32,128]{3,2,1,0:T(8,128)(2,1)S(1)}, u32[]{:S(2)}, u32[]{:S(2)}) collective-permute-start(bf16[4,4,32,128]{3,2,1,0:T(8,128)(2,1)S(1)} %reshape_squeeze.51), channel_id=1, source_target_pairs={{0,1},{1,2},{2,3},{3,4},{4,5},{5,6},{6,7},{8,9},{9,10},{10,11},{11... | collective-permute-start | bytes 393224 | tf_op jit(solution)/shard_map/ppermute | solution.py:21
  33.7 8.4 %collective-permute-start.4 = (bf16[4,4,32,128]{3,2,1,0:T(8,128)(2,1)S(1)}, bf16[4,4,32,128]{3,2,1,0:T(8,128)(2,1)S(1)}, u32[]{:S(2)}, u32[]{:S(2)}) collective-permute-start(bf16[4,4,32,128]{3,2,1,0:T(8,128)(2,1)S(1)} %reshape_squeeze.52), channel_id=1, source_target_pairs={{1,0},{2,1},{3,2},{4,3},{5,4},{6,5},{7,6},{9,8},{10,9},{11,10},{12... | collective-permute-start | bytes 393224 | tf_op jit(solution)/shard_map/ppermute | solution.py:21
  36.1 8.0 %copy-start.1 = (bf16[1,6,4,64,64]{4,3,2,1,0:T(8,128)(2,1)}, bf16[1,6,4,64,64]{4,3,2,1,0:T(8,128)(2,1)S(1)}, u32[]{:S(2)}) copy-start(bf16[1,6,4,64,64]{4,3,2,1,0:T(8,128)(2,1)S(1)} %maximum_bitcast_fusion) | copy-start | bytes 589828
  36.4 7.7 %copy-start.3 = (bf16[4,1,4,64,64]{4,3,2,0,1:T(8,128)(2,1)}, bf16[4,1,4,64,64]{4,3,2,0,1:T(8,128)(2,1)S(1)}, u32[]{:S(2)}) copy-start(bf16[4,1,4,64,64]{4,3,2,0,1:T(8,128)(2,1)S(1)} %broadcast_in_dim_reshape.33) | copy-start | bytes 393220
  36.5 17.6 %copy-start.2 = (bf16[1,6,4,64,64]{4,3,2,1,0:T(8,128)(2,1)}, bf16[1,6,4,64,64]{4,3,2,1,0:T(8,128)(2,1)S(1)}, u32[]{:S(2)}) copy-start(bf16[1,6,4,64,64]{4,3,2,1,0:T(8,128)(2,1)S(1)} %maximum_bitcast_fusion.1) | copy-start | bytes 589828
  42.2 11.8 %copy-start.4 = (bf16[4,1,4,64,64]{4,3,2,0,1:T(8,128)(2,1)}, bf16[4,1,4,64,64]{4,3,2,0,1:T(8,128)(2,1)S(1)}, u32[]{:S(2)}) copy-start(bf16[4,1,4,64,64]{4,3,2,0,1:T(8,128)(2,1)S(1)} %broadcast_in_dim_reshape.34) | copy-start | bytes 393220
  54.1 4.2 %copy-start = (bf16[16,9,64,64]{3,2,1,0:T(8,128)(2,1)S(1)}, bf16[16,9,64,64]{3,2,1,0:T(8,128)(2,1)}, u32[]{:S(2)}) copy-start(bf16[16,9,64,64]{3,2,1,0:T(8,128)(2,1)} %shard_map.55.ap_ref) | copy-start | bytes 3538948
  60.2 38.8 %collective-permute-start.8 = (bf16[9,32,128]{2,1,0:T(8,128)(2,1)}, bf16[9,32,128]{2,1,0:T(8,128)(2,1)}, u32[]{:S(2)}, u32[]{:S(2)}) collective-permute-start(bf16[9,32,128]{2,1,0:T(8,128)(2,1)} %reshape_squeeze.56), channel_id=1, source_target_pairs={{0,9},{1,10},{2,11},{3,12},{4,13},{5,14},{6,15},{8,17},{9,18},{10,... | collective-permute-start | bytes 221192 | tf_op jit(solution)/shard_map/ppermute | solution.py:28
  63.1 47.3 %collective-permute-start.9 = (bf16[4,9,32,128]{3,2,1,0:T(8,128)(2,1)}, bf16[4,9,32,128]{3,2,1,0:T(8,128)(2,1)}, u32[]{:S(2)}, u32[]{:S(2)}) collective-permute-start(bf16[4,9,32,128]{3,2,1,0:T(8,128)(2,1)} %reshape_squeeze.57), channel_id=1, source_target_pairs={{0,8},{8,16},{16,24},{1,9},{9,17},{17,25},{2,10},{10,18},{18,26},{... | collective-permute-start | bytes 884744 | tf_op jit(solution)/shard_map/ppermute | solution.py:18
  67.9 36.2 %collective-permute-start.10 = (bf16[9,32,128]{2,1,0:T(8,128)(2,1)S(1)}, bf16[9,32,128]{2,1,0:T(8,128)(2,1)S(1)}, u32[]{:S(2)}, u32[]{:S(2)}) collective-permute-start(bf16[9,32,128]{2,1,0:T(8,128)(2,1)S(1)} %reshape_squeeze.58), channel_id=1, source_target_pairs={{1,8},{2,9},{3,10},{4,11},{5,12},{6,13},{7,14},{9,16},{10,17},{11,... | collective-permute-start | bytes 221192 | tf_op jit(solution)/shard_map/ppermute | solution.py:28
  70.9 36.0 %collective-permute-start.11 = (bf16[9,32,128]{2,1,0:T(8,128)(2,1)S(1)}, bf16[9,32,128]{2,1,0:T(8,128)(2,1)S(1)}, u32[]{:S(2)}, u32[]{:S(2)}) collective-permute-start(bf16[9,32,128]{2,1,0:T(8,128)(2,1)S(1)} %reshape_squeeze.59), channel_id=1, source_target_pairs={{8,1},{9,2},{10,3},{11,4},{12,5},{13,6},{14,7},{16,9},{17,10},{18,... | collective-permute-start | bytes 221192 | tf_op jit(solution)/shard_map/ppermute | solution.py:28
  78.5 34.6 %collective-permute-start.12 = (bf16[4,9,32,128]{3,2,1,0:T(8,128)(2,1)}, bf16[4,9,32,128]{3,2,1,0:T(8,128)(2,1)}, u32[]{:S(2)}, u32[]{:S(2)}) collective-permute-start(bf16[4,9,32,128]{3,2,1,0:T(8,128)(2,1)} %reshape_squeeze.60), channel_id=1, source_target_pairs={{8,0},{16,8},{24,16},{9,1},{17,9},{25,17},{10,2},{18,10},{26,18},{... | collective-permute-start | bytes 884744 | tf_op jit(solution)/shard_map/ppermute | solution.py:18
  98.9 11.3 %collective-permute-start.13 = (bf16[9,32,128]{2,1,0:T(8,128)(2,1)S(1)}, bf16[9,32,128]{2,1,0:T(8,128)(2,1)S(1)}, u32[]{:S(2)}, u32[]{:S(2)}) collective-permute-start(bf16[9,32,128]{2,1,0:T(8,128)(2,1)S(1)} %reshape_squeeze.61), channel_id=1, source_target_pairs={{9,0},{10,1},{11,2},{12,3},{13,4},{14,5},{15,6},{17,8},{18,9},{19,... | collective-permute-start | bytes 221192 | tf_op jit(solution)/shard_map/ppermute | solution.py:28
  104.1 18.0 %collective-permute-start.14 = (bf16[4,9,32,128]{3,2,1,0:T(8,128)(2,1)}, bf16[4,9,32,128]{3,2,1,0:T(8,128)(2,1)S(1)}, u32[]{:S(2)}, u32[]{:S(2)}) collective-permute-start(bf16[4,9,32,128]{3,2,1,0:T(8,128)(2,1)} %reshape_squeeze.62), channel_id=1, source_target_pairs={{0,1},{1,2},{2,3},{3,4},{4,5},{5,6},{6,7},{8,9},{9,10},{10,11},{11... | collective-permute-start | bytes 884744 | tf_op jit(solution)/shard_map/ppermute | solution.py:21
  106.9 17.1 %collective-permute-start.15 = (bf16[4,9,32,128]{3,2,1,0:T(8,128)(2,1)}, bf16[4,9,32,128]{3,2,1,0:T(8,128)(2,1)S(1)}, u32[]{:S(2)}, u32[]{:S(2)}) collective-permute-start(bf16[4,9,32,128]{3,2,1,0:T(8,128)(2,1)} %reshape_squeeze.63), channel_id=1, source_target_pairs={{1,0},{2,1},{3,2},{4,3},{5,4},{6,5},{7,6},{9,8},{10,9},{11,10},{12... | collective-permute-start | bytes 884744 | tf_op jit(solution)/shard_map/ppermute | solution.py:21

commit v6 on v5

--- a/solution.py
+++ b/solution.py
@@ -112,14 +112,12 @@
     lax.fori_loop(0, ap_ref.shape[0], one_tile, 0)
 
 
-def own_kernel(where_ref, target_ref, ap_ref, pt_ref, acc_ref):
+def coarse_kernel(
+    own_where_ref, own_target_ref, ring_where_ref, ring_target_ref, pick_ref, own_ref, ring_ref, pt_ref, out_ref, acc_ref
+):
     acc_ref[...] = jnp.zeros(acc_ref.shape, jnp.float32)
-    add_terms(where_ref, target_ref, ap_ref, pt_ref, acc_ref)
-
-
-def ring_kernel(where_ref, target_ref, pick_ref, ap_ref, pt_ref, part_ref, out_ref, acc_ref):
-    acc_ref[...] = part_ref[...]
-    add_terms(where_ref, target_ref, ap_ref, pt_ref, acc_ref)
+    add_terms(own_where_ref, own_target_ref, own_ref, pt_ref, acc_ref)
+    add_terms(ring_where_ref, ring_target_ref, ring_ref, pt_ref, acc_ref)
     owned, stencil = out_ref.shape[0], out_ref.shape[1]
 
     def one_pick(i, carry):
@@ -212,39 +210,22 @@
 
     p_t = jnp.swapaxes(p_ext, -1, -2).reshape(ext_r * ext_c * 4, bs, bs)
     stencil = c_cols.shape[-1]
-    acc_shape = jax.ShapeDtypeStruct((o_r * o_c * 25, bs, bs), jnp.float32)
-    dot_cost = 2 * bs * bs * bs * 9
-    part = pl.pallas_call(
-        own_kernel,
-        out_shape=acc_shape,
-        in_specs=[pl.BlockSpec(memory_space=pltpu.SMEM)] * 2 + [pl.BlockSpec(memory_space=pltpu.VMEM)] * 2,
+    ring_tiles = 2 * ext_c + 2 * n_r
+    out = pl.pallas_call(
+        coarse_kernel,
+        out_shape=jax.ShapeDtypeStruct((o_r * o_c, stencil, bs, bs), jnp.bfloat16),
+        in_specs=[pl.BlockSpec(memory_space=pltpu.SMEM)] * 5 + [pl.BlockSpec(memory_space=pltpu.VMEM)] * 3,
         out_specs=pl.BlockSpec(memory_space=pltpu.VMEM),
-        cost_estimate=pl.CostEstimate(
-            flops=dot_cost * n_r * n_c * 4, bytes_accessed=4 * 1024 * 1024, transcendentals=0
-        ),
+        scratch_shapes=[pltpu.VMEM((o_r * o_c * 25, bs, bs), jnp.float32)],
     )(
         place[1:-1, 1:-1].reshape(-1),
         target[1:-1, 1:-1].reshape(-1),
-        ap.reshape(n_r * n_c, 9, bs, bs),
-        p_t,
-    )
-    ring_tiles = 2 * ext_c + 2 * n_r
-    out = pl.pallas_call(
-        ring_kernel,
-        out_shape=jax.ShapeDtypeStruct((o_r * o_c, stencil, bs, bs), jnp.bfloat16),
-        in_specs=[pl.BlockSpec(memory_space=pltpu.SMEM)] * 3 + [pl.BlockSpec(memory_space=pltpu.VMEM)] * 3,
-        out_specs=pl.BlockSpec(memory_space=pltpu.VMEM),
-        scratch_shapes=[pltpu.VMEM(acc_shape.shape, jnp.float32)],
-        cost_estimate=pl.CostEstimate(
-            flops=dot_cost * ring_tiles * 4, bytes_accessed=5 * 1024 * 1024, transcendentals=0
-        ),
-    )(
         ring_of(place),
         ring_of(target).reshape(-1),
         pick,
+        ap.reshape(n_r * n_c, 9, bs, bs),
         halo_ring(ap),
         p_t,
-        part,
     )
     return out.reshape(o_r, o_c, stencil, bs, bs)
 

time: 138 us -> 135 us (0.978)
  Pallas kernels: 33 us -> 28.5 us
  local copies, waits for them, and re-layouts: 35.6 us -> 39.6 us
  waiting for transfers between devices: 11.8 us -> 8.54 us
    pallas_call x2 -> x1, Pallas kernels: 23 us -> 18.5 us  [body(): pl.pallas_call(coarse_kernel, out_shape=jax.ShapeDtypeStruct((o_r * o_c,...]
    ppermute x4, waiting for transfers between devices: 11.8 us -> 8.51 us  [shifted(): return lax.ppermute(piece, 'col', pairs)]
    reshape x6, local copies, waits for them, and re-layouts: 3.28 us -> 5.21 us  [dense_shifted(): return shifted(packed, down, right).reshape(piece.shape)]
    another operation x1, local copies, waits for them, and re-layouts: 0.1 us -> 1.66 us  [halo_ring(): h['top_right'][None]]
    another operation x1, local copies, waits for them, and re-layouts: 0.1 us -> 1.65 us  [halo_ring(): h['bottom_left'][None]]
    unnamed x21 -> x25, local copies, waits for them, and re-layouts: 5.31 us -> 4.66 us
  transfers between devices with their start and end apart: 16 -> 16, of which waited for: 2 -> 2; matrix products, arithmetic and copies ran while one was open for 23% -> 26% of each run, Pallas kernels for 8% -> 0%
where the time goes in v6:
time: 135 us; the launch traced here: 134 us
  starting transfers between devices  47.1 us (35%)
  local copies, waits for them, and re-layouts  39.6 us (29%)
  Pallas kernels  28.5 us (21%)
  other arithmetic  9.56 us (7%)
  waiting for transfers between devices  8.54 us (6%)
    ppermute x8, starting transfers between devices, shifted(): return lax.ppermute(piece, ('row', 'col'), pairs)  24.6 us
    pallas_call x1, Pallas kernels, body(): pl.pallas_call(coarse_kernel, out_shape=jax.ShapeDtypeStruct((o_r * o_c,...  18.5 us
    ppermute x4, starting transfers between devices, shifted(): return lax.ppermute(piece, 'col', pairs)  12.8 us
    another operation x16, local copies, waits for them, and re-layouts, dense_shifted(): packed = piece.reshape(piece.shape[:-2] + (rows * cols // lanes, lanes))  12.1 us
    pallas_call x1, Pallas kernels, body(): pl.pallas_call(ap_kernel, out_shape=jax.ShapeDtypeStruct((n_r * n_c, 9, b...  10 us
    ppermute x4, starting transfers between devices, shifted(): return lax.ppermute(piece, 'row', pairs)  9.68 us
    ppermute x4, waiting for transfers between devices, shifted(): return lax.ppermute(piece, 'col', pairs)  8.51 us
    reshape x6, local copies, waits for them, and re-layouts, dense_shifted(): return shifted(packed, down, right).reshape(piece.shape)  5.21 us
  transfers between devices with their start and end apart: 16, of which 2 were waited for; matrix products, arithmetic and copies ran while one was open for 26% of the time, Pallas kernels for 0%

profile of v6, /device:TPU:6, one launch (start us, length us, event | category | flops | bytes accessed | tf_op | source)
XLA Modules:
  0.0 134.3 jit_solution(6822270417983063989)
XLA Ops:
  1.1 2.8 %select_reduce_fusion = bf16[4,4,4,64,64]{4,3,2,1,0:T(8,128)(2,1)S(1)} fusion(pred[4,4,4,4]{3,2,1,0:T(4,128)(4,1)S(1)} %broadcast_compare_fusion, bf16[4,4,4,64,64]{4,3,2,1,0:T(8,128)(2,1)} %param.7), kind=kLoop, calls=%fused_computation | loop fusion | flops 1835008 | bytes 1048832 | tf_op jit(solution)/shard_map/reduce_sum | solution.py:152
  4.0 2.9 %collective-permute-start = (bf16[4,32,128]{2,1,0:T(8,128)(2,1)S(1)}, bf16[4,32,128]{2,1,0:T(8,128)(2,1)S(1)}, u32[]{:S(2)}, u32[]{:S(2)}) collective-permute-start(bf16[4,32,128]{2,1,0:T(8,128)(2,1)S(1)} %reshape_squeeze.48), channel_id=1, source_target_pairs={{0,9},{1,10},{2,11},{3,12},{4,13},{5,14},{6,15},{8,17},{9,18},{10,... | collective-permute-start | bytes 98312 | tf_op jit(solution)/shard_map/ppermute | solution.py:28
  7.0 1.9 %collective-permute-start.2 = (bf16[4,32,128]{2,1,0:T(8,128)(2,1)S(1)}, bf16[4,32,128]{2,1,0:T(8,128)(2,1)S(1)}, u32[]{:S(2)}, u32[]{:S(2)}) collective-permute-start(bf16[4,32,128]{2,1,0:T(8,128)(2,1)S(1)} %reshape_squeeze.50), channel_id=1, source_target_pairs={{1,8},{2,9},{3,10},{4,11},{5,12},{6,13},{7,14},{9,16},{10,17},{11,... | collective-permute-start | bytes 98312 | tf_op jit(solution)/shard_map/ppermute | solution.py:28
  9.1 1.9 %collective-permute-start.1 = (bf16[4,4,32,128]{3,2,1,0:T(8,128)(2,1)S(1)}, bf16[4,4,32,128]{3,2,1,0:T(8,128)(2,1)S(1)}, u32[]{:S(2)}, u32[]{:S(2)}) collective-permute-start(bf16[4,4,32,128]{3,2,1,0:T(8,128)(2,1)S(1)} %reshape_squeeze.49), channel_id=1, source_target_pairs={{0,8},{8,16},{16,24},{1,9},{9,17},{17,25},{2,10},{10,18},{18,26},{... | collective-permute-start | bytes 393224 | tf_op jit(solution)/shard_map/ppermute | solution.py:18
  11.1 5.4 %collective-permute-start.5 = (bf16[4,32,128]{2,1,0:T(8,128)(2,1)S(1)}, bf16[4,32,128]{2,1,0:T(8,128)(2,1)S(1)}, u32[]{:S(2)}, u32[]{:S(2)}) collective-permute-start(bf16[4,32,128]{2,1,0:T(8,128)(2,1)S(1)} %reshape_squeeze.53), channel_id=1, source_target_pairs={{8,1},{9,2},{10,3},{11,4},{12,5},{13,6},{14,7},{16,9},{17,10},{18,... | collective-permute-start | bytes 98312 | tf_op jit(solution)/shard_map/ppermute | solution.py:28
  16.7 1.9 %collective-permute-start.7 = (bf16[4,32,128]{2,1,0:T(8,128)(2,1)S(1)}, bf16[4,32,128]{2,1,0:T(8,128)(2,1)S(1)}, u32[]{:S(2)}, u32[]{:S(2)}) collective-permute-start(bf16[4,32,128]{2,1,0:T(8,128)(2,1)S(1)} %reshape_squeeze.55), channel_id=1, source_target_pairs={{9,0},{10,1},{11,2},{12,3},{13,4},{14,5},{15,6},{17,8},{18,9},{19,... | collective-permute-start | bytes 98312 | tf_op jit(solution)/shard_map/ppermute | solution.py:28
  22.5 2.6 %collective-permute-start.6 = (bf16[4,4,32,128]{3,2,1,0:T(8,128)(2,1)S(1)}, bf16[4,4,32,128]{3,2,1,0:T(8,128)(2,1)S(1)}, u32[]{:S(2)}, u32[]{:S(2)}) collective-permute-start(bf16[4,4,32,128]{3,2,1,0:T(8,128)(2,1)S(1)} %reshape_squeeze.54), channel_id=1, source_target_pairs={{8,0},{16,8},{24,16},{9,1},{17,9},{25,17},{10,2},{18,10},{26,18},{... | collective-permute-start | bytes 393224 | tf_op jit(solution)/shard_map/ppermute | solution.py:18
  25.0 4.3 %collective-permute-start.3 = (bf16[4,4,32,128]{3,2,1,0:T(8,128)(2,1)S(1)}, bf16[4,4,32,128]{3,2,1,0:T(8,128)(2,1)S(1)}, u32[]{:S(2)}, u32[]{:S(2)}) collective-permute-start(bf16[4,4,32,128]{3,2,1,0:T(8,128)(2,1)S(1)} %reshape_squeeze.51), channel_id=1, source_target_pairs={{0,1},{1,2},{2,3},{3,4},{4,5},{5,6},{6,7},{8,9},{9,10},{10,11},{11... | collective-permute-start | bytes 393224 | tf_op jit(solution)/shard_map/ppermute | solution.py:21
  33.7 1.9 %collective-permute-start.4 = (bf16[4,4,32,128]{3,2,1,0:T(8,128)(2,1)S(1)}, bf16[4,4,32,128]{3,2,1,0:T(8,128)(2,1)S(1)}, u32[]{:S(2)}, u32[]{:S(2)}) collective-permute-start(bf16[4,4,32,128]{3,2,1,0:T(8,128)(2,1)S(1)} %reshape_squeeze.52), channel_id=1, source_target_pairs={{1,0},{2,1},{3,2},{4,3},{5,4},{6,5},{7,6},{9,8},{10,9},{11,10},{12... | collective-permute-start | bytes 393224 | tf_op jit(solution)/shard_map/ppermute | solution.py:21
  36.5 5.6 %collective-permute-done.4 = bf16[4,4,32,128]{3,2,1,0:T(8,128)(2,1)S(1)} collective-permute-done((bf16[4,4,32,128]{3,2,1,0:T(8,128)(2,1)S(1)}, bf16[4,4,32,128]{3,2,1,0:T(8,128)(2,1)S(1)}, u32[]{:S(2)}, u32[]{:S(2)}) %collective-permute-start.4) | collective-permute-done | bytes 131104 | tf_op jit(solution)/shard_map/ppermute | solution.py:21
  42.3 1.8 %pad_maximum_fusion = bf16[6,6,4,64,64]{4,3,2,1,0:T(8,128)(2,1)} fusion(bf16[1,6,4,64,64]{4,3,2,1,0:T(8,128)(2,1)S(1)} %maximum_bitcast_fusion.1, bf16[4,1,4,64,64]{4,3,2,1,0:T(8,128)(2,1)S(1)} %bitcast.92, bf16[4,4,4,64,64]{4,3,2,1,0:T(8,128)(2,1)S(1)} %select_reduce_fusion, bf16[4,1,4,64,64]{4,3,2,1,0:T(8,128)(2,1)S(1)} %bitcast.90, ...), kind=kLoop, calls=%fused_computation.1 | loop fusion | flops 2359296 | bytes 2359296 | tf_op jit(solution)/shard_map/concatenate | solution.py:56
  44.1 10.0 %shard_map.55.own_ref = bf16[16,9,64,64]{3,2,1,0:T(8,128)(2,1)} custom-call(s32[144]{0:T(256)} %reshape.685.near_ref, s32[576]{0:T(1024)} %and_select_fusion.1.slot_ref, bf16[16,9,64,64]{3,2,1,0:T(8,128)(2,1)} %bitcast.89, bf16[36,4,64,64]{3,2,1,0:T(8,128)(2,1)} %bitcast.87), custom_call_target="tpu_custom_call" | custom-call | tf_op jit(solution)/shard_map/pallas_call | solution.py:170
  54.1 2.3 %fusion.17 = (bf16[4,9,64,64]{3,2,1,0:T(8,128)(2,1)}, bf16[4,9,64,64]{3,2,1,0:T(8,128)(2,1)S(1)}) fusion(bf16[16,9,64,64]{3,2,1,0:T(8,128)(2,1)} %shard_map.55.own_ref), kind=kLoop, calls=%fused_computation.126 | loop fusion | bytes 1179648 | tf_op jit(solution)/shard_map/slice | solution.py:43
  59.1 1.9 %collective-permute-start.8 = (bf16[9,32,128]{2,1,0:T(8,128)(2,1)}, bf16[9,32,128]{2,1,0:T(8,128)(2,1)}, u32[]{:S(2)}, u32[]{:S(2)}) collective-permute-start(bf16[9,32,128]{2,1,0:T(8,128)(2,1)} %reshape_squeeze.56), channel_id=1, source_target_pairs={{0,9},{1,10},{2,11},{3,12},{4,13},{5,14},{6,15},{8,17},{9,18},{10,... | collective-permute-start | bytes 221192 | tf_op jit(solution)/shard_map/ppermute | solution.py:28
  62.0 1.9 %collective-permute-start.9 = (bf16[4,9,32,128]{3,2,1,0:T(8,128)(2,1)}, bf16[4,9,32,128]{3,2,1,0:T(8,128)(2,1)}, u32[]{:S(2)}, u32[]{:S(2)}) collective-permute-start(bf16[4,9,32,128]{3,2,1,0:T(8,128)(2,1)} %reshape_squeeze.57), channel_id=1, source_target_pairs={{0,8},{8,16},{16,24},{1,9},{9,17},{17,25},{2,10},{10,18},{18,26},{... | collective-permute-start | bytes 884744 | tf_op jit(solution)/shard_map/ppermute | solution.py:18
  63.9 1.9 %fusion.22 = bf16[6,6,4,64,64]{3,4,2,1,0:T(8,128)(2,1)S(1)} fusion(bf16[1,6,4,64,64]{4,3,2,1,0:T(8,128)(2,1)} %copy-done.2, bf16[4,1,4,64,64]{4,3,2,1,0:T(8,128)(2,1)} %bitcast.93, bf16[4,4,4,64,64]{4,3,2,1,0:T(8,128)(2,1)S(1)} %select_reduce_fusion, bf16[4,1,4,64,64]{4,3,2,1,0:T(8,128)(2,1)} %bitcast.91, bf16[1,6,4,64,64]{4,3,2,1,0:T(8,128)(2,1)} %copy-done.1), kind=kLoop, calls=%fused_computation.131 | loop fusion | flops 2359296 | bytes 2359296 | tf_op jit(solution)/shard_map/transpose | solution.py:211
  65.8 1.7 %reshape_squeeze.58 = bf16[9,32,128]{2,1,0:T(8,128)(2,1)} reshape(bf16[1,1,9,64,64]{4,3,2,1,0:T(8,128)(2,1)} %get-tuple-element.11) | data formatting | bytes 147456 | tf_op jit(solution)/shard_map/reshape;squeeze | solution.py:34
  67.5 1.9 %collective-permute-start.10 = (bf16[9,32,128]{2,1,0:T(8,128)(2,1)}, bf16[9,32,128]{2,1,0:T(8,128)(2,1)}, u32[]{:S(2)}, u32[]{:S(2)}) collective-permute-start(bf16[9,32,128]{2,1,0:T(8,128)(2,1)} %reshape_squeeze.58), channel_id=1, source_target_pairs={{1,8},{2,9},{3,10},{4,11},{5,12},{6,13},{7,14},{9,16},{10,17},{11,... | collective-permute-start | bytes 221192 | tf_op jit(solution)/shard_map/ppermute | solution.py:28
  69.5 1.7 %reshape_squeeze.59 = bf16[9,32,128]{2,1,0:T(8,128)(2,1)} reshape(bf16[1,1,9,64,64]{4,3,2,1,0:T(8,128)(2,1)} %get-tuple-element.10) | data formatting | bytes 147456 | tf_op jit(solution)/shard_map/reshape;squeeze | solution.py:34
  71.1 5.5 %collective-permute-start.11 = (bf16[9,32,128]{2,1,0:T(8,128)(2,1)}, bf16[9,32,128]{2,1,0:T(8,128)(2,1)}, u32[]{:S(2)}, u32[]{:S(2)}) collective-permute-start(bf16[9,32,128]{2,1,0:T(8,128)(2,1)} %reshape_squeeze.59), channel_id=1, source_target_pairs={{8,1},{9,2},{10,3},{11,4},{12,5},{13,6},{14,7},{16,9},{17,10},{18,... | collective-permute-start | bytes 221192 | tf_op jit(solution)/shard_map/ppermute | solution.py:28
  76.7 2.1 %reshape_squeeze.60 = bf16[4,9,32,128]{3,2,1,0:T(8,128)(2,1)} reshape(bf16[4,9,64,64]{3,2,1,0:T(8,128)(2,1)} %get-tuple-element.13) | data formatting | bytes 589824 | tf_op jit(solution)/shard_map/reshape;squeeze | solution.py:34
  78.8 3.3 %collective-permute-start.12 = (bf16[4,9,32,128]{3,2,1,0:T(8,128)(2,1)}, bf16[4,9,32,128]{3,2,1,0:T(8,128)(2,1)}, u32[]{:S(2)}, u32[]{:S(2)}) collective-permute-start(bf16[4,9,32,128]{3,2,1,0:T(8,128)(2,1)} %reshape_squeeze.60), channel_id=1, source_target_pairs={{8,0},{16,8},{24,16},{9,1},{17,9},{25,17},{10,2},{18,10},{26,18},{... | collective-permute-start | bytes 884744 | tf_op jit(solution)/shard_map/ppermute | solution.py:18
  82.8 2.1 %reshape_squeeze.62 = bf16[4,9,32,128]{3,2,1,0:T(8,128)(2,1)} reshape(bf16[4,1,9,64,64]{4,3,2,1,0:T(8,128)(2,1)} %get-tuple-element.8) | data formatting | bytes 589824 | tf_op jit(solution)/shard_map/reshape;squeeze | solution.py:34
  85.9 2.4 %copy.60 = bf16[6,6,4,64,64]{4,3,2,1,0:T(8,128)(2,1)} copy(bf16[6,6,4,64,64]{3,4,2,1,0:T(8,128)(2,1)S(1)} %fusion.22) | data formatting | bytes 2359296 | tf_op jit(solution)/shard_map/transpose | solution.py:211
  88.3 3.1 %collective-permute-start.13 = (bf16[9,32,128]{2,1,0:T(8,128)(2,1)}, bf16[9,32,128]{2,1,0:T(8,128)(2,1)S(1)}, u32[]{:S(2)}, u32[]{:S(2)}) collective-permute-start(bf16[9,32,128]{2,1,0:T(8,128)(2,1)} %reshape_squeeze.61), channel_id=1, source_target_pairs={{9,0},{10,1},{11,2},{12,3},{13,4},{14,5},{15,6},{17,8},{18,9},{19,... | collective-permute-start | bytes 221192 | tf_op jit(solution)/shard_map/ppermute | solution.py:28
  92.5 3.0 %collective-permute-start.14 = (bf16[4,9,32,128]{3,2,1,0:T(8,128)(2,1)}, bf16[4,9,32,128]{3,2,1,0:T(8,128)(2,1)}, u32[]{:S(2)}, u32[]{:S(2)}) collective-permute-start(bf16[4,9,32,128]{3,2,1,0:T(8,128)(2,1)} %reshape_squeeze.62), channel_id=1, source_target_pairs={{0,1},{1,2},{2,3},{3,4},{4,5},{5,6},{6,7},{8,9},{9,10},{10,11},{11... | collective-permute-start | bytes 884744 | tf_op jit(solution)/shard_map/ppermute | solution.py:21
  95.6 1.7 %broadcast_in_dim_reshape.38 = bf16[1,9,64,64]{3,2,1,0:T(8,128)(2,1)} reshape(bf16[9,32,128]{2,1,0:T(8,128)(2,1)} %collective-permute-done.10) | data formatting | bytes 147456 | tf_op jit(solution)/shard_map/broadcast_in_dim;reshape | solution.py:65
  97.2 3.5 %collective-permute-start.15 = (bf16[4,9,32,128]{3,2,1,0:T(8,128)(2,1)}, bf16[4,9,32,128]{3,2,1,0:T(8,128)(2,1)}, u32[]{:S(2)}, u32[]{:S(2)}) collective-permute-start(bf16[4,9,32,128]{3,2,1,0:T(8,128)(2,1)} %reshape_squeeze.63), channel_id=1, source_target_pairs={{1,0},{2,1},{3,2},{4,3},{5,4},{6,5},{7,6},{9,8},{10,9},{11,10},{12... | collective-permute-start | bytes 884744 | tf_op jit(solution)/shard_map/ppermute | solution.py:21
  100.7 1.7 %broadcast_in_dim_reshape.39 = bf16[1,9,64,64]{3,2,1,0:T(8,128)(2,1)} reshape(bf16[9,32,128]{2,1,0:T(8,128)(2,1)} %collective-permute-done.11) | data formatting | bytes 147456 | tf_op jit(solution)/shard_map/broadcast_in_dim;reshape | solution.py:66
  107.7 2.9 %collective-permute-done.14 = bf16[4,9,32,128]{3,2,1,0:T(8,128)(2,1)} collective-permute-done((bf16[4,9,32,128]{3,2,1,0:T(8,128)(2,1)}, bf16[4,9,32,128]{3,2,1,0:T(8,128)(2,1)}, u32[]{:S(2)}, u32[]{:S(2)}) %collective-permute-start.14) | collective-permute-done | bytes 294944 | tf_op jit(solution)/shard_map/ppermute | solution.py:21
  114.2 1.6 %copy-done.3 = bf16[20,9,64,64]{3,2,1,0:T(8,128)(2,1)} copy-done((bf16[20,9,64,64]{3,2,1,0:T(8,128)(2,1)}, bf16[20,9,64,64]{3,2,1,0:T(8,128)(2,1)S(1)}, u32[]{:S(2)}) %copy-start.3) | copy-done | bytes 1474584
  115.8 18.5 %shard_map.56 = bf16[4,25,64,64]{3,2,1,0:T(8,128)(2,1)} custom-call(s32[16]{0:T(128)} %reshape.681.own_where_ref, s32[64]{0:T(128)} %reshape.682.own_target_ref, s32[20]{0:T(128)} %pad_add_fusion.1.ring_where_ref, s32[80]{0:T(128)} %reshape.683.ring_target_ref, s32[100]{0:T(128)} %reshape.684.pick_ref, bf16[16,9,64,64]{3,2,1,0:T(8,128)(2,1)} %shard_map.55.own_ref, ...), custom_call_target="tpu_custom_call" | custom-call | tf_op jit(solution)/shard_map/pallas_call | solution.py:214
  (138 shorter events, 25.5 us)
Async XLA Ops:
  1.1 18.2 %copy-start.7 = (s32[4,4,9]{2,1,0:T(4,128)S(1)}, s32[4,4,9]{2,1,0:T(4,128)}, u32[]{:S(2)}) copy-start(s32[4,4,9]{2,1,0:T(4,128)} %param.6) | copy-start | bytes 1732
  3.8 18.1 %copy-start.8 = (s32[2,2,25]{2,1,0:T(2,128)S(1)}, s32[2,2,25]{2,1,0:T(2,128)}, u32[]{:S(2)}) copy-start(s32[2,2,25]{2,1,0:T(2,128)} %param.9) | copy-start | bytes 1204
  4.0 18.5 %collective-permute-start = (bf16[4,32,128]{2,1,0:T(8,128)(2,1)S(1)}, bf16[4,32,128]{2,1,0:T(8,128)(2,1)S(1)}, u32[]{:S(2)}, u32[]{:S(2)}) collective-permute-start(bf16[4,32,128]{2,1,0:T(8,128)(2,1)S(1)} %reshape_squeeze.48), channel_id=1, source_target_pairs={{0,9},{1,10},{2,11},{3,12},{4,13},{5,14},{6,15},{8,17},{9,18},{10,... | collective-permute-start | bytes 98312 | tf_op jit(solution)/shard_map/ppermute | solution.py:28
  7.0 18.1 %collective-permute-start.2 = (bf16[4,32,128]{2,1,0:T(8,128)(2,1)S(1)}, bf16[4,32,128]{2,1,0:T(8,128)(2,1)S(1)}, u32[]{:S(2)}, u32[]{:S(2)}) collective-permute-start(bf16[4,32,128]{2,1,0:T(8,128)(2,1)S(1)} %reshape_squeeze.50), channel_id=1, source_target_pairs={{1,8},{2,9},{3,10},{4,11},{5,12},{6,13},{7,14},{9,16},{10,17},{11,... | collective-permute-start | bytes 98312 | tf_op jit(solution)/shard_map/ppermute | solution.py:28
  9.1 26.7 %collective-permute-start.1 = (bf16[4,4,32,128]{3,2,1,0:T(8,128)(2,1)S(1)}, bf16[4,4,32,128]{3,2,1,0:T(8,128)(2,1)S(1)}, u32[]{:S(2)}, u32[]{:S(2)}) collective-permute-start(bf16[4,4,32,128]{3,2,1,0:T(8,128)(2,1)S(1)} %reshape_squeeze.49), channel_id=1, source_target_pairs={{0,8},{8,16},{16,24},{1,9},{9,17},{17,25},{2,10},{10,18},{18,26},{... | collective-permute-start | bytes 393224 | tf_op jit(solution)/shard_map/ppermute | solution.py:18
  11.1 22.6 %collective-permute-start.5 = (bf16[4,32,128]{2,1,0:T(8,128)(2,1)S(1)}, bf16[4,32,128]{2,1,0:T(8,128)(2,1)S(1)}, u32[]{:S(2)}, u32[]{:S(2)}) collective-permute-start(bf16[4,32,128]{2,1,0:T(8,128)(2,1)S(1)} %reshape_squeeze.53), channel_id=1, source_target_pairs={{8,1},{9,2},{10,3},{11,4},{12,5},{13,6},{14,7},{16,9},{17,10},{18,... | collective-permute-start | bytes 98312 | tf_op jit(solution)/shard_map/ppermute | solution.py:28
  16.7 19.1 %collective-permute-start.7 = (bf16[4,32,128]{2,1,0:T(8,128)(2,1)S(1)}, bf16[4,32,128]{2,1,0:T(8,128)(2,1)S(1)}, u32[]{:S(2)}, u32[]{:S(2)}) collective-permute-start(bf16[4,32,128]{2,1,0:T(8,128)(2,1)S(1)} %reshape_squeeze.55), channel_id=1, source_target_pairs={{9,0},{10,1},{11,2},{12,3},{13,4},{14,5},{15,6},{17,8},{18,9},{19,... | collective-permute-start | bytes 98312 | tf_op jit(solution)/shard_map/ppermute | solution.py:28
  22.5 13.6 %collective-permute-start.6 = (bf16[4,4,32,128]{3,2,1,0:T(8,128)(2,1)S(1)}, bf16[4,4,32,128]{3,2,1,0:T(8,128)(2,1)S(1)}, u32[]{:S(2)}, u32[]{:S(2)}) collective-permute-start(bf16[4,4,32,128]{3,2,1,0:T(8,128)(2,1)S(1)} %reshape_squeeze.54), channel_id=1, source_target_pairs={{8,0},{16,8},{24,16},{9,1},{17,9},{25,17},{10,2},{18,10},{26,18},{... | collective-permute-start | bytes 393224 | tf_op jit(solution)/shard_map/ppermute | solution.py:18
  25.0 11.2 %collective-permute-start.3 = (bf16[4,4,32,128]{3,2,1,0:T(8,128)(2,1)S(1)}, bf16[4,4,32,128]{3,2,1,0:T(8,128)(2,1)S(1)}, u32[]{:S(2)}, u32[]{:S(2)}) collective-permute-start(bf16[4,4,32,128]{3,2,1,0:T(8,128)(2,1)S(1)} %reshape_squeeze.51), channel_id=1, source_target_pairs={{0,1},{1,2},{2,3},{3,4},{4,5},{5,6},{6,7},{8,9},{9,10},{10,11},{11... | collective-permute-start | bytes 393224 | tf_op jit(solution)/shard_map/ppermute | solution.py:21
  33.7 8.4 %collective-permute-start.4 = (bf16[4,4,32,128]{3,2,1,0:T(8,128)(2,1)S(1)}, bf16[4,4,32,128]{3,2,1,0:T(8,128)(2,1)S(1)}, u32[]{:S(2)}, u32[]{:S(2)}) collective-permute-start(bf16[4,4,32,128]{3,2,1,0:T(8,128)(2,1)S(1)} %reshape_squeeze.52), channel_id=1, source_target_pairs={{1,0},{2,1},{3,2},{4,3},{5,4},{6,5},{7,6},{9,8},{10,9},{11,10},{12... | collective-permute-start | bytes 393224 | tf_op jit(solution)/shard_map/ppermute | solution.py:21
  36.1 8.0 %copy-start.1 = (bf16[1,6,4,64,64]{4,3,2,1,0:T(8,128)(2,1)}, bf16[1,6,4,64,64]{4,3,2,1,0:T(8,128)(2,1)S(1)}, u32[]{:S(2)}) copy-start(bf16[1,6,4,64,64]{4,3,2,1,0:T(8,128)(2,1)S(1)} %maximum_bitcast_fusion) | copy-start | bytes 589828
  36.4 7.7 %copy-start.4 = (bf16[4,1,4,64,64]{4,3,2,0,1:T(8,128)(2,1)}, bf16[4,1,4,64,64]{4,3,2,0,1:T(8,128)(2,1)S(1)}, u32[]{:S(2)}) copy-start(bf16[4,1,4,64,64]{4,3,2,0,1:T(8,128)(2,1)S(1)} %broadcast_in_dim_reshape.33) | copy-start | bytes 393220
  36.5 7.6 %copy-start.2 = (bf16[1,6,4,64,64]{4,3,2,1,0:T(8,128)(2,1)}, bf16[1,6,4,64,64]{4,3,2,1,0:T(8,128)(2,1)S(1)}, u32[]{:S(2)}) copy-start(bf16[1,6,4,64,64]{4,3,2,1,0:T(8,128)(2,1)S(1)} %maximum_bitcast_fusion.1) | copy-start | bytes 589828
  42.3 1.8 %copy-start.5 = (bf16[4,1,4,64,64]{4,3,2,0,1:T(8,128)(2,1)}, bf16[4,1,4,64,64]{4,3,2,0,1:T(8,128)(2,1)S(1)}, u32[]{:S(2)}) copy-start(bf16[4,1,4,64,64]{4,3,2,0,1:T(8,128)(2,1)S(1)} %broadcast_in_dim_reshape.34) | copy-start | bytes 393220
  54.1 2.3 %copy-start = (bf16[16,9,64,64]{3,2,1,0:T(8,128)(2,1)S(1)}, bf16[16,9,64,64]{3,2,1,0:T(8,128)(2,1)}, u32[]{:S(2)}) copy-start(bf16[16,9,64,64]{3,2,1,0:T(8,128)(2,1)} %shard_map.55.own_ref) | copy-start | bytes 3538948
  59.1 29.2 %collective-permute-start.8 = (bf16[9,32,128]{2,1,0:T(8,128)(2,1)}, bf16[9,32,128]{2,1,0:T(8,128)(2,1)}, u32[]{:S(2)}, u32[]{:S(2)}) collective-permute-start(bf16[9,32,128]{2,1,0:T(8,128)(2,1)} %reshape_squeeze.56), channel_id=1, source_target_pairs={{0,9},{1,10},{2,11},{3,12},{4,13},{5,14},{6,15},{8,17},{9,18},{10,... | collective-permute-start | bytes 221192 | tf_op jit(solution)/shard_map/ppermute | solution.py:28
  62.0 41.2 %collective-permute-start.9 = (bf16[4,9,32,128]{3,2,1,0:T(8,128)(2,1)}, bf16[4,9,32,128]{3,2,1,0:T(8,128)(2,1)}, u32[]{:S(2)}, u32[]{:S(2)}) collective-permute-start(bf16[4,9,32,128]{3,2,1,0:T(8,128)(2,1)} %reshape_squeeze.57), channel_id=1, source_target_pairs={{0,8},{8,16},{16,24},{1,9},{9,17},{17,25},{2,10},{10,18},{18,26},{... | collective-permute-start | bytes 884744 | tf_op jit(solution)/shard_map/ppermute | solution.py:18
  65.8 19.1 %copy-start.6 = (bf16[4,1,9,64,64]{4,3,2,1,0:T(8,128)(2,1)S(1)}, bf16[4,1,9,64,64]{4,3,2,1,0:T(8,128)(2,1)}, u32[]{:S(2)}) copy-start(bf16[4,1,9,64,64]{4,3,2,1,0:T(8,128)(2,1)} %get-tuple-element.7) | copy-start | bytes 884740
  67.5 24.9 %collective-permute-start.10 = (bf16[9,32,128]{2,1,0:T(8,128)(2,1)}, bf16[9,32,128]{2,1,0:T(8,128)(2,1)}, u32[]{:S(2)}, u32[]{:S(2)}) collective-permute-start(bf16[9,32,128]{2,1,0:T(8,128)(2,1)} %reshape_squeeze.58), channel_id=1, source_target_pairs={{1,8},{2,9},{3,10},{4,11},{5,12},{6,13},{7,14},{9,16},{10,17},{11,... | collective-permute-start | bytes 221192 | tf_op jit(solution)/shard_map/ppermute | solution.py:28
  71.1 26.1 %collective-permute-start.11 = (bf16[9,32,128]{2,1,0:T(8,128)(2,1)}, bf16[9,32,128]{2,1,0:T(8,128)(2,1)}, u32[]{:S(2)}, u32[]{:S(2)}) collective-permute-start(bf16[9,32,128]{2,1,0:T(8,128)(2,1)} %reshape_squeeze.59), channel_id=1, source_target_pairs={{8,1},{9,2},{10,3},{11,4},{12,5},{13,6},{14,7},{16,9},{17,10},{18,... | collective-permute-start | bytes 221192 | tf_op jit(solution)/shard_map/ppermute | solution.py:28
  78.8 26.7 %collective-permute-start.12 = (bf16[4,9,32,128]{3,2,1,0:T(8,128)(2,1)}, bf16[4,9,32,128]{3,2,1,0:T(8,128)(2,1)}, u32[]{:S(2)}, u32[]{:S(2)}) collective-permute-start(bf16[4,9,32,128]{3,2,1,0:T(8,128)(2,1)} %reshape_squeeze.60), channel_id=1, source_target_pairs={{8,0},{16,8},{24,16},{9,1},{17,9},{25,17},{10,2},{18,10},{26,18},{... | collective-permute-start | bytes 884744 | tf_op jit(solution)/shard_map/ppermute | solution.py:18
  88.3 14.1 %collective-permute-start.13 = (bf16[9,32,128]{2,1,0:T(8,128)(2,1)}, bf16[9,32,128]{2,1,0:T(8,128)(2,1)S(1)}, u32[]{:S(2)}, u32[]{:S(2)}) collective-permute-start(bf16[9,32,128]{2,1,0:T(8,128)(2,1)} %reshape_squeeze.61), channel_id=1, source_target_pairs={{9,0},{10,1},{11,2},{12,3},{13,4},{14,5},{15,6},{17,8},{18,9},{19,... | collective-permute-start | bytes 221192 | tf_op jit(solution)/shard_map/ppermute | solution.py:28
  92.5 18.1 %collective-permute-start.14 = (bf16[4,9,32,128]{3,2,1,0:T(8,128)(2,1)}, bf16[4,9,32,128]{3,2,1,0:T(8,128)(2,1)}, u32[]{:S(2)}, u32[]{:S(2)}) collective-permute-start(bf16[4,9,32,128]{3,2,1,0:T(8,128)(2,1)} %reshape_squeeze.62), channel_id=1, source_target_pairs={{0,1},{1,2},{2,3},{3,4},{4,5},{5,6},{6,7},{8,9},{9,10},{10,11},{11... | collective-permute-start | bytes 884744 | tf_op jit(solution)/shard_map/ppermute | solution.py:21
  97.2 15.7 %collective-permute-start.15 = (bf16[4,9,32,128]{3,2,1,0:T(8,128)(2,1)}, bf16[4,9,32,128]{3,2,1,0:T(8,128)(2,1)}, u32[]{:S(2)}, u32[]{:S(2)}) collective-permute-start(bf16[4,9,32,128]{3,2,1,0:T(8,128)(2,1)} %reshape_squeeze.63), channel_id=1, source_target_pairs={{1,0},{2,1},{3,2},{4,3},{5,4},{6,5},{7,6},{9,8},{10,9},{11,10},{12... | collective-permute-start | bytes 884744 | tf_op jit(solution)/shard_map/ppermute | solution.py:21
  114.2 1.6 %copy-start.3 = (bf16[20,9,64,64]{3,2,1,0:T(8,128)(2,1)}, bf16[20,9,64,64]{3,2,1,0:T(8,128)(2,1)S(1)}, u32[]{:S(2)}) copy-start(bf16[20,9,64,64]{3,2,1,0:T(8,128)(2,1)S(1)} %constant_dynamic-update-slice_fusion.ring_ref) | copy-start | bytes 4423684

commit v7 on v6

--- a/solution.py
+++ b/solution.py
@@ -73,7 +73,7 @@
     )
 
 
-def ap_kernel(near_ref, slot_ref, a_ref, p_ref, out_ref, acc_ref):
+def ap_kernel(near_ref, slot_ref, a_ref, p_ref, out_ref, dense_ref, acc_ref):
     tiles, terms = a_ref.shape[0], a_ref.shape[1]
 
     def one_tile(t, carry):
@@ -87,7 +87,9 @@
                 prod = jnp.dot(a, p_ref[j, q], preferred_element_type=jnp.float32)
                 acc_ref[jnp.clip(e, 0, 8)] += prod * keep
 
-        out_ref[t] = acc_ref[...].astype(out_ref.dtype)
+        ap = acc_ref[...].astype(out_ref.dtype)
+        out_ref[t] = ap
+        dense_ref[t] = ap.reshape(dense_ref.shape[1:])
         return carry
 
     lax.fori_loop(0, tiles, one_tile, 0)
@@ -103,9 +105,8 @@
             def _():
                 pt = pt_ref[w * 4 + q]
                 for e in range(9):
-                    acc_ref[g + (e // 3) * 5 + e % 3] += jnp.dot(
-                        pt, ap_ref[t, e], preferred_element_type=jnp.float32
-                    )
+                    block = ap_ref[t, e].reshape(pt.shape)
+                    acc_ref[g + (e // 3) * 5 + e % 3] += jnp.dot(pt, block, preferred_element_type=jnp.float32)
 
         return carry
 
@@ -167,16 +168,19 @@
     slot = (slot_y[..., :, None] * 3 + slot_x[..., None, :]).reshape(n_r, n_c, terms, 4)
     slot = jnp.where((slot >= 0) & (slot < 9), slot, -1)
 
-    ap = pl.pallas_call(
+    ap, ap_dense = pl.pallas_call(
         ap_kernel,
-        out_shape=jax.ShapeDtypeStruct((n_r * n_c, 9, bs, bs), jnp.bfloat16),
+        out_shape=(
+            jax.ShapeDtypeStruct((n_r * n_c, 9, bs, bs), jnp.bfloat16),
+            jax.ShapeDtypeStruct((n_r * n_c, 9, bs * bs // 128, 128), jnp.bfloat16),
+        ),
         in_specs=[
             pl.BlockSpec(memory_space=pltpu.SMEM),
             pl.BlockSpec(memory_space=pltpu.SMEM),
             pl.BlockSpec(memory_space=pltpu.VMEM),
             pl.BlockSpec(memory_space=pltpu.VMEM),
         ],
-        out_specs=pl.BlockSpec(memory_space=pltpu.VMEM),
+        out_specs=(pl.BlockSpec(memory_space=pltpu.VMEM), pl.BlockSpec(memory_space=pltpu.VMEM)),
         scratch_shapes=[pltpu.VMEM((9, bs, bs), jnp.float32)],
     )(
         near.reshape(-1),
@@ -185,6 +189,7 @@
         p_ext.reshape(ext_r * ext_c, 4, bs, bs),
     )
     ap = ap.reshape(n_r, n_c, 9, bs, bs)
+    ap_dense = ap_dense.reshape((n_r, n_c) + ap_dense.shape[1:])
 
     o_r, o_c = n_r // 2, n_c // 2
     ey = y0 - 1 + jnp.arange(ext_r, dtype=jnp.int32)
@@ -224,7 +229,7 @@
         ring_of(target).reshape(-1),
         pick,
         ap.reshape(n_r * n_c, 9, bs, bs),
-        halo_ring(ap),
+        halo_ring(ap_dense),
         p_t,
     )
     return out.reshape(o_r, o_c, stencil, bs, bs)

time: 135 us -> 131 us (0.970)
  the two profiles are of different devices: /device:TPU:6 before, /device:TPU:9 now
where the time goes in v7:
time: 131 us; the launch traced here: 129 us
  starting transfers between devices  48.9 us (37%)
  Pallas kernels  42.7 us (33%)
  local copies, waits for them, and re-layouts  16.3 us (12%)
  other arithmetic  11.1 us (8%)
  waiting for transfers between devices  9.27 us (7%)
    ppermute x8, starting transfers between devices, shifted(): return lax.ppermute(piece, ('row', 'col'), pairs)  28.3 us
    pallas_call x1, Pallas kernels, body(): pl.pallas_call(coarse_kernel, out_shape=jax.ShapeDtypeStruct((o_r * o_c,...  27 us
    pallas_call x1, Pallas kernels, body(): pl.pallas_call(ap_kernel, out_shape=(jax.ShapeDtypeStruct((n_r * n_c, 9,...  15.8 us
    ppermute x4, starting transfers between devices, shifted(): return lax.ppermute(piece, 'col', pairs)  10.5 us
    ppermute x4, starting transfers between devices, shifted(): return lax.ppermute(piece, 'row', pairs)  10.1 us
    ppermute x4, waiting for transfers between devices, shifted(): return lax.ppermute(piece, 'row', pairs)  6.28 us
    ppermute x4, waiting for transfers between devices, shifted(): return lax.ppermute(piece, 'col', pairs)  2.97 us
    reduce_sum x1, other arithmetic, body(): jnp.sum(jnp.where(match[..., None, None], p_blocks[:, :, None], jnp.zeros...  2.77 us
  transfers between devices with their start and end apart: 16, of which 3 were waited for; matrix products, arithmetic and copies ran while one was open for 11% of the time, Pallas kernels for 0%

profile of v7, /device:TPU:9, one launch (start us, length us, event | category | flops | bytes accessed | tf_op | source)
XLA Modules:
  0.0 129.3 jit_solution(17027811375115999931)
XLA Ops:
  1.1 2.8 %select_reduce_fusion = bf16[4,4,4,64,64]{4,3,2,1,0:T(8,128)(2,1)S(1)} fusion(pred[4,4,4,4]{3,2,1,0:T(4,128)(4,1)S(1)} %broadcast_compare_fusion, bf16[4,4,4,64,64]{4,3,2,1,0:T(8,128)(2,1)} %param.7), kind=kLoop, calls=%fused_computation | loop fusion | flops 1835008 | bytes 1048832 | tf_op jit(solution)/shard_map/reduce_sum | solution.py:153
  4.0 4.5 %collective-permute-start.2 = (bf16[4,32,128]{2,1,0:T(8,128)(2,1)S(1)}, bf16[4,32,128]{2,1,0:T(8,128)(2,1)S(1)}, u32[]{:S(2)}, u32[]{:S(2)}) collective-permute-start(bf16[4,32,128]{2,1,0:T(8,128)(2,1)S(1)} %reshape_squeeze.26), channel_id=1, source_target_pairs={{1,8},{2,9},{3,10},{4,11},{5,12},{6,13},{7,14},{9,16},{10,17},{11,... | collective-permute-start | bytes 98312 | tf_op jit(solution)/shard_map/ppermute | solution.py:28
  8.6 1.9 %collective-permute-start.5 = (bf16[4,32,128]{2,1,0:T(8,128)(2,1)S(1)}, bf16[4,32,128]{2,1,0:T(8,128)(2,1)S(1)}, u32[]{:S(2)}, u32[]{:S(2)}) collective-permute-start(bf16[4,32,128]{2,1,0:T(8,128)(2,1)S(1)} %reshape_squeeze.29), channel_id=1, source_target_pairs={{8,1},{9,2},{10,3},{11,4},{12,5},{13,6},{14,7},{16,9},{17,10},{18,... | collective-permute-start | bytes 98312 | tf_op jit(solution)/shard_map/ppermute | solution.py:28
  10.6 1.9 %collective-permute-start.7 = (bf16[4,32,128]{2,1,0:T(8,128)(2,1)S(1)}, bf16[4,32,128]{2,1,0:T(8,128)(2,1)S(1)}, u32[]{:S(2)}, u32[]{:S(2)}) collective-permute-start(bf16[4,32,128]{2,1,0:T(8,128)(2,1)S(1)} %reshape_squeeze.31), channel_id=1, source_target_pairs={{9,0},{10,1},{11,2},{12,3},{13,4},{14,5},{15,6},{17,8},{18,9},{19,... | collective-permute-start | bytes 98312 | tf_op jit(solution)/shard_map/ppermute | solution.py:28
  12.7 5.6 %collective-permute-start = (bf16[4,32,128]{2,1,0:T(8,128)(2,1)S(1)}, bf16[4,32,128]{2,1,0:T(8,128)(2,1)S(1)}, u32[]{:S(2)}, u32[]{:S(2)}) collective-permute-start(bf16[4,32,128]{2,1,0:T(8,128)(2,1)S(1)} %reshape_squeeze.24), channel_id=1, source_target_pairs={{0,9},{1,10},{2,11},{3,12},{4,13},{5,14},{6,15},{8,17},{9,18},{10,... | collective-permute-start | bytes 98312 | tf_op jit(solution)/shard_map/ppermute | solution.py:28
  18.4 1.9 %collective-permute-start.6 = (bf16[4,4,32,128]{3,2,1,0:T(8,128)(2,1)S(1)}, bf16[4,4,32,128]{3,2,1,0:T(8,128)(2,1)S(1)}, u32[]{:S(2)}, u32[]{:S(2)}) collective-permute-start(bf16[4,4,32,128]{3,2,1,0:T(8,128)(2,1)S(1)} %reshape_squeeze.30), channel_id=1, source_target_pairs={{8,0},{16,8},{24,16},{9,1},{17,9},{25,17},{10,2},{18,10},{26,18},{... | collective-permute-start | bytes 393224 | tf_op jit(solution)/shard_map/ppermute | solution.py:18
  24.3 2.9 %collective-permute-start.4 = (bf16[4,4,32,128]{3,2,1,0:T(8,128)(2,1)S(1)}, bf16[4,4,32,128]{3,2,1,0:T(8,128)(2,1)S(1)}, u32[]{:S(2)}, u32[]{:S(2)}) collective-permute-start(bf16[4,4,32,128]{3,2,1,0:T(8,128)(2,1)S(1)} %reshape_squeeze.28), channel_id=1, source_target_pairs={{1,0},{2,1},{3,2},{4,3},{5,4},{6,5},{7,6},{9,8},{10,9},{11,10},{12... | collective-permute-start | bytes 393224 | tf_op jit(solution)/shard_map/ppermute | solution.py:21
  27.3 4.0 %collective-permute-start.1 = (bf16[4,4,32,128]{3,2,1,0:T(8,128)(2,1)S(1)}, bf16[4,4,32,128]{3,2,1,0:T(8,128)(2,1)S(1)}, u32[]{:S(2)}, u32[]{:S(2)}) collective-permute-start(bf16[4,4,32,128]{3,2,1,0:T(8,128)(2,1)S(1)} %reshape_squeeze.25), channel_id=1, source_target_pairs={{0,8},{8,16},{16,24},{1,9},{9,17},{17,25},{2,10},{10,18},{18,26},{... | collective-permute-start | bytes 393224 | tf_op jit(solution)/shard_map/ppermute | solution.py:18
  35.7 2.3 %collective-permute-start.3 = (bf16[4,4,32,128]{3,2,1,0:T(8,128)(2,1)S(1)}, bf16[4,4,32,128]{3,2,1,0:T(8,128)(2,1)S(1)}, u32[]{:S(2)}, u32[]{:S(2)}) collective-permute-start(bf16[4,4,32,128]{3,2,1,0:T(8,128)(2,1)S(1)} %reshape_squeeze.27), channel_id=1, source_target_pairs={{0,1},{1,2},{2,3},{3,4},{4,5},{5,6},{6,7},{8,9},{9,10},{10,11},{11... | collective-permute-start | bytes 393224 | tf_op jit(solution)/shard_map/ppermute | solution.py:21
  38.3 0.8 maximum_bitcast_fusion.1
  39.2 0.8 broadcast_in_dim_reshape.22
  41.0 1.6 %collective-permute-done.3 = bf16[4,4,32,128]{3,2,1,0:T(8,128)(2,1)S(1)} collective-permute-done((bf16[4,4,32,128]{3,2,1,0:T(8,128)(2,1)S(1)}, bf16[4,4,32,128]{3,2,1,0:T(8,128)(2,1)S(1)}, u32[]{:S(2)}, u32[]{:S(2)}) %collective-permute-start.3) | collective-permute-done | bytes 131104 | tf_op jit(solution)/shard_map/ppermute | solution.py:21
  42.6 0.8 broadcast_in_dim_reshape.21
  43.5 2.0 %fusion.20 = bf16[6,6,4,64,64]{3,4,2,1,0:T(8,128)(2,1)S(1)} fusion(bf16[1,6,4,64,64]{4,3,2,1,0:T(8,128)(2,1)} %maximum_bitcast_fusion.1, bf16[4,1,4,64,64]{4,3,2,1,0:T(8,128)(2,1)} %bitcast.87, bf16[4,4,4,64,64]{4,3,2,1,0:T(8,128)(2,1)S(1)} %select_reduce_fusion, bf16[4,1,4,64,64]{4,3,2,1,0:T(8,128)(2,1)} %bitcast.89, ...), kind=kLoop, calls=%fused_computation.135 | loop fusion | flops 2359296 | bytes 2359296 | tf_op jit(solution)/shard_map/transpose | solution.py:216
  45.5 1.8 %pad_maximum_fusion = bf16[6,6,4,64,64]{4,3,2,1,0:T(8,128)(2,1)} fusion(bf16[1,6,4,64,64]{4,3,2,1,0:T(8,128)(2,1)S(1)} %copy-done, bf16[4,1,4,64,64]{4,3,2,1,0:T(8,128)(2,1)S(1)} %bitcast.88, bf16[4,4,4,64,64]{4,3,2,1,0:T(8,128)(2,1)S(1)} %select_reduce_fusion, bf16[4,1,4,64,64]{4,3,2,1,0:T(8,128)(2,1)S(1)} %bitcast.90, ...), kind=kLoop, calls=%fused_computation.1 | loop fusion | flops 2359296 | bytes 2359296 | tf_op jit(solution)/shard_map/concatenate | solution.py:56
  47.3 15.8 %shard_map.55 = (bf16[16,9,64,64]{3,2,1,0:T(8,128)(2,1)}, bf16[16,9,32,128]{3,2,1,0:T(8,128)(2,1)}) custom-call(s32[144]{0:T(256)} %reshape.673.near_ref, s32[576]{0:T(1024)} %and_select_fusion.1.slot_ref, bf16[16,9,64,64]{3,2,1,0:T(8,128)(2,1)} %bitcast.91, bf16[36,4,64,64]{3,2,1,0:T(8,128)(2,1)} %bitcast.86), custom_call_target="tpu_custom_call" | custom-call | tf_op jit(solution)/shard_map/pallas_call | solution.py:171
  63.1 1.9 %fusion.15 = (bf16[4,9,32,128]{3,2,1,0:T(8,128)(2,1)}, bf16[4,9,32,128]{3,2,1,0:T(8,128)(2,1)S(1)}) fusion(bf16[16,9,32,128]{3,2,1,0:T(8,128)(2,1)} %get-tuple-element.8), kind=kLoop, calls=%fused_computation.130 | loop fusion | bytes 1179648 | tf_op jit(solution)/shard_map/slice | solution.py:43
  64.9 1.0 slice_bitcast_fusion.2
  66.0 2.6 %collective-permute-start.8 = (bf16[9,32,128]{2,1,0:T(8,128)(2,1)S(1)}, bf16[9,32,128]{2,1,0:T(8,128)(2,1)S(1)}, u32[]{:S(2)}, u32[]{:S(2)}) collective-permute-start(bf16[9,32,128]{2,1,0:T(8,128)(2,1)S(1)} %get-tuple-element.16), channel_id=1, source_target_pairs={{0,9},{1,10},{2,11},{3,12},{4,13},{5,14},{6,15},{8,17},{9,18},{10,... | collective-permute-start | bytes 221192 | tf_op jit(solution)/shard_map/ppermute | solution.py:28
  68.6 2.3 %collective-permute-start.9 = (bf16[4,9,32,128]{3,2,1,0:T(8,128)(2,1)S(1)}, bf16[4,9,32,128]{3,2,1,0:T(8,128)(2,1)S(1)}, u32[]{:S(2)}, u32[]{:S(2)}) collective-permute-start(bf16[4,9,32,128]{3,2,1,0:T(8,128)(2,1)S(1)} %get-tuple-element.18), channel_id=1, source_target_pairs={{0,8},{8,16},{16,24},{1,9},{9,17},{17,25},{2,10},{10,18},{18,26},{... | collective-permute-start | bytes 884744 | tf_op jit(solution)/shard_map/ppermute | solution.py:18
  70.9 0.9 slice_bitcast_fusion
  71.8 2.4 %copy.64 = bf16[6,6,4,64,64]{4,3,2,1,0:T(8,128)(2,1)} copy(bf16[6,6,4,64,64]{3,4,2,1,0:T(8,128)(2,1)S(1)} %fusion.20) | data formatting | bytes 2359296 | tf_op jit(solution)/shard_map/transpose | solution.py:216
  74.2 4.4 %collective-permute-start.13 = (bf16[9,32,128]{2,1,0:T(8,128)(2,1)S(1)}, bf16[9,32,128]{2,1,0:T(8,128)(2,1)S(1)}, u32[]{:S(2)}, u32[]{:S(2)}) collective-permute-start(bf16[9,32,128]{2,1,0:T(8,128)(2,1)S(1)} %get-tuple-element.13), channel_id=1, source_target_pairs={{9,0},{10,1},{11,2},{12,3},{13,4},{14,5},{15,6},{17,8},{18,9},{19,... | collective-permute-start | bytes 221192 | tf_op jit(solution)/shard_map/ppermute | solution.py:28
  78.6 1.9 %collective-permute-start.11 = (bf16[9,32,128]{2,1,0:T(8,128)(2,1)S(1)}, bf16[9,32,128]{2,1,0:T(8,128)(2,1)S(1)}, u32[]{:S(2)}, u32[]{:S(2)}) collective-permute-start(bf16[9,32,128]{2,1,0:T(8,128)(2,1)S(1)} %get-tuple-element.14), channel_id=1, source_target_pairs={{8,1},{9,2},{10,3},{11,4},{12,5},{13,6},{14,7},{16,9},{17,10},{18,... | collective-permute-start | bytes 221192 | tf_op jit(solution)/shard_map/ppermute | solution.py:28
  80.5 5.4 %collective-permute-start.10 = (bf16[9,32,128]{2,1,0:T(8,128)(2,1)S(1)}, bf16[9,32,128]{2,1,0:T(8,128)(2,1)S(1)}, u32[]{:S(2)}, u32[]{:S(2)}) collective-permute-start(bf16[9,32,128]{2,1,0:T(8,128)(2,1)S(1)} %get-tuple-element.15), channel_id=1, source_target_pairs={{1,8},{2,9},{3,10},{4,11},{5,12},{6,13},{7,14},{9,16},{10,17},{11,... | collective-permute-start | bytes 221192 | tf_op jit(solution)/shard_map/ppermute | solution.py:28
  86.0 1.9 %collective-permute-start.15 = (bf16[4,9,32,128]{3,2,1,0:T(8,128)(2,1)}, bf16[4,9,32,128]{3,2,1,0:T(8,128)(2,1)S(1)}, u32[]{:S(2)}, u32[]{:S(2)}) collective-permute-start(bf16[4,9,32,128]{3,2,1,0:T(8,128)(2,1)} %get-tuple-element.11), channel_id=1, source_target_pairs={{1,0},{2,1},{3,2},{4,3},{5,4},{6,5},{7,6},{9,8},{10,9},{11,10},{12... | collective-permute-start | bytes 884744 | tf_op jit(solution)/shard_map/ppermute | solution.py:21
  87.9 3.4 %collective-permute-start.14 = (bf16[4,9,32,128]{3,2,1,0:T(8,128)(2,1)}, bf16[4,9,32,128]{3,2,1,0:T(8,128)(2,1)S(1)}, u32[]{:S(2)}, u32[]{:S(2)}) collective-permute-start(bf16[4,9,32,128]{3,2,1,0:T(8,128)(2,1)} %get-tuple-element.12), channel_id=1, source_target_pairs={{0,1},{1,2},{2,3},{3,4},{4,5},{5,6},{6,7},{8,9},{9,10},{10,11},{11... | collective-permute-start | bytes 884744 | tf_op jit(solution)/shard_map/ppermute | solution.py:21
  91.4 1.9 %collective-permute-start.12 = (bf16[4,9,32,128]{3,2,1,0:T(8,128)(2,1)}, bf16[4,9,32,128]{3,2,1,0:T(8,128)(2,1)S(1)}, u32[]{:S(2)}, u32[]{:S(2)}) collective-permute-start(bf16[4,9,32,128]{3,2,1,0:T(8,128)(2,1)} %get-tuple-element.17), channel_id=1, source_target_pairs={{8,0},{16,8},{24,16},{9,1},{17,9},{25,17},{10,2},{18,10},{26,18},{... | collective-permute-start | bytes 884744 | tf_op jit(solution)/shard_map/ppermute | solution.py:18
  93.3 6.3 %collective-permute-done.12 = bf16[4,9,32,128]{3,2,1,0:T(8,128)(2,1)S(1)} collective-permute-done((bf16[4,9,32,128]{3,2,1,0:T(8,128)(2,1)}, bf16[4,9,32,128]{3,2,1,0:T(8,128)(2,1)S(1)}, u32[]{:S(2)}, u32[]{:S(2)}) %collective-permute-start.12) | collective-permute-done | bytes 294944 | tf_op jit(solution)/shard_map/ppermute | solution.py:18
  99.7 1.4 %collective-permute-done.14 = bf16[4,9,32,128]{3,2,1,0:T(8,128)(2,1)S(1)} collective-permute-done((bf16[4,9,32,128]{3,2,1,0:T(8,128)(2,1)}, bf16[4,9,32,128]{3,2,1,0:T(8,128)(2,1)S(1)}, u32[]{:S(2)}, u32[]{:S(2)}) %collective-permute-start.14) | collective-permute-done | bytes 294944 | tf_op jit(solution)/shard_map/ppermute | solution.py:21
  101.2 1.1 copy-done.5
  102.3 27.0 %shard_map.56 = bf16[4,25,64,64]{3,2,1,0:T(8,128)(2,1)} custom-call(s32[16]{0:T(128)} %reshape.669.own_where_ref, s32[64]{0:T(128)} %reshape.670.own_target_ref, s32[20]{0:T(128)} %pad_add_fusion.1.ring_where_ref, s32[80]{0:T(128)} %reshape.671.ring_target_ref, s32[100]{0:T(128)} %reshape.672.pick_ref, bf16[16,9,64,64]{3,2,1,0:T(8,128)(2,1)} %get-tuple-element.7.own_ref, ...), custom_call_target="tpu_custom_call" | custom-call | tf_op jit(solution)/shard_map/pallas_call | solution.py:219
  (120 shorter events, 11.0 us)
Async XLA Ops:
  3.9 18.7 %copy-start.6 = (s32[4,4,9]{2,1,0:T(4,128)S(1)}, s32[4,4,9]{2,1,0:T(4,128)}, u32[]{:S(2)}) copy-start(s32[4,4,9]{2,1,0:T(4,128)} %param.6) | copy-start | bytes 1732
  4.0 20.3 %collective-permute-start.2 = (bf16[4,32,128]{2,1,0:T(8,128)(2,1)S(1)}, bf16[4,32,128]{2,1,0:T(8,128)(2,1)S(1)}, u32[]{:S(2)}, u32[]{:S(2)}) collective-permute-start(bf16[4,32,128]{2,1,0:T(8,128)(2,1)S(1)} %reshape_squeeze.26), channel_id=1, source_target_pairs={{1,8},{2,9},{3,10},{4,11},{5,12},{6,13},{7,14},{9,16},{10,17},{11,... | collective-permute-start | bytes 98312 | tf_op jit(solution)/shard_map/ppermute | solution.py:28
  8.6 18.7 %collective-permute-start.5 = (bf16[4,32,128]{2,1,0:T(8,128)(2,1)S(1)}, bf16[4,32,128]{2,1,0:T(8,128)(2,1)S(1)}, u32[]{:S(2)}, u32[]{:S(2)}) collective-permute-start(bf16[4,32,128]{2,1,0:T(8,128)(2,1)S(1)} %reshape_squeeze.29), channel_id=1, source_target_pairs={{8,1},{9,2},{10,3},{11,4},{12,5},{13,6},{14,7},{16,9},{17,10},{18,... | collective-permute-start | bytes 98312 | tf_op jit(solution)/shard_map/ppermute | solution.py:28
  10.6 25.0 %collective-permute-start.7 = (bf16[4,32,128]{2,1,0:T(8,128)(2,1)S(1)}, bf16[4,32,128]{2,1,0:T(8,128)(2,1)S(1)}, u32[]{:S(2)}, u32[]{:S(2)}) collective-permute-start(bf16[4,32,128]{2,1,0:T(8,128)(2,1)S(1)} %reshape_squeeze.31), channel_id=1, source_target_pairs={{9,0},{10,1},{11,2},{12,3},{13,4},{14,5},{15,6},{17,8},{18,9},{19,... | collective-permute-start | bytes 98312 | tf_op jit(solution)/shard_map/ppermute | solution.py:28
  12.7 11.2 %copy-start.7 = (s32[2,2,25]{2,1,0:T(2,128)S(1)}, s32[2,2,25]{2,1,0:T(2,128)}, u32[]{:S(2)}) copy-start(s32[2,2,25]{2,1,0:T(2,128)} %param.9) | copy-start | bytes 1204
  12.7 25.4 %collective-permute-start = (bf16[4,32,128]{2,1,0:T(8,128)(2,1)S(1)}, bf16[4,32,128]{2,1,0:T(8,128)(2,1)S(1)}, u32[]{:S(2)}, u32[]{:S(2)}) collective-permute-start(bf16[4,32,128]{2,1,0:T(8,128)(2,1)S(1)} %reshape_squeeze.24), channel_id=1, source_target_pairs={{0,9},{1,10},{2,11},{3,12},{4,13},{5,14},{6,15},{8,17},{9,18},{10,... | collective-permute-start | bytes 98312 | tf_op jit(solution)/shard_map/ppermute | solution.py:28
  18.4 19.7 %collective-permute-start.6 = (bf16[4,4,32,128]{3,2,1,0:T(8,128)(2,1)S(1)}, bf16[4,4,32,128]{3,2,1,0:T(8,128)(2,1)S(1)}, u32[]{:S(2)}, u32[]{:S(2)}) collective-permute-start(bf16[4,4,32,128]{3,2,1,0:T(8,128)(2,1)S(1)} %reshape_squeeze.30), channel_id=1, source_target_pairs={{8,0},{16,8},{24,16},{9,1},{17,9},{25,17},{10,2},{18,10},{26,18},{... | collective-permute-start | bytes 393224 | tf_op jit(solution)/shard_map/ppermute | solution.py:18
  24.3 14.9 %collective-permute-start.4 = (bf16[4,4,32,128]{3,2,1,0:T(8,128)(2,1)S(1)}, bf16[4,4,32,128]{3,2,1,0:T(8,128)(2,1)S(1)}, u32[]{:S(2)}, u32[]{:S(2)}) collective-permute-start(bf16[4,4,32,128]{3,2,1,0:T(8,128)(2,1)S(1)} %reshape_squeeze.28), channel_id=1, source_target_pairs={{1,0},{2,1},{3,2},{4,3},{5,4},{6,5},{7,6},{9,8},{10,9},{11,10},{12... | collective-permute-start | bytes 393224 | tf_op jit(solution)/shard_map/ppermute | solution.py:21
  27.3 12.7 %collective-permute-start.1 = (bf16[4,4,32,128]{3,2,1,0:T(8,128)(2,1)S(1)}, bf16[4,4,32,128]{3,2,1,0:T(8,128)(2,1)S(1)}, u32[]{:S(2)}, u32[]{:S(2)}) collective-permute-start(bf16[4,4,32,128]{3,2,1,0:T(8,128)(2,1)S(1)} %reshape_squeeze.25), channel_id=1, source_target_pairs={{0,8},{8,16},{16,24},{1,9},{9,17},{17,25},{2,10},{10,18},{18,26},{... | collective-permute-start | bytes 393224 | tf_op jit(solution)/shard_map/ppermute | solution.py:18
  35.7 6.9 %collective-permute-start.3 = (bf16[4,4,32,128]{3,2,1,0:T(8,128)(2,1)S(1)}, bf16[4,4,32,128]{3,2,1,0:T(8,128)(2,1)S(1)}, u32[]{:S(2)}, u32[]{:S(2)}) collective-permute-start(bf16[4,4,32,128]{3,2,1,0:T(8,128)(2,1)S(1)} %reshape_squeeze.27), channel_id=1, source_target_pairs={{0,1},{1,2},{2,3},{3,4},{4,5},{5,6},{6,7},{8,9},{9,10},{10,11},{11... | collective-permute-start | bytes 393224 | tf_op jit(solution)/shard_map/ppermute | solution.py:21
  43.5 2.0 %copy-start = (bf16[1,6,4,64,64]{4,3,2,1,0:T(8,128)(2,1)S(1)}, bf16[1,6,4,64,64]{4,3,2,1,0:T(8,128)(2,1)}, u32[]{:S(2)}) copy-start(bf16[1,6,4,64,64]{4,3,2,1,0:T(8,128)(2,1)} %maximum_bitcast_fusion.1) | copy-start | bytes 589828
  43.5 2.0 %copy-start.1 = (bf16[1,6,4,64,64]{4,3,2,1,0:T(8,128)(2,1)S(1)}, bf16[1,6,4,64,64]{4,3,2,1,0:T(8,128)(2,1)}, u32[]{:S(2)}) copy-start(bf16[1,6,4,64,64]{4,3,2,1,0:T(8,128)(2,1)} %maximum_bitcast_fusion) | copy-start | bytes 589828
  43.5 2.0 %copy-start.2 = (bf16[4,1,4,64,64]{4,3,2,0,1:T(8,128)(2,1)S(1)}, bf16[4,1,4,64,64]{4,3,2,0,1:T(8,128)(2,1)}, u32[]{:S(2)}) copy-start(bf16[4,1,4,64,64]{4,3,2,0,1:T(8,128)(2,1)} %broadcast_in_dim_reshape.22) | copy-start | bytes 393220
  43.5 2.0 %copy-start.3 = (bf16[4,1,4,64,64]{4,3,2,0,1:T(8,128)(2,1)S(1)}, bf16[4,1,4,64,64]{4,3,2,0,1:T(8,128)(2,1)}, u32[]{:S(2)}) copy-start(bf16[4,1,4,64,64]{4,3,2,0,1:T(8,128)(2,1)} %broadcast_in_dim_reshape.21) | copy-start | bytes 393220
  63.1 7.8 %copy-start.4 = (bf16[16,9,32,128]{3,2,1,0:T(8,128)(2,1)S(1)}, bf16[16,9,32,128]{3,2,1,0:T(8,128)(2,1)}, u32[]{:S(2)}) copy-start(bf16[16,9,32,128]{3,2,1,0:T(8,128)(2,1)} %get-tuple-element.8) | copy-start | bytes 3538948
  66.0 20.0 %collective-permute-start.8 = (bf16[9,32,128]{2,1,0:T(8,128)(2,1)S(1)}, bf16[9,32,128]{2,1,0:T(8,128)(2,1)S(1)}, u32[]{:S(2)}, u32[]{:S(2)}) collective-permute-start(bf16[9,32,128]{2,1,0:T(8,128)(2,1)S(1)} %get-tuple-element.16), channel_id=1, source_target_pairs={{0,9},{1,10},{2,11},{3,12},{4,13},{5,14},{6,15},{8,17},{9,18},{10,... | collective-permute-start | bytes 221192 | tf_op jit(solution)/shard_map/ppermute | solution.py:28
  68.6 19.3 %collective-permute-start.9 = (bf16[4,9,32,128]{3,2,1,0:T(8,128)(2,1)S(1)}, bf16[4,9,32,128]{3,2,1,0:T(8,128)(2,1)S(1)}, u32[]{:S(2)}, u32[]{:S(2)}) collective-permute-start(bf16[4,9,32,128]{3,2,1,0:T(8,128)(2,1)S(1)} %get-tuple-element.18), channel_id=1, source_target_pairs={{0,8},{8,16},{16,24},{1,9},{9,17},{17,25},{2,10},{10,18},{18,26},{... | collective-permute-start | bytes 884744 | tf_op jit(solution)/shard_map/ppermute | solution.py:18
  74.2 25.5 %collective-permute-start.13 = (bf16[9,32,128]{2,1,0:T(8,128)(2,1)S(1)}, bf16[9,32,128]{2,1,0:T(8,128)(2,1)S(1)}, u32[]{:S(2)}, u32[]{:S(2)}) collective-permute-start(bf16[9,32,128]{2,1,0:T(8,128)(2,1)S(1)} %get-tuple-element.13), channel_id=1, source_target_pairs={{9,0},{10,1},{11,2},{12,3},{13,4},{14,5},{15,6},{17,8},{18,9},{19,... | collective-permute-start | bytes 221192 | tf_op jit(solution)/shard_map/ppermute | solution.py:28
  78.6 14.7 %collective-permute-start.11 = (bf16[9,32,128]{2,1,0:T(8,128)(2,1)S(1)}, bf16[9,32,128]{2,1,0:T(8,128)(2,1)S(1)}, u32[]{:S(2)}, u32[]{:S(2)}) collective-permute-start(bf16[9,32,128]{2,1,0:T(8,128)(2,1)S(1)} %get-tuple-element.14), channel_id=1, source_target_pairs={{8,1},{9,2},{10,3},{11,4},{12,5},{13,6},{14,7},{16,9},{17,10},{18,... | collective-permute-start | bytes 221192 | tf_op jit(solution)/shard_map/ppermute | solution.py:28
  80.5 10.8 %collective-permute-start.10 = (bf16[9,32,128]{2,1,0:T(8,128)(2,1)S(1)}, bf16[9,32,128]{2,1,0:T(8,128)(2,1)S(1)}, u32[]{:S(2)}, u32[]{:S(2)}) collective-permute-start(bf16[9,32,128]{2,1,0:T(8,128)(2,1)S(1)} %get-tuple-element.15), channel_id=1, source_target_pairs={{1,8},{2,9},{3,10},{4,11},{5,12},{6,13},{7,14},{9,16},{10,17},{11,... | collective-permute-start | bytes 221192 | tf_op jit(solution)/shard_map/ppermute | solution.py:28
  86.0 15.1 %collective-permute-start.15 = (bf16[4,9,32,128]{3,2,1,0:T(8,128)(2,1)}, bf16[4,9,32,128]{3,2,1,0:T(8,128)(2,1)S(1)}, u32[]{:S(2)}, u32[]{:S(2)}) collective-permute-start(bf16[4,9,32,128]{3,2,1,0:T(8,128)(2,1)} %get-tuple-element.11), channel_id=1, source_target_pairs={{1,0},{2,1},{3,2},{4,3},{5,4},{6,5},{7,6},{9,8},{10,9},{11,10},{12... | collective-permute-start | bytes 884744 | tf_op jit(solution)/shard_map/ppermute | solution.py:21
  87.9 13.1 %collective-permute-start.14 = (bf16[4,9,32,128]{3,2,1,0:T(8,128)(2,1)}, bf16[4,9,32,128]{3,2,1,0:T(8,128)(2,1)S(1)}, u32[]{:S(2)}, u32[]{:S(2)}) collective-permute-start(bf16[4,9,32,128]{3,2,1,0:T(8,128)(2,1)} %get-tuple-element.12), channel_id=1, source_target_pairs={{0,1},{1,2},{2,3},{3,4},{4,5},{5,6},{6,7},{8,9},{9,10},{10,11},{11... | collective-permute-start | bytes 884744 | tf_op jit(solution)/shard_map/ppermute | solution.py:21
  91.4 8.3 %collective-permute-start.12 = (bf16[4,9,32,128]{3,2,1,0:T(8,128)(2,1)}, bf16[4,9,32,128]{3,2,1,0:T(8,128)(2,1)S(1)}, u32[]{:S(2)}, u32[]{:S(2)}) collective-permute-start(bf16[4,9,32,128]{3,2,1,0:T(8,128)(2,1)} %get-tuple-element.17), channel_id=1, source_target_pairs={{8,0},{16,8},{24,16},{9,1},{17,9},{25,17},{10,2},{18,10},{26,18},{... | collective-permute-start | bytes 884744 | tf_op jit(solution)/shard_map/ppermute | solution.py:18
  101.1 1.2 copy-start.5

commit v8 on v7

--- a/solution.py
+++ b/solution.py
@@ -98,6 +98,7 @@
 def add_terms(where_ref, target_ref, ap_ref, pt_ref, acc_ref):
     def one_tile(t, carry):
         w = where_ref[t]
+        blocks = [ap_ref[t, e].reshape(pt_ref.shape[1:]) for e in range(9)]
         for q in range(4):
             g = target_ref[t * 4 + q]
 
@@ -105,8 +106,7 @@
             def _():
                 pt = pt_ref[w * 4 + q]
                 for e in range(9):
-                    block = ap_ref[t, e].reshape(pt.shape)
-                    acc_ref[g + (e // 3) * 5 + e % 3] += jnp.dot(pt, block, preferred_element_type=jnp.float32)
+                    acc_ref[g + (e // 3) * 5 + e % 3] += jnp.dot(pt, blocks[e], preferred_element_type=jnp.float32)
 
         return carry
 

time: 131 us -> 129 us (0.985)
  Pallas kernels: 42.7 us -> 41.1 us
    pallas_call x1, Pallas kernels: 27 us -> 25.3 us  [body(): pl.pallas_call(coarse_kernel, out_shape=jax.ShapeDtypeStruct((o_r * o_c,...]
  transfers between devices with their start and end apart: 16 -> 16, of which waited for: 3 -> 3; matrix products, arithmetic and copies ran while one was open for 11% -> 12% of each run, Pallas kernels for 0% -> 0%
where the time goes in v8:
time: 129 us; the launch traced here: 128 us
  starting transfers between devices  48.8 us (38%)
  Pallas kernels  41.1 us (32%)
  local copies, waits for them, and re-layouts  16.3 us (13%)
  other arithmetic  11.1 us (9%)
  waiting for transfers between devices  9.27 us (7%)
    ppermute x8, starting transfers between devices, shifted(): return lax.ppermute(piece, ('row', 'col'), pairs)  28.2 us
    pallas_call x1, Pallas kernels, body(): pl.pallas_call(coarse_kernel, out_shape=jax.ShapeDtypeStruct((o_r * o_c,...  25.3 us
    pallas_call x1, Pallas kernels, body(): pl.pallas_call(ap_kernel, out_shape=(jax.ShapeDtypeStruct((n_r * n_c, 9,...  15.8 us
    ppermute x4, starting transfers between devices, shifted(): return lax.ppermute(piece, 'col', pairs)  10.5 us
    ppermute x4, starting transfers between devices, shifted(): return lax.ppermute(piece, 'row', pairs)  10.1 us
    ppermute x4, waiting for transfers between devices, shifted(): return lax.ppermute(piece, 'row', pairs)  6.28 us
    ppermute x4, waiting for transfers between devices, shifted(): return lax.ppermute(piece, 'col', pairs)  2.97 us
    reduce_sum x1, other arithmetic, body(): jnp.sum(jnp.where(match[..., None, None], p_blocks[:, :, None], jnp.zeros...  2.77 us
  transfers between devices with their start and end apart: 16, of which 3 were waited for; matrix products, arithmetic and copies ran while one was open for 12% of the time, Pallas kernels for 0%

profile of v8, /device:TPU:9, one launch (start us, length us, event | category | flops | bytes accessed | tf_op | source)
XLA Modules:
  0.0 127.6 jit_solution(8051080049153087518)
XLA Ops:
  1.1 2.8 %select_reduce_fusion = bf16[4,4,4,64,64]{4,3,2,1,0:T(8,128)(2,1)S(1)} fusion(pred[4,4,4,4]{3,2,1,0:T(4,128)(4,1)S(1)} %broadcast_compare_fusion, bf16[4,4,4,64,64]{4,3,2,1,0:T(8,128)(2,1)} %param.7), kind=kLoop, calls=%fused_computation | loop fusion | flops 1835008 | bytes 1048832 | tf_op jit(solution)/shard_map/reduce_sum | solution.py:153
  4.0 4.5 %collective-permute-start.2 = (bf16[4,32,128]{2,1,0:T(8,128)(2,1)S(1)}, bf16[4,32,128]{2,1,0:T(8,128)(2,1)S(1)}, u32[]{:S(2)}, u32[]{:S(2)}) collective-permute-start(bf16[4,32,128]{2,1,0:T(8,128)(2,1)S(1)} %reshape_squeeze.26), channel_id=1, source_target_pairs={{1,8},{2,9},{3,10},{4,11},{5,12},{6,13},{7,14},{9,16},{10,17},{11,... | collective-permute-start | bytes 98312 | tf_op jit(solution)/shard_map/ppermute | solution.py:28
  8.6 1.9 %collective-permute-start.5 = (bf16[4,32,128]{2,1,0:T(8,128)(2,1)S(1)}, bf16[4,32,128]{2,1,0:T(8,128)(2,1)S(1)}, u32[]{:S(2)}, u32[]{:S(2)}) collective-permute-start(bf16[4,32,128]{2,1,0:T(8,128)(2,1)S(1)} %reshape_squeeze.29), channel_id=1, source_target_pairs={{8,1},{9,2},{10,3},{11,4},{12,5},{13,6},{14,7},{16,9},{17,10},{18,... | collective-permute-start | bytes 98312 | tf_op jit(solution)/shard_map/ppermute | solution.py:28
  10.6 1.9 %collective-permute-start.7 = (bf16[4,32,128]{2,1,0:T(8,128)(2,1)S(1)}, bf16[4,32,128]{2,1,0:T(8,128)(2,1)S(1)}, u32[]{:S(2)}, u32[]{:S(2)}) collective-permute-start(bf16[4,32,128]{2,1,0:T(8,128)(2,1)S(1)} %reshape_squeeze.31), channel_id=1, source_target_pairs={{9,0},{10,1},{11,2},{12,3},{13,4},{14,5},{15,6},{17,8},{18,9},{19,... | collective-permute-start | bytes 98312 | tf_op jit(solution)/shard_map/ppermute | solution.py:28
  12.7 5.6 %collective-permute-start = (bf16[4,32,128]{2,1,0:T(8,128)(2,1)S(1)}, bf16[4,32,128]{2,1,0:T(8,128)(2,1)S(1)}, u32[]{:S(2)}, u32[]{:S(2)}) collective-permute-start(bf16[4,32,128]{2,1,0:T(8,128)(2,1)S(1)} %reshape_squeeze.24), channel_id=1, source_target_pairs={{0,9},{1,10},{2,11},{3,12},{4,13},{5,14},{6,15},{8,17},{9,18},{10,... | collective-permute-start | bytes 98312 | tf_op jit(solution)/shard_map/ppermute | solution.py:28
  18.4 1.9 %collective-permute-start.6 = (bf16[4,4,32,128]{3,2,1,0:T(8,128)(2,1)S(1)}, bf16[4,4,32,128]{3,2,1,0:T(8,128)(2,1)S(1)}, u32[]{:S(2)}, u32[]{:S(2)}) collective-permute-start(bf16[4,4,32,128]{3,2,1,0:T(8,128)(2,1)S(1)} %reshape_squeeze.30), channel_id=1, source_target_pairs={{8,0},{16,8},{24,16},{9,1},{17,9},{25,17},{10,2},{18,10},{26,18},{... | collective-permute-start | bytes 393224 | tf_op jit(solution)/shard_map/ppermute | solution.py:18
  24.3 2.9 %collective-permute-start.4 = (bf16[4,4,32,128]{3,2,1,0:T(8,128)(2,1)S(1)}, bf16[4,4,32,128]{3,2,1,0:T(8,128)(2,1)S(1)}, u32[]{:S(2)}, u32[]{:S(2)}) collective-permute-start(bf16[4,4,32,128]{3,2,1,0:T(8,128)(2,1)S(1)} %reshape_squeeze.28), channel_id=1, source_target_pairs={{1,0},{2,1},{3,2},{4,3},{5,4},{6,5},{7,6},{9,8},{10,9},{11,10},{12... | collective-permute-start | bytes 393224 | tf_op jit(solution)/shard_map/ppermute | solution.py:21
  27.3 4.0 %collective-permute-start.1 = (bf16[4,4,32,128]{3,2,1,0:T(8,128)(2,1)S(1)}, bf16[4,4,32,128]{3,2,1,0:T(8,128)(2,1)S(1)}, u32[]{:S(2)}, u32[]{:S(2)}) collective-permute-start(bf16[4,4,32,128]{3,2,1,0:T(8,128)(2,1)S(1)} %reshape_squeeze.25), channel_id=1, source_target_pairs={{0,8},{8,16},{16,24},{1,9},{9,17},{17,25},{2,10},{10,18},{18,26},{... | collective-permute-start | bytes 393224 | tf_op jit(solution)/shard_map/ppermute | solution.py:18
  35.7 2.3 %collective-permute-start.3 = (bf16[4,4,32,128]{3,2,1,0:T(8,128)(2,1)S(1)}, bf16[4,4,32,128]{3,2,1,0:T(8,128)(2,1)S(1)}, u32[]{:S(2)}, u32[]{:S(2)}) collective-permute-start(bf16[4,4,32,128]{3,2,1,0:T(8,128)(2,1)S(1)} %reshape_squeeze.27), channel_id=1, source_target_pairs={{0,1},{1,2},{2,3},{3,4},{4,5},{5,6},{6,7},{8,9},{9,10},{10,11},{11... | collective-permute-start | bytes 393224 | tf_op jit(solution)/shard_map/ppermute | solution.py:21
  38.3 0.8 maximum_bitcast_fusion.1
  39.2 0.8 broadcast_in_dim_reshape.22
  41.0 1.6 %collective-permute-done.3 = bf16[4,4,32,128]{3,2,1,0:T(8,128)(2,1)S(1)} collective-permute-done((bf16[4,4,32,128]{3,2,1,0:T(8,128)(2,1)S(1)}, bf16[4,4,32,128]{3,2,1,0:T(8,128)(2,1)S(1)}, u32[]{:S(2)}, u32[]{:S(2)}) %collective-permute-start.3) | collective-permute-done | bytes 131104 | tf_op jit(solution)/shard_map/ppermute | solution.py:21
  42.6 0.8 broadcast_in_dim_reshape.21
  43.5 2.0 %fusion.20 = bf16[6,6,4,64,64]{3,4,2,1,0:T(8,128)(2,1)S(1)} fusion(bf16[1,6,4,64,64]{4,3,2,1,0:T(8,128)(2,1)} %maximum_bitcast_fusion.1, bf16[4,1,4,64,64]{4,3,2,1,0:T(8,128)(2,1)} %bitcast.87, bf16[4,4,4,64,64]{4,3,2,1,0:T(8,128)(2,1)S(1)} %select_reduce_fusion, bf16[4,1,4,64,64]{4,3,2,1,0:T(8,128)(2,1)} %bitcast.89, ...), kind=kLoop, calls=%fused_computation.135 | loop fusion | flops 2359296 | bytes 2359296 | tf_op jit(solution)/shard_map/transpose | solution.py:216
  45.5 1.8 %pad_maximum_fusion = bf16[6,6,4,64,64]{4,3,2,1,0:T(8,128)(2,1)} fusion(bf16[1,6,4,64,64]{4,3,2,1,0:T(8,128)(2,1)S(1)} %copy-done, bf16[4,1,4,64,64]{4,3,2,1,0:T(8,128)(2,1)S(1)} %bitcast.88, bf16[4,4,4,64,64]{4,3,2,1,0:T(8,128)(2,1)S(1)} %select_reduce_fusion, bf16[4,1,4,64,64]{4,3,2,1,0:T(8,128)(2,1)S(1)} %bitcast.90, ...), kind=kLoop, calls=%fused_computation.1 | loop fusion | flops 2359296 | bytes 2359296 | tf_op jit(solution)/shard_map/concatenate | solution.py:56
  47.3 15.8 %shard_map.55 = (bf16[16,9,64,64]{3,2,1,0:T(8,128)(2,1)}, bf16[16,9,32,128]{3,2,1,0:T(8,128)(2,1)}) custom-call(s32[144]{0:T(256)} %reshape.673.near_ref, s32[576]{0:T(1024)} %and_select_fusion.1.slot_ref, bf16[16,9,64,64]{3,2,1,0:T(8,128)(2,1)} %bitcast.91, bf16[36,4,64,64]{3,2,1,0:T(8,128)(2,1)} %bitcast.86), custom_call_target="tpu_custom_call" | custom-call | tf_op jit(solution)/shard_map/pallas_call | solution.py:171
  63.1 1.9 %fusion.15 = (bf16[4,9,32,128]{3,2,1,0:T(8,128)(2,1)}, bf16[4,9,32,128]{3,2,1,0:T(8,128)(2,1)S(1)}) fusion(bf16[16,9,32,128]{3,2,1,0:T(8,128)(2,1)} %get-tuple-element.8), kind=kLoop, calls=%fused_computation.130 | loop fusion | bytes 1179648 | tf_op jit(solution)/shard_map/slice | solution.py:43
  65.0 1.0 slice_bitcast_fusion.2
  66.0 2.6 %collective-permute-start.8 = (bf16[9,32,128]{2,1,0:T(8,128)(2,1)S(1)}, bf16[9,32,128]{2,1,0:T(8,128)(2,1)S(1)}, u32[]{:S(2)}, u32[]{:S(2)}) collective-permute-start(bf16[9,32,128]{2,1,0:T(8,128)(2,1)S(1)} %get-tuple-element.16), channel_id=1, source_target_pairs={{0,9},{1,10},{2,11},{3,12},{4,13},{5,14},{6,15},{8,17},{9,18},{10,... | collective-permute-start | bytes 221192 | tf_op jit(solution)/shard_map/ppermute | solution.py:28
  68.6 2.3 %collective-permute-start.9 = (bf16[4,9,32,128]{3,2,1,0:T(8,128)(2,1)S(1)}, bf16[4,9,32,128]{3,2,1,0:T(8,128)(2,1)S(1)}, u32[]{:S(2)}, u32[]{:S(2)}) collective-permute-start(bf16[4,9,32,128]{3,2,1,0:T(8,128)(2,1)S(1)} %get-tuple-element.18), channel_id=1, source_target_pairs={{0,8},{8,16},{16,24},{1,9},{9,17},{17,25},{2,10},{10,18},{18,26},{... | collective-permute-start | bytes 884744 | tf_op jit(solution)/shard_map/ppermute | solution.py:18
  70.9 0.9 slice_bitcast_fusion
  71.7 2.4 %copy.64 = bf16[6,6,4,64,64]{4,3,2,1,0:T(8,128)(2,1)} copy(bf16[6,6,4,64,64]{3,4,2,1,0:T(8,128)(2,1)S(1)} %fusion.20) | data formatting | bytes 2359296 | tf_op jit(solution)/shard_map/transpose | solution.py:216
  74.2 4.4 %collective-permute-start.13 = (bf16[9,32,128]{2,1,0:T(8,128)(2,1)S(1)}, bf16[9,32,128]{2,1,0:T(8,128)(2,1)S(1)}, u32[]{:S(2)}, u32[]{:S(2)}) collective-permute-start(bf16[9,32,128]{2,1,0:T(8,128)(2,1)S(1)} %get-tuple-element.13), channel_id=1, source_target_pairs={{9,0},{10,1},{11,2},{12,3},{13,4},{14,5},{15,6},{17,8},{18,9},{19,... | collective-permute-start | bytes 221192 | tf_op jit(solution)/shard_map/ppermute | solution.py:28
  78.6 1.9 %collective-permute-start.11 = (bf16[9,32,128]{2,1,0:T(8,128)(2,1)S(1)}, bf16[9,32,128]{2,1,0:T(8,128)(2,1)S(1)}, u32[]{:S(2)}, u32[]{:S(2)}) collective-permute-start(bf16[9,32,128]{2,1,0:T(8,128)(2,1)S(1)} %get-tuple-element.14), channel_id=1, source_target_pairs={{8,1},{9,2},{10,3},{11,4},{12,5},{13,6},{14,7},{16,9},{17,10},{18,... | collective-permute-start | bytes 221192 | tf_op jit(solution)/shard_map/ppermute | solution.py:28
  80.5 5.4 %collective-permute-start.10 = (bf16[9,32,128]{2,1,0:T(8,128)(2,1)S(1)}, bf16[9,32,128]{2,1,0:T(8,128)(2,1)S(1)}, u32[]{:S(2)}, u32[]{:S(2)}) collective-permute-start(bf16[9,32,128]{2,1,0:T(8,128)(2,1)S(1)} %get-tuple-element.15), channel_id=1, source_target_pairs={{1,8},{2,9},{3,10},{4,11},{5,12},{6,13},{7,14},{9,16},{10,17},{11,... | collective-permute-start | bytes 221192 | tf_op jit(solution)/shard_map/ppermute | solution.py:28
  86.0 1.9 %collective-permute-start.15 = (bf16[4,9,32,128]{3,2,1,0:T(8,128)(2,1)}, bf16[4,9,32,128]{3,2,1,0:T(8,128)(2,1)S(1)}, u32[]{:S(2)}, u32[]{:S(2)}) collective-permute-start(bf16[4,9,32,128]{3,2,1,0:T(8,128)(2,1)} %get-tuple-element.11), channel_id=1, source_target_pairs={{1,0},{2,1},{3,2},{4,3},{5,4},{6,5},{7,6},{9,8},{10,9},{11,10},{12... | collective-permute-start | bytes 884744 | tf_op jit(solution)/shard_map/ppermute | solution.py:21
  87.9 3.4 %collective-permute-start.14 = (bf16[4,9,32,128]{3,2,1,0:T(8,128)(2,1)}, bf16[4,9,32,128]{3,2,1,0:T(8,128)(2,1)S(1)}, u32[]{:S(2)}, u32[]{:S(2)}) collective-permute-start(bf16[4,9,32,128]{3,2,1,0:T(8,128)(2,1)} %get-tuple-element.12), channel_id=1, source_target_pairs={{0,1},{1,2},{2,3},{3,4},{4,5},{5,6},{6,7},{8,9},{9,10},{10,11},{11... | collective-permute-start | bytes 884744 | tf_op jit(solution)/shard_map/ppermute | solution.py:21
  91.3 1.9 %collective-permute-start.12 = (bf16[4,9,32,128]{3,2,1,0:T(8,128)(2,1)}, bf16[4,9,32,128]{3,2,1,0:T(8,128)(2,1)S(1)}, u32[]{:S(2)}, u32[]{:S(2)}) collective-permute-start(bf16[4,9,32,128]{3,2,1,0:T(8,128)(2,1)} %get-tuple-element.17), channel_id=1, source_target_pairs={{8,0},{16,8},{24,16},{9,1},{17,9},{25,17},{10,2},{18,10},{26,18},{... | collective-permute-start | bytes 884744 | tf_op jit(solution)/shard_map/ppermute | solution.py:18
  93.3 6.3 %collective-permute-done.12 = bf16[4,9,32,128]{3,2,1,0:T(8,128)(2,1)S(1)} collective-permute-done((bf16[4,9,32,128]{3,2,1,0:T(8,128)(2,1)}, bf16[4,9,32,128]{3,2,1,0:T(8,128)(2,1)S(1)}, u32[]{:S(2)}, u32[]{:S(2)}) %collective-permute-start.12) | collective-permute-done | bytes 294944 | tf_op jit(solution)/shard_map/ppermute | solution.py:18
  99.7 1.4 %collective-permute-done.14 = bf16[4,9,32,128]{3,2,1,0:T(8,128)(2,1)S(1)} collective-permute-done((bf16[4,9,32,128]{3,2,1,0:T(8,128)(2,1)}, bf16[4,9,32,128]{3,2,1,0:T(8,128)(2,1)S(1)}, u32[]{:S(2)}, u32[]{:S(2)}) %collective-permute-start.14) | collective-permute-done | bytes 294944 | tf_op jit(solution)/shard_map/ppermute | solution.py:21
  101.1 1.1 copy-done.5
  102.3 25.3 %shard_map.56 = bf16[4,25,64,64]{3,2,1,0:T(8,128)(2,1)} custom-call(s32[16]{0:T(128)} %reshape.669.own_where_ref, s32[64]{0:T(128)} %reshape.670.own_target_ref, s32[20]{0:T(128)} %pad_add_fusion.1.ring_where_ref, s32[80]{0:T(128)} %reshape.671.ring_target_ref, s32[100]{0:T(128)} %reshape.672.pick_ref, bf16[16,9,64,64]{3,2,1,0:T(8,128)(2,1)} %get-tuple-element.7.own_ref, ...), custom_call_target="tpu_custom_call" | custom-call | tf_op jit(solution)/shard_map/pallas_call | solution.py:219
  (120 shorter events, 11.0 us)
Async XLA Ops:
  3.9 18.7 %copy-start.6 = (s32[4,4,9]{2,1,0:T(4,128)S(1)}, s32[4,4,9]{2,1,0:T(4,128)}, u32[]{:S(2)}) copy-start(s32[4,4,9]{2,1,0:T(4,128)} %param.6) | copy-start | bytes 1732
  4.0 20.3 %collective-permute-start.2 = (bf16[4,32,128]{2,1,0:T(8,128)(2,1)S(1)}, bf16[4,32,128]{2,1,0:T(8,128)(2,1)S(1)}, u32[]{:S(2)}, u32[]{:S(2)}) collective-permute-start(bf16[4,32,128]{2,1,0:T(8,128)(2,1)S(1)} %reshape_squeeze.26), channel_id=1, source_target_pairs={{1,8},{2,9},{3,10},{4,11},{5,12},{6,13},{7,14},{9,16},{10,17},{11,... | collective-permute-start | bytes 98312 | tf_op jit(solution)/shard_map/ppermute | solution.py:28
  8.6 18.7 %collective-permute-start.5 = (bf16[4,32,128]{2,1,0:T(8,128)(2,1)S(1)}, bf16[4,32,128]{2,1,0:T(8,128)(2,1)S(1)}, u32[]{:S(2)}, u32[]{:S(2)}) collective-permute-start(bf16[4,32,128]{2,1,0:T(8,128)(2,1)S(1)} %reshape_squeeze.29), channel_id=1, source_target_pairs={{8,1},{9,2},{10,3},{11,4},{12,5},{13,6},{14,7},{16,9},{17,10},{18,... | collective-permute-start | bytes 98312 | tf_op jit(solution)/shard_map/ppermute | solution.py:28
  10.6 25.0 %collective-permute-start.7 = (bf16[4,32,128]{2,1,0:T(8,128)(2,1)S(1)}, bf16[4,32,128]{2,1,0:T(8,128)(2,1)S(1)}, u32[]{:S(2)}, u32[]{:S(2)}) collective-permute-start(bf16[4,32,128]{2,1,0:T(8,128)(2,1)S(1)} %reshape_squeeze.31), channel_id=1, source_target_pairs={{9,0},{10,1},{11,2},{12,3},{13,4},{14,5},{15,6},{17,8},{18,9},{19,... | collective-permute-start | bytes 98312 | tf_op jit(solution)/shard_map/ppermute | solution.py:28
  12.7 11.2 %copy-start.7 = (s32[2,2,25]{2,1,0:T(2,128)S(1)}, s32[2,2,25]{2,1,0:T(2,128)}, u32[]{:S(2)}) copy-start(s32[2,2,25]{2,1,0:T(2,128)} %param.9) | copy-start | bytes 1204
  12.7 25.4 %collective-permute-start = (bf16[4,32,128]{2,1,0:T(8,128)(2,1)S(1)}, bf16[4,32,128]{2,1,0:T(8,128)(2,1)S(1)}, u32[]{:S(2)}, u32[]{:S(2)}) collective-permute-start(bf16[4,32,128]{2,1,0:T(8,128)(2,1)S(1)} %reshape_squeeze.24), channel_id=1, source_target_pairs={{0,9},{1,10},{2,11},{3,12},{4,13},{5,14},{6,15},{8,17},{9,18},{10,... | collective-permute-start | bytes 98312 | tf_op jit(solution)/shard_map/ppermute | solution.py:28
  18.4 19.7 %collective-permute-start.6 = (bf16[4,4,32,128]{3,2,1,0:T(8,128)(2,1)S(1)}, bf16[4,4,32,128]{3,2,1,0:T(8,128)(2,1)S(1)}, u32[]{:S(2)}, u32[]{:S(2)}) collective-permute-start(bf16[4,4,32,128]{3,2,1,0:T(8,128)(2,1)S(1)} %reshape_squeeze.30), channel_id=1, source_target_pairs={{8,0},{16,8},{24,16},{9,1},{17,9},{25,17},{10,2},{18,10},{26,18},{... | collective-permute-start | bytes 393224 | tf_op jit(solution)/shard_map/ppermute | solution.py:18
  24.3 14.9 %collective-permute-start.4 = (bf16[4,4,32,128]{3,2,1,0:T(8,128)(2,1)S(1)}, bf16[4,4,32,128]{3,2,1,0:T(8,128)(2,1)S(1)}, u32[]{:S(2)}, u32[]{:S(2)}) collective-permute-start(bf16[4,4,32,128]{3,2,1,0:T(8,128)(2,1)S(1)} %reshape_squeeze.28), channel_id=1, source_target_pairs={{1,0},{2,1},{3,2},{4,3},{5,4},{6,5},{7,6},{9,8},{10,9},{11,10},{12... | collective-permute-start | bytes 393224 | tf_op jit(solution)/shard_map/ppermute | solution.py:21
  27.3 12.7 %collective-permute-start.1 = (bf16[4,4,32,128]{3,2,1,0:T(8,128)(2,1)S(1)}, bf16[4,4,32,128]{3,2,1,0:T(8,128)(2,1)S(1)}, u32[]{:S(2)}, u32[]{:S(2)}) collective-permute-start(bf16[4,4,32,128]{3,2,1,0:T(8,128)(2,1)S(1)} %reshape_squeeze.25), channel_id=1, source_target_pairs={{0,8},{8,16},{16,24},{1,9},{9,17},{17,25},{2,10},{10,18},{18,26},{... | collective-permute-start | bytes 393224 | tf_op jit(solution)/shard_map/ppermute | solution.py:18
  35.7 6.9 %collective-permute-start.3 = (bf16[4,4,32,128]{3,2,1,0:T(8,128)(2,1)S(1)}, bf16[4,4,32,128]{3,2,1,0:T(8,128)(2,1)S(1)}, u32[]{:S(2)}, u32[]{:S(2)}) collective-permute-start(bf16[4,4,32,128]{3,2,1,0:T(8,128)(2,1)S(1)} %reshape_squeeze.27), channel_id=1, source_target_pairs={{0,1},{1,2},{2,3},{3,4},{4,5},{5,6},{6,7},{8,9},{9,10},{10,11},{11... | collective-permute-start | bytes 393224 | tf_op jit(solution)/shard_map/ppermute | solution.py:21
  43.5 2.0 %copy-start = (bf16[1,6,4,64,64]{4,3,2,1,0:T(8,128)(2,1)S(1)}, bf16[1,6,4,64,64]{4,3,2,1,0:T(8,128)(2,1)}, u32[]{:S(2)}) copy-start(bf16[1,6,4,64,64]{4,3,2,1,0:T(8,128)(2,1)} %maximum_bitcast_fusion.1) | copy-start | bytes 589828
  43.5 2.0 %copy-start.1 = (bf16[1,6,4,64,64]{4,3,2,1,0:T(8,128)(2,1)S(1)}, bf16[1,6,4,64,64]{4,3,2,1,0:T(8,128)(2,1)}, u32[]{:S(2)}) copy-start(bf16[1,6,4,64,64]{4,3,2,1,0:T(8,128)(2,1)} %maximum_bitcast_fusion) | copy-start | bytes 589828
  43.5 2.0 %copy-start.2 = (bf16[4,1,4,64,64]{4,3,2,0,1:T(8,128)(2,1)S(1)}, bf16[4,1,4,64,64]{4,3,2,0,1:T(8,128)(2,1)}, u32[]{:S(2)}) copy-start(bf16[4,1,4,64,64]{4,3,2,0,1:T(8,128)(2,1)} %broadcast_in_dim_reshape.22) | copy-start | bytes 393220
  43.5 2.0 %copy-start.3 = (bf16[4,1,4,64,64]{4,3,2,0,1:T(8,128)(2,1)S(1)}, bf16[4,1,4,64,64]{4,3,2,0,1:T(8,128)(2,1)}, u32[]{:S(2)}) copy-start(bf16[4,1,4,64,64]{4,3,2,0,1:T(8,128)(2,1)} %broadcast_in_dim_reshape.21) | copy-start | bytes 393220
  63.1 7.8 %copy-start.4 = (bf16[16,9,32,128]{3,2,1,0:T(8,128)(2,1)S(1)}, bf16[16,9,32,128]{3,2,1,0:T(8,128)(2,1)}, u32[]{:S(2)}) copy-start(bf16[16,9,32,128]{3,2,1,0:T(8,128)(2,1)} %get-tuple-element.8) | copy-start | bytes 3538948
  66.0 19.9 %collective-permute-start.8 = (bf16[9,32,128]{2,1,0:T(8,128)(2,1)S(1)}, bf16[9,32,128]{2,1,0:T(8,128)(2,1)S(1)}, u32[]{:S(2)}, u32[]{:S(2)}) collective-permute-start(bf16[9,32,128]{2,1,0:T(8,128)(2,1)S(1)} %get-tuple-element.16), channel_id=1, source_target_pairs={{0,9},{1,10},{2,11},{3,12},{4,13},{5,14},{6,15},{8,17},{9,18},{10,... | collective-permute-start | bytes 221192 | tf_op jit(solution)/shard_map/ppermute | solution.py:28
  68.6 19.3 %collective-permute-start.9 = (bf16[4,9,32,128]{3,2,1,0:T(8,128)(2,1)S(1)}, bf16[4,9,32,128]{3,2,1,0:T(8,128)(2,1)S(1)}, u32[]{:S(2)}, u32[]{:S(2)}) collective-permute-start(bf16[4,9,32,128]{3,2,1,0:T(8,128)(2,1)S(1)} %get-tuple-element.18), channel_id=1, source_target_pairs={{0,8},{8,16},{16,24},{1,9},{9,17},{17,25},{2,10},{10,18},{18,26},{... | collective-permute-start | bytes 884744 | tf_op jit(solution)/shard_map/ppermute | solution.py:18
  74.2 25.5 %collective-permute-start.13 = (bf16[9,32,128]{2,1,0:T(8,128)(2,1)S(1)}, bf16[9,32,128]{2,1,0:T(8,128)(2,1)S(1)}, u32[]{:S(2)}, u32[]{:S(2)}) collective-permute-start(bf16[9,32,128]{2,1,0:T(8,128)(2,1)S(1)} %get-tuple-element.13), channel_id=1, source_target_pairs={{9,0},{10,1},{11,2},{12,3},{13,4},{14,5},{15,6},{17,8},{18,9},{19,... | collective-permute-start | bytes 221192 | tf_op jit(solution)/shard_map/ppermute | solution.py:28
  78.6 14.7 %collective-permute-start.11 = (bf16[9,32,128]{2,1,0:T(8,128)(2,1)S(1)}, bf16[9,32,128]{2,1,0:T(8,128)(2,1)S(1)}, u32[]{:S(2)}, u32[]{:S(2)}) collective-permute-start(bf16[9,32,128]{2,1,0:T(8,128)(2,1)S(1)} %get-tuple-element.14), channel_id=1, source_target_pairs={{8,1},{9,2},{10,3},{11,4},{12,5},{13,6},{14,7},{16,9},{17,10},{18,... | collective-permute-start | bytes 221192 | tf_op jit(solution)/shard_map/ppermute | solution.py:28
  80.5 10.8 %collective-permute-start.10 = (bf16[9,32,128]{2,1,0:T(8,128)(2,1)S(1)}, bf16[9,32,128]{2,1,0:T(8,128)(2,1)S(1)}, u32[]{:S(2)}, u32[]{:S(2)}) collective-permute-start(bf16[9,32,128]{2,1,0:T(8,128)(2,1)S(1)} %get-tuple-element.15), channel_id=1, source_target_pairs={{1,8},{2,9},{3,10},{4,11},{5,12},{6,13},{7,14},{9,16},{10,17},{11,... | collective-permute-start | bytes 221192 | tf_op jit(solution)/shard_map/ppermute | solution.py:28
  86.0 15.1 %collective-permute-start.15 = (bf16[4,9,32,128]{3,2,1,0:T(8,128)(2,1)}, bf16[4,9,32,128]{3,2,1,0:T(8,128)(2,1)S(1)}, u32[]{:S(2)}, u32[]{:S(2)}) collective-permute-start(bf16[4,9,32,128]{3,2,1,0:T(8,128)(2,1)} %get-tuple-element.11), channel_id=1, source_target_pairs={{1,0},{2,1},{3,2},{4,3},{5,4},{6,5},{7,6},{9,8},{10,9},{11,10},{12... | collective-permute-start | bytes 884744 | tf_op jit(solution)/shard_map/ppermute | solution.py:21
  87.9 13.1 %collective-permute-start.14 = (bf16[4,9,32,128]{3,2,1,0:T(8,128)(2,1)}, bf16[4,9,32,128]{3,2,1,0:T(8,128)(2,1)S(1)}, u32[]{:S(2)}, u32[]{:S(2)}) collective-permute-start(bf16[4,9,32,128]{3,2,1,0:T(8,128)(2,1)} %get-tuple-element.12), channel_id=1, source_target_pairs={{0,1},{1,2},{2,3},{3,4},{4,5},{5,6},{6,7},{8,9},{9,10},{10,11},{11... | collective-permute-start | bytes 884744 | tf_op jit(solution)/shard_map/ppermute | solution.py:21
  91.3 8.3 %collective-permute-start.12 = (bf16[4,9,32,128]{3,2,1,0:T(8,128)(2,1)}, bf16[4,9,32,128]{3,2,1,0:T(8,128)(2,1)S(1)}, u32[]{:S(2)}, u32[]{:S(2)}) collective-permute-start(bf16[4,9,32,128]{3,2,1,0:T(8,128)(2,1)} %get-tuple-element.17), channel_id=1, source_target_pairs={{8,0},{16,8},{24,16},{9,1},{17,9},{25,17},{10,2},{18,10},{26,18},{... | collective-permute-start | bytes 884744 | tf_op jit(solution)/shard_map/ppermute | solution.py:18
  101.1 1.2 copy-start.5

commit v9 on v8

--- a/solution.py
+++ b/solution.py
@@ -56,25 +56,27 @@
     return jnp.concatenate([first[None], middle, last[None]], axis=0)
 
 
-def halo_ring(x):
-    h = halo_pieces(x)
+def halo_ring(top, bottom, left, right):
     return jnp.concatenate(
         [
-            h["top_left"][None],
-            h["top"],
-            h["top_right"][None],
-            h["bottom_left"][None],
-            h["bottom"],
-            h["bottom_right"][None],
-            h["left"],
-            h["right"],
+            dense_shifted(bottom[-1], 1, 1)[None],
+            dense_shifted(bottom, 1, 0),
+            dense_shifted(bottom[0], 1, -1)[None],
+            dense_shifted(top[-1], -1, 1)[None],
+            dense_shifted(top, -1, 0),
+            dense_shifted(top[0], -1, -1)[None],
+            dense_shifted(right, 0, 1),
+            dense_shifted(left, 0, -1),
         ],
         axis=0,
     )
 
 
-def ap_kernel(near_ref, slot_ref, a_ref, p_ref, out_ref, dense_ref, acc_ref):
+def ap_kernel(near_ref, slot_ref, a_ref, p_ref, out_ref, top_ref, bottom_ref, left_ref, right_ref, acc_ref):
     tiles, terms = a_ref.shape[0], a_ref.shape[1]
+    n_c = top_ref.shape[0]
+    n_r = left_ref.shape[0]
+    dense = top_ref.shape[1:]
 
     def one_tile(t, carry):
         acc_ref[...] = jnp.zeros(acc_ref.shape, jnp.float32)
@@ -87,9 +89,19 @@
                 prod = jnp.dot(a, p_ref[j, q], preferred_element_type=jnp.float32)
                 acc_ref[jnp.clip(e, 0, 8)] += prod * keep
 
-        ap = acc_ref[...].astype(out_ref.dtype)
-        out_ref[t] = ap
-        dense_ref[t] = ap.reshape(dense_ref.shape[1:])
+        out_ref[t] = acc_ref[...].astype(out_ref.dtype)
+        row, col = t // n_c, t % n_c
+        for ref, at, index in (
+            (top_ref, row == 0, col),
+            (bottom_ref, row == n_r - 1, col),
+            (left_ref, col == 0, row),
+            (right_ref, col == n_c - 1, row),
+        ):
+
+            @pl.when(at)
+            def _():
+                ref[index] = out_ref[t].reshape(dense)
+
         return carry
 
     lax.fori_loop(0, tiles, one_tile, 0)
@@ -168,11 +180,15 @@
     slot = (slot_y[..., :, None] * 3 + slot_x[..., None, :]).reshape(n_r, n_c, terms, 4)
     slot = jnp.where((slot >= 0) & (slot < 9), slot, -1)
 
-    ap, ap_dense = pl.pallas_call(
+    dense = (9, bs * bs // 128, 128)
+    ap, top, bottom, left, right = pl.pallas_call(
         ap_kernel,
         out_shape=(
             jax.ShapeDtypeStruct((n_r * n_c, 9, bs, bs), jnp.bfloat16),
-            jax.ShapeDtypeStruct((n_r * n_c, 9, bs * bs // 128, 128), jnp.bfloat16),
+            jax.ShapeDtypeStruct((n_c,) + dense, jnp.bfloat16),
+            jax.ShapeDtypeStruct((n_c,) + dense, jnp.bfloat16),
+            jax.ShapeDtypeStruct((n_r,) + dense, jnp.bfloat16),
+            jax.ShapeDtypeStruct((n_r,) + dense, jnp.bfloat16),
         ),
         in_specs=[
             pl.BlockSpec(memory_space=pltpu.SMEM),
@@ -180,7 +196,7 @@
             pl.BlockSpec(memory_space=pltpu.VMEM),
             pl.BlockSpec(memory_space=pltpu.VMEM),
         ],
-        out_specs=(pl.BlockSpec(memory_space=pltpu.VMEM), pl.BlockSpec(memory_space=pltpu.VMEM)),
+        out_specs=tuple(pl.BlockSpec(memory_space=pltpu.VMEM) for _ in range(5)),
         scratch_shapes=[pltpu.VMEM((9, bs, bs), jnp.float32)],
     )(
         near.reshape(-1),
@@ -189,7 +205,6 @@
         p_ext.reshape(ext_r * ext_c, 4, bs, bs),
     )
     ap = ap.reshape(n_r, n_c, 9, bs, bs)
-    ap_dense = ap_dense.reshape((n_r, n_c) + ap_dense.shape[1:])
 
     o_r, o_c = n_r // 2, n_c // 2
     ey = y0 - 1 + jnp.arange(ext_r, dtype=jnp.int32)
@@ -229,7 +244,7 @@
         ring_of(target).reshape(-1),
         pick,
         ap.reshape(n_r * n_c, 9, bs, bs),
-        halo_ring(ap_dense),
+        halo_ring(top, bottom, left, right),
         p_t,
     )
     return out.reshape(o_r, o_c, stencil, bs, bs)

time: 129 us -> 132 us (1.023)
  the two profiles are of different devices: /device:TPU:9 before, /device:TPU:19 now
where the time goes in v9:
time: 132 us
  starting transfers between devices  50.2 us (38%)
  Pallas kernels  42 us (32%)
  local copies, waits for them, and re-layouts  15.2 us (12%)
  waiting for transfers between devices  13.8 us (10%)
  other arithmetic  9.55 us (7%)
    ppermute x8, starting transfers between devices, shifted(): return lax.ppermute(piece, ('row', 'col'), pairs)  27.9 us
    pallas_call x1, Pallas kernels, body(): pl.pallas_call(coarse_kernel, out_shape=jax.ShapeDtypeStruct((o_r * o_c,...  25.3 us
    pallas_call x1, Pallas kernels, body(): pl.pallas_call(ap_kernel, out_shape=(jax.ShapeDtypeStruct((n_r * n_c, 9,...  16.7 us
    ppermute x4, waiting for transfers between devices, shifted(): return lax.ppermute(piece, 'col', pairs)  13.7 us
    ppermute x4, starting transfers between devices, shifted(): return lax.ppermute(piece, 'col', pairs)  12.4 us
    ppermute x4, starting transfers between devices, shifted(): return lax.ppermute(piece, 'row', pairs)  9.9 us
    reduce_sum x1, other arithmetic, body(): jnp.sum(jnp.where(match[..., None, None], p_blocks[:, :, None], jnp.zeros...  2.77 us
  transfers between devices with their start and end apart: 16, of which 3 were waited for; matrix products, arithmetic and copies ran while one was open for 12% of the time, Pallas kernels for 0%

profile of v9, /device:TPU:19, one launch (start us, length us, event | category | flops | bytes accessed | tf_op | source)
XLA Modules:
  0.0 131.6 jit_solution(16156351186516068042)
XLA Ops:
  0.3 0.8 broadcast_compare_fusion
  1.1 2.8 %select_reduce_fusion = bf16[4,4,4,64,64]{4,3,2,1,0:T(8,128)(2,1)S(1)} fusion(pred[4,4,4,4]{3,2,1,0:T(4,128)(4,1)S(1)} %broadcast_compare_fusion, bf16[4,4,4,64,64]{4,3,2,1,0:T(8,128)(2,1)} %param.7), kind=kLoop, calls=%fused_computation | loop fusion | flops 1835008 | bytes 1048832 | tf_op jit(solution)/shard_map/reduce_sum | solution.py:165
  4.0 1.3 collective-permute-start
  5.4 1.3 collective-permute-start.2
  6.9 1.3 collective-permute-start.1
  8.3 6.5 %collective-permute-start.5 = (bf16[4,32,128]{2,1,0:T(8,128)(2,1)S(1)}, bf16[4,32,128]{2,1,0:T(8,128)(2,1)S(1)}, u32[]{:S(2)}, u32[]{:S(2)}) collective-permute-start(bf16[4,32,128]{2,1,0:T(8,128)(2,1)S(1)} %reshape_squeeze.29), channel_id=1, source_target_pairs={{8,1},{9,2},{10,3},{11,4},{12,5},{13,6},{14,7},{16,9},{17,10},{18,... | collective-permute-start | bytes 98312 | tf_op jit(solution)/shard_map/ppermute | solution.py:28
  14.9 5.3 %collective-permute-start.7 = (bf16[4,32,128]{2,1,0:T(8,128)(2,1)S(1)}, bf16[4,32,128]{2,1,0:T(8,128)(2,1)S(1)}, u32[]{:S(2)}, u32[]{:S(2)}) collective-permute-start(bf16[4,32,128]{2,1,0:T(8,128)(2,1)S(1)} %reshape_squeeze.31), channel_id=1, source_target_pairs={{9,0},{10,1},{11,2},{12,3},{13,4},{14,5},{15,6},{17,8},{18,9},{19,... | collective-permute-start | bytes 98312 | tf_op jit(solution)/shard_map/ppermute | solution.py:28
  24.1 2.4 %collective-permute-start.6 = (bf16[4,4,32,128]{3,2,1,0:T(8,128)(2,1)S(1)}, bf16[4,4,32,128]{3,2,1,0:T(8,128)(2,1)S(1)}, u32[]{:S(2)}, u32[]{:S(2)}) collective-permute-start(bf16[4,4,32,128]{3,2,1,0:T(8,128)(2,1)S(1)} %reshape_squeeze.30), channel_id=1, source_target_pairs={{8,0},{16,8},{24,16},{9,1},{17,9},{25,17},{10,2},{18,10},{26,18},{... | collective-permute-start | bytes 393224 | tf_op jit(solution)/shard_map/ppermute | solution.py:18
  26.6 1.9 %collective-permute-start.3 = (bf16[4,4,32,128]{3,2,1,0:T(8,128)(2,1)S(1)}, bf16[4,4,32,128]{3,2,1,0:T(8,128)(2,1)S(1)}, u32[]{:S(2)}, u32[]{:S(2)}) collective-permute-start(bf16[4,4,32,128]{3,2,1,0:T(8,128)(2,1)S(1)} %reshape_squeeze.27), channel_id=1, source_target_pairs={{0,1},{1,2},{2,3},{3,4},{4,5},{5,6},{6,7},{8,9},{9,10},{10,11},{11... | collective-permute-start | bytes 393224 | tf_op jit(solution)/shard_map/ppermute | solution.py:21
  29.3 0.7 reshape.666.near_ref
  30.7 0.7 reshape.664.ring_target_ref
  32.9 4.3 %collective-permute-start.4 = (bf16[4,4,32,128]{3,2,1,0:T(8,128)(2,1)S(1)}, bf16[4,4,32,128]{3,2,1,0:T(8,128)(2,1)S(1)}, u32[]{:S(2)}, u32[]{:S(2)}) collective-permute-start(bf16[4,4,32,128]{3,2,1,0:T(8,128)(2,1)S(1)} %reshape_squeeze.28), channel_id=1, source_target_pairs={{1,0},{2,1},{3,2},{4,3},{5,4},{6,5},{7,6},{9,8},{10,9},{11,10},{12... | collective-permute-start | bytes 393224 | tf_op jit(solution)/shard_map/ppermute | solution.py:21
  38.1 2.9 %collective-permute-done.4 = bf16[4,4,32,128]{3,2,1,0:T(8,128)(2,1)S(1)} collective-permute-done((bf16[4,4,32,128]{3,2,1,0:T(8,128)(2,1)S(1)}, bf16[4,4,32,128]{3,2,1,0:T(8,128)(2,1)S(1)}, u32[]{:S(2)}, u32[]{:S(2)}) %collective-permute-start.4) | collective-permute-done | bytes 131104 | tf_op jit(solution)/shard_map/ppermute | solution.py:21
  41.1 1.8 %pad_maximum_fusion = bf16[6,6,4,64,64]{4,3,2,1,0:T(8,128)(2,1)} fusion(bf16[1,6,4,64,64]{4,3,2,1,0:T(8,128)(2,1)S(1)} %maximum_bitcast_fusion.1, bf16[4,1,4,64,64]{4,3,2,1,0:T(8,128)(2,1)S(1)} %bitcast.80, bf16[4,4,4,64,64]{4,3,2,1,0:T(8,128)(2,1)S(1)} %select_reduce_fusion, bf16[4,1,4,64,64]{4,3,2,1,0:T(8,128)(2,1)S(1)} %bitcast.78, ...), kind=kLoop, calls=%fused_computation.1 | loop fusion | flops 2359296 | bytes 2359296 | tf_op jit(solution)/shard_map/concatenate | solution.py:56
  43.0 16.7 %shard_map.55 = (bf16[16,9,64,64]{3,2,1,0:T(8,128)(2,1)}, bf16[4,9,32,128]{3,2,1,0:T(8,128)(2,1)}, bf16[4,9,32,128]{3,2,1,0:T(8,128)(2,1)}, bf16[4,9,32,128]{3,2,1,0:T(8,128)(2,1)}, bf16[4,9,32,128]{3,2,1,0:T(8,128)(2,1)}) custom-call(s32[144]{0:T(256)} %reshape.666.near_ref, s32[576]{0:T(1024)} %and_select_fusion.1.slot_ref, ...), custom_call_target="tpu_custom_call" | custom-call | tf_op jit(solution)/shard_map/pallas_call | solution.py:184
  59.6 1.6 %slice_bitcast_fusion.2 = (bf16[9,32,128]{2,1,0:T(8,128)(2,1)}, bf16[9,32,128]{2,1,0:T(8,128)(2,1)}) fusion(bf16[4,9,32,128]{3,2,1,0:T(8,128)(2,1)} %get-tuple-element.11), kind=kLoop, calls=%fused_computation.17 | loop fusion | bytes 294912 | tf_op jit(solution)/shard_map/squeeze | solution.py:64
  61.2 1.3 collective-permute-start.9
  62.5 1.9 %fusion.19 = bf16[6,6,4,64,64]{3,4,2,1,0:T(8,128)(2,1)S(1)} fusion(bf16[1,6,4,64,64]{4,3,2,1,0:T(8,128)(2,1)} %copy-done.1, bf16[4,1,4,64,64]{4,3,2,1,0:T(8,128)(2,1)} %bitcast.81, bf16[4,4,4,64,64]{4,3,2,1,0:T(8,128)(2,1)S(1)} %select_reduce_fusion, bf16[4,1,4,64,64]{4,3,2,1,0:T(8,128)(2,1)} %bitcast.79, bf16[1,6,4,64,64]{4,3,2,1,0:T(8,128)(2,1)} %copy-done), kind=kLoop, calls=%fused_computation.132 | loop fusion | flops 2359296 | bytes 2359296 | tf_op jit(solution)/shard_map/transpose | solution.py:231
  64.4 1.3 collective-permute-start.8
  65.7 1.6 %slice_bitcast_fusion = (bf16[9,32,128]{2,1,0:T(8,128)(2,1)S(1)}, bf16[9,32,128]{2,1,0:T(8,128)(2,1)}) fusion(bf16[4,9,32,128]{3,2,1,0:T(8,128)(2,1)} %get-tuple-element.12), kind=kLoop, calls=%fused_computation.15 | loop fusion | bytes 294912 | tf_op jit(solution)/shard_map/squeeze | solution.py:67
  67.2 4.9 %collective-permute-start.12 = (bf16[4,9,32,128]{3,2,1,0:T(8,128)(2,1)}, bf16[4,9,32,128]{3,2,1,0:T(8,128)(2,1)S(1)}, u32[]{:S(2)}, u32[]{:S(2)}) collective-permute-start(bf16[4,9,32,128]{3,2,1,0:T(8,128)(2,1)} %get-tuple-element.12), channel_id=1, source_target_pairs={{8,0},{16,8},{24,16},{9,1},{17,9},{25,17},{10,2},{18,10},{26,18},{... | collective-permute-start | bytes 884744 | tf_op jit(solution)/shard_map/ppermute | solution.py:18
  72.2 1.3 collective-permute-start.10
  73.5 5.6 %collective-permute-start.11 = (bf16[9,32,128]{2,1,0:T(8,128)(2,1)}, bf16[9,32,128]{2,1,0:T(8,128)(2,1)S(1)}, u32[]{:S(2)}, u32[]{:S(2)}) collective-permute-start(bf16[9,32,128]{2,1,0:T(8,128)(2,1)} %get-tuple-element.26), channel_id=1, source_target_pairs={{8,1},{9,2},{10,3},{11,4},{12,5},{13,6},{14,7},{16,9},{17,10},{18,... | collective-permute-start | bytes 221192 | tf_op jit(solution)/shard_map/ppermute | solution.py:28
  79.0 2.5 %copy.60 = bf16[6,6,4,64,64]{4,3,2,1,0:T(8,128)(2,1)} copy(bf16[6,6,4,64,64]{3,4,2,1,0:T(8,128)(2,1)S(1)} %fusion.19) | data formatting | bytes 2359296 | tf_op jit(solution)/shard_map/transpose | solution.py:231
  81.5 5.3 %collective-permute-start.13 = (bf16[9,32,128]{2,1,0:T(8,128)(2,1)S(1)}, bf16[9,32,128]{2,1,0:T(8,128)(2,1)S(1)}, u32[]{:S(2)}, u32[]{:S(2)}) collective-permute-start(bf16[9,32,128]{2,1,0:T(8,128)(2,1)S(1)} %get-tuple-element.25), channel_id=1, source_target_pairs={{9,0},{10,1},{11,2},{12,3},{13,4},{14,5},{15,6},{17,8},{18,9},{19,... | collective-permute-start | bytes 221192 | tf_op jit(solution)/shard_map/ppermute | solution.py:28
  86.8 2.3 %collective-permute-start.14 = (bf16[4,9,32,128]{3,2,1,0:T(8,128)(2,1)}, bf16[4,9,32,128]{3,2,1,0:T(8,128)(2,1)S(1)}, u32[]{:S(2)}, u32[]{:S(2)}) collective-permute-start(bf16[4,9,32,128]{3,2,1,0:T(8,128)(2,1)} %get-tuple-element.13), channel_id=1, source_target_pairs={{0,1},{1,2},{2,3},{3,4},{4,5},{5,6},{6,7},{8,9},{9,10},{10,11},{11... | collective-permute-start | bytes 884744 | tf_op jit(solution)/shard_map/ppermute | solution.py:21
  89.1 1.0 constant_dynamic-update-slice_fusion.3
  90.2 3.9 %collective-permute-start.15 = (bf16[4,9,32,128]{3,2,1,0:T(8,128)(2,1)}, bf16[4,9,32,128]{3,2,1,0:T(8,128)(2,1)S(1)}, u32[]{:S(2)}, u32[]{:S(2)}) collective-permute-start(bf16[4,9,32,128]{3,2,1,0:T(8,128)(2,1)} %get-tuple-element.14), channel_id=1, source_target_pairs={{1,0},{2,1},{3,2},{4,3},{5,4},{6,5},{7,6},{9,8},{10,9},{11,10},{12... | collective-permute-start | bytes 884744 | tf_op jit(solution)/shard_map/ppermute | solution.py:21
  94.2 4.5 %collective-permute-done.14 = bf16[4,9,32,128]{3,2,1,0:T(8,128)(2,1)S(1)} collective-permute-done((bf16[4,9,32,128]{3,2,1,0:T(8,128)(2,1)}, bf16[4,9,32,128]{3,2,1,0:T(8,128)(2,1)S(1)}, u32[]{:S(2)}, u32[]{:S(2)}) %collective-permute-start.14) | collective-permute-done | bytes 294944 | tf_op jit(solution)/shard_map/ppermute | solution.py:21
  98.8 6.3 %collective-permute-done.15 = bf16[4,9,32,128]{3,2,1,0:T(8,128)(2,1)S(1)} collective-permute-done((bf16[4,9,32,128]{3,2,1,0:T(8,128)(2,1)}, bf16[4,9,32,128]{3,2,1,0:T(8,128)(2,1)S(1)}, u32[]{:S(2)}, u32[]{:S(2)}) %collective-permute-start.15) | collective-permute-done | bytes 294944 | tf_op jit(solution)/shard_map/ppermute | solution.py:21
  105.1 1.2 copy-done.4
  106.3 25.3 %shard_map.56 = bf16[4,25,64,64]{3,2,1,0:T(8,128)(2,1)} custom-call(s32[16]{0:T(128)} %reshape.662.own_where_ref, s32[64]{0:T(128)} %reshape.663.own_target_ref, s32[20]{0:T(128)} %pad_add_fusion.1.ring_where_ref, s32[80]{0:T(128)} %reshape.664.ring_target_ref, s32[100]{0:T(128)} %reshape.665.pick_ref, bf16[16,9,64,64]{3,2,1,0:T(8,128)(2,1)} %get-tuple-element.10.own_ref, ...), custom_call_target="tpu_custom_call" | custom-call | tf_op jit(solution)/shard_map/pallas_call | solution.py:234
  (117 shorter events, 8.4 us)
Async XLA Ops:
  1.1 19.9 %copy-start.5 = (s32[4,4,9]{2,1,0:T(4,128)S(1)}, s32[4,4,9]{2,1,0:T(4,128)}, u32[]{:S(2)}) copy-start(s32[4,4,9]{2,1,0:T(4,128)} %param.6) | copy-start | bytes 1732
  3.8 19.8 %copy-start.6 = (s32[2,2,25]{2,1,0:T(2,128)S(1)}, s32[2,2,25]{2,1,0:T(2,128)}, u32[]{:S(2)}) copy-start(s32[2,2,25]{2,1,0:T(2,128)} %param.9) | copy-start | bytes 1204
  4.0 20.1 %collective-permute-start = (bf16[4,32,128]{2,1,0:T(8,128)(2,1)S(1)}, bf16[4,32,128]{2,1,0:T(8,128)(2,1)S(1)}, u32[]{:S(2)}, u32[]{:S(2)}) collective-permute-start(bf16[4,32,128]{2,1,0:T(8,128)(2,1)S(1)} %reshape_squeeze.24), channel_id=1, source_target_pairs={{0,9},{1,10},{2,11},{3,12},{4,13},{5,14},{6,15},{8,17},{9,18},{10,... | collective-permute-start | bytes 98312 | tf_op jit(solution)/shard_map/ppermute | solution.py:28
  5.4 21.2 %collective-permute-start.2 = (bf16[4,32,128]{2,1,0:T(8,128)(2,1)S(1)}, bf16[4,32,128]{2,1,0:T(8,128)(2,1)S(1)}, u32[]{:S(2)}, u32[]{:S(2)}) collective-permute-start(bf16[4,32,128]{2,1,0:T(8,128)(2,1)S(1)} %reshape_squeeze.26), channel_id=1, source_target_pairs={{1,8},{2,9},{3,10},{4,11},{5,12},{6,13},{7,14},{9,16},{10,17},{11,... | collective-permute-start | bytes 98312 | tf_op jit(solution)/shard_map/ppermute | solution.py:28
  6.9 30.5 %collective-permute-start.1 = (bf16[4,4,32,128]{3,2,1,0:T(8,128)(2,1)S(1)}, bf16[4,4,32,128]{3,2,1,0:T(8,128)(2,1)S(1)}, u32[]{:S(2)}, u32[]{:S(2)}) collective-permute-start(bf16[4,4,32,128]{3,2,1,0:T(8,128)(2,1)S(1)} %reshape_squeeze.25), channel_id=1, source_target_pairs={{0,8},{8,16},{16,24},{1,9},{9,17},{17,25},{2,10},{10,18},{18,26},{... | collective-permute-start | bytes 393224 | tf_op jit(solution)/shard_map/ppermute | solution.py:18
  8.3 24.6 %collective-permute-start.5 = (bf16[4,32,128]{2,1,0:T(8,128)(2,1)S(1)}, bf16[4,32,128]{2,1,0:T(8,128)(2,1)S(1)}, u32[]{:S(2)}, u32[]{:S(2)}) collective-permute-start(bf16[4,32,128]{2,1,0:T(8,128)(2,1)S(1)} %reshape_squeeze.29), channel_id=1, source_target_pairs={{8,1},{9,2},{10,3},{11,4},{12,5},{13,6},{14,7},{16,9},{17,10},{18,... | collective-permute-start | bytes 98312 | tf_op jit(solution)/shard_map/ppermute | solution.py:28
  14.9 22.3 %collective-permute-start.7 = (bf16[4,32,128]{2,1,0:T(8,128)(2,1)S(1)}, bf16[4,32,128]{2,1,0:T(8,128)(2,1)S(1)}, u32[]{:S(2)}, u32[]{:S(2)}) collective-permute-start(bf16[4,32,128]{2,1,0:T(8,128)(2,1)S(1)} %reshape_squeeze.31), channel_id=1, source_target_pairs={{9,0},{10,1},{11,2},{12,3},{13,4},{14,5},{15,6},{17,8},{18,9},{19,... | collective-permute-start | bytes 98312 | tf_op jit(solution)/shard_map/ppermute | solution.py:28
  24.1 13.5 %collective-permute-start.6 = (bf16[4,4,32,128]{3,2,1,0:T(8,128)(2,1)S(1)}, bf16[4,4,32,128]{3,2,1,0:T(8,128)(2,1)S(1)}, u32[]{:S(2)}, u32[]{:S(2)}) collective-permute-start(bf16[4,4,32,128]{3,2,1,0:T(8,128)(2,1)S(1)} %reshape_squeeze.30), channel_id=1, source_target_pairs={{8,0},{16,8},{24,16},{9,1},{17,9},{25,17},{10,2},{18,10},{26,18},{... | collective-permute-start | bytes 393224 | tf_op jit(solution)/shard_map/ppermute | solution.py:18
  26.6 11.2 %collective-permute-start.3 = (bf16[4,4,32,128]{3,2,1,0:T(8,128)(2,1)S(1)}, bf16[4,4,32,128]{3,2,1,0:T(8,128)(2,1)S(1)}, u32[]{:S(2)}, u32[]{:S(2)}) collective-permute-start(bf16[4,4,32,128]{3,2,1,0:T(8,128)(2,1)S(1)} %reshape_squeeze.27), channel_id=1, source_target_pairs={{0,1},{1,2},{2,3},{3,4},{4,5},{5,6},{6,7},{8,9},{9,10},{10,11},{11... | collective-permute-start | bytes 393224 | tf_op jit(solution)/shard_map/ppermute | solution.py:21
  32.9 8.0 %collective-permute-start.4 = (bf16[4,4,32,128]{3,2,1,0:T(8,128)(2,1)S(1)}, bf16[4,4,32,128]{3,2,1,0:T(8,128)(2,1)S(1)}, u32[]{:S(2)}, u32[]{:S(2)}) collective-permute-start(bf16[4,4,32,128]{3,2,1,0:T(8,128)(2,1)S(1)} %reshape_squeeze.28), channel_id=1, source_target_pairs={{1,0},{2,1},{3,2},{4,3},{5,4},{6,5},{7,6},{9,8},{10,9},{11,10},{12... | collective-permute-start | bytes 393224 | tf_op jit(solution)/shard_map/ppermute | solution.py:21
  37.6 5.3 %copy-start = (bf16[1,6,4,64,64]{4,3,2,1,0:T(8,128)(2,1)}, bf16[1,6,4,64,64]{4,3,2,1,0:T(8,128)(2,1)S(1)}, u32[]{:S(2)}) copy-start(bf16[1,6,4,64,64]{4,3,2,1,0:T(8,128)(2,1)S(1)} %maximum_bitcast_fusion) | copy-start | bytes 589828
  37.9 5.0 %copy-start.2 = (bf16[4,1,4,64,64]{4,3,2,0,1:T(8,128)(2,1)}, bf16[4,1,4,64,64]{4,3,2,0,1:T(8,128)(2,1)S(1)}, u32[]{:S(2)}) copy-start(bf16[4,1,4,64,64]{4,3,2,0,1:T(8,128)(2,1)S(1)} %broadcast_in_dim_reshape.21) | copy-start | bytes 393220
  38.0 4.9 %copy-start.1 = (bf16[1,6,4,64,64]{4,3,2,1,0:T(8,128)(2,1)}, bf16[1,6,4,64,64]{4,3,2,1,0:T(8,128)(2,1)S(1)}, u32[]{:S(2)}) copy-start(bf16[1,6,4,64,64]{4,3,2,1,0:T(8,128)(2,1)S(1)} %maximum_bitcast_fusion.1) | copy-start | bytes 589828
  41.1 1.9 %copy-start.3 = (bf16[4,1,4,64,64]{4,3,2,0,1:T(8,128)(2,1)}, bf16[4,1,4,64,64]{4,3,2,0,1:T(8,128)(2,1)S(1)}, u32[]{:S(2)}) copy-start(bf16[4,1,4,64,64]{4,3,2,0,1:T(8,128)(2,1)S(1)} %broadcast_in_dim_reshape.22) | copy-start | bytes 393220
  61.2 25.6 %collective-permute-start.9 = (bf16[4,9,32,128]{3,2,1,0:T(8,128)(2,1)}, bf16[4,9,32,128]{3,2,1,0:T(8,128)(2,1)}, u32[]{:S(2)}, u32[]{:S(2)}) collective-permute-start(bf16[4,9,32,128]{3,2,1,0:T(8,128)(2,1)} %get-tuple-element.11), channel_id=1, source_target_pairs={{0,8},{8,16},{16,24},{1,9},{9,17},{17,25},{2,10},{10,18},{18,26},{... | collective-permute-start | bytes 884744 | tf_op jit(solution)/shard_map/ppermute | solution.py:18
  64.4 17.1 %collective-permute-start.8 = (bf16[9,32,128]{2,1,0:T(8,128)(2,1)}, bf16[9,32,128]{2,1,0:T(8,128)(2,1)S(1)}, u32[]{:S(2)}, u32[]{:S(2)}) collective-permute-start(bf16[9,32,128]{2,1,0:T(8,128)(2,1)} %get-tuple-element.28), channel_id=1, source_target_pairs={{0,9},{1,10},{2,11},{3,12},{4,13},{5,14},{6,15},{8,17},{9,18},{10,... | collective-permute-start | bytes 221192 | tf_op jit(solution)/shard_map/ppermute | solution.py:28
  67.2 26.9 %collective-permute-start.12 = (bf16[4,9,32,128]{3,2,1,0:T(8,128)(2,1)}, bf16[4,9,32,128]{3,2,1,0:T(8,128)(2,1)S(1)}, u32[]{:S(2)}, u32[]{:S(2)}) collective-permute-start(bf16[4,9,32,128]{3,2,1,0:T(8,128)(2,1)} %get-tuple-element.12), channel_id=1, source_target_pairs={{8,0},{16,8},{24,16},{9,1},{17,9},{25,17},{10,2},{18,10},{26,18},{... | collective-permute-start | bytes 884744 | tf_op jit(solution)/shard_map/ppermute | solution.py:18
  72.2 18.0 %collective-permute-start.10 = (bf16[9,32,128]{2,1,0:T(8,128)(2,1)}, bf16[9,32,128]{2,1,0:T(8,128)(2,1)S(1)}, u32[]{:S(2)}, u32[]{:S(2)}) collective-permute-start(bf16[9,32,128]{2,1,0:T(8,128)(2,1)} %get-tuple-element.27), channel_id=1, source_target_pairs={{1,8},{2,9},{3,10},{4,11},{5,12},{6,13},{7,14},{9,16},{10,17},{11,... | collective-permute-start | bytes 221192 | tf_op jit(solution)/shard_map/ppermute | solution.py:28
  73.5 20.6 %collective-permute-start.11 = (bf16[9,32,128]{2,1,0:T(8,128)(2,1)}, bf16[9,32,128]{2,1,0:T(8,128)(2,1)S(1)}, u32[]{:S(2)}, u32[]{:S(2)}) collective-permute-start(bf16[9,32,128]{2,1,0:T(8,128)(2,1)} %get-tuple-element.26), channel_id=1, source_target_pairs={{8,1},{9,2},{10,3},{11,4},{12,5},{13,6},{14,7},{16,9},{17,10},{18,... | collective-permute-start | bytes 221192 | tf_op jit(solution)/shard_map/ppermute | solution.py:28
  81.5 12.7 %collective-permute-start.13 = (bf16[9,32,128]{2,1,0:T(8,128)(2,1)S(1)}, bf16[9,32,128]{2,1,0:T(8,128)(2,1)S(1)}, u32[]{:S(2)}, u32[]{:S(2)}) collective-permute-start(bf16[9,32,128]{2,1,0:T(8,128)(2,1)S(1)} %get-tuple-element.25), channel_id=1, source_target_pairs={{9,0},{10,1},{11,2},{12,3},{13,4},{14,5},{15,6},{17,8},{18,9},{19,... | collective-permute-start | bytes 221192 | tf_op jit(solution)/shard_map/ppermute | solution.py:28
  86.8 11.9 %collective-permute-start.14 = (bf16[4,9,32,128]{3,2,1,0:T(8,128)(2,1)}, bf16[4,9,32,128]{3,2,1,0:T(8,128)(2,1)S(1)}, u32[]{:S(2)}, u32[]{:S(2)}) collective-permute-start(bf16[4,9,32,128]{3,2,1,0:T(8,128)(2,1)} %get-tuple-element.13), channel_id=1, source_target_pairs={{0,1},{1,2},{2,3},{3,4},{4,5},{5,6},{6,7},{8,9},{9,10},{10,11},{11... | collective-permute-start | bytes 884744 | tf_op jit(solution)/shard_map/ppermute | solution.py:21
  90.2 14.9 %collective-permute-start.15 = (bf16[4,9,32,128]{3,2,1,0:T(8,128)(2,1)}, bf16[4,9,32,128]{3,2,1,0:T(8,128)(2,1)S(1)}, u32[]{:S(2)}, u32[]{:S(2)}) collective-permute-start(bf16[4,9,32,128]{3,2,1,0:T(8,128)(2,1)} %get-tuple-element.14), channel_id=1, source_target_pairs={{1,0},{2,1},{3,2},{4,3},{5,4},{6,5},{7,6},{9,8},{10,9},{11,10},{12... | collective-permute-start | bytes 884744 | tf_op jit(solution)/shard_map/ppermute | solution.py:21
  105.1 1.2 copy-start.4

commit v10 on v8

--- a/solution.py
+++ b/solution.py
@@ -35,41 +35,24 @@
     return shifted(packed, down, right).reshape(piece.shape)
 
 
-def halo_pieces(x):
-    return {
-        "left": dense_shifted(x[:, -1], 0, 1),
-        "right": dense_shifted(x[:, 0], 0, -1),
-        "top": dense_shifted(x[-1], 1, 0),
-        "bottom": dense_shifted(x[0], -1, 0),
-        "top_left": dense_shifted(x[-1, -1], 1, 1),
-        "top_right": dense_shifted(x[-1, 0], 1, -1),
-        "bottom_left": dense_shifted(x[0, -1], -1, 1),
-        "bottom_right": dense_shifted(x[0, 0], -1, -1),
-    }
+def halo_sides(x):
+    top = dense_shifted(x[-1], 1, 0)
+    bottom = dense_shifted(x[0], -1, 0)
+    left = dense_shifted(jnp.concatenate([top[-1:], x[:, -1], bottom[-1:]], axis=0), 0, 1)
+    right = dense_shifted(jnp.concatenate([top[:1], x[:, 0], bottom[:1]], axis=0), 0, -1)
+    return top, bottom, left, right
 
 
 def with_halo(x):
-    h = halo_pieces(x)
-    first = jnp.concatenate([h["top_left"][None], h["top"], h["top_right"][None]], axis=0)
-    last = jnp.concatenate([h["bottom_left"][None], h["bottom"], h["bottom_right"][None]], axis=0)
-    middle = jnp.concatenate([h["left"][:, None], x, h["right"][:, None]], axis=1)
-    return jnp.concatenate([first[None], middle, last[None]], axis=0)
+    top, bottom, left, right = halo_sides(x)
+    middle = jnp.concatenate([top[None], x, bottom[None]], axis=0)
+    return jnp.concatenate([left[:, None], middle, right[:, None]], axis=1)
 
 
 def halo_ring(x):
-    h = halo_pieces(x)
+    top, bottom, left, right = halo_sides(x)
     return jnp.concatenate(
-        [
-            h["top_left"][None],
-            h["top"],
-            h["top_right"][None],
-            h["bottom_left"][None],
-            h["bottom"],
-            h["bottom_right"][None],
-            h["left"],
-            h["right"],
-        ],
-        axis=0,
+        [left[:1], top, right[:1], left[-1:], bottom, right[-1:], left[1:-1], right[1:-1]], axis=0
     )
 
 

time: 129 us -> 111 us (0.86)
  starting transfers between devices: 48.8 us -> 23.8 us
  waiting for transfers between devices: 9.27 us -> 15.2 us
  local copies, waits for them, and re-layouts: 16.3 us -> 18.2 us
    ppermute x8 -> x0, starting transfers between devices: 28.2 us -> none  [shifted(): return lax.ppermute(piece, ('row', 'col'), pairs)]
    ppermute x4, waiting for transfers between devices: 2.97 us -> 10.2 us  [shifted(): return lax.ppermute(piece, 'col', pairs)]
    unnamed x23 -> x29, local copies, waits for them, and re-layouts: 1.36 us -> 5.87 us
    ppermute x4, starting transfers between devices: 10.5 us -> 12.3 us  [shifted(): return lax.ppermute(piece, 'col', pairs)]
    concatenate x1 -> x5, other arithmetic: 1.8 us -> 3.55 us  [the longest x1 1.82 us: with_halo(): return jnp.concatenate([left[:, None], middle, right[:, None]], axis=1)]
    broadcast_in_dim x2 -> x0, other arithmetic: 1.67 us -> none  [with_halo(): return jnp.concatenate([first[None], middle, last[None]], axis=0)]
    another operation x6 -> x4, local copies, waits for them, and re-layouts: 2.04 us -> 0.62 us  [the longest x2 0.35 us: with_halo(): return jnp.concatenate([left[:, None], middle, right[:, None]], axis=1)]
    ppermute x4, starting transfers between devices: 10.1 us -> 11.5 us  [shifted(): return lax.ppermute(piece, 'row', pairs)]
  transfers between devices with their start and end apart: 16 -> 8, of which waited for: 3 -> 5; matrix products, arithmetic and copies ran while one was open for 12% -> 14% of each run, Pallas kernels for 0% -> 0%
where the time goes in v10:
time: 111 us; the launch traced here: 110 us
  Pallas kernels  41.1 us (37%)
  starting transfers between devices  23.8 us (21%)
  local copies, waits for them, and re-layouts  18.2 us (16%)
  waiting for transfers between devices  15.2 us (14%)
  other arithmetic  11.1 us (10%)
    pallas_call x1, Pallas kernels, body(): pl.pallas_call(coarse_kernel, out_shape=jax.ShapeDtypeStruct((o_r * o_c,...  25.3 us
    pallas_call x1, Pallas kernels, body(): pl.pallas_call(ap_kernel, out_shape=(jax.ShapeDtypeStruct((n_r * n_c, 9,...  15.8 us
    ppermute x4, starting transfers between devices, shifted(): return lax.ppermute(piece, 'col', pairs)  12.3 us
    ppermute x4, starting transfers between devices, shifted(): return lax.ppermute(piece, 'row', pairs)  11.5 us
    ppermute x4, waiting for transfers between devices, shifted(): return lax.ppermute(piece, 'col', pairs)  10.2 us
    unnamed x29, local copies, waits for them, and re-layouts  5.87 us
    ppermute x4, waiting for transfers between devices, shifted(): return lax.ppermute(piece, 'row', pairs)  5 us
    reduce_sum x1, other arithmetic, body(): jnp.sum(jnp.where(match[..., None, None], p_blocks[:, :, None], jnp.zeros...  2.77 us
  transfers between devices with their start and end apart: 8, of which 5 were waited for; matrix products, arithmetic and copies ran while one was open for 14% of the time, Pallas kernels for 0%

profile of v10, /device:TPU:9, one launch (start us, length us, event | category | flops | bytes accessed | tf_op | source)
XLA Modules:
  0.0 110.1 jit_solution(15997370680119397104)
XLA Ops:
  0.3 0.8 broadcast_compare_fusion
  1.1 2.8 %select_reduce_fusion = bf16[4,4,4,64,64]{4,3,2,1,0:T(8,128)(2,1)S(1)} fusion(pred[4,4,4,4]{3,2,1,0:T(4,128)(4,1)S(1)} %broadcast_compare_fusion, bf16[4,4,4,64,64]{4,3,2,1,0:T(8,128)(2,1)} %param.7), kind=kLoop, calls=%fused_computation | loop fusion | flops 1835008 | bytes 1048832 | tf_op jit(solution)/shard_map/reduce_sum | solution.py:136
  4.1 3.7 %collective-permute-start = (bf16[4,4,32,128]{3,2,1,0:T(8,128)(2,1)S(1)}, bf16[4,4,32,128]{3,2,1,0:T(8,128)(2,1)S(1)}, u32[]{:S(2)}, u32[]{:S(2)}) collective-permute-start(bf16[4,4,32,128]{3,2,1,0:T(8,128)(2,1)S(1)} %reshape_squeeze.6), channel_id=1, source_target_pairs={{0,8},{8,16},{16,24},{1,9},{9,17},{17,25},{2,10},{10,18},{18,26},{... | collective-permute-start | bytes 393224 | tf_op jit(solution)/shard_map/ppermute | solution.py:18
  7.9 1.9 %collective-permute-start.1 = (bf16[4,4,32,128]{3,2,1,0:T(8,128)(2,1)S(1)}, bf16[4,4,32,128]{3,2,1,0:T(8,128)(2,1)S(1)}, u32[]{:S(2)}, u32[]{:S(2)}) collective-permute-start(bf16[4,4,32,128]{3,2,1,0:T(8,128)(2,1)S(1)} %reshape_squeeze.7), channel_id=1, source_target_pairs={{8,0},{16,8},{24,16},{9,1},{17,9},{25,17},{10,2},{18,10},{26,18},{... | collective-permute-start | bytes 393224 | tf_op jit(solution)/shard_map/ppermute | solution.py:18
  13.2 0.7 reshape.687.near_ref
  14.3 3.1 %collective-permute-start.2 = (bf16[6,4,32,128]{3,2,1,0:T(8,128)(2,1)S(1)}, bf16[6,4,32,128]{3,2,1,0:T(8,128)(2,1)S(1)}, u32[]{:S(2)}, u32[]{:S(2)}) collective-permute-start(bf16[6,4,32,128]{3,2,1,0:T(8,128)(2,1)S(1)} %pad_maximum_fusion.3), channel_id=1, source_target_pairs={{0,1},{1,2},{2,3},{3,4},{4,5},{5,6},{6,7},{8,9},{9,10},{10,11},{11... | collective-permute-start | bytes 589832 | tf_op jit(solution)/shard_map/ppermute | solution.py:21
  17.5 3.0 %collective-permute-start.3 = (bf16[6,4,32,128]{3,2,1,0:T(8,128)(2,1)S(1)}, bf16[6,4,32,128]{3,2,1,0:T(8,128)(2,1)S(1)}, u32[]{:S(2)}, u32[]{:S(2)}) collective-permute-start(bf16[6,4,32,128]{3,2,1,0:T(8,128)(2,1)S(1)} %pad_maximum_fusion.4), channel_id=1, source_target_pairs={{1,0},{2,1},{3,2},{4,3},{5,4},{6,5},{7,6},{9,8},{10,9},{11,10},{12... | collective-permute-start | bytes 589832 | tf_op jit(solution)/shard_map/ppermute | solution.py:21
  20.9 1.5 %collective-permute-done.2 = bf16[6,4,32,128]{3,2,1,0:T(8,128)(2,1)S(1)} collective-permute-done((bf16[6,4,32,128]{3,2,1,0:T(8,128)(2,1)S(1)}, bf16[6,4,32,128]{3,2,1,0:T(8,128)(2,1)S(1)}, u32[]{:S(2)}, u32[]{:S(2)}) %collective-permute-start.2) | collective-permute-done | bytes 196640 | tf_op jit(solution)/shard_map/ppermute | solution.py:21
  22.6 4.1 %collective-permute-done.3 = bf16[6,4,32,128]{3,2,1,0:T(8,128)(2,1)S(1)} collective-permute-done((bf16[6,4,32,128]{3,2,1,0:T(8,128)(2,1)S(1)}, bf16[6,4,32,128]{3,2,1,0:T(8,128)(2,1)S(1)}, u32[]{:S(2)}, u32[]{:S(2)}) %collective-permute-start.3) | collective-permute-done | bytes 196640 | tf_op jit(solution)/shard_map/ppermute | solution.py:21
  26.9 1.8 %pad_maximum_fusion = bf16[6,6,4,64,64]{4,3,2,1,0:T(8,128)(2,1)} fusion(bf16[6,1,4,64,64]{4,3,2,1,0:T(8,128)(2,1)S(1)} %bitcast.61, bf16[1,4,4,64,64]{4,3,2,1,0:T(8,128)(2,1)S(1)} %broadcast_in_dim_reshape.15, bf16[4,4,4,64,64]{4,3,2,1,0:T(8,128)(2,1)S(1)} %select_reduce_fusion, bf16[1,4,4,64,64]{4,3,2,1,0:T(8,128)(2,1)S(1)} %broadcast_in_dim_reshape.14, ...), kind=kLoop, calls=%fused_computation.1 | loop fusion | flops 2359296 | bytes 2359296 | tf_op jit(solution)/shard_map/concatenate | solution.py:49
  28.7 15.8 %shard_map.55 = (bf16[16,9,64,64]{3,2,1,0:T(8,128)(2,1)}, bf16[16,9,32,128]{3,2,1,0:T(8,128)(2,1)}) custom-call(s32[144]{0:T(256)} %reshape.687.near_ref, s32[576]{0:T(1024)} %and_select_fusion.1.slot_ref, bf16[16,9,64,64]{3,2,1,0:T(8,128)(2,1)} %bitcast.63, bf16[36,4,64,64]{3,2,1,0:T(8,128)(2,1)} %bitcast.58), custom_call_target="tpu_custom_call" | custom-call | tf_op jit(solution)/shard_map/pallas_call | solution.py:154
  44.5 1.1 fusion.15
  45.6 4.0 %collective-permute-start.4 = (bf16[4,9,32,128]{3,2,1,0:T(8,128)(2,1)S(1)}, bf16[4,9,32,128]{3,2,1,0:T(8,128)(2,1)S(1)}, u32[]{:S(2)}, u32[]{:S(2)}) collective-permute-start(bf16[4,9,32,128]{3,2,1,0:T(8,128)(2,1)S(1)} %get-tuple-element.13), channel_id=1, source_target_pairs={{0,8},{8,16},{16,24},{1,9},{9,17},{17,25},{2,10},{10,18},{18,26},{... | collective-permute-start | bytes 884744 | tf_op jit(solution)/shard_map/ppermute | solution.py:18
  49.6 1.9 %collective-permute-start.5 = (bf16[4,9,32,128]{3,2,1,0:T(8,128)(2,1)S(1)}, bf16[4,9,32,128]{3,2,1,0:T(8,128)(2,1)S(1)}, u32[]{:S(2)}, u32[]{:S(2)}) collective-permute-start(bf16[4,9,32,128]{3,2,1,0:T(8,128)(2,1)S(1)} %get-tuple-element.14), channel_id=1, source_target_pairs={{8,0},{16,8},{24,16},{9,1},{17,9},{25,17},{10,2},{18,10},{26,18},{... | collective-permute-start | bytes 884744 | tf_op jit(solution)/shard_map/ppermute | solution.py:18
  51.6 1.1 slice_bitcast_fusion
  53.2 4.4 %collective-permute-done.5 = bf16[4,9,32,128]{3,2,1,0:T(8,128)(2,1)S(1)} collective-permute-done((bf16[4,9,32,128]{3,2,1,0:T(8,128)(2,1)S(1)}, bf16[4,9,32,128]{3,2,1,0:T(8,128)(2,1)S(1)}, u32[]{:S(2)}, u32[]{:S(2)}) %collective-permute-start.5) | collective-permute-done | bytes 294944 | tf_op jit(solution)/shard_map/ppermute | solution.py:18
  57.7 0.8 pad_maximum_fusion.1
  58.5 2.4 %collective-permute-start.6 = (bf16[6,9,32,128]{3,2,1,0:T(8,128)(2,1)}, bf16[6,9,32,128]{3,2,1,0:T(8,128)(2,1)}, u32[]{:S(2)}, u32[]{:S(2)}) collective-permute-start(bf16[6,9,32,128]{3,2,1,0:T(8,128)(2,1)} %pad_maximum_fusion.1), channel_id=1, source_target_pairs={{0,1},{1,2},{2,3},{3,4},{4,5},{5,6},{6,7},{8,9},{9,10},{10,11},{11... | collective-permute-start | bytes 1327112 | tf_op jit(solution)/shard_map/ppermute | solution.py:21
  62.3 0.7 reshape.685.ring_target_ref
  64.4 0.8 pad_maximum_fusion.2
  65.3 3.8 %collective-permute-start.7 = (bf16[6,9,32,128]{3,2,1,0:T(8,128)(2,1)}, bf16[6,9,32,128]{3,2,1,0:T(8,128)(2,1)}, u32[]{:S(2)}, u32[]{:S(2)}) collective-permute-start(bf16[6,9,32,128]{3,2,1,0:T(8,128)(2,1)} %pad_maximum_fusion.2), channel_id=1, source_target_pairs={{1,0},{2,1},{3,2},{4,3},{5,4},{6,5},{7,6},{9,8},{10,9},{11,10},{12... | collective-permute-start | bytes 1327112 | tf_op jit(solution)/shard_map/ppermute | solution.py:21
  69.1 1.9 %fusion.23 = bf16[6,6,4,64,64]{3,4,2,1,0:T(8,128)(2,1)S(1)} fusion(bf16[6,1,4,64,64]{4,3,2,1,0:T(8,128)(2,1)} %bitcast.62, bf16[1,4,4,64,64]{4,3,2,1,0:T(8,128)(2,1)} %copy-done.3, bf16[4,4,4,64,64]{4,3,2,1,0:T(8,128)(2,1)S(1)} %select_reduce_fusion, bf16[1,4,4,64,64]{4,3,2,1,0:T(8,128)(2,1)} %copy-done.2, bf16[6,1,4,64,64]{4,3,2,1,0:T(8,128)(2,1)} %bitcast.60), kind=kLoop, calls=%fused_computation.136 | loop fusion | flops 2359296 | bytes 2359296 | tf_op jit(solution)/shard_map/transpose | solution.py:199
  71.0 2.4 %copy.65 = bf16[6,6,4,64,64]{4,3,2,1,0:T(8,128)(2,1)} copy(bf16[6,6,4,64,64]{3,4,2,1,0:T(8,128)(2,1)S(1)} %fusion.23) | data formatting | bytes 2359296 | tf_op jit(solution)/shard_map/transpose | solution.py:199
  73.4 0.9 slice_dynamic-update-slice_fusion.5
  74.3 4.6 %collective-permute-done.7 = bf16[6,9,32,128]{3,2,1,0:T(8,128)(2,1)} collective-permute-done((bf16[6,9,32,128]{3,2,1,0:T(8,128)(2,1)}, bf16[6,9,32,128]{3,2,1,0:T(8,128)(2,1)}, u32[]{:S(2)}, u32[]{:S(2)}) %collective-permute-start.7) | collective-permute-done | bytes 442400 | tf_op jit(solution)/shard_map/ppermute | solution.py:21
  78.9 0.9 slice_dynamic-update-slice_fusion.4
  79.8 0.9 slice_dynamic-update-slice_fusion.3
  80.8 0.9 slice_dynamic-update-slice_fusion.2
  81.7 1.0 slice_dynamic-update-slice_fusion.1
  82.7 1.0 slice_dynamic-update-slice_fusion.ring_ref
  83.7 1.2 %copy-done.4 = bf16[20,9,32,128]{3,2,1,0:T(8,128)(2,1)} copy-done((bf16[20,9,32,128]{3,2,1,0:T(8,128)(2,1)}, bf16[20,9,32,128]{3,2,1,0:T(8,128)(2,1)S(1)}, u32[]{:S(2)}) %copy-start.4) | copy-done | bytes 1474584
  84.9 25.3 %shard_map.56 = bf16[4,25,64,64]{3,2,1,0:T(8,128)(2,1)} custom-call(s32[16]{0:T(128)} %reshape.683.own_where_ref, s32[64]{0:T(128)} %reshape.684.own_target_ref, s32[20]{0:T(128)} %pad_add_fusion.1.ring_where_ref, s32[80]{0:T(128)} %reshape.685.ring_target_ref, s32[100]{0:T(128)} %reshape.686.pick_ref, bf16[16,9,64,64]{3,2,1,0:T(8,128)(2,1)} %get-tuple-element.7.own_ref, ...), custom_call_target="tpu_custom_call" | custom-call | tf_op jit(solution)/shard_map/pallas_call | solution.py:202
  (106 shorter events, 8.2 us)
Async XLA Ops:
  3.8 6.5 %copy-start.9 = (s32[4,4,9]{2,1,0:T(4,128)S(1)}, s32[4,4,9]{2,1,0:T(4,128)}, u32[]{:S(2)}) copy-start(s32[4,4,9]{2,1,0:T(4,128)} %param.6) | copy-start | bytes 1732
  4.1 10.2 %collective-permute-start = (bf16[4,4,32,128]{3,2,1,0:T(8,128)(2,1)S(1)}, bf16[4,4,32,128]{3,2,1,0:T(8,128)(2,1)S(1)}, u32[]{:S(2)}, u32[]{:S(2)}) collective-permute-start(bf16[4,4,32,128]{3,2,1,0:T(8,128)(2,1)S(1)} %reshape_squeeze.6), channel_id=1, source_target_pairs={{0,8},{8,16},{16,24},{1,9},{9,17},{17,25},{2,10},{10,18},{18,26},{... | collective-permute-start | bytes 393224 | tf_op jit(solution)/shard_map/ppermute | solution.py:18
  7.9 6.3 %collective-permute-start.1 = (bf16[4,4,32,128]{3,2,1,0:T(8,128)(2,1)S(1)}, bf16[4,4,32,128]{3,2,1,0:T(8,128)(2,1)S(1)}, u32[]{:S(2)}, u32[]{:S(2)}) collective-permute-start(bf16[4,4,32,128]{3,2,1,0:T(8,128)(2,1)S(1)} %reshape_squeeze.7), channel_id=1, source_target_pairs={{8,0},{16,8},{24,16},{9,1},{17,9},{25,17},{10,2},{18,10},{26,18},{... | collective-permute-start | bytes 393224 | tf_op jit(solution)/shard_map/ppermute | solution.py:18
  9.9 10.6 %copy-start.10 = (s32[2,2,25]{2,1,0:T(2,128)S(1)}, s32[2,2,25]{2,1,0:T(2,128)}, u32[]{:S(2)}) copy-start(s32[2,2,25]{2,1,0:T(2,128)} %param.9) | copy-start | bytes 1204
  14.3 8.1 %collective-permute-start.2 = (bf16[6,4,32,128]{3,2,1,0:T(8,128)(2,1)S(1)}, bf16[6,4,32,128]{3,2,1,0:T(8,128)(2,1)S(1)}, u32[]{:S(2)}, u32[]{:S(2)}) collective-permute-start(bf16[6,4,32,128]{3,2,1,0:T(8,128)(2,1)S(1)} %pad_maximum_fusion.3), channel_id=1, source_target_pairs={{0,1},{1,2},{2,3},{3,4},{4,5},{5,6},{6,7},{8,9},{9,10},{10,11},{11... | collective-permute-start | bytes 589832 | tf_op jit(solution)/shard_map/ppermute | solution.py:21
  17.5 9.2 %collective-permute-start.3 = (bf16[6,4,32,128]{3,2,1,0:T(8,128)(2,1)S(1)}, bf16[6,4,32,128]{3,2,1,0:T(8,128)(2,1)S(1)}, u32[]{:S(2)}, u32[]{:S(2)}) collective-permute-start(bf16[6,4,32,128]{3,2,1,0:T(8,128)(2,1)S(1)} %pad_maximum_fusion.4), channel_id=1, source_target_pairs={{1,0},{2,1},{3,2},{4,3},{5,4},{6,5},{7,6},{9,8},{10,9},{11,10},{12... | collective-permute-start | bytes 589832 | tf_op jit(solution)/shard_map/ppermute | solution.py:21
  20.8 8.0 %copy-start.2 = (bf16[1,4,4,64,64]{4,3,2,1,0:T(8,128)(2,1)}, bf16[1,4,4,64,64]{4,3,2,1,0:T(8,128)(2,1)S(1)}, u32[]{:S(2)}) copy-start(bf16[1,4,4,64,64]{4,3,2,1,0:T(8,128)(2,1)S(1)} %broadcast_in_dim_reshape.14) | copy-start | bytes 393220
  20.9 7.8 %copy-start.3 = (bf16[1,4,4,64,64]{4,3,2,1,0:T(8,128)(2,1)}, bf16[1,4,4,64,64]{4,3,2,1,0:T(8,128)(2,1)S(1)}, u32[]{:S(2)}) copy-start(bf16[1,4,4,64,64]{4,3,2,1,0:T(8,128)(2,1)S(1)} %broadcast_in_dim_reshape.15) | copy-start | bytes 393220
  22.6 6.1 %copy-start = (bf16[6,1,4,64,64]{4,3,2,0,1:T(8,128)(2,1)}, bf16[6,1,4,64,64]{4,3,2,0,1:T(8,128)(2,1)S(1)}, u32[]{:S(2)}) copy-start(bf16[6,1,4,64,64]{4,3,2,0,1:T(8,128)(2,1)S(1)} %broadcast_in_dim_reshape.13) | copy-start | bytes 589828
  26.9 1.8 %copy-start.1 = (bf16[6,1,4,64,64]{4,3,2,0,1:T(8,128)(2,1)}, bf16[6,1,4,64,64]{4,3,2,0,1:T(8,128)(2,1)S(1)}, u32[]{:S(2)}) copy-start(bf16[6,1,4,64,64]{4,3,2,0,1:T(8,128)(2,1)S(1)} %broadcast_in_dim_reshape.16) | copy-start | bytes 589828
  45.6 7.6 %collective-permute-start.4 = (bf16[4,9,32,128]{3,2,1,0:T(8,128)(2,1)S(1)}, bf16[4,9,32,128]{3,2,1,0:T(8,128)(2,1)S(1)}, u32[]{:S(2)}, u32[]{:S(2)}) collective-permute-start(bf16[4,9,32,128]{3,2,1,0:T(8,128)(2,1)S(1)} %get-tuple-element.13), channel_id=1, source_target_pairs={{0,8},{8,16},{16,24},{1,9},{9,17},{17,25},{2,10},{10,18},{18,26},{... | collective-permute-start | bytes 884744 | tf_op jit(solution)/shard_map/ppermute | solution.py:18
  49.6 8.0 %collective-permute-start.5 = (bf16[4,9,32,128]{3,2,1,0:T(8,128)(2,1)S(1)}, bf16[4,9,32,128]{3,2,1,0:T(8,128)(2,1)S(1)}, u32[]{:S(2)}, u32[]{:S(2)}) collective-permute-start(bf16[4,9,32,128]{3,2,1,0:T(8,128)(2,1)S(1)} %get-tuple-element.14), channel_id=1, source_target_pairs={{8,0},{16,8},{24,16},{9,1},{17,9},{25,17},{10,2},{18,10},{26,18},{... | collective-permute-start | bytes 884744 | tf_op jit(solution)/shard_map/ppermute | solution.py:18
  53.2 5.3 %copy-start.5 = (bf16[4,9,32,128]{3,2,1,0:T(8,128)(2,1)}, bf16[4,9,32,128]{3,2,1,0:T(8,128)(2,1)S(1)}, u32[]{:S(2)}) copy-start(bf16[4,9,32,128]{3,2,1,0:T(8,128)(2,1)S(1)} %collective-permute-done.4) | copy-start | bytes 884740
  57.7 3.2 %copy-start.7 = (bf16[4,9,32,128]{3,2,1,0:T(8,128)(2,1)}, bf16[4,9,32,128]{3,2,1,0:T(8,128)(2,1)S(1)}, u32[]{:S(2)}) copy-start(bf16[4,9,32,128]{3,2,1,0:T(8,128)(2,1)S(1)} %collective-permute-done.5) | copy-start | bytes 884740
  58.5 14.9 %collective-permute-start.6 = (bf16[6,9,32,128]{3,2,1,0:T(8,128)(2,1)}, bf16[6,9,32,128]{3,2,1,0:T(8,128)(2,1)}, u32[]{:S(2)}, u32[]{:S(2)}) collective-permute-start(bf16[6,9,32,128]{3,2,1,0:T(8,128)(2,1)} %pad_maximum_fusion.1), channel_id=1, source_target_pairs={{0,1},{1,2},{2,3},{3,4},{4,5},{5,6},{6,7},{8,9},{9,10},{10,11},{11... | collective-permute-start | bytes 1327112 | tf_op jit(solution)/shard_map/ppermute | solution.py:21
  65.3 13.7 %collective-permute-start.7 = (bf16[6,9,32,128]{3,2,1,0:T(8,128)(2,1)}, bf16[6,9,32,128]{3,2,1,0:T(8,128)(2,1)}, u32[]{:S(2)}, u32[]{:S(2)}) collective-permute-start(bf16[6,9,32,128]{3,2,1,0:T(8,128)(2,1)} %pad_maximum_fusion.2), channel_id=1, source_target_pairs={{1,0},{2,1},{3,2},{4,3},{5,4},{6,5},{7,6},{9,8},{10,9},{11,10},{12... | collective-permute-start | bytes 1327112 | tf_op jit(solution)/shard_map/ppermute | solution.py:21
  70.9 3.4 %copy-start.6 = (bf16[4,9,32,128]{3,2,1,0:T(8,128)(2,1)S(1)}, bf16[4,9,32,128]{3,2,1,0:T(8,128)(2,1)}, u32[]{:S(2)}) copy-start(bf16[4,9,32,128]{3,2,1,0:T(8,128)(2,1)} %copy-done.5) | copy-start | bytes 884740
  70.9 9.8 %copy-start.8 = (bf16[4,9,32,128]{3,2,1,0:T(8,128)(2,1)S(1)}, bf16[4,9,32,128]{3,2,1,0:T(8,128)(2,1)}, u32[]{:S(2)}) copy-start(bf16[4,9,32,128]{3,2,1,0:T(8,128)(2,1)} %copy-done.7) | copy-start | bytes 884740
  83.7 1.2 %copy-start.4 = (bf16[20,9,32,128]{3,2,1,0:T(8,128)(2,1)}, bf16[20,9,32,128]{3,2,1,0:T(8,128)(2,1)S(1)}, u32[]{:S(2)}) copy-start(bf16[20,9,32,128]{3,2,1,0:T(8,128)(2,1)S(1)} %slice_dynamic-update-slice_fusion.ring_ref) | copy-start | bytes 4423684

commit v11 on v10

--- a/solution.py
+++ b/solution.py
@@ -96,12 +96,13 @@
     lax.fori_loop(0, ap_ref.shape[0], one_tile, 0)
 
 
-def coarse_kernel(
-    own_where_ref, own_target_ref, ring_where_ref, ring_target_ref, pick_ref, own_ref, ring_ref, pt_ref, out_ref, acc_ref
-):
+def coarse_kernel(*refs):
+    groups = (len(refs) - 4) // 3
+    tables, pick_ref = refs[: 2 * groups], refs[2 * groups]
+    blocks, pt_ref, out_ref, acc_ref = refs[2 * groups + 1 : 3 * groups + 1], refs[-3], refs[-2], refs[-1]
     acc_ref[...] = jnp.zeros(acc_ref.shape, jnp.float32)
-    add_terms(own_where_ref, own_target_ref, own_ref, pt_ref, acc_ref)
-    add_terms(ring_where_ref, ring_target_ref, ring_ref, pt_ref, acc_ref)
+    for i in range(groups):
+        add_terms(tables[2 * i], tables[2 * i + 1], blocks[i], pt_ref, acc_ref)
     owned, stencil = out_ref.shape[0], out_ref.shape[1]
 
     def one_pick(i, carry):
@@ -198,21 +199,25 @@
 
     p_t = jnp.swapaxes(p_ext, -1, -2).reshape(ext_r * ext_c * 4, bs, bs)
     stencil = c_cols.shape[-1]
-    ring_tiles = 2 * ext_c + 2 * n_r
+    top, bottom, left, right = halo_sides(ap_dense)
+    parts = [
+        (place[1:-1, 1:-1], target[1:-1, 1:-1], ap.reshape(n_r * n_c, 9, bs, bs)),
+        (place[0, 1:-1], target[0, 1:-1], top),
+        (place[-1, 1:-1], target[-1, 1:-1], bottom),
+        (place[:, 0], target[:, 0], left),
+        (place[:, -1], target[:, -1], right),
+    ]
     out = pl.pallas_call(
         coarse_kernel,
         out_shape=jax.ShapeDtypeStruct((o_r * o_c, stencil, bs, bs), jnp.bfloat16),
-        in_specs=[pl.BlockSpec(memory_space=pltpu.SMEM)] * 5 + [pl.BlockSpec(memory_space=pltpu.VMEM)] * 3,
+        in_specs=[pl.BlockSpec(memory_space=pltpu.SMEM)] * (2 * len(parts) + 1)
+        + [pl.BlockSpec(memory_space=pltpu.VMEM)] * (len(parts) + 1),
         out_specs=pl.BlockSpec(memory_space=pltpu.VMEM),
         scratch_shapes=[pltpu.VMEM((o_r * o_c * 25, bs, bs), jnp.float32)],
     )(
-        place[1:-1, 1:-1].reshape(-1),
-        target[1:-1, 1:-1].reshape(-1),
-        ring_of(place),
-        ring_of(target).reshape(-1),
+        *[t for w, g, _ in parts for t in (w.reshape(-1), g.reshape(-1))],
         pick,
-        ap.reshape(n_r * n_c, 9, bs, bs),
-        halo_ring(ap_dense),
+        *[b for _, _, b in parts],
         p_t,
     )
     return out.reshape(o_r, o_c, stencil, bs, bs)

time: 111 us -> 108 us (0.973)
  local copies, waits for them, and re-layouts: 18.2 us -> 13.4 us
  waiting for transfers between devices: 15.2 us -> 19.4 us
  starting transfers between devices: 23.8 us -> 22.6 us
    ppermute x4, waiting for transfers between devices: 10.2 us -> 16.9 us  [shifted(): return lax.ppermute(piece, 'col', pairs)]
    unnamed x29 -> x16, local copies, waits for them, and re-layouts: 5.87 us -> 0.04 us
    ppermute x4, waiting for transfers between devices: 5 us -> 2.51 us  [shifted(): return lax.ppermute(piece, 'row', pairs)]
    another operation x0 -> x4, local copies, waits for them, and re-layouts: none -> 2.36 us  [body(): g.reshape(-1)]
    slice x6 -> x8, local copies, waits for them, and re-layouts: 0.34 us -> 2.06 us  [the longest x1 1.09 us: halo_sides(): bottom = dense_shifted(x[0], -1, 0)]
  transfers between devices with their start and end apart: 8 -> 8, of which waited for: 5 -> 5; matrix products, arithmetic and copies ran while one was open for 14% -> 15% of each run, Pallas kernels for 0% -> 0%
where the time goes in v11:
time: 108 us
  Pallas kernels  41.1 us (38%)
  starting transfers between devices  22.6 us (21%)
  waiting for transfers between devices  19.4 us (18%)
  local copies, waits for them, and re-layouts  13.4 us (12%)
  other arithmetic  10.3 us (10%)
    pallas_call x1, Pallas kernels, body(): pl.pallas_call(coarse_kernel, out_shape=jax.ShapeDtypeStruct((o_r * o_c,...  25.3 us
    ppermute x4, waiting for transfers between devices, shifted(): return lax.ppermute(piece, 'col', pairs)  16.9 us
    pallas_call x1, Pallas kernels, body(): pl.pallas_call(ap_kernel, out_shape=(jax.ShapeDtypeStruct((n_r * n_c, 9,...  15.8 us
    ppermute x4, starting transfers between devices, shifted(): return lax.ppermute(piece, 'col', pairs)  11.4 us
    ppermute x4, starting transfers between devices, shifted(): return lax.ppermute(piece, 'row', pairs)  11.2 us
    reduce_sum x1, other arithmetic, body(): jnp.sum(jnp.where(match[..., None, None], p_blocks[:, :, None], jnp.zeros...  2.77 us
    ppermute x4, waiting for transfers between devices, shifted(): return lax.ppermute(piece, 'row', pairs)  2.51 us
    transpose x1, local copies, waits for them, and re-layouts, body(): p_t = jnp.swapaxes(p_ext, -1, -2).reshape(ext_r * ext_c * 4, bs, bs)  2.45 us
  transfers between devices with their start and end apart: 8, of which 5 were waited for; matrix products, arithmetic and copies ran while one was open for 15% of the time, Pallas kernels for 0%

profile of v11, /device:TPU:9, one launch (start us, length us, event | category | flops | bytes accessed | tf_op | source)
XLA Modules:
  0.0 107.7 jit_solution(17950037488395105628)
XLA Ops:
  0.3 0.8 broadcast_compare_fusion
  1.1 2.8 %select_reduce_fusion = bf16[4,4,4,64,64]{4,3,2,1,0:T(8,128)(2,1)S(1)} fusion(pred[4,4,4,4]{3,2,1,0:T(4,128)(4,1)S(1)} %broadcast_compare_fusion, bf16[4,4,4,64,64]{4,3,2,1,0:T(8,128)(2,1)} %param.7), kind=kLoop, calls=%fused_computation | loop fusion | flops 1835008 | bytes 1048832 | tf_op jit(solution)/shard_map/reduce_sum | solution.py:137
  4.1 2.6 %collective-permute-start.1 = (bf16[4,4,32,128]{3,2,1,0:T(8,128)(2,1)S(1)}, bf16[4,4,32,128]{3,2,1,0:T(8,128)(2,1)S(1)}, u32[]{:S(2)}, u32[]{:S(2)}) collective-permute-start(bf16[4,4,32,128]{3,2,1,0:T(8,128)(2,1)S(1)} %reshape_squeeze.23), channel_id=1, source_target_pairs={{8,0},{16,8},{24,16},{9,1},{17,9},{25,17},{10,2},{18,10},{26,18},{... | collective-permute-start | bytes 393224 | tf_op jit(solution)/shard_map/ppermute | solution.py:18
  6.8 3.0 %collective-permute-start = (bf16[4,4,32,128]{3,2,1,0:T(8,128)(2,1)S(1)}, bf16[4,4,32,128]{3,2,1,0:T(8,128)(2,1)S(1)}, u32[]{:S(2)}, u32[]{:S(2)}) collective-permute-start(bf16[4,4,32,128]{3,2,1,0:T(8,128)(2,1)S(1)} %reshape_squeeze.22), channel_id=1, source_target_pairs={{0,8},{8,16},{16,24},{1,9},{9,17},{17,25},{2,10},{10,18},{18,26},{... | collective-permute-start | bytes 393224 | tf_op jit(solution)/shard_map/ppermute | solution.py:18
  11.8 0.6 and_select_fusion.slot_ref
  12.4 0.7 reshape.679.near_ref
  13.5 3.0 %collective-permute-start.3 = (bf16[6,4,32,128]{3,2,1,0:T(8,128)(2,1)S(1)}, bf16[6,4,32,128]{3,2,1,0:T(8,128)(2,1)S(1)}, u32[]{:S(2)}, u32[]{:S(2)}) collective-permute-start(bf16[6,4,32,128]{3,2,1,0:T(8,128)(2,1)S(1)} %pad_maximum_fusion.4), channel_id=1, source_target_pairs={{1,0},{2,1},{3,2},{4,3},{5,4},{6,5},{7,6},{9,8},{10,9},{11,10},{12... | collective-permute-start | bytes 589832 | tf_op jit(solution)/shard_map/ppermute | solution.py:21
  16.6 2.2 %collective-permute-start.2 = (bf16[6,4,32,128]{3,2,1,0:T(8,128)(2,1)S(1)}, bf16[6,4,32,128]{3,2,1,0:T(8,128)(2,1)S(1)}, u32[]{:S(2)}, u32[]{:S(2)}) collective-permute-start(bf16[6,4,32,128]{3,2,1,0:T(8,128)(2,1)S(1)} %pad_maximum_fusion.3), channel_id=1, source_target_pairs={{0,1},{1,2},{2,3},{3,4},{4,5},{5,6},{6,7},{8,9},{9,10},{10,11},{11... | collective-permute-start | bytes 589832 | tf_op jit(solution)/shard_map/ppermute | solution.py:21
  19.2 2.8 %collective-permute-done.3 = bf16[6,4,32,128]{3,2,1,0:T(8,128)(2,1)S(1)} collective-permute-done((bf16[6,4,32,128]{3,2,1,0:T(8,128)(2,1)S(1)}, bf16[6,4,32,128]{3,2,1,0:T(8,128)(2,1)S(1)}, u32[]{:S(2)}, u32[]{:S(2)}) %collective-permute-start.3) | collective-permute-done | bytes 196640 | tf_op jit(solution)/shard_map/ppermute | solution.py:21
  22.3 4.1 %collective-permute-done.2 = bf16[6,4,32,128]{3,2,1,0:T(8,128)(2,1)S(1)} collective-permute-done((bf16[6,4,32,128]{3,2,1,0:T(8,128)(2,1)S(1)}, bf16[6,4,32,128]{3,2,1,0:T(8,128)(2,1)S(1)}, u32[]{:S(2)}, u32[]{:S(2)}) %collective-permute-start.2) | collective-permute-done | bytes 196640 | tf_op jit(solution)/shard_map/ppermute | solution.py:21
  26.5 1.8 %pad_maximum_fusion = bf16[6,6,4,64,64]{4,3,2,1,0:T(8,128)(2,1)} fusion(bf16[6,1,4,64,64]{4,3,2,1,0:T(8,128)(2,1)S(1)} %bitcast.57, bf16[1,4,4,64,64]{4,3,2,1,0:T(8,128)(2,1)S(1)} %broadcast_in_dim_reshape.15, bf16[4,4,4,64,64]{4,3,2,1,0:T(8,128)(2,1)S(1)} %select_reduce_fusion, bf16[1,4,4,64,64]{4,3,2,1,0:T(8,128)(2,1)S(1)} %broadcast_in_dim_reshape.14, ...), kind=kLoop, calls=%fused_computation.1 | loop fusion | flops 2359296 | bytes 2359296 | tf_op jit(solution)/shard_map/concatenate | solution.py:49
  28.4 15.8 %shard_map.55 = (bf16[16,9,64,64]{3,2,1,0:T(8,128)(2,1)}, bf16[16,9,32,128]{3,2,1,0:T(8,128)(2,1)}) custom-call(s32[144]{0:T(256)} %reshape.679.near_ref, s32[576]{0:T(1024)} %and_select_fusion.slot_ref, bf16[16,9,64,64]{3,2,1,0:T(8,128)(2,1)} %bitcast.61, bf16[36,4,64,64]{3,2,1,0:T(8,128)(2,1)} %bitcast.55), custom_call_target="tpu_custom_call" | custom-call | tf_op jit(solution)/shard_map/pallas_call | solution.py:155
  44.2 1.1 %fusion.15 = (bf16[4,9,32,128]{3,2,1,0:T(8,128)(2,1)S(1)}, bf16[4,9,32,128]{3,2,1,0:T(8,128)(2,1)S(1)}) fusion(bf16[16,9,32,128]{3,2,1,0:T(8,128)(2,1)} %get-tuple-element.8), kind=kLoop, calls=%fused_computation.117 | loop fusion | bytes 1179648 | tf_op jit(solution)/shard_map/slice | solution.py:40
  45.3 2.4 %collective-permute-start.5 = (bf16[4,9,32,128]{3,2,1,0:T(8,128)(2,1)S(1)}, bf16[4,9,32,128]{3,2,1,0:T(8,128)(2,1)S(1)}, u32[]{:S(2)}, u32[]{:S(2)}) collective-permute-start(bf16[4,9,32,128]{3,2,1,0:T(8,128)(2,1)S(1)} %get-tuple-element.15), channel_id=1, source_target_pairs={{8,0},{16,8},{24,16},{9,1},{17,9},{25,17},{10,2},{18,10},{26,18},{... | collective-permute-start | bytes 884744 | tf_op jit(solution)/shard_map/ppermute | solution.py:18
  47.6 0.8 slice_reduce_fusion.2
  49.1 0.6 reshape.676.refs_0_
  49.7 0.6 reshape_squeeze.19.refs_5_
  50.9 0.6 reshape_squeeze.21.refs_9_
  51.5 0.6 reshape.677.refs_1_
  52.1 0.6 reshape_squeeze.20.refs_7_
  52.7 3.2 %collective-permute-start.4 = (bf16[4,9,32,128]{3,2,1,0:T(8,128)(2,1)S(1)}, bf16[4,9,32,128]{3,2,1,0:T(8,128)(2,1)S(1)}, u32[]{:S(2)}, u32[]{:S(2)}) collective-permute-start(bf16[4,9,32,128]{3,2,1,0:T(8,128)(2,1)S(1)} %get-tuple-element.16), channel_id=1, source_target_pairs={{0,8},{8,16},{16,24},{1,9},{9,17},{17,25},{2,10},{10,18},{18,26},{... | collective-permute-start | bytes 884744 | tf_op jit(solution)/shard_map/ppermute | solution.py:18
  55.9 1.1 %slice_bitcast_fusion = (bf16[4,9,32,128]{3,2,1,0:T(8,128)(2,1)S(1)}, bf16[4,9,32,128]{3,2,1,0:T(8,128)(2,1)S(1)}) fusion(bf16[4,4,9,32,128]{4,3,2,1,0:T(8,128)(2,1)} %bitcast.62), kind=kLoop, calls=%fused_computation.8 | loop fusion | bytes 1179648 | tf_op jit(solution)/shard_map/squeeze | solution.py:42
  57.1 2.5 %collective-permute-done.4.refs_12_ = bf16[4,9,32,128]{3,2,1,0:T(8,128)(2,1)S(1)} collective-permute-done((bf16[4,9,32,128]{3,2,1,0:T(8,128)(2,1)S(1)}, bf16[4,9,32,128]{3,2,1,0:T(8,128)(2,1)S(1)}, u32[]{:S(2)}, u32[]{:S(2)}) %collective-permute-start.4) | collective-permute-done | bytes 294944 | tf_op jit(solution)/shard_map/ppermute | solution.py:18
  59.6 0.8 pad_maximum_fusion.1
  60.4 4.1 %collective-permute-start.6 = (bf16[6,9,32,128]{3,2,1,0:T(8,128)(2,1)}, bf16[6,9,32,128]{3,2,1,0:T(8,128)(2,1)}, u32[]{:S(2)}, u32[]{:S(2)}) collective-permute-start(bf16[6,9,32,128]{3,2,1,0:T(8,128)(2,1)} %pad_maximum_fusion.1), channel_id=1, source_target_pairs={{0,1},{1,2},{2,3},{3,4},{4,5},{5,6},{6,7},{8,9},{9,10},{10,11},{11... | collective-permute-start | bytes 1327112 | tf_op jit(solution)/shard_map/ppermute | solution.py:21
  64.5 0.8 pad_maximum_fusion.2
  65.3 2.1 %collective-permute-start.7 = (bf16[6,9,32,128]{3,2,1,0:T(8,128)(2,1)}, bf16[6,9,32,128]{3,2,1,0:T(8,128)(2,1)}, u32[]{:S(2)}, u32[]{:S(2)}) collective-permute-start(bf16[6,9,32,128]{3,2,1,0:T(8,128)(2,1)} %pad_maximum_fusion.2), channel_id=1, source_target_pairs={{1,0},{2,1},{3,2},{4,3},{5,4},{6,5},{7,6},{9,8},{10,9},{11,10},{12... | collective-permute-start | bytes 1327112 | tf_op jit(solution)/shard_map/ppermute | solution.py:21
  68.0 1.8 %fusion.23 = bf16[6,6,4,64,64]{3,4,2,1,0:T(8,128)(2,1)S(1)} fusion(bf16[6,1,4,64,64]{4,3,2,1,0:T(8,128)(2,1)} %bitcast.58, bf16[1,4,4,64,64]{4,3,2,1,0:T(8,128)(2,1)} %copy-done.2, bf16[4,4,4,64,64]{4,3,2,1,0:T(8,128)(2,1)S(1)} %select_reduce_fusion, bf16[1,4,4,64,64]{4,3,2,1,0:T(8,128)(2,1)} %copy-done.3, bf16[6,1,4,64,64]{4,3,2,1,0:T(8,128)(2,1)} %bitcast.60), kind=kLoop, calls=%fused_computation.125 | loop fusion | flops 2359296 | bytes 2359296 | tf_op jit(solution)/shard_map/transpose | solution.py:200
  69.9 2.5 %copy.47 = bf16[6,6,4,64,64]{4,3,2,1,0:T(8,128)(2,1)} copy(bf16[6,6,4,64,64]{3,4,2,1,0:T(8,128)(2,1)S(1)} %fusion.23) | data formatting | bytes 2359296 | tf_op jit(solution)/shard_map/transpose | solution.py:200
  72.3 9.1 %collective-permute-done.6.refs_14_ = bf16[6,9,32,128]{3,2,1,0:T(8,128)(2,1)} collective-permute-done((bf16[6,9,32,128]{3,2,1,0:T(8,128)(2,1)}, bf16[6,9,32,128]{3,2,1,0:T(8,128)(2,1)}, u32[]{:S(2)}, u32[]{:S(2)}) %collective-permute-start.6) | collective-permute-done | bytes 442400 | tf_op jit(solution)/shard_map/ppermute | solution.py:21
  81.5 0.9 collective-permute-done.7.refs_15_
  82.4 25.3 %shard_map.56 = bf16[4,25,64,64]{3,2,1,0:T(8,128)(2,1)} custom-call(s32[16]{0:T(128)} %reshape.676.refs_0_, s32[64]{0:T(128)} %reshape.677.refs_1_, s32[4]{0:T(128)} %get-tuple-element.12.refs_2_, s32[16]{0:T(128)} %reshape_squeeze.18.refs_3_, s32[4]{0:T(128)} %get-tuple-element.11.refs_4_, s32[16]{0:T(128)} %reshape_squeeze.19.refs_5_, ...), custom_call_target="tpu_custom_call" | custom-call | tf_op jit(solution)/shard_map/pallas_call | solution.py:210
  (86 shorter events, 5.1 us)
Async XLA Ops:
  1.1 10.1 %copy-start.6 = (s32[4,4,9]{2,1,0:T(4,128)S(1)}, s32[4,4,9]{2,1,0:T(4,128)}, u32[]{:S(2)}) copy-start(s32[4,4,9]{2,1,0:T(4,128)} %param.6) | copy-start | bytes 1732
  3.9 15.0 %copy-start.7 = (s32[2,2,25]{2,1,0:T(2,128)S(1)}, s32[2,2,25]{2,1,0:T(2,128)}, u32[]{:S(2)}) copy-start(s32[2,2,25]{2,1,0:T(2,128)} %param.9) | copy-start | bytes 1204
  4.1 9.4 %collective-permute-start.1 = (bf16[4,4,32,128]{3,2,1,0:T(8,128)(2,1)S(1)}, bf16[4,4,32,128]{3,2,1,0:T(8,128)(2,1)S(1)}, u32[]{:S(2)}, u32[]{:S(2)}) collective-permute-start(bf16[4,4,32,128]{3,2,1,0:T(8,128)(2,1)S(1)} %reshape_squeeze.23), channel_id=1, source_target_pairs={{8,0},{16,8},{24,16},{9,1},{17,9},{25,17},{10,2},{18,10},{26,18},{... | collective-permute-start | bytes 393224 | tf_op jit(solution)/shard_map/ppermute | solution.py:18
  6.8 6.7 %collective-permute-start = (bf16[4,4,32,128]{3,2,1,0:T(8,128)(2,1)S(1)}, bf16[4,4,32,128]{3,2,1,0:T(8,128)(2,1)S(1)}, u32[]{:S(2)}, u32[]{:S(2)}) collective-permute-start(bf16[4,4,32,128]{3,2,1,0:T(8,128)(2,1)S(1)} %reshape_squeeze.22), channel_id=1, source_target_pairs={{0,8},{8,16},{16,24},{1,9},{9,17},{17,25},{2,10},{10,18},{18,26},{... | collective-permute-start | bytes 393224 | tf_op jit(solution)/shard_map/ppermute | solution.py:18
  13.5 8.5 %collective-permute-start.3 = (bf16[6,4,32,128]{3,2,1,0:T(8,128)(2,1)S(1)}, bf16[6,4,32,128]{3,2,1,0:T(8,128)(2,1)S(1)}, u32[]{:S(2)}, u32[]{:S(2)}) collective-permute-start(bf16[6,4,32,128]{3,2,1,0:T(8,128)(2,1)S(1)} %pad_maximum_fusion.4), channel_id=1, source_target_pairs={{1,0},{2,1},{3,2},{4,3},{5,4},{6,5},{7,6},{9,8},{10,9},{11,10},{12... | collective-permute-start | bytes 589832 | tf_op jit(solution)/shard_map/ppermute | solution.py:21
  16.6 9.7 %collective-permute-start.2 = (bf16[6,4,32,128]{3,2,1,0:T(8,128)(2,1)S(1)}, bf16[6,4,32,128]{3,2,1,0:T(8,128)(2,1)S(1)}, u32[]{:S(2)}, u32[]{:S(2)}) collective-permute-start(bf16[6,4,32,128]{3,2,1,0:T(8,128)(2,1)S(1)} %pad_maximum_fusion.3), channel_id=1, source_target_pairs={{0,1},{1,2},{2,3},{3,4},{4,5},{5,6},{6,7},{8,9},{9,10},{10,11},{11... | collective-permute-start | bytes 589832 | tf_op jit(solution)/shard_map/ppermute | solution.py:21
  19.1 9.3 %copy-start.2 = (bf16[1,4,4,64,64]{4,3,2,1,0:T(8,128)(2,1)}, bf16[1,4,4,64,64]{4,3,2,1,0:T(8,128)(2,1)S(1)}, u32[]{:S(2)}) copy-start(bf16[1,4,4,64,64]{4,3,2,1,0:T(8,128)(2,1)S(1)} %broadcast_in_dim_reshape.15) | copy-start | bytes 393220
  19.2 9.1 %copy-start.3 = (bf16[1,4,4,64,64]{4,3,2,1,0:T(8,128)(2,1)}, bf16[1,4,4,64,64]{4,3,2,1,0:T(8,128)(2,1)S(1)}, u32[]{:S(2)}) copy-start(bf16[1,4,4,64,64]{4,3,2,1,0:T(8,128)(2,1)S(1)} %broadcast_in_dim_reshape.14) | copy-start | bytes 393220
  22.2 6.1 %copy-start = (bf16[6,1,4,64,64]{4,3,2,0,1:T(8,128)(2,1)}, bf16[6,1,4,64,64]{4,3,2,0,1:T(8,128)(2,1)S(1)}, u32[]{:S(2)}) copy-start(bf16[6,1,4,64,64]{4,3,2,0,1:T(8,128)(2,1)S(1)} %broadcast_in_dim_reshape.16) | copy-start | bytes 589828
  26.5 1.8 %copy-start.1 = (bf16[6,1,4,64,64]{4,3,2,0,1:T(8,128)(2,1)}, bf16[6,1,4,64,64]{4,3,2,0,1:T(8,128)(2,1)S(1)}, u32[]{:S(2)}) copy-start(bf16[6,1,4,64,64]{4,3,2,0,1:T(8,128)(2,1)S(1)} %broadcast_in_dim_reshape.13) | copy-start | bytes 589828
  45.3 11.8 %collective-permute-start.5 = (bf16[4,9,32,128]{3,2,1,0:T(8,128)(2,1)S(1)}, bf16[4,9,32,128]{3,2,1,0:T(8,128)(2,1)S(1)}, u32[]{:S(2)}, u32[]{:S(2)}) collective-permute-start(bf16[4,9,32,128]{3,2,1,0:T(8,128)(2,1)S(1)} %get-tuple-element.15), channel_id=1, source_target_pairs={{8,0},{16,8},{24,16},{9,1},{17,9},{25,17},{10,2},{18,10},{26,18},{... | collective-permute-start | bytes 884744 | tf_op jit(solution)/shard_map/ppermute | solution.py:18
  52.7 6.8 %collective-permute-start.4 = (bf16[4,9,32,128]{3,2,1,0:T(8,128)(2,1)S(1)}, bf16[4,9,32,128]{3,2,1,0:T(8,128)(2,1)S(1)}, u32[]{:S(2)}, u32[]{:S(2)}) collective-permute-start(bf16[4,9,32,128]{3,2,1,0:T(8,128)(2,1)S(1)} %get-tuple-element.16), channel_id=1, source_target_pairs={{0,8},{8,16},{16,24},{1,9},{9,17},{17,25},{2,10},{10,18},{18,26},{... | collective-permute-start | bytes 884744 | tf_op jit(solution)/shard_map/ppermute | solution.py:18
  57.0 10.4 %copy-start.4 = (bf16[4,9,32,128]{3,2,1,0:T(8,128)(2,1)}, bf16[4,9,32,128]{3,2,1,0:T(8,128)(2,1)S(1)}, u32[]{:S(2)}) copy-start(bf16[4,9,32,128]{3,2,1,0:T(8,128)(2,1)S(1)} %collective-permute-done.5.refs_13_) | copy-start | bytes 884740
  59.6 7.9 %copy-start.5 = (bf16[4,9,32,128]{3,2,1,0:T(8,128)(2,1)}, bf16[4,9,32,128]{3,2,1,0:T(8,128)(2,1)S(1)}, u32[]{:S(2)}) copy-start(bf16[4,9,32,128]{3,2,1,0:T(8,128)(2,1)S(1)} %collective-permute-done.4.refs_12_) | copy-start | bytes 884740
  60.4 21.0 %collective-permute-start.6 = (bf16[6,9,32,128]{3,2,1,0:T(8,128)(2,1)}, bf16[6,9,32,128]{3,2,1,0:T(8,128)(2,1)}, u32[]{:S(2)}, u32[]{:S(2)}) collective-permute-start(bf16[6,9,32,128]{3,2,1,0:T(8,128)(2,1)} %pad_maximum_fusion.1), channel_id=1, source_target_pairs={{0,1},{1,2},{2,3},{3,4},{4,5},{5,6},{6,7},{8,9},{9,10},{10,11},{11... | collective-permute-start | bytes 1327112 | tf_op jit(solution)/shard_map/ppermute | solution.py:21
  65.3 17.0 %collective-permute-start.7 = (bf16[6,9,32,128]{3,2,1,0:T(8,128)(2,1)}, bf16[6,9,32,128]{3,2,1,0:T(8,128)(2,1)}, u32[]{:S(2)}, u32[]{:S(2)}) collective-permute-start(bf16[6,9,32,128]{3,2,1,0:T(8,128)(2,1)} %pad_maximum_fusion.2), channel_id=1, source_target_pairs={{1,0},{2,1},{3,2},{4,3},{5,4},{6,5},{7,6},{9,8},{10,9},{11,10},{12... | collective-permute-start | bytes 1327112 | tf_op jit(solution)/shard_map/ppermute | solution.py:21

commit v12 on v11

--- a/solution.py
+++ b/solution.py
@@ -96,11 +96,17 @@
     lax.fori_loop(0, ap_ref.shape[0], one_tile, 0)
 
 
+def own_kernel(where_ref, target_ref, ap_ref, pt_ref, acc_ref):
+    acc_ref[...] = jnp.zeros(acc_ref.shape, jnp.float32)
+    add_terms(where_ref, target_ref, ap_ref, pt_ref, acc_ref)
+
+
 def coarse_kernel(*refs):
-    groups = (len(refs) - 4) // 3
+    groups = (len(refs) - 5) // 3
     tables, pick_ref = refs[: 2 * groups], refs[2 * groups]
-    blocks, pt_ref, out_ref, acc_ref = refs[2 * groups + 1 : 3 * groups + 1], refs[-3], refs[-2], refs[-1]
-    acc_ref[...] = jnp.zeros(acc_ref.shape, jnp.float32)
+    blocks = refs[2 * groups + 1 : 3 * groups + 1]
+    pt_ref, part_ref, out_ref, acc_ref = refs[-4], refs[-3], refs[-2], refs[-1]
+    acc_ref[...] = part_ref[...]
     for i in range(groups):
         add_terms(tables[2 * i], tables[2 * i + 1], blocks[i], pt_ref, acc_ref)
     owned, stencil = out_ref.shape[0], out_ref.shape[1]
@@ -199,9 +205,20 @@
 
     p_t = jnp.swapaxes(p_ext, -1, -2).reshape(ext_r * ext_c * 4, bs, bs)
     stencil = c_cols.shape[-1]
+    smem = pl.BlockSpec(memory_space=pltpu.SMEM)
+    vmem = pl.BlockSpec(memory_space=pltpu.VMEM)
+    acc_shape = (o_r * o_c * 25, bs, bs)
+    part = pl.pallas_call(
+        own_kernel,
+        out_shape=jax.ShapeDtypeStruct(acc_shape, jnp.float32),
+        in_specs=[smem, smem, vmem, vmem],
+        out_specs=vmem,
+        cost_estimate=pl.CostEstimate(
+            flops=2 * bs * bs * bs * 9 * n_r * n_c * 4, bytes_accessed=6 * 1024 * 1024, transcendentals=0
+        ),
+    )(place[1:-1, 1:-1].reshape(-1), target[1:-1, 1:-1].reshape(-1), ap.reshape(n_r * n_c, 9, bs, bs), p_t)
     top, bottom, left, right = halo_sides(ap_dense)
     parts = [
-        (place[1:-1, 1:-1], target[1:-1, 1:-1], ap.reshape(n_r * n_c, 9, bs, bs)),
         (place[0, 1:-1], target[0, 1:-1], top),
         (place[-1, 1:-1], target[-1, 1:-1], bottom),
         (place[:, 0], target[:, 0], left),
@@ -210,15 +227,15 @@
     out = pl.pallas_call(
         coarse_kernel,
         out_shape=jax.ShapeDtypeStruct((o_r * o_c, stencil, bs, bs), jnp.bfloat16),
-        in_specs=[pl.BlockSpec(memory_space=pltpu.SMEM)] * (2 * len(parts) + 1)
-        + [pl.BlockSpec(memory_space=pltpu.VMEM)] * (len(parts) + 1),
-        out_specs=pl.BlockSpec(memory_space=pltpu.VMEM),
-        scratch_shapes=[pltpu.VMEM((o_r * o_c * 25, bs, bs), jnp.float32)],
+        in_specs=[smem] * (2 * len(parts) + 1) + [vmem] * (len(parts) + 2),
+        out_specs=vmem,
+        scratch_shapes=[pltpu.VMEM(acc_shape, jnp.float32)],
     )(
         *[t for w, g, _ in parts for t in (w.reshape(-1), g.reshape(-1))],
         pick,
         *[b for _, _, b in parts],
         p_t,
+        part,
     )
     return out.reshape(o_r, o_c, stencil, bs, bs)
 

time: 108 us -> 104 us (0.963)
  waiting for transfers between devices: 19.4 us -> 10.2 us
  Pallas kernels: 41.1 us -> 45.6 us
    ppermute x4, waiting for transfers between devices: 16.9 us -> 4.32 us  [shifted(): return lax.ppermute(piece, 'col', pairs)]
    pallas_call x0 -> x1, Pallas kernels: none -> 11.1 us  [body(): pl.pallas_call(own_kernel, out_shape=jax.ShapeDtypeStruct(acc_shape, jnp....]
    pallas_call x1, Pallas kernels: 25.3 us -> 18.7 us  [body(): pl.pallas_call(coarse_kernel, out_shape=jax.ShapeDtypeStruct((o_r * o_c,...]
    ppermute x4, waiting for transfers between devices: 2.51 us -> 5.88 us  [shifted(): return lax.ppermute(piece, 'row', pairs)]
  transfers between devices with their start and end apart: 8 -> 8, of which waited for: 5 -> 5; matrix products, arithmetic and copies ran while one was open for 15% -> 15% of each run, Pallas kernels for 0% -> 11%
where the time goes in v12:
time: 104 us; the launch traced here: 103 us
  Pallas kernels  45.6 us (44%)
  starting transfers between devices  22.8 us (22%)
  local copies, waits for them, and re-layouts  13.4 us (13%)
  other arithmetic  10.3 us (10%)
  waiting for transfers between devices  10.2 us (10%)
    pallas_call x1, Pallas kernels, body(): pl.pallas_call(coarse_kernel, out_shape=jax.ShapeDtypeStruct((o_r * o_c,...  18.7 us
    pallas_call x1, Pallas kernels, body(): pl.pallas_call(ap_kernel, out_shape=(jax.ShapeDtypeStruct((n_r * n_c, 9,...  15.8 us
    ppermute x4, starting transfers between devices, shifted(): return lax.ppermute(piece, 'col', pairs)  11.4 us
    ppermute x4, starting transfers between devices, shifted(): return lax.ppermute(piece, 'row', pairs)  11.3 us
    pallas_call x1, Pallas kernels, body(): pl.pallas_call(own_kernel, out_shape=jax.ShapeDtypeStruct(acc_shape, jnp....  11.1 us
    ppermute x4, waiting for transfers between devices, shifted(): return lax.ppermute(piece, 'row', pairs)  5.88 us
    ppermute x4, waiting for transfers between devices, shifted(): return lax.ppermute(piece, 'col', pairs)  4.32 us
    reduce_sum x1, other arithmetic, body(): jnp.sum(jnp.where(match[..., None, None], p_blocks[:, :, None], jnp.zeros...  2.77 us
  transfers between devices with their start and end apart: 8, of which 5 were waited for; matrix products, arithmetic and copies ran while one was open for 15% of the time, Pallas kernels for 11%

profile of v12, /device:TPU:9, one launch (start us, length us, event | category | flops | bytes accessed | tf_op | source)
XLA Modules:
  0.0 103.0 jit_solution(11297144989630136327)
XLA Ops:
  0.3 0.8 broadcast_compare_fusion
  1.1 2.8 %select_reduce_fusion = bf16[4,4,4,64,64]{4,3,2,1,0:T(8,128)(2,1)S(1)} fusion(pred[4,4,4,4]{3,2,1,0:T(4,128)(4,1)S(1)} %broadcast_compare_fusion, bf16[4,4,4,64,64]{4,3,2,1,0:T(8,128)(2,1)} %param.7), kind=kLoop, calls=%fused_computation | loop fusion | flops 1835008 | bytes 1048832 | tf_op jit(solution)/shard_map/reduce_sum | solution.py:143
  4.1 3.7 %collective-permute-start = (bf16[4,4,32,128]{3,2,1,0:T(8,128)(2,1)S(1)}, bf16[4,4,32,128]{3,2,1,0:T(8,128)(2,1)S(1)}, u32[]{:S(2)}, u32[]{:S(2)}) collective-permute-start(bf16[4,4,32,128]{3,2,1,0:T(8,128)(2,1)S(1)} %reshape_squeeze.22), channel_id=1, source_target_pairs={{0,8},{8,16},{16,24},{1,9},{9,17},{17,25},{2,10},{10,18},{18,26},{... | collective-permute-start | bytes 393224 | tf_op jit(solution)/shard_map/ppermute | solution.py:18
  7.9 1.9 %collective-permute-start.1 = (bf16[4,4,32,128]{3,2,1,0:T(8,128)(2,1)S(1)}, bf16[4,4,32,128]{3,2,1,0:T(8,128)(2,1)S(1)}, u32[]{:S(2)}, u32[]{:S(2)}) collective-permute-start(bf16[4,4,32,128]{3,2,1,0:T(8,128)(2,1)S(1)} %reshape_squeeze.23), channel_id=1, source_target_pairs={{8,0},{16,8},{24,16},{9,1},{17,9},{25,17},{10,2},{18,10},{26,18},{... | collective-permute-start | bytes 393224 | tf_op jit(solution)/shard_map/ppermute | solution.py:18
  11.0 0.6 and_select_fusion.slot_ref
  12.7 0.6 reshape.677.near_ref
  13.3 0.9 collective-permute-done.1
  14.2 3.1 %collective-permute-start.2 = (bf16[6,4,32,128]{3,2,1,0:T(8,128)(2,1)S(1)}, bf16[6,4,32,128]{3,2,1,0:T(8,128)(2,1)S(1)}, u32[]{:S(2)}, u32[]{:S(2)}) collective-permute-start(bf16[6,4,32,128]{3,2,1,0:T(8,128)(2,1)S(1)} %pad_maximum_fusion.3), channel_id=1, source_target_pairs={{0,1},{1,2},{2,3},{3,4},{4,5},{5,6},{6,7},{8,9},{9,10},{10,11},{11... | collective-permute-start | bytes 589832 | tf_op jit(solution)/shard_map/ppermute | solution.py:21
  17.4 3.0 %collective-permute-start.3 = (bf16[6,4,32,128]{3,2,1,0:T(8,128)(2,1)S(1)}, bf16[6,4,32,128]{3,2,1,0:T(8,128)(2,1)S(1)}, u32[]{:S(2)}, u32[]{:S(2)}) collective-permute-start(bf16[6,4,32,128]{3,2,1,0:T(8,128)(2,1)S(1)} %pad_maximum_fusion.4), channel_id=1, source_target_pairs={{1,0},{2,1},{3,2},{4,3},{5,4},{6,5},{7,6},{9,8},{10,9},{11,10},{12... | collective-permute-start | bytes 589832 | tf_op jit(solution)/shard_map/ppermute | solution.py:21
  20.4 0.6 slice_bitcast_fusion.2
  21.8 4.0 %collective-permute-done.3 = bf16[6,4,32,128]{3,2,1,0:T(8,128)(2,1)S(1)} collective-permute-done((bf16[6,4,32,128]{3,2,1,0:T(8,128)(2,1)S(1)}, bf16[6,4,32,128]{3,2,1,0:T(8,128)(2,1)S(1)}, u32[]{:S(2)}, u32[]{:S(2)}) %collective-permute-start.3) | collective-permute-done | bytes 196640 | tf_op jit(solution)/shard_map/ppermute | solution.py:21
  26.0 1.8 %pad_maximum_fusion = bf16[6,6,4,64,64]{4,3,2,1,0:T(8,128)(2,1)} fusion(bf16[6,1,4,64,64]{4,3,2,1,0:T(8,128)(2,1)S(1)} %bitcast.56, bf16[1,4,4,64,64]{4,3,2,1,0:T(8,128)(2,1)S(1)} %broadcast_in_dim_reshape.15, bf16[4,4,4,64,64]{4,3,2,1,0:T(8,128)(2,1)S(1)} %select_reduce_fusion, bf16[1,4,4,64,64]{4,3,2,1,0:T(8,128)(2,1)S(1)} %broadcast_in_dim_reshape.14, ...), kind=kLoop, calls=%fused_computation.1 | loop fusion | flops 2359296 | bytes 2359296 | tf_op jit(solution)/shard_map/concatenate | solution.py:49
  27.9 15.8 %shard_map.55 = (bf16[16,9,64,64]{3,2,1,0:T(8,128)(2,1)}, bf16[16,9,32,128]{3,2,1,0:T(8,128)(2,1)}) custom-call(s32[144]{0:T(256)} %reshape.677.near_ref, s32[576]{0:T(1024)} %and_select_fusion.slot_ref, bf16[16,9,64,64]{3,2,1,0:T(8,128)(2,1)} %bitcast.58, bf16[36,4,64,64]{3,2,1,0:T(8,128)(2,1)} %bitcast.53), custom_call_target="tpu_custom_call" | custom-call | tf_op jit(solution)/shard_map/pallas_call | solution.py:161
  43.7 1.1 %fusion.15 = (bf16[4,9,32,128]{3,2,1,0:T(8,128)(2,1)S(1)}, bf16[4,9,32,128]{3,2,1,0:T(8,128)(2,1)S(1)}) fusion(bf16[16,9,32,128]{3,2,1,0:T(8,128)(2,1)} %get-tuple-element.7), kind=kLoop, calls=%fused_computation.117 | loop fusion | bytes 1179648 | tf_op jit(solution)/shard_map/slice | solution.py:40
  44.8 3.8 %collective-permute-start.4 = (bf16[4,9,32,128]{3,2,1,0:T(8,128)(2,1)S(1)}, bf16[4,9,32,128]{3,2,1,0:T(8,128)(2,1)S(1)}, u32[]{:S(2)}, u32[]{:S(2)}) collective-permute-start(bf16[4,9,32,128]{3,2,1,0:T(8,128)(2,1)S(1)} %get-tuple-element.16), channel_id=1, source_target_pairs={{0,8},{8,16},{16,24},{1,9},{9,17},{17,25},{2,10},{10,18},{18,26},{... | collective-permute-start | bytes 884744 | tf_op jit(solution)/shard_map/ppermute | solution.py:18
  48.7 1.9 %collective-permute-start.5 = (bf16[4,9,32,128]{3,2,1,0:T(8,128)(2,1)S(1)}, bf16[4,9,32,128]{3,2,1,0:T(8,128)(2,1)S(1)}, u32[]{:S(2)}, u32[]{:S(2)}) collective-permute-start(bf16[4,9,32,128]{3,2,1,0:T(8,128)(2,1)S(1)} %get-tuple-element.15), channel_id=1, source_target_pairs={{8,0},{16,8},{24,16},{9,1},{17,9},{25,17},{10,2},{18,10},{26,18},{... | collective-permute-start | bytes 884744 | tf_op jit(solution)/shard_map/ppermute | solution.py:18
  50.6 1.1 %slice_bitcast_fusion = (bf16[4,9,32,128]{3,2,1,0:T(8,128)(2,1)S(1)}, bf16[4,9,32,128]{3,2,1,0:T(8,128)(2,1)S(1)}) fusion(bf16[4,4,9,32,128]{4,3,2,1,0:T(8,128)(2,1)} %bitcast.59), kind=kLoop, calls=%fused_computation.8 | loop fusion | bytes 1179648 | tf_op jit(solution)/shard_map/squeeze | solution.py:42
  52.3 4.5 %collective-permute-done.5.refs_10_ = bf16[4,9,32,128]{3,2,1,0:T(8,128)(2,1)S(1)} collective-permute-done((bf16[4,9,32,128]{3,2,1,0:T(8,128)(2,1)S(1)}, bf16[4,9,32,128]{3,2,1,0:T(8,128)(2,1)S(1)}, u32[]{:S(2)}, u32[]{:S(2)}) %collective-permute-start.5) | collective-permute-done | bytes 294944 | tf_op jit(solution)/shard_map/ppermute | solution.py:18
  56.8 0.9 pad_maximum_fusion.2
  57.6 2.3 %collective-permute-start.7 = (bf16[6,9,32,128]{3,2,1,0:T(8,128)(2,1)}, bf16[6,9,32,128]{3,2,1,0:T(8,128)(2,1)}, u32[]{:S(2)}, u32[]{:S(2)}) collective-permute-start(bf16[6,9,32,128]{3,2,1,0:T(8,128)(2,1)} %pad_maximum_fusion.2), channel_id=1, source_target_pairs={{1,0},{2,1},{3,2},{4,3},{5,4},{6,5},{7,6},{9,8},{10,9},{11,10},{12... | collective-permute-start | bytes 1327112 | tf_op jit(solution)/shard_map/ppermute | solution.py:21
  59.9 0.8 pad_maximum_fusion.1
  60.8 3.0 %collective-permute-start.6 = (bf16[6,9,32,128]{3,2,1,0:T(8,128)(2,1)}, bf16[6,9,32,128]{3,2,1,0:T(8,128)(2,1)}, u32[]{:S(2)}, u32[]{:S(2)}) collective-permute-start(bf16[6,9,32,128]{3,2,1,0:T(8,128)(2,1)} %pad_maximum_fusion.1), channel_id=1, source_target_pairs={{0,1},{1,2},{2,3},{3,4},{4,5},{5,6},{6,7},{8,9},{9,10},{10,11},{11... | collective-permute-start | bytes 1327112 | tf_op jit(solution)/shard_map/ppermute | solution.py:21
  63.9 0.7 reshape.683.target_ref
  64.5 0.6 reshape.682.where_ref
  65.7 0.6 reshape_squeeze.20.refs_5_
  66.3 0.6 reshape_squeeze.21.refs_7_
  67.5 0.6 reshape_squeeze.19.refs_3_
  68.1 0.8 slice_reduce_fusion
  68.9 1.8 %fusion.23 = bf16[6,6,4,64,64]{3,4,2,1,0:T(8,128)(2,1)S(1)} fusion(bf16[6,1,4,64,64]{4,3,2,1,0:T(8,128)(2,1)} %bitcast.57, bf16[1,4,4,64,64]{4,3,2,1,0:T(8,128)(2,1)} %copy-done.3, bf16[4,4,4,64,64]{4,3,2,1,0:T(8,128)(2,1)S(1)} %select_reduce_fusion, bf16[1,4,4,64,64]{4,3,2,1,0:T(8,128)(2,1)} %copy-done.2, bf16[6,1,4,64,64]{4,3,2,1,0:T(8,128)(2,1)} %bitcast.55), kind=kLoop, calls=%fused_computation.125 | loop fusion | flops 2359296 | bytes 2359296 | tf_op jit(solution)/shard_map/transpose | solution.py:206
  70.7 2.5 %copy.41 = bf16[6,6,4,64,64]{4,3,2,1,0:T(8,128)(2,1)} copy(bf16[6,6,4,64,64]{3,4,2,1,0:T(8,128)(2,1)S(1)} %fusion.23) | data formatting | bytes 2359296 | tf_op jit(solution)/shard_map/transpose | solution.py:206
  73.2 11.1 %shard_map.56.refs_14_ = f32[100,64,64]{2,1,0:T(8,128)} custom-call(s32[16]{0:T(128)} %reshape.682.where_ref, s32[64]{0:T(128)} %reshape.683.target_ref, bf16[16,9,64,64]{3,2,1,0:T(8,128)(2,1)} %get-tuple-element.8.ap_ref, bf16[144,64,64]{2,1,0:T(8,128)(2,1)} %bitcast.51), custom_call_target="tpu_custom_call" | custom-call | flops 301989888 | bytes 6291456 | tf_op jit(solution)/shard_map/pallas_call | solution.py:211
  84.3 18.7 %shard_map.57 = bf16[4,25,64,64]{3,2,1,0:T(8,128)(2,1)} custom-call(s32[4]{0:T(128)} %get-tuple-element.35.refs_0_, s32[16]{0:T(128)} %reshape_squeeze.18.refs_1_, s32[4]{0:T(128)} %get-tuple-element.34.refs_2_, s32[16]{0:T(128)} %reshape_squeeze.19.refs_3_, s32[6]{0:T(128)} %get-tuple-element.12.refs_4_, s32[24]{0:T(128)} %reshape_squeeze.20.refs_5_, ...), custom_call_target="tpu_custom_call" | custom-call | tf_op jit(solution)/shard_map/pallas_call | solution.py:227
  (85 shorter events, 5.3 us)
Async XLA Ops:
  1.1 9.2 %copy-start.6 = (s32[4,4,9]{2,1,0:T(4,128)S(1)}, s32[4,4,9]{2,1,0:T(4,128)}, u32[]{:S(2)}) copy-start(s32[4,4,9]{2,1,0:T(4,128)} %param.6) | copy-start | bytes 1732
  4.1 9.2 %collective-permute-start = (bf16[4,4,32,128]{3,2,1,0:T(8,128)(2,1)S(1)}, bf16[4,4,32,128]{3,2,1,0:T(8,128)(2,1)S(1)}, u32[]{:S(2)}, u32[]{:S(2)}) collective-permute-start(bf16[4,4,32,128]{3,2,1,0:T(8,128)(2,1)S(1)} %reshape_squeeze.22), channel_id=1, source_target_pairs={{0,8},{8,16},{16,24},{1,9},{9,17},{17,25},{2,10},{10,18},{18,26},{... | collective-permute-start | bytes 393224 | tf_op jit(solution)/shard_map/ppermute | solution.py:18
  7.9 6.3 %collective-permute-start.1 = (bf16[4,4,32,128]{3,2,1,0:T(8,128)(2,1)S(1)}, bf16[4,4,32,128]{3,2,1,0:T(8,128)(2,1)S(1)}, u32[]{:S(2)}, u32[]{:S(2)}) collective-permute-start(bf16[4,4,32,128]{3,2,1,0:T(8,128)(2,1)S(1)} %reshape_squeeze.23), channel_id=1, source_target_pairs={{8,0},{16,8},{24,16},{9,1},{17,9},{25,17},{10,2},{18,10},{26,18},{... | collective-permute-start | bytes 393224 | tf_op jit(solution)/shard_map/ppermute | solution.py:18
  14.2 7.4 %collective-permute-start.2 = (bf16[6,4,32,128]{3,2,1,0:T(8,128)(2,1)S(1)}, bf16[6,4,32,128]{3,2,1,0:T(8,128)(2,1)S(1)}, u32[]{:S(2)}, u32[]{:S(2)}) collective-permute-start(bf16[6,4,32,128]{3,2,1,0:T(8,128)(2,1)S(1)} %pad_maximum_fusion.3), channel_id=1, source_target_pairs={{0,1},{1,2},{2,3},{3,4},{4,5},{5,6},{6,7},{8,9},{9,10},{10,11},{11... | collective-permute-start | bytes 589832 | tf_op jit(solution)/shard_map/ppermute | solution.py:21
  17.4 8.4 %collective-permute-start.3 = (bf16[6,4,32,128]{3,2,1,0:T(8,128)(2,1)S(1)}, bf16[6,4,32,128]{3,2,1,0:T(8,128)(2,1)S(1)}, u32[]{:S(2)}, u32[]{:S(2)}) collective-permute-start(bf16[6,4,32,128]{3,2,1,0:T(8,128)(2,1)S(1)} %pad_maximum_fusion.4), channel_id=1, source_target_pairs={{1,0},{2,1},{3,2},{4,3},{5,4},{6,5},{7,6},{9,8},{10,9},{11,10},{12... | collective-permute-start | bytes 589832 | tf_op jit(solution)/shard_map/ppermute | solution.py:21
  21.2 6.7 %copy-start.2 = (bf16[1,4,4,64,64]{4,3,2,1,0:T(8,128)(2,1)}, bf16[1,4,4,64,64]{4,3,2,1,0:T(8,128)(2,1)S(1)}, u32[]{:S(2)}) copy-start(bf16[1,4,4,64,64]{4,3,2,1,0:T(8,128)(2,1)S(1)} %broadcast_in_dim_reshape.14) | copy-start | bytes 393220
  21.3 6.5 %copy-start.3 = (bf16[1,4,4,64,64]{4,3,2,1,0:T(8,128)(2,1)}, bf16[1,4,4,64,64]{4,3,2,1,0:T(8,128)(2,1)S(1)}, u32[]{:S(2)}) copy-start(bf16[1,4,4,64,64]{4,3,2,1,0:T(8,128)(2,1)S(1)} %broadcast_in_dim_reshape.15) | copy-start | bytes 393220
  21.8 6.0 %copy-start = (bf16[6,1,4,64,64]{4,3,2,0,1:T(8,128)(2,1)}, bf16[6,1,4,64,64]{4,3,2,0,1:T(8,128)(2,1)S(1)}, u32[]{:S(2)}) copy-start(bf16[6,1,4,64,64]{4,3,2,0,1:T(8,128)(2,1)S(1)} %broadcast_in_dim_reshape.13) | copy-start | bytes 589828
  26.0 1.8 %copy-start.1 = (bf16[6,1,4,64,64]{4,3,2,0,1:T(8,128)(2,1)}, bf16[6,1,4,64,64]{4,3,2,0,1:T(8,128)(2,1)S(1)}, u32[]{:S(2)}) copy-start(bf16[6,1,4,64,64]{4,3,2,0,1:T(8,128)(2,1)S(1)} %broadcast_in_dim_reshape.16) | copy-start | bytes 589828
  27.9 20.7 %copy-start.7 = (s32[2,2,25]{2,1,0:T(2,128)S(1)}, s32[2,2,25]{2,1,0:T(2,128)}, u32[]{:S(2)}) copy-start(s32[2,2,25]{2,1,0:T(2,128)} %param.9) | copy-start | bytes 1204
  44.8 7.5 %collective-permute-start.4 = (bf16[4,9,32,128]{3,2,1,0:T(8,128)(2,1)S(1)}, bf16[4,9,32,128]{3,2,1,0:T(8,128)(2,1)S(1)}, u32[]{:S(2)}, u32[]{:S(2)}) collective-permute-start(bf16[4,9,32,128]{3,2,1,0:T(8,128)(2,1)S(1)} %get-tuple-element.16), channel_id=1, source_target_pairs={{0,8},{8,16},{16,24},{1,9},{9,17},{17,25},{2,10},{10,18},{18,26},{... | collective-permute-start | bytes 884744 | tf_op jit(solution)/shard_map/ppermute | solution.py:18
  48.7 8.0 %collective-permute-start.5 = (bf16[4,9,32,128]{3,2,1,0:T(8,128)(2,1)S(1)}, bf16[4,9,32,128]{3,2,1,0:T(8,128)(2,1)S(1)}, u32[]{:S(2)}, u32[]{:S(2)}) collective-permute-start(bf16[4,9,32,128]{3,2,1,0:T(8,128)(2,1)S(1)} %get-tuple-element.15), channel_id=1, source_target_pairs={{8,0},{16,8},{24,16},{9,1},{17,9},{25,17},{10,2},{18,10},{26,18},{... | collective-permute-start | bytes 884744 | tf_op jit(solution)/shard_map/ppermute | solution.py:18
  52.3 8.5 %copy-start.4 = (bf16[4,9,32,128]{3,2,1,0:T(8,128)(2,1)}, bf16[4,9,32,128]{3,2,1,0:T(8,128)(2,1)S(1)}, u32[]{:S(2)}) copy-start(bf16[4,9,32,128]{3,2,1,0:T(8,128)(2,1)S(1)} %collective-permute-done.4.refs_9_) | copy-start | bytes 884740
  56.7 7.0 %copy-start.5 = (bf16[4,9,32,128]{3,2,1,0:T(8,128)(2,1)}, bf16[4,9,32,128]{3,2,1,0:T(8,128)(2,1)S(1)}, u32[]{:S(2)}) copy-start(bf16[4,9,32,128]{3,2,1,0:T(8,128)(2,1)S(1)} %collective-permute-done.5.refs_10_) | copy-start | bytes 884740
  57.6 26.7 %collective-permute-start.7 = (bf16[6,9,32,128]{3,2,1,0:T(8,128)(2,1)}, bf16[6,9,32,128]{3,2,1,0:T(8,128)(2,1)}, u32[]{:S(2)}, u32[]{:S(2)}) collective-permute-start(bf16[6,9,32,128]{3,2,1,0:T(8,128)(2,1)} %pad_maximum_fusion.2), channel_id=1, source_target_pairs={{1,0},{2,1},{3,2},{4,3},{5,4},{6,5},{7,6},{9,8},{10,9},{11,10},{12... | collective-permute-start | bytes 1327112 | tf_op jit(solution)/shard_map/ppermute | solution.py:21
  60.8 23.6 %collective-permute-start.6 = (bf16[6,9,32,128]{3,2,1,0:T(8,128)(2,1)}, bf16[6,9,32,128]{3,2,1,0:T(8,128)(2,1)}, u32[]{:S(2)}, u32[]{:S(2)}) collective-permute-start(bf16[6,9,32,128]{3,2,1,0:T(8,128)(2,1)} %pad_maximum_fusion.1), channel_id=1, source_target_pairs={{0,1},{1,2},{2,3},{3,4},{4,5},{5,6},{6,7},{8,9},{9,10},{10,11},{11... | collective-permute-start | bytes 1327112 | tf_op jit(solution)/shard_map/ppermute | solution.py:21

commit v13 on v12

--- a/solution.py
+++ b/solution.py
@@ -1,3 +1,5 @@
+import functools
+
 import jax
 import jax.numpy as jnp
 from jax import lax
@@ -56,7 +58,7 @@
     )
 
 
-def ap_kernel(near_ref, slot_ref, a_ref, p_ref, out_ref, dense_ref, acc_ref):
+def ap_kernel(near_ref, slot_ref, a_ref, p_ref, out_ref, dense_ref, acc_ref, *, n_r, n_c):
     tiles, terms = a_ref.shape[0], a_ref.shape[1]
 
     def one_tile(t, carry):
@@ -72,7 +74,12 @@
 
         ap = acc_ref[...].astype(out_ref.dtype)
         out_ref[t] = ap
-        dense_ref[t] = ap.reshape(dense_ref.shape[1:])
+        row, col = t // n_c, t % n_c
+
+        @pl.when((row == 0) | (row == n_r - 1) | (col == 0) | (col == n_c - 1))
+        def _():
+            dense_ref[t] = ap.reshape(dense_ref.shape[1:])
+
         return carry
 
     lax.fori_loop(0, tiles, one_tile, 0)
@@ -87,9 +94,11 @@
 
             @pl.when(g >= 0)
             def _():
-                pt = pt_ref[w * 4 + q]
+                p = pt_ref[w * 4 + q]
                 for e in range(9):
-                    acc_ref[g + (e // 3) * 5 + e % 3] += jnp.dot(pt, blocks[e], preferred_element_type=jnp.float32)
+                    acc_ref[g + (e // 3) * 5 + e % 3] += lax.dot_general(
+                        p, blocks[e], (((0,), (0,)), ((), ())), preferred_element_type=jnp.float32
+                    )
 
         return carry
 
@@ -159,7 +168,7 @@
     slot = jnp.where((slot >= 0) & (slot < 9), slot, -1)
 
     ap, ap_dense = pl.pallas_call(
-        ap_kernel,
+        functools.partial(ap_kernel, n_r=n_r, n_c=n_c),
         out_shape=(
             jax.ShapeDtypeStruct((n_r * n_c, 9, bs, bs), jnp.bfloat16),
             jax.ShapeDtypeStruct((n_r * n_c, 9, bs * bs // 128, 128), jnp.bfloat16),
@@ -203,7 +212,7 @@
     pick = (c_cols // coarse_cols - cy[:, None, None] + 2) * 5 + (c_cols % coarse_cols - cx[None, :, None] + 2)
     pick = jnp.clip(pick, 0, 24).reshape(-1)
 
-    p_t = jnp.swapaxes(p_ext, -1, -2).reshape(ext_r * ext_c * 4, bs, bs)
+    p_t = p_ext.reshape(ext_r * ext_c * 4, bs, bs)
     stencil = c_cols.shape[-1]
     smem = pl.BlockSpec(memory_space=pltpu.SMEM)
     vmem = pl.BlockSpec(memory_space=pltpu.VMEM)

time: 104 us -> 102 us (0.981)
  other arithmetic: 10.3 us -> 6.86 us
  Pallas kernels: 45.6 us -> 48 us
  local copies, waits for them, and re-layouts: 13.4 us -> 11.9 us
    transpose x1 -> x0, local copies, waits for them, and re-layouts: 2.47 us -> none  [body(): p_t = jnp.swapaxes(p_ext, -1, -2).reshape(ext_r * ext_c * 4, bs, bs)]
    transpose x1 -> x0, other arithmetic: 1.84 us -> none  [body(): p_t = jnp.swapaxes(p_ext, -1, -2).reshape(ext_r * ext_c * 4, bs, bs)]
    pallas_call x1, Pallas kernels: 11.1 us -> 12.8 us  [body(): pl.pallas_call(own_kernel, out_shape=jax.ShapeDtypeStruct(acc_shape, jnp....]
    pallas_call x1, Pallas kernels: 18.7 us -> 20.1 us  [body(): pl.pallas_call(coarse_kernel, out_shape=jax.ShapeDtypeStruct((o_r * o_c,...]
  transfers between devices with their start and end apart: 8 -> 8, of which waited for: 5 -> 4; matrix products, arithmetic and copies ran while one was open for 15% -> 11% of each run, Pallas kernels for 11% -> 13%
where the time goes in v13:
time: 102 us; the launch traced here: 101 us
  Pallas kernels  48 us (47%)
  starting transfers between devices  22.8 us (22%)
  local copies, waits for them, and re-layouts  11.9 us (12%)
  waiting for transfers between devices  10.7 us (10%)
  other arithmetic  6.86 us (7%)
    pallas_call x1, Pallas kernels, body(): pl.pallas_call(coarse_kernel, out_shape=jax.ShapeDtypeStruct((o_r * o_c,...  20.1 us
    pallas_call x1, Pallas kernels, body(): pl.pallas_call(functools.partial(ap_kernel, n_r=n_r, n_c=n_c), out_shape=...  15.1 us
    pallas_call x1, Pallas kernels, body(): pl.pallas_call(own_kernel, out_shape=jax.ShapeDtypeStruct(acc_shape, jnp....  12.8 us
    ppermute x4, starting transfers between devices, shifted(): return lax.ppermute(piece, 'col', pairs)  11.5 us
    ppermute x4, starting transfers between devices, shifted(): return lax.ppermute(piece, 'row', pairs)  11.3 us
    ppermute x4, waiting for transfers between devices, shifted(): return lax.ppermute(piece, 'row', pairs)  5.87 us
    ppermute x4, waiting for transfers between devices, shifted(): return lax.ppermute(piece, 'col', pairs)  4.85 us
    reduce_sum x1, other arithmetic, body(): jnp.sum(jnp.where(match[..., None, None], p_blocks[:, :, None], jnp.zeros...  2.77 us
  transfers between devices with their start and end apart: 8, of which 4 were waited for; matrix products, arithmetic and copies ran while one was open for 11% of the time, Pallas kernels for 13%

profile of v13, /device:TPU:9, one launch (start us, length us, event | category | flops | bytes accessed | tf_op | source)
XLA Modules:
  0.0 101.0 jit_solution(1762770666319175162)
XLA Ops:
  0.3 0.8 broadcast_compare_fusion
  1.1 2.8 %select_reduce_fusion = bf16[4,4,4,64,64]{4,3,2,1,0:T(8,128)(2,1)S(1)} fusion(pred[4,4,4,4]{3,2,1,0:T(4,128)(4,1)S(1)} %broadcast_compare_fusion, bf16[4,4,4,64,64]{4,3,2,1,0:T(8,128)(2,1)} %param.7), kind=kLoop, calls=%fused_computation | loop fusion | flops 1835008 | bytes 1048832 | tf_op jit(solution)/shard_map/reduce_sum | solution.py:152
  4.1 3.7 %collective-permute-start = (bf16[4,4,32,128]{3,2,1,0:T(8,128)(2,1)S(1)}, bf16[4,4,32,128]{3,2,1,0:T(8,128)(2,1)S(1)}, u32[]{:S(2)}, u32[]{:S(2)}) collective-permute-start(bf16[4,4,32,128]{3,2,1,0:T(8,128)(2,1)S(1)} %reshape_squeeze.22), channel_id=1, source_target_pairs={{0,8},{8,16},{16,24},{1,9},{9,17},{17,25},{2,10},{10,18},{18,26},{... | collective-permute-start | bytes 393224 | tf_op jit(solution)/shard_map/ppermute | solution.py:20
  7.9 1.9 %collective-permute-start.1 = (bf16[4,4,32,128]{3,2,1,0:T(8,128)(2,1)S(1)}, bf16[4,4,32,128]{3,2,1,0:T(8,128)(2,1)S(1)}, u32[]{:S(2)}, u32[]{:S(2)}) collective-permute-start(bf16[4,4,32,128]{3,2,1,0:T(8,128)(2,1)S(1)} %reshape_squeeze.23), channel_id=1, source_target_pairs={{8,0},{16,8},{24,16},{9,1},{17,9},{25,17},{10,2},{18,10},{26,18},{... | collective-permute-start | bytes 393224 | tf_op jit(solution)/shard_map/ppermute | solution.py:20
  10.7 0.6 and_select_fusion.slot_ref
  12.6 0.6 reshape.677.near_ref
  13.3 0.9 collective-permute-done.1
  14.2 3.1 %collective-permute-start.2 = (bf16[6,4,32,128]{3,2,1,0:T(8,128)(2,1)S(1)}, bf16[6,4,32,128]{3,2,1,0:T(8,128)(2,1)S(1)}, u32[]{:S(2)}, u32[]{:S(2)}) collective-permute-start(bf16[6,4,32,128]{3,2,1,0:T(8,128)(2,1)S(1)} %pad_maximum_fusion.3), channel_id=1, source_target_pairs={{0,1},{1,2},{2,3},{3,4},{4,5},{5,6},{6,7},{8,9},{9,10},{10,11},{11... | collective-permute-start | bytes 589832 | tf_op jit(solution)/shard_map/ppermute | solution.py:23
  17.4 3.0 %collective-permute-start.3 = (bf16[6,4,32,128]{3,2,1,0:T(8,128)(2,1)S(1)}, bf16[6,4,32,128]{3,2,1,0:T(8,128)(2,1)S(1)}, u32[]{:S(2)}, u32[]{:S(2)}) collective-permute-start(bf16[6,4,32,128]{3,2,1,0:T(8,128)(2,1)S(1)} %pad_maximum_fusion.4), channel_id=1, source_target_pairs={{1,0},{2,1},{3,2},{4,3},{5,4},{6,5},{7,6},{9,8},{10,9},{11,10},{12... | collective-permute-start | bytes 589832 | tf_op jit(solution)/shard_map/ppermute | solution.py:23
  20.8 0.8 collective-permute-done.2
  21.8 4.0 %collective-permute-done.3 = bf16[6,4,32,128]{3,2,1,0:T(8,128)(2,1)S(1)} collective-permute-done((bf16[6,4,32,128]{3,2,1,0:T(8,128)(2,1)S(1)}, bf16[6,4,32,128]{3,2,1,0:T(8,128)(2,1)S(1)}, u32[]{:S(2)}, u32[]{:S(2)}) %collective-permute-start.3) | collective-permute-done | bytes 196640 | tf_op jit(solution)/shard_map/ppermute | solution.py:23
  26.0 1.8 %pad_maximum_fusion = bf16[6,6,4,64,64]{4,3,2,1,0:T(8,128)(2,1)} fusion(bf16[6,1,4,64,64]{4,3,2,1,0:T(8,128)(2,1)S(1)} %broadcast_in_dim_reshape.16, bf16[1,4,4,64,64]{4,3,2,1,0:T(8,128)(2,1)S(1)} %broadcast_in_dim_reshape.15, bf16[4,4,4,64,64]{4,3,2,1,0:T(8,128)(2,1)S(1)} %select_reduce_fusion, bf16[1,4,4,64,64]{4,3,2,1,0:T(8,128)(2,1)S(1)} %broadcast_in_dim_reshape.14, ...), kind=kLoop, calls=%fused_computation.1 | loop fusion | flops 2359296 | bytes 2359296 | tf_op jit(solution)/shard_map/concatenate | solution.py:51
  27.9 15.1 %shard_map.55 = (bf16[16,9,64,64]{3,2,1,0:T(8,128)(2,1)}, bf16[16,9,32,128]{3,2,1,0:T(8,128)(2,1)}) custom-call(s32[144]{0:T(256)} %reshape.677.near_ref, s32[576]{0:T(1024)} %and_select_fusion.slot_ref, bf16[16,9,64,64]{3,2,1,0:T(8,128)(2,1)} %bitcast.50, bf16[36,4,64,64]{3,2,1,0:T(8,128)(2,1)} %bitcast.47), custom_call_target="tpu_custom_call" | custom-call | tf_op jit(solution)/shard_map/pallas_call | solution.py:170
  43.0 1.1 %fusion.15 = (bf16[4,9,32,128]{3,2,1,0:T(8,128)(2,1)S(1)}, bf16[4,9,32,128]{3,2,1,0:T(8,128)(2,1)S(1)}) fusion(bf16[16,9,32,128]{3,2,1,0:T(8,128)(2,1)} %get-tuple-element.7), kind=kLoop, calls=%fused_computation.117 | loop fusion | bytes 1179648 | tf_op jit(solution)/shard_map/slice | solution.py:42
  44.1 3.8 %collective-permute-start.4 = (bf16[4,9,32,128]{3,2,1,0:T(8,128)(2,1)S(1)}, bf16[4,9,32,128]{3,2,1,0:T(8,128)(2,1)S(1)}, u32[]{:S(2)}, u32[]{:S(2)}) collective-permute-start(bf16[4,9,32,128]{3,2,1,0:T(8,128)(2,1)S(1)} %get-tuple-element.16), channel_id=1, source_target_pairs={{0,8},{8,16},{16,24},{1,9},{9,17},{17,25},{2,10},{10,18},{18,26},{... | collective-permute-start | bytes 884744 | tf_op jit(solution)/shard_map/ppermute | solution.py:20
  47.9 0.7 reshape.683.target_ref
  48.6 0.6 reshape.682.where_ref
  49.2 0.6 reshape.676.refs_8_
  49.8 1.9 %collective-permute-start.5 = (bf16[4,9,32,128]{3,2,1,0:T(8,128)(2,1)S(1)}, bf16[4,9,32,128]{3,2,1,0:T(8,128)(2,1)S(1)}, u32[]{:S(2)}, u32[]{:S(2)}) collective-permute-start(bf16[4,9,32,128]{3,2,1,0:T(8,128)(2,1)S(1)} %get-tuple-element.15), channel_id=1, source_target_pairs={{8,0},{16,8},{24,16},{9,1},{17,9},{25,17},{10,2},{18,10},{26,18},{... | collective-permute-start | bytes 884744 | tf_op jit(solution)/shard_map/ppermute | solution.py:20
  51.7 1.1 %slice_bitcast_fusion = (bf16[4,9,32,128]{3,2,1,0:T(8,128)(2,1)S(1)}, bf16[4,9,32,128]{3,2,1,0:T(8,128)(2,1)S(1)}) fusion(bf16[4,4,9,32,128]{4,3,2,1,0:T(8,128)(2,1)} %bitcast.51), kind=kLoop, calls=%fused_computation.8 | loop fusion | bytes 1179648 | tf_op jit(solution)/shard_map/squeeze | solution.py:44
  52.8 5.0 %collective-permute-done.5.refs_10_ = bf16[4,9,32,128]{3,2,1,0:T(8,128)(2,1)S(1)} collective-permute-done((bf16[4,9,32,128]{3,2,1,0:T(8,128)(2,1)S(1)}, bf16[4,9,32,128]{3,2,1,0:T(8,128)(2,1)S(1)}, u32[]{:S(2)}, u32[]{:S(2)}) %collective-permute-start.5) | collective-permute-done | bytes 294944 | tf_op jit(solution)/shard_map/ppermute | solution.py:20
  57.9 2.3 %collective-permute-start.7 = (bf16[6,9,32,128]{3,2,1,0:T(8,128)(2,1)S(1)}, bf16[6,9,32,128]{3,2,1,0:T(8,128)(2,1)S(1)}, u32[]{:S(2)}, u32[]{:S(2)}) collective-permute-start(bf16[6,9,32,128]{3,2,1,0:T(8,128)(2,1)S(1)} %pad_maximum_fusion.2), channel_id=1, source_target_pairs={{1,0},{2,1},{3,2},{4,3},{5,4},{6,5},{7,6},{9,8},{10,9},{11,10},{12... | collective-permute-start | bytes 1327112 | tf_op jit(solution)/shard_map/ppermute | solution.py:23
  60.3 3.0 %collective-permute-start.6 = (bf16[6,9,32,128]{3,2,1,0:T(8,128)(2,1)S(1)}, bf16[6,9,32,128]{3,2,1,0:T(8,128)(2,1)S(1)}, u32[]{:S(2)}, u32[]{:S(2)}) collective-permute-start(bf16[6,9,32,128]{3,2,1,0:T(8,128)(2,1)S(1)} %pad_maximum_fusion.1), channel_id=1, source_target_pairs={{0,1},{1,2},{2,3},{3,4},{4,5},{5,6},{6,7},{8,9},{9,10},{10,11},{11... | collective-permute-start | bytes 1327112 | tf_op jit(solution)/shard_map/ppermute | solution.py:23
  63.3 0.6 reshape_squeeze.20.refs_5_
  63.9 0.7 reshape_squeeze.21.refs_7_
  64.6 0.6 reshape_squeeze.18.refs_1_
  65.2 0.6 reshape_squeeze.19.refs_3_
  65.8 0.7 slice_reduce_fusion
  66.5 0.6 slice_bitcast_fusion.2
  67.1 12.8 %shard_map.56.refs_14_ = f32[100,64,64]{2,1,0:T(8,128)} custom-call(s32[16]{0:T(128)} %reshape.682.where_ref, s32[64]{0:T(128)} %reshape.683.target_ref, bf16[16,9,64,64]{3,2,1,0:T(8,128)(2,1)} %get-tuple-element.8.ap_ref, bf16[144,64,64]{2,1,0:T(8,128)(2,1)} %bitcast.48), custom_call_target="tpu_custom_call" | custom-call | flops 301989888 | bytes 6291456 | tf_op jit(solution)/shard_map/pallas_call | solution.py:220
  80.0 0.7 copy-done.2
  80.9 20.1 %shard_map.57 = bf16[4,25,64,64]{3,2,1,0:T(8,128)(2,1)} custom-call(s32[4]{0:T(128)} %get-tuple-element.35.refs_0_, s32[16]{0:T(128)} %reshape_squeeze.18.refs_1_, s32[4]{0:T(128)} %get-tuple-element.34.refs_2_, s32[16]{0:T(128)} %reshape_squeeze.19.refs_3_, s32[6]{0:T(128)} %get-tuple-element.12.refs_4_, s32[24]{0:T(128)} %reshape_squeeze.20.refs_5_, ...), custom_call_target="tpu_custom_call" | custom-call | tf_op jit(solution)/shard_map/pallas_call | solution.py:236
  (79 shorter events, 3.5 us)
Async XLA Ops:
  1.1 8.9 %copy-start.4 = (s32[4,4,9]{2,1,0:T(4,128)S(1)}, s32[4,4,9]{2,1,0:T(4,128)}, u32[]{:S(2)}) copy-start(s32[4,4,9]{2,1,0:T(4,128)} %param.6) | copy-start | bytes 1732
  3.9 16.6 %copy-start.5 = (s32[2,2,25]{2,1,0:T(2,128)S(1)}, s32[2,2,25]{2,1,0:T(2,128)}, u32[]{:S(2)}) copy-start(s32[2,2,25]{2,1,0:T(2,128)} %param.9) | copy-start | bytes 1204
  4.1 9.2 %collective-permute-start = (bf16[4,4,32,128]{3,2,1,0:T(8,128)(2,1)S(1)}, bf16[4,4,32,128]{3,2,1,0:T(8,128)(2,1)S(1)}, u32[]{:S(2)}, u32[]{:S(2)}) collective-permute-start(bf16[4,4,32,128]{3,2,1,0:T(8,128)(2,1)S(1)} %reshape_squeeze.22), channel_id=1, source_target_pairs={{0,8},{8,16},{16,24},{1,9},{9,17},{17,25},{2,10},{10,18},{18,26},{... | collective-permute-start | bytes 393224 | tf_op jit(solution)/shard_map/ppermute | solution.py:20
  7.9 6.3 %collective-permute-start.1 = (bf16[4,4,32,128]{3,2,1,0:T(8,128)(2,1)S(1)}, bf16[4,4,32,128]{3,2,1,0:T(8,128)(2,1)S(1)}, u32[]{:S(2)}, u32[]{:S(2)}) collective-permute-start(bf16[4,4,32,128]{3,2,1,0:T(8,128)(2,1)S(1)} %reshape_squeeze.23), channel_id=1, source_target_pairs={{8,0},{16,8},{24,16},{9,1},{17,9},{25,17},{10,2},{18,10},{26,18},{... | collective-permute-start | bytes 393224 | tf_op jit(solution)/shard_map/ppermute | solution.py:20
  14.2 7.4 %collective-permute-start.2 = (bf16[6,4,32,128]{3,2,1,0:T(8,128)(2,1)S(1)}, bf16[6,4,32,128]{3,2,1,0:T(8,128)(2,1)S(1)}, u32[]{:S(2)}, u32[]{:S(2)}) collective-permute-start(bf16[6,4,32,128]{3,2,1,0:T(8,128)(2,1)S(1)} %pad_maximum_fusion.3), channel_id=1, source_target_pairs={{0,1},{1,2},{2,3},{3,4},{4,5},{5,6},{6,7},{8,9},{9,10},{10,11},{11... | collective-permute-start | bytes 589832 | tf_op jit(solution)/shard_map/ppermute | solution.py:23
  17.4 8.4 %collective-permute-start.3 = (bf16[6,4,32,128]{3,2,1,0:T(8,128)(2,1)S(1)}, bf16[6,4,32,128]{3,2,1,0:T(8,128)(2,1)S(1)}, u32[]{:S(2)}, u32[]{:S(2)}) collective-permute-start(bf16[6,4,32,128]{3,2,1,0:T(8,128)(2,1)S(1)} %pad_maximum_fusion.4), channel_id=1, source_target_pairs={{1,0},{2,1},{3,2},{4,3},{5,4},{6,5},{7,6},{9,8},{10,9},{11,10},{12... | collective-permute-start | bytes 589832 | tf_op jit(solution)/shard_map/ppermute | solution.py:23
  44.1 8.7 %collective-permute-start.4 = (bf16[4,9,32,128]{3,2,1,0:T(8,128)(2,1)S(1)}, bf16[4,9,32,128]{3,2,1,0:T(8,128)(2,1)S(1)}, u32[]{:S(2)}, u32[]{:S(2)}) collective-permute-start(bf16[4,9,32,128]{3,2,1,0:T(8,128)(2,1)S(1)} %get-tuple-element.16), channel_id=1, source_target_pairs={{0,8},{8,16},{16,24},{1,9},{9,17},{17,25},{2,10},{10,18},{18,26},{... | collective-permute-start | bytes 884744 | tf_op jit(solution)/shard_map/ppermute | solution.py:20
  49.8 8.0 %collective-permute-start.5 = (bf16[4,9,32,128]{3,2,1,0:T(8,128)(2,1)S(1)}, bf16[4,9,32,128]{3,2,1,0:T(8,128)(2,1)S(1)}, u32[]{:S(2)}, u32[]{:S(2)}) collective-permute-start(bf16[4,9,32,128]{3,2,1,0:T(8,128)(2,1)S(1)} %get-tuple-element.15), channel_id=1, source_target_pairs={{8,0},{16,8},{24,16},{9,1},{17,9},{25,17},{10,2},{18,10},{26,18},{... | collective-permute-start | bytes 884744 | tf_op jit(solution)/shard_map/ppermute | solution.py:20
  52.8 27.1 %copy-start = (bf16[4,9,32,128]{3,2,1,0:T(8,128)(2,1)}, bf16[4,9,32,128]{3,2,1,0:T(8,128)(2,1)S(1)}, u32[]{:S(2)}) copy-start(bf16[4,9,32,128]{3,2,1,0:T(8,128)(2,1)S(1)} %collective-permute-done.4.refs_9_) | copy-start | bytes 884740
  57.8 22.1 %copy-start.1 = (bf16[4,9,32,128]{3,2,1,0:T(8,128)(2,1)}, bf16[4,9,32,128]{3,2,1,0:T(8,128)(2,1)S(1)}, u32[]{:S(2)}) copy-start(bf16[4,9,32,128]{3,2,1,0:T(8,128)(2,1)S(1)} %collective-permute-done.5.refs_10_) | copy-start | bytes 884740
  57.9 22.0 %collective-permute-start.7 = (bf16[6,9,32,128]{3,2,1,0:T(8,128)(2,1)S(1)}, bf16[6,9,32,128]{3,2,1,0:T(8,128)(2,1)S(1)}, u32[]{:S(2)}, u32[]{:S(2)}) collective-permute-start(bf16[6,9,32,128]{3,2,1,0:T(8,128)(2,1)S(1)} %pad_maximum_fusion.2), channel_id=1, source_target_pairs={{1,0},{2,1},{3,2},{4,3},{5,4},{6,5},{7,6},{9,8},{10,9},{11,10},{12... | collective-permute-start | bytes 1327112 | tf_op jit(solution)/shard_map/ppermute | solution.py:23
  60.3 19.7 %collective-permute-start.6 = (bf16[6,9,32,128]{3,2,1,0:T(8,128)(2,1)S(1)}, bf16[6,9,32,128]{3,2,1,0:T(8,128)(2,1)S(1)}, u32[]{:S(2)}, u32[]{:S(2)}) collective-permute-start(bf16[6,9,32,128]{3,2,1,0:T(8,128)(2,1)S(1)} %pad_maximum_fusion.1), channel_id=1, source_target_pairs={{0,1},{1,2},{2,3},{3,4},{4,5},{5,6},{6,7},{8,9},{9,10},{10,11},{11... | collective-permute-start | bytes 1327112 | tf_op jit(solution)/shard_map/ppermute | solution.py:23
  80.0 0.8 copy-start.2
  80.0 0.9 copy-start.3

commit v14 on v13

--- a/solution.py
+++ b/solution.py
@@ -82,7 +82,7 @@
 
         return carry
 
-    lax.fori_loop(0, tiles, one_tile, 0)
+    lax.fori_loop(0, tiles, one_tile, 0, unroll=2)
 
 
 def add_terms(where_ref, target_ref, ap_ref, pt_ref, acc_ref):
@@ -102,7 +102,7 @@
 
         return carry
 
-    lax.fori_loop(0, ap_ref.shape[0], one_tile, 0)
+    lax.fori_loop(0, ap_ref.shape[0], one_tile, 0, unroll=2)
 
 
 def own_kernel(where_ref, target_ref, ap_ref, pt_ref, acc_ref):

time: 102 us -> 103 us (level)
  transfers between devices with their start and end apart: 8 -> 8, of which waited for: 4 -> 4; matrix products, arithmetic and copies ran while one was open for 11% -> 10% of each run, Pallas kernels for 13% -> 13%
where the time goes in v14:
time: 103 us; the launch traced here: 102 us
  Pallas kernels  49 us (48%)
  starting transfers between devices  22.9 us (22%)
  local copies, waits for them, and re-layouts  11.9 us (12%)
  waiting for transfers between devices  10.7 us (10%)
  other arithmetic  6.86 us (7%)
    pallas_call x1, Pallas kernels, body(): pl.pallas_call(coarse_kernel, out_shape=jax.ShapeDtypeStruct((o_r * o_c,...  20.1 us
    pallas_call x1, Pallas kernels, body(): pl.pallas_call(functools.partial(ap_kernel, n_r=n_r, n_c=n_c), out_shape=...  16.1 us
    pallas_call x1, Pallas kernels, body(): pl.pallas_call(own_kernel, out_shape=jax.ShapeDtypeStruct(acc_shape, jnp....  12.8 us
    ppermute x4, starting transfers between devices, shifted(): return lax.ppermute(piece, 'col', pairs)  11.6 us
    ppermute x4, starting transfers between devices, shifted(): return lax.ppermute(piece, 'row', pairs)  11.3 us
    ppermute x4, waiting for transfers between devices, shifted(): return lax.ppermute(piece, 'row', pairs)  5.87 us
    ppermute x4, waiting for transfers between devices, shifted(): return lax.ppermute(piece, 'col', pairs)  4.85 us
    reduce_sum x1, other arithmetic, body(): jnp.sum(jnp.where(match[..., None, None], p_blocks[:, :, None], jnp.zeros...  2.77 us
  transfers between devices with their start and end apart: 8, of which 4 were waited for; matrix products, arithmetic and copies ran while one was open for 10% of the time, Pallas kernels for 13%

profile of v14, /device:TPU:9, one launch (start us, length us, event | category | flops | bytes accessed | tf_op | source)
XLA Modules:
  0.0 102.1 jit_solution(9898905838157603045)
XLA Ops:
  0.3 0.8 broadcast_compare_fusion
  1.1 2.8 %select_reduce_fusion = bf16[4,4,4,64,64]{4,3,2,1,0:T(8,128)(2,1)S(1)} fusion(pred[4,4,4,4]{3,2,1,0:T(4,128)(4,1)S(1)} %broadcast_compare_fusion, bf16[4,4,4,64,64]{4,3,2,1,0:T(8,128)(2,1)} %param.7), kind=kLoop, calls=%fused_computation | loop fusion | flops 1835008 | bytes 1048832 | tf_op jit(solution)/shard_map/reduce_sum | solution.py:152
  4.1 3.7 %collective-permute-start = (bf16[4,4,32,128]{3,2,1,0:T(8,128)(2,1)S(1)}, bf16[4,4,32,128]{3,2,1,0:T(8,128)(2,1)S(1)}, u32[]{:S(2)}, u32[]{:S(2)}) collective-permute-start(bf16[4,4,32,128]{3,2,1,0:T(8,128)(2,1)S(1)} %reshape_squeeze.22), channel_id=1, source_target_pairs={{0,8},{8,16},{16,24},{1,9},{9,17},{17,25},{2,10},{10,18},{18,26},{... | collective-permute-start | bytes 393224 | tf_op jit(solution)/shard_map/ppermute | solution.py:20
  7.9 1.9 %collective-permute-start.1 = (bf16[4,4,32,128]{3,2,1,0:T(8,128)(2,1)S(1)}, bf16[4,4,32,128]{3,2,1,0:T(8,128)(2,1)S(1)}, u32[]{:S(2)}, u32[]{:S(2)}) collective-permute-start(bf16[4,4,32,128]{3,2,1,0:T(8,128)(2,1)S(1)} %reshape_squeeze.23), channel_id=1, source_target_pairs={{8,0},{16,8},{24,16},{9,1},{17,9},{25,17},{10,2},{18,10},{26,18},{... | collective-permute-start | bytes 393224 | tf_op jit(solution)/shard_map/ppermute | solution.py:20
  10.7 0.6 and_select_fusion.slot_ref
  12.6 0.6 reshape.677.near_ref
  13.3 0.9 collective-permute-done.1
  14.2 3.1 %collective-permute-start.2 = (bf16[6,4,32,128]{3,2,1,0:T(8,128)(2,1)S(1)}, bf16[6,4,32,128]{3,2,1,0:T(8,128)(2,1)S(1)}, u32[]{:S(2)}, u32[]{:S(2)}) collective-permute-start(bf16[6,4,32,128]{3,2,1,0:T(8,128)(2,1)S(1)} %pad_maximum_fusion.3), channel_id=1, source_target_pairs={{0,1},{1,2},{2,3},{3,4},{4,5},{5,6},{6,7},{8,9},{9,10},{10,11},{11... | collective-permute-start | bytes 589832 | tf_op jit(solution)/shard_map/ppermute | solution.py:23
  17.4 3.0 %collective-permute-start.3 = (bf16[6,4,32,128]{3,2,1,0:T(8,128)(2,1)S(1)}, bf16[6,4,32,128]{3,2,1,0:T(8,128)(2,1)S(1)}, u32[]{:S(2)}, u32[]{:S(2)}) collective-permute-start(bf16[6,4,32,128]{3,2,1,0:T(8,128)(2,1)S(1)} %pad_maximum_fusion.4), channel_id=1, source_target_pairs={{1,0},{2,1},{3,2},{4,3},{5,4},{6,5},{7,6},{9,8},{10,9},{11,10},{12... | collective-permute-start | bytes 589832 | tf_op jit(solution)/shard_map/ppermute | solution.py:23
  20.8 0.8 collective-permute-done.2
  21.8 4.0 %collective-permute-done.3 = bf16[6,4,32,128]{3,2,1,0:T(8,128)(2,1)S(1)} collective-permute-done((bf16[6,4,32,128]{3,2,1,0:T(8,128)(2,1)S(1)}, bf16[6,4,32,128]{3,2,1,0:T(8,128)(2,1)S(1)}, u32[]{:S(2)}, u32[]{:S(2)}) %collective-permute-start.3) | collective-permute-done | bytes 196640 | tf_op jit(solution)/shard_map/ppermute | solution.py:23
  26.0 1.8 %pad_maximum_fusion = bf16[6,6,4,64,64]{4,3,2,1,0:T(8,128)(2,1)} fusion(bf16[6,1,4,64,64]{4,3,2,1,0:T(8,128)(2,1)S(1)} %broadcast_in_dim_reshape.16, bf16[1,4,4,64,64]{4,3,2,1,0:T(8,128)(2,1)S(1)} %broadcast_in_dim_reshape.15, bf16[4,4,4,64,64]{4,3,2,1,0:T(8,128)(2,1)S(1)} %select_reduce_fusion, bf16[1,4,4,64,64]{4,3,2,1,0:T(8,128)(2,1)S(1)} %broadcast_in_dim_reshape.14, ...), kind=kLoop, calls=%fused_computation.1 | loop fusion | flops 2359296 | bytes 2359296 | tf_op jit(solution)/shard_map/concatenate | solution.py:51
  27.9 16.1 %shard_map.55 = (bf16[16,9,64,64]{3,2,1,0:T(8,128)(2,1)}, bf16[16,9,32,128]{3,2,1,0:T(8,128)(2,1)}) custom-call(s32[144]{0:T(256)} %reshape.677.near_ref, s32[576]{0:T(1024)} %and_select_fusion.slot_ref, bf16[16,9,64,64]{3,2,1,0:T(8,128)(2,1)} %bitcast.50, bf16[36,4,64,64]{3,2,1,0:T(8,128)(2,1)} %bitcast.47), custom_call_target="tpu_custom_call" | custom-call | tf_op jit(solution)/shard_map/pallas_call | solution.py:170
  43.9 1.1 %fusion.15 = (bf16[4,9,32,128]{3,2,1,0:T(8,128)(2,1)S(1)}, bf16[4,9,32,128]{3,2,1,0:T(8,128)(2,1)S(1)}) fusion(bf16[16,9,32,128]{3,2,1,0:T(8,128)(2,1)} %get-tuple-element.7), kind=kLoop, calls=%fused_computation.117 | loop fusion | bytes 1179648 | tf_op jit(solution)/shard_map/slice | solution.py:42
  45.0 3.8 %collective-permute-start.4 = (bf16[4,9,32,128]{3,2,1,0:T(8,128)(2,1)S(1)}, bf16[4,9,32,128]{3,2,1,0:T(8,128)(2,1)S(1)}, u32[]{:S(2)}, u32[]{:S(2)}) collective-permute-start(bf16[4,9,32,128]{3,2,1,0:T(8,128)(2,1)S(1)} %get-tuple-element.16), channel_id=1, source_target_pairs={{0,8},{8,16},{16,24},{1,9},{9,17},{17,25},{2,10},{10,18},{18,26},{... | collective-permute-start | bytes 884744 | tf_op jit(solution)/shard_map/ppermute | solution.py:20
  48.9 0.7 reshape.683.target_ref
  49.6 0.6 reshape.682.where_ref
  50.2 0.6 reshape.676.refs_8_
  50.8 1.9 %collective-permute-start.5 = (bf16[4,9,32,128]{3,2,1,0:T(8,128)(2,1)S(1)}, bf16[4,9,32,128]{3,2,1,0:T(8,128)(2,1)S(1)}, u32[]{:S(2)}, u32[]{:S(2)}) collective-permute-start(bf16[4,9,32,128]{3,2,1,0:T(8,128)(2,1)S(1)} %get-tuple-element.15), channel_id=1, source_target_pairs={{8,0},{16,8},{24,16},{9,1},{17,9},{25,17},{10,2},{18,10},{26,18},{... | collective-permute-start | bytes 884744 | tf_op jit(solution)/shard_map/ppermute | solution.py:20
  52.7 1.1 %slice_bitcast_fusion = (bf16[4,9,32,128]{3,2,1,0:T(8,128)(2,1)S(1)}, bf16[4,9,32,128]{3,2,1,0:T(8,128)(2,1)S(1)}) fusion(bf16[4,4,9,32,128]{4,3,2,1,0:T(8,128)(2,1)} %bitcast.51), kind=kLoop, calls=%fused_computation.8 | loop fusion | bytes 1179648 | tf_op jit(solution)/shard_map/squeeze | solution.py:44
  53.8 5.0 %collective-permute-done.5.refs_10_ = bf16[4,9,32,128]{3,2,1,0:T(8,128)(2,1)S(1)} collective-permute-done((bf16[4,9,32,128]{3,2,1,0:T(8,128)(2,1)S(1)}, bf16[4,9,32,128]{3,2,1,0:T(8,128)(2,1)S(1)}, u32[]{:S(2)}, u32[]{:S(2)}) %collective-permute-start.5) | collective-permute-done | bytes 294944 | tf_op jit(solution)/shard_map/ppermute | solution.py:20
  58.9 2.3 %collective-permute-start.7 = (bf16[6,9,32,128]{3,2,1,0:T(8,128)(2,1)S(1)}, bf16[6,9,32,128]{3,2,1,0:T(8,128)(2,1)S(1)}, u32[]{:S(2)}, u32[]{:S(2)}) collective-permute-start(bf16[6,9,32,128]{3,2,1,0:T(8,128)(2,1)S(1)} %pad_maximum_fusion.2), channel_id=1, source_target_pairs={{1,0},{2,1},{3,2},{4,3},{5,4},{6,5},{7,6},{9,8},{10,9},{11,10},{12... | collective-permute-start | bytes 1327112 | tf_op jit(solution)/shard_map/ppermute | solution.py:23
  61.2 3.2 %collective-permute-start.6 = (bf16[6,9,32,128]{3,2,1,0:T(8,128)(2,1)S(1)}, bf16[6,9,32,128]{3,2,1,0:T(8,128)(2,1)S(1)}, u32[]{:S(2)}, u32[]{:S(2)}) collective-permute-start(bf16[6,9,32,128]{3,2,1,0:T(8,128)(2,1)S(1)} %pad_maximum_fusion.1), channel_id=1, source_target_pairs={{0,1},{1,2},{2,3},{3,4},{4,5},{5,6},{6,7},{8,9},{9,10},{10,11},{11... | collective-permute-start | bytes 1327112 | tf_op jit(solution)/shard_map/ppermute | solution.py:23
  64.4 0.6 reshape_squeeze.20.refs_5_
  65.0 0.7 reshape_squeeze.21.refs_7_
  65.7 0.6 reshape_squeeze.18.refs_1_
  66.3 0.6 reshape_squeeze.19.refs_3_
  66.9 0.7 slice_reduce_fusion
  67.6 0.6 slice_bitcast_fusion.2
  68.3 12.8 %shard_map.56.refs_14_ = f32[100,64,64]{2,1,0:T(8,128)} custom-call(s32[16]{0:T(128)} %reshape.682.where_ref, s32[64]{0:T(128)} %reshape.683.target_ref, bf16[16,9,64,64]{3,2,1,0:T(8,128)(2,1)} %get-tuple-element.8.ap_ref, bf16[144,64,64]{2,1,0:T(8,128)(2,1)} %bitcast.48), custom_call_target="tpu_custom_call" | custom-call | flops 301989888 | bytes 6291456 | tf_op jit(solution)/shard_map/pallas_call | solution.py:220
  81.1 0.7 copy-done.2
  82.0 20.1 %shard_map.57 = bf16[4,25,64,64]{3,2,1,0:T(8,128)(2,1)} custom-call(s32[4]{0:T(128)} %get-tuple-element.35.refs_0_, s32[16]{0:T(128)} %reshape_squeeze.18.refs_1_, s32[4]{0:T(128)} %get-tuple-element.34.refs_2_, s32[16]{0:T(128)} %reshape_squeeze.19.refs_3_, s32[6]{0:T(128)} %get-tuple-element.12.refs_4_, s32[24]{0:T(128)} %reshape_squeeze.20.refs_5_, ...), custom_call_target="tpu_custom_call" | custom-call | tf_op jit(solution)/shard_map/pallas_call | solution.py:236
  (79 shorter events, 3.5 us)
Async XLA Ops:
  1.1 8.9 %copy-start.4 = (s32[4,4,9]{2,1,0:T(4,128)S(1)}, s32[4,4,9]{2,1,0:T(4,128)}, u32[]{:S(2)}) copy-start(s32[4,4,9]{2,1,0:T(4,128)} %param.6) | copy-start | bytes 1732
  3.9 16.6 %copy-start.5 = (s32[2,2,25]{2,1,0:T(2,128)S(1)}, s32[2,2,25]{2,1,0:T(2,128)}, u32[]{:S(2)}) copy-start(s32[2,2,25]{2,1,0:T(2,128)} %param.9) | copy-start | bytes 1204
  4.1 9.2 %collective-permute-start = (bf16[4,4,32,128]{3,2,1,0:T(8,128)(2,1)S(1)}, bf16[4,4,32,128]{3,2,1,0:T(8,128)(2,1)S(1)}, u32[]{:S(2)}, u32[]{:S(2)}) collective-permute-start(bf16[4,4,32,128]{3,2,1,0:T(8,128)(2,1)S(1)} %reshape_squeeze.22), channel_id=1, source_target_pairs={{0,8},{8,16},{16,24},{1,9},{9,17},{17,25},{2,10},{10,18},{18,26},{... | collective-permute-start | bytes 393224 | tf_op jit(solution)/shard_map/ppermute | solution.py:20
  7.9 6.3 %collective-permute-start.1 = (bf16[4,4,32,128]{3,2,1,0:T(8,128)(2,1)S(1)}, bf16[4,4,32,128]{3,2,1,0:T(8,128)(2,1)S(1)}, u32[]{:S(2)}, u32[]{:S(2)}) collective-permute-start(bf16[4,4,32,128]{3,2,1,0:T(8,128)(2,1)S(1)} %reshape_squeeze.23), channel_id=1, source_target_pairs={{8,0},{16,8},{24,16},{9,1},{17,9},{25,17},{10,2},{18,10},{26,18},{... | collective-permute-start | bytes 393224 | tf_op jit(solution)/shard_map/ppermute | solution.py:20
  14.2 7.4 %collective-permute-start.2 = (bf16[6,4,32,128]{3,2,1,0:T(8,128)(2,1)S(1)}, bf16[6,4,32,128]{3,2,1,0:T(8,128)(2,1)S(1)}, u32[]{:S(2)}, u32[]{:S(2)}) collective-permute-start(bf16[6,4,32,128]{3,2,1,0:T(8,128)(2,1)S(1)} %pad_maximum_fusion.3), channel_id=1, source_target_pairs={{0,1},{1,2},{2,3},{3,4},{4,5},{5,6},{6,7},{8,9},{9,10},{10,11},{11... | collective-permute-start | bytes 589832 | tf_op jit(solution)/shard_map/ppermute | solution.py:23
  17.4 8.4 %collective-permute-start.3 = (bf16[6,4,32,128]{3,2,1,0:T(8,128)(2,1)S(1)}, bf16[6,4,32,128]{3,2,1,0:T(8,128)(2,1)S(1)}, u32[]{:S(2)}, u32[]{:S(2)}) collective-permute-start(bf16[6,4,32,128]{3,2,1,0:T(8,128)(2,1)S(1)} %pad_maximum_fusion.4), channel_id=1, source_target_pairs={{1,0},{2,1},{3,2},{4,3},{5,4},{6,5},{7,6},{9,8},{10,9},{11,10},{12... | collective-permute-start | bytes 589832 | tf_op jit(solution)/shard_map/ppermute | solution.py:23
  45.0 8.7 %collective-permute-start.4 = (bf16[4,9,32,128]{3,2,1,0:T(8,128)(2,1)S(1)}, bf16[4,9,32,128]{3,2,1,0:T(8,128)(2,1)S(1)}, u32[]{:S(2)}, u32[]{:S(2)}) collective-permute-start(bf16[4,9,32,128]{3,2,1,0:T(8,128)(2,1)S(1)} %get-tuple-element.16), channel_id=1, source_target_pairs={{0,8},{8,16},{16,24},{1,9},{9,17},{17,25},{2,10},{10,18},{18,26},{... | collective-permute-start | bytes 884744 | tf_op jit(solution)/shard_map/ppermute | solution.py:20
  50.8 8.0 %collective-permute-start.5 = (bf16[4,9,32,128]{3,2,1,0:T(8,128)(2,1)S(1)}, bf16[4,9,32,128]{3,2,1,0:T(8,128)(2,1)S(1)}, u32[]{:S(2)}, u32[]{:S(2)}) collective-permute-start(bf16[4,9,32,128]{3,2,1,0:T(8,128)(2,1)S(1)} %get-tuple-element.15), channel_id=1, source_target_pairs={{8,0},{16,8},{24,16},{9,1},{17,9},{25,17},{10,2},{18,10},{26,18},{... | collective-permute-start | bytes 884744 | tf_op jit(solution)/shard_map/ppermute | solution.py:20
  53.8 27.3 %copy-start = (bf16[4,9,32,128]{3,2,1,0:T(8,128)(2,1)}, bf16[4,9,32,128]{3,2,1,0:T(8,128)(2,1)S(1)}, u32[]{:S(2)}) copy-start(bf16[4,9,32,128]{3,2,1,0:T(8,128)(2,1)S(1)} %collective-permute-done.4.refs_9_) | copy-start | bytes 884740
  58.8 22.3 %copy-start.1 = (bf16[4,9,32,128]{3,2,1,0:T(8,128)(2,1)}, bf16[4,9,32,128]{3,2,1,0:T(8,128)(2,1)S(1)}, u32[]{:S(2)}) copy-start(bf16[4,9,32,128]{3,2,1,0:T(8,128)(2,1)S(1)} %collective-permute-done.5.refs_10_) | copy-start | bytes 884740
  58.9 22.2 %collective-permute-start.7 = (bf16[6,9,32,128]{3,2,1,0:T(8,128)(2,1)S(1)}, bf16[6,9,32,128]{3,2,1,0:T(8,128)(2,1)S(1)}, u32[]{:S(2)}, u32[]{:S(2)}) collective-permute-start(bf16[6,9,32,128]{3,2,1,0:T(8,128)(2,1)S(1)} %pad_maximum_fusion.2), channel_id=1, source_target_pairs={{1,0},{2,1},{3,2},{4,3},{5,4},{6,5},{7,6},{9,8},{10,9},{11,10},{12... | collective-permute-start | bytes 1327112 | tf_op jit(solution)/shard_map/ppermute | solution.py:23
  61.2 19.9 %collective-permute-start.6 = (bf16[6,9,32,128]{3,2,1,0:T(8,128)(2,1)S(1)}, bf16[6,9,32,128]{3,2,1,0:T(8,128)(2,1)S(1)}, u32[]{:S(2)}, u32[]{:S(2)}) collective-permute-start(bf16[6,9,32,128]{3,2,1,0:T(8,128)(2,1)S(1)} %pad_maximum_fusion.1), channel_id=1, source_target_pairs={{0,1},{1,2},{2,3},{3,4},{4,5},{5,6},{6,7},{8,9},{9,10},{10,11},{11... | collective-permute-start | bytes 1327112 | tf_op jit(solution)/shard_map/ppermute | solution.py:23
  81.1 0.8 copy-start.2
  81.1 0.9 copy-start.3

commit v15 on v13

--- a/solution.py
+++ b/solution.py
@@ -85,7 +85,7 @@
     lax.fori_loop(0, tiles, one_tile, 0)
 
 
-def add_terms(where_ref, target_ref, ap_ref, pt_ref, acc_ref):
+def add_terms(where_ref, target_ref, ap_ref, pt_ref, acc_ref, transposed=True):
     def one_tile(t, carry):
         w = where_ref[t]
         blocks = [ap_ref[t, e].reshape(pt_ref.shape[1:]) for e in range(9)]
@@ -95,9 +95,10 @@
             @pl.when(g >= 0)
             def _():
                 p = pt_ref[w * 4 + q]
+                pair = (((0 if transposed else 1,), (0,)), ((), ()))
                 for e in range(9):
                     acc_ref[g + (e // 3) * 5 + e % 3] += lax.dot_general(
-                        p, blocks[e], (((0,), (0,)), ((), ())), preferred_element_type=jnp.float32
+                        p, blocks[e], pair, preferred_element_type=jnp.float32
                     )
 
         return carry
@@ -107,7 +108,7 @@
 
 def own_kernel(where_ref, target_ref, ap_ref, pt_ref, acc_ref):
     acc_ref[...] = jnp.zeros(acc_ref.shape, jnp.float32)
-    add_terms(where_ref, target_ref, ap_ref, pt_ref, acc_ref)
+    add_terms(where_ref, target_ref, ap_ref, pt_ref, acc_ref, transposed=False)
 
 
 def coarse_kernel(*refs):
@@ -225,7 +226,12 @@
         cost_estimate=pl.CostEstimate(
             flops=2 * bs * bs * bs * 9 * n_r * n_c * 4, bytes_accessed=6 * 1024 * 1024, transcendentals=0
         ),
-    )(place[1:-1, 1:-1].reshape(-1), target[1:-1, 1:-1].reshape(-1), ap.reshape(n_r * n_c, 9, bs, bs), p_t)
+    )(
+        jnp.arange(n_r * n_c, dtype=jnp.int32),
+        target[1:-1, 1:-1].reshape(-1),
+        ap.reshape(n_r * n_c, 9, bs, bs),
+        jnp.swapaxes(canon, -1, -2).reshape(n_r * n_c * 4, bs, bs),
+    )
     top, bottom, left, right = halo_sides(ap_dense)
     parts = [
         (place[0, 1:-1], target[0, 1:-1], top),

time: 102 us -> 102 us (level)
  waiting for transfers between devices: 10.7 us -> 13.3 us
  Pallas kernels: 48 us -> 45.9 us
    ppermute x4, waiting for transfers between devices: 4.85 us -> 9.77 us  [shifted(): return lax.ppermute(piece, 'col', pairs)]
    ppermute x4, waiting for transfers between devices: 5.87 us -> 3.55 us  [shifted(): return lax.ppermute(piece, 'row', pairs)]
    pallas_call x1, Pallas kernels: 12.8 us -> 10.7 us  [body(): pl.pallas_call(own_kernel, out_shape=jax.ShapeDtypeStruct(acc_shape, jnp....]
    transpose x0 -> x1, local copies, waits for them, and re-layouts: none -> 1.38 us  [body(): jnp.swapaxes(canon, -1, -2).reshape(n_r * n_c * 4, bs, bs)]
    squeeze x1, local copies, waits for them, and re-layouts: 1.1 us -> 0.04 us  [halo_sides(): x[:, 0]]
  transfers between devices with their start and end apart: 8 -> 8, of which waited for: 4 -> 5; matrix products, arithmetic and copies ran while one was open for 11% -> 11% of each run, Pallas kernels for 13% -> 11%
where the time goes in v15:
time: 102 us
  Pallas kernels  45.9 us (45%)
  starting transfers between devices  22.6 us (22%)
  waiting for transfers between devices  13.3 us (13%)
  local copies, waits for them, and re-layouts  12 us (12%)
  other arithmetic  6.81 us (7%)
    pallas_call x1, Pallas kernels, body(): pl.pallas_call(coarse_kernel, out_shape=jax.ShapeDtypeStruct((o_r * o_c,...  20.1 us
    pallas_call x1, Pallas kernels, body(): pl.pallas_call(functools.partial(ap_kernel, n_r=n_r, n_c=n_c), out_shape=...  15.1 us
    ppermute x4, starting transfers between devices, shifted(): return lax.ppermute(piece, 'col', pairs)  11.5 us
    ppermute x4, starting transfers between devices, shifted(): return lax.ppermute(piece, 'row', pairs)  11.2 us
    pallas_call x1, Pallas kernels, body(): pl.pallas_call(own_kernel, out_shape=jax.ShapeDtypeStruct(acc_shape, jnp....  10.7 us
    ppermute x4, waiting for transfers between devices, shifted(): return lax.ppermute(piece, 'col', pairs)  9.77 us
    ppermute x4, waiting for transfers between devices, shifted(): return lax.ppermute(piece, 'row', pairs)  3.55 us
    reduce_sum x1, other arithmetic, body(): jnp.sum(jnp.where(match[..., None, None], p_blocks[:, :, None], jnp.zeros...  2.77 us
  transfers between devices with their start and end apart: 8, of which 5 were waited for; matrix products, arithmetic and copies ran while one was open for 11% of the time, Pallas kernels for 11%

profile of v15, /device:TPU:9, one launch (start us, length us, event | category | flops | bytes accessed | tf_op | source)
XLA Modules:
  0.0 101.5 jit_solution(13986696105366283632)
XLA Ops:
  0.3 0.8 broadcast_compare_fusion
  1.1 2.8 %select_reduce_fusion = bf16[4,4,4,64,64]{4,3,2,1,0:T(8,128)(2,1)S(1)} fusion(pred[4,4,4,4]{3,2,1,0:T(4,128)(4,1)S(1)} %broadcast_compare_fusion, bf16[4,4,4,64,64]{4,3,2,1,0:T(8,128)(2,1)} %param.7), kind=kLoop, calls=%fused_computation | loop fusion | flops 1835008 | bytes 1048832 | tf_op jit(solution)/shard_map/reduce_sum | solution.py:153
  4.1 2.6 %collective-permute-start.1 = (bf16[4,4,32,128]{3,2,1,0:T(8,128)(2,1)S(1)}, bf16[4,4,32,128]{3,2,1,0:T(8,128)(2,1)S(1)}, u32[]{:S(2)}, u32[]{:S(2)}) collective-permute-start(bf16[4,4,32,128]{3,2,1,0:T(8,128)(2,1)S(1)} %reshape_squeeze.23), channel_id=1, source_target_pairs={{8,0},{16,8},{24,16},{9,1},{17,9},{25,17},{10,2},{18,10},{26,18},{... | collective-permute-start | bytes 393224 | tf_op jit(solution)/shard_map/ppermute | solution.py:20
  6.8 3.0 %collective-permute-start = (bf16[4,4,32,128]{3,2,1,0:T(8,128)(2,1)S(1)}, bf16[4,4,32,128]{3,2,1,0:T(8,128)(2,1)S(1)}, u32[]{:S(2)}, u32[]{:S(2)}) collective-permute-start(bf16[4,4,32,128]{3,2,1,0:T(8,128)(2,1)S(1)} %reshape_squeeze.22), channel_id=1, source_target_pairs={{0,8},{8,16},{16,24},{1,9},{9,17},{17,25},{2,10},{10,18},{18,26},{... | collective-permute-start | bytes 393224 | tf_op jit(solution)/shard_map/ppermute | solution.py:20
  11.5 0.6 and_select_fusion.slot_ref
  12.4 0.6 reshape.673.near_ref
  13.4 3.0 %collective-permute-start.3 = (bf16[6,4,32,128]{3,2,1,0:T(8,128)(2,1)S(1)}, bf16[6,4,32,128]{3,2,1,0:T(8,128)(2,1)S(1)}, u32[]{:S(2)}, u32[]{:S(2)}) collective-permute-start(bf16[6,4,32,128]{3,2,1,0:T(8,128)(2,1)S(1)} %pad_maximum_fusion.4), channel_id=1, source_target_pairs={{1,0},{2,1},{3,2},{4,3},{5,4},{6,5},{7,6},{9,8},{10,9},{11,10},{12... | collective-permute-start | bytes 589832 | tf_op jit(solution)/shard_map/ppermute | solution.py:23
  16.5 2.2 %collective-permute-start.2 = (bf16[6,4,32,128]{3,2,1,0:T(8,128)(2,1)S(1)}, bf16[6,4,32,128]{3,2,1,0:T(8,128)(2,1)S(1)}, u32[]{:S(2)}, u32[]{:S(2)}) collective-permute-start(bf16[6,4,32,128]{3,2,1,0:T(8,128)(2,1)S(1)} %pad_maximum_fusion.3), channel_id=1, source_target_pairs={{0,1},{1,2},{2,3},{3,4},{4,5},{5,6},{6,7},{8,9},{9,10},{10,11},{11... | collective-permute-start | bytes 589832 | tf_op jit(solution)/shard_map/ppermute | solution.py:23
  19.1 2.8 %collective-permute-done.3 = bf16[6,4,32,128]{3,2,1,0:T(8,128)(2,1)S(1)} collective-permute-done((bf16[6,4,32,128]{3,2,1,0:T(8,128)(2,1)S(1)}, bf16[6,4,32,128]{3,2,1,0:T(8,128)(2,1)S(1)}, u32[]{:S(2)}, u32[]{:S(2)}) %collective-permute-start.3) | collective-permute-done | bytes 196640 | tf_op jit(solution)/shard_map/ppermute | solution.py:23
  22.2 4.1 %collective-permute-done.2 = bf16[6,4,32,128]{3,2,1,0:T(8,128)(2,1)S(1)} collective-permute-done((bf16[6,4,32,128]{3,2,1,0:T(8,128)(2,1)S(1)}, bf16[6,4,32,128]{3,2,1,0:T(8,128)(2,1)S(1)}, u32[]{:S(2)}, u32[]{:S(2)}) %collective-permute-start.2) | collective-permute-done | bytes 196640 | tf_op jit(solution)/shard_map/ppermute | solution.py:23
  26.4 1.8 %pad_maximum_fusion = bf16[6,6,4,64,64]{4,3,2,1,0:T(8,128)(2,1)} fusion(bf16[6,1,4,64,64]{4,3,2,1,0:T(8,128)(2,1)S(1)} %broadcast_in_dim_reshape.16, bf16[1,4,4,64,64]{4,3,2,1,0:T(8,128)(2,1)S(1)} %broadcast_in_dim_reshape.15, bf16[4,4,4,64,64]{4,3,2,1,0:T(8,128)(2,1)S(1)} %select_reduce_fusion, bf16[1,4,4,64,64]{4,3,2,1,0:T(8,128)(2,1)S(1)} %broadcast_in_dim_reshape.14, ...), kind=kLoop, calls=%fused_computation.1 | loop fusion | flops 2359296 | bytes 2359296 | tf_op jit(solution)/shard_map/concatenate | solution.py:51
  28.2 15.1 %shard_map.55 = (bf16[16,9,64,64]{3,2,1,0:T(8,128)(2,1)}, bf16[16,9,32,128]{3,2,1,0:T(8,128)(2,1)}) custom-call(s32[144]{0:T(256)} %reshape.673.near_ref, s32[576]{0:T(1024)} %and_select_fusion.slot_ref, bf16[16,9,64,64]{3,2,1,0:T(8,128)(2,1)} %bitcast.53, bf16[36,4,64,64]{3,2,1,0:T(8,128)(2,1)} %bitcast.49), custom_call_target="tpu_custom_call" | custom-call | tf_op jit(solution)/shard_map/pallas_call | solution.py:171
  43.3 1.2 %fusion.15 = (bf16[4,9,32,128]{3,2,1,0:T(8,128)(2,1)S(1)}, bf16[4,9,32,128]{3,2,1,0:T(8,128)(2,1)S(1)}) fusion(bf16[16,9,32,128]{3,2,1,0:T(8,128)(2,1)} %get-tuple-element.7), kind=kLoop, calls=%fused_computation.117 | loop fusion | bytes 1179648 | tf_op jit(solution)/shard_map/slice | solution.py:42
  44.5 2.4 %collective-permute-start.5 = (bf16[4,9,32,128]{3,2,1,0:T(8,128)(2,1)S(1)}, bf16[4,9,32,128]{3,2,1,0:T(8,128)(2,1)S(1)}, u32[]{:S(2)}, u32[]{:S(2)}) collective-permute-start(bf16[4,9,32,128]{3,2,1,0:T(8,128)(2,1)S(1)} %get-tuple-element.15), channel_id=1, source_target_pairs={{8,0},{16,8},{24,16},{9,1},{17,9},{25,17},{10,2},{18,10},{26,18},{... | collective-permute-start | bytes 884744 | tf_op jit(solution)/shard_map/ppermute | solution.py:20
  46.9 0.7 reshape.672.refs_8_
  47.6 0.6 reshape_squeeze.19.refs_3_
  48.2 0.7 reshape_squeeze.18.refs_1_
  48.9 0.6 reshape.678.target_ref
  49.5 0.6 reshape_squeeze.21.refs_7_
  50.1 0.7 reshape_squeeze.20.refs_5_
  50.7 1.4 %copy.36 = bf16[4,4,4,64,64]{4,3,2,1,0:T(8,128)(2,1)} copy(bf16[4,4,4,64,64]{3,4,2,1,0:T(8,128)(2,1)S(1)} %bitcast.51) | data formatting | bytes 1048576 | tf_op jit(solution)/shard_map/transpose | solution.py:233
  52.1 3.2 %collective-permute-start.4 = (bf16[4,9,32,128]{3,2,1,0:T(8,128)(2,1)S(1)}, bf16[4,9,32,128]{3,2,1,0:T(8,128)(2,1)S(1)}, u32[]{:S(2)}, u32[]{:S(2)}) collective-permute-start(bf16[4,9,32,128]{3,2,1,0:T(8,128)(2,1)S(1)} %get-tuple-element.16), channel_id=1, source_target_pairs={{0,8},{8,16},{16,24},{1,9},{9,17},{17,25},{2,10},{10,18},{18,26},{... | collective-permute-start | bytes 884744 | tf_op jit(solution)/shard_map/ppermute | solution.py:20
  55.4 3.5 %collective-permute-done.4.refs_9_ = bf16[4,9,32,128]{3,2,1,0:T(8,128)(2,1)S(1)} collective-permute-done((bf16[4,9,32,128]{3,2,1,0:T(8,128)(2,1)S(1)}, bf16[4,9,32,128]{3,2,1,0:T(8,128)(2,1)S(1)}, u32[]{:S(2)}, u32[]{:S(2)}) %collective-permute-start.4) | collective-permute-done | bytes 294944 | tf_op jit(solution)/shard_map/ppermute | solution.py:20
  59.0 4.1 %collective-permute-start.6 = (bf16[6,9,32,128]{3,2,1,0:T(8,128)(2,1)S(1)}, bf16[6,9,32,128]{3,2,1,0:T(8,128)(2,1)S(1)}, u32[]{:S(2)}, u32[]{:S(2)}) collective-permute-start(bf16[6,9,32,128]{3,2,1,0:T(8,128)(2,1)S(1)} %pad_maximum_fusion.1), channel_id=1, source_target_pairs={{0,1},{1,2},{2,3},{3,4},{4,5},{5,6},{6,7},{8,9},{9,10},{10,11},{11... | collective-permute-start | bytes 1327112 | tf_op jit(solution)/shard_map/ppermute | solution.py:23
  63.2 2.1 %collective-permute-start.7 = (bf16[6,9,32,128]{3,2,1,0:T(8,128)(2,1)S(1)}, bf16[6,9,32,128]{3,2,1,0:T(8,128)(2,1)S(1)}, u32[]{:S(2)}, u32[]{:S(2)}) collective-permute-start(bf16[6,9,32,128]{3,2,1,0:T(8,128)(2,1)S(1)} %pad_maximum_fusion.2), channel_id=1, source_target_pairs={{1,0},{2,1},{3,2},{4,3},{5,4},{6,5},{7,6},{9,8},{10,9},{11,10},{12... | collective-permute-start | bytes 1327112 | tf_op jit(solution)/shard_map/ppermute | solution.py:23
  65.3 0.7 slice_reduce_fusion.2
  66.0 0.5 slice_bitcast_fusion.2
  67.1 10.7 %shard_map.56.refs_14_ = f32[100,64,64]{2,1,0:T(8,128)} custom-call(s32[16]{0:T(128)} %iota.117.where_ref, s32[64]{0:T(128)} %reshape.678.target_ref, bf16[16,9,64,64]{3,2,1,0:T(8,128)(2,1)} %get-tuple-element.8.ap_ref, bf16[64,64,64]{2,1,0:T(8,128)(2,1)} %bitcast.52), custom_call_target="tpu_custom_call" | custom-call | flops 301989888 | bytes 6291456 | tf_op jit(solution)/shard_map/pallas_call | solution.py:221
  77.8 2.0 %collective-permute-done.6.refs_11_ = bf16[6,9,32,128]{3,2,1,0:T(8,128)(2,1)S(1)} collective-permute-done((bf16[6,9,32,128]{3,2,1,0:T(8,128)(2,1)S(1)}, bf16[6,9,32,128]{3,2,1,0:T(8,128)(2,1)S(1)}, u32[]{:S(2)}, u32[]{:S(2)}) %collective-permute-start.6) | collective-permute-done | bytes 442400 | tf_op jit(solution)/shard_map/ppermute | solution.py:23
  79.8 0.8 collective-permute-done.7.refs_12_
  80.6 0.8 copy-done.4
  81.4 20.1 %shard_map.57 = bf16[4,25,64,64]{3,2,1,0:T(8,128)(2,1)} custom-call(s32[4]{0:T(128)} %get-tuple-element.12.refs_0_, s32[16]{0:T(128)} %reshape_squeeze.18.refs_1_, s32[4]{0:T(128)} %get-tuple-element.11.refs_2_, s32[16]{0:T(128)} %reshape_squeeze.19.refs_3_, s32[6]{0:T(128)} %get-tuple-element.35.refs_4_, s32[24]{0:T(128)} %reshape_squeeze.20.refs_5_, ...), custom_call_target="tpu_custom_call" | custom-call | tf_op jit(solution)/shard_map/pallas_call | solution.py:242
  (81 shorter events, 3.9 us)
Async XLA Ops:
  1.1 9.7 %copy-start.5 = (s32[4,4,9]{2,1,0:T(4,128)S(1)}, s32[4,4,9]{2,1,0:T(4,128)}, u32[]{:S(2)}) copy-start(s32[4,4,9]{2,1,0:T(4,128)} %param.6) | copy-start | bytes 1732
  3.9 14.9 %copy-start.6 = (s32[2,2,25]{2,1,0:T(2,128)S(1)}, s32[2,2,25]{2,1,0:T(2,128)}, u32[]{:S(2)}) copy-start(s32[2,2,25]{2,1,0:T(2,128)} %param.9) | copy-start | bytes 1204
  4.1 9.3 %collective-permute-start.1 = (bf16[4,4,32,128]{3,2,1,0:T(8,128)(2,1)S(1)}, bf16[4,4,32,128]{3,2,1,0:T(8,128)(2,1)S(1)}, u32[]{:S(2)}, u32[]{:S(2)}) collective-permute-start(bf16[4,4,32,128]{3,2,1,0:T(8,128)(2,1)S(1)} %reshape_squeeze.23), channel_id=1, source_target_pairs={{8,0},{16,8},{24,16},{9,1},{17,9},{25,17},{10,2},{18,10},{26,18},{... | collective-permute-start | bytes 393224 | tf_op jit(solution)/shard_map/ppermute | solution.py:20
  6.8 6.6 %collective-permute-start = (bf16[4,4,32,128]{3,2,1,0:T(8,128)(2,1)S(1)}, bf16[4,4,32,128]{3,2,1,0:T(8,128)(2,1)S(1)}, u32[]{:S(2)}, u32[]{:S(2)}) collective-permute-start(bf16[4,4,32,128]{3,2,1,0:T(8,128)(2,1)S(1)} %reshape_squeeze.22), channel_id=1, source_target_pairs={{0,8},{8,16},{16,24},{1,9},{9,17},{17,25},{2,10},{10,18},{18,26},{... | collective-permute-start | bytes 393224 | tf_op jit(solution)/shard_map/ppermute | solution.py:20
  13.4 8.5 %collective-permute-start.3 = (bf16[6,4,32,128]{3,2,1,0:T(8,128)(2,1)S(1)}, bf16[6,4,32,128]{3,2,1,0:T(8,128)(2,1)S(1)}, u32[]{:S(2)}, u32[]{:S(2)}) collective-permute-start(bf16[6,4,32,128]{3,2,1,0:T(8,128)(2,1)S(1)} %pad_maximum_fusion.4), channel_id=1, source_target_pairs={{1,0},{2,1},{3,2},{4,3},{5,4},{6,5},{7,6},{9,8},{10,9},{11,10},{12... | collective-permute-start | bytes 589832 | tf_op jit(solution)/shard_map/ppermute | solution.py:23
  16.5 9.7 %collective-permute-start.2 = (bf16[6,4,32,128]{3,2,1,0:T(8,128)(2,1)S(1)}, bf16[6,4,32,128]{3,2,1,0:T(8,128)(2,1)S(1)}, u32[]{:S(2)}, u32[]{:S(2)}) collective-permute-start(bf16[6,4,32,128]{3,2,1,0:T(8,128)(2,1)S(1)} %pad_maximum_fusion.3), channel_id=1, source_target_pairs={{0,1},{1,2},{2,3},{3,4},{4,5},{5,6},{6,7},{8,9},{9,10},{10,11},{11... | collective-permute-start | bytes 589832 | tf_op jit(solution)/shard_map/ppermute | solution.py:23
  43.3 12.0 %copy-start = (bf16[16,9,32,128]{3,2,1,0:T(8,128)(2,1)S(1)}, bf16[16,9,32,128]{3,2,1,0:T(8,128)(2,1)}, u32[]{:S(2)}) copy-start(bf16[16,9,32,128]{3,2,1,0:T(8,128)(2,1)} %get-tuple-element.7) | copy-start | bytes 3538948
  44.5 10.8 %collective-permute-start.5 = (bf16[4,9,32,128]{3,2,1,0:T(8,128)(2,1)S(1)}, bf16[4,9,32,128]{3,2,1,0:T(8,128)(2,1)S(1)}, u32[]{:S(2)}, u32[]{:S(2)}) collective-permute-start(bf16[4,9,32,128]{3,2,1,0:T(8,128)(2,1)S(1)} %get-tuple-element.15), channel_id=1, source_target_pairs={{8,0},{16,8},{24,16},{9,1},{17,9},{25,17},{10,2},{18,10},{26,18},{... | collective-permute-start | bytes 884744 | tf_op jit(solution)/shard_map/ppermute | solution.py:20
  52.1 6.9 %collective-permute-start.4 = (bf16[4,9,32,128]{3,2,1,0:T(8,128)(2,1)S(1)}, bf16[4,9,32,128]{3,2,1,0:T(8,128)(2,1)S(1)}, u32[]{:S(2)}, u32[]{:S(2)}) collective-permute-start(bf16[4,9,32,128]{3,2,1,0:T(8,128)(2,1)S(1)} %get-tuple-element.16), channel_id=1, source_target_pairs={{0,8},{8,16},{16,24},{1,9},{9,17},{17,25},{2,10},{10,18},{18,26},{... | collective-permute-start | bytes 884744 | tf_op jit(solution)/shard_map/ppermute | solution.py:20
  55.4 22.4 %copy-start.1 = (bf16[4,9,32,128]{3,2,1,0:T(8,128)(2,1)}, bf16[4,9,32,128]{3,2,1,0:T(8,128)(2,1)S(1)}, u32[]{:S(2)}) copy-start(bf16[4,9,32,128]{3,2,1,0:T(8,128)(2,1)S(1)} %collective-permute-done.5.refs_10_) | copy-start | bytes 884740
  59.0 18.8 %copy-start.2 = (bf16[4,9,32,128]{3,2,1,0:T(8,128)(2,1)}, bf16[4,9,32,128]{3,2,1,0:T(8,128)(2,1)S(1)}, u32[]{:S(2)}) copy-start(bf16[4,9,32,128]{3,2,1,0:T(8,128)(2,1)S(1)} %collective-permute-done.4.refs_9_) | copy-start | bytes 884740
  59.0 20.7 %collective-permute-start.6 = (bf16[6,9,32,128]{3,2,1,0:T(8,128)(2,1)S(1)}, bf16[6,9,32,128]{3,2,1,0:T(8,128)(2,1)S(1)}, u32[]{:S(2)}, u32[]{:S(2)}) collective-permute-start(bf16[6,9,32,128]{3,2,1,0:T(8,128)(2,1)S(1)} %pad_maximum_fusion.1), channel_id=1, source_target_pairs={{0,1},{1,2},{2,3},{3,4},{4,5},{5,6},{6,7},{8,9},{9,10},{10,11},{11... | collective-permute-start | bytes 1327112 | tf_op jit(solution)/shard_map/ppermute | solution.py:23
  63.2 17.4 %collective-permute-start.7 = (bf16[6,9,32,128]{3,2,1,0:T(8,128)(2,1)S(1)}, bf16[6,9,32,128]{3,2,1,0:T(8,128)(2,1)S(1)}, u32[]{:S(2)}, u32[]{:S(2)}) collective-permute-start(bf16[6,9,32,128]{3,2,1,0:T(8,128)(2,1)S(1)} %pad_maximum_fusion.2), channel_id=1, source_target_pairs={{1,0},{2,1},{3,2},{4,3},{5,4},{6,5},{7,6},{9,8},{10,9},{11,10},{12... | collective-permute-start | bytes 1327112 | tf_op jit(solution)/shard_map/ppermute | solution.py:23
  79.8 0.8 copy-start.3
  80.6 0.8 copy-start.4

commit v16 on v13

--- a/solution.py
+++ b/solution.py
@@ -88,7 +88,8 @@
 def add_terms(where_ref, target_ref, ap_ref, pt_ref, acc_ref):
     def one_tile(t, carry):
         w = where_ref[t]
-        blocks = [ap_ref[t, e].reshape(pt_ref.shape[1:]) for e in range(9)]
+        dense = ap_ref.shape[-2:] != pt_ref.shape[1:]
+        blocks = [ap_ref[t, e].reshape(pt_ref.shape[1:]) for e in range(9)] if dense else None
         for q in range(4):
             g = target_ref[t * 4 + q]
 
@@ -96,8 +97,9 @@
             def _():
                 p = pt_ref[w * 4 + q]
                 for e in range(9):
+                    block = blocks[e] if dense else ap_ref[t, e]
                     acc_ref[g + (e // 3) * 5 + e % 3] += lax.dot_general(
-                        p, blocks[e], (((0,), (0,)), ((), ())), preferred_element_type=jnp.float32
+                        p, block, (((0,), (0,)), ((), ())), preferred_element_type=jnp.float32
                     )
 
         return carry

time: 102 us -> 101 us (level)
  transfers between devices with their start and end apart: 8 -> 8, of which waited for: 4 -> 4; matrix products, arithmetic and copies ran while one was open for 11% -> 11% of each run, Pallas kernels for 13% -> 12%
where the time goes in v16:
time: 101 us
  Pallas kernels  47.8 us (47%)
  starting transfers between devices  22.8 us (23%)
  local copies, waits for them, and re-layouts  11.9 us (12%)
  waiting for transfers between devices  10.7 us (11%)
  other arithmetic  6.86 us (7%)
    pallas_call x1, Pallas kernels, body(): pl.pallas_call(coarse_kernel, out_shape=jax.ShapeDtypeStruct((o_r * o_c,...  20.1 us
    pallas_call x1, Pallas kernels, body(): pl.pallas_call(functools.partial(ap_kernel, n_r=n_r, n_c=n_c), out_shape=...  15.1 us
    pallas_call x1, Pallas kernels, body(): pl.pallas_call(own_kernel, out_shape=jax.ShapeDtypeStruct(acc_shape, jnp....  12.6 us
    ppermute x4, starting transfers between devices, shifted(): return lax.ppermute(piece, 'col', pairs)  11.5 us
    ppermute x4, starting transfers between devices, shifted(): return lax.ppermute(piece, 'row', pairs)  11.3 us
    ppermute x4, waiting for transfers between devices, shifted(): return lax.ppermute(piece, 'row', pairs)  5.87 us
    ppermute x4, waiting for transfers between devices, shifted(): return lax.ppermute(piece, 'col', pairs)  4.85 us
    reduce_sum x1, other arithmetic, body(): jnp.sum(jnp.where(match[..., None, None], p_blocks[:, :, None], jnp.zeros...  2.77 us
  transfers between devices with their start and end apart: 8, of which 4 were waited for; matrix products, arithmetic and copies ran while one was open for 11% of the time, Pallas kernels for 12%

profile of v16, /device:TPU:9, one launch (start us, length us, event | category | flops | bytes accessed | tf_op | source)
XLA Modules:
  0.0 100.8 jit_solution(17718583868863378485)
XLA Ops:
  0.3 0.8 broadcast_compare_fusion
  1.1 2.8 %select_reduce_fusion = bf16[4,4,4,64,64]{4,3,2,1,0:T(8,128)(2,1)S(1)} fusion(pred[4,4,4,4]{3,2,1,0:T(4,128)(4,1)S(1)} %broadcast_compare_fusion, bf16[4,4,4,64,64]{4,3,2,1,0:T(8,128)(2,1)} %param.7), kind=kLoop, calls=%fused_computation | loop fusion | flops 1835008 | bytes 1048832 | tf_op jit(solution)/shard_map/reduce_sum | solution.py:154
  4.1 3.7 %collective-permute-start = (bf16[4,4,32,128]{3,2,1,0:T(8,128)(2,1)S(1)}, bf16[4,4,32,128]{3,2,1,0:T(8,128)(2,1)S(1)}, u32[]{:S(2)}, u32[]{:S(2)}) collective-permute-start(bf16[4,4,32,128]{3,2,1,0:T(8,128)(2,1)S(1)} %reshape_squeeze.22), channel_id=1, source_target_pairs={{0,8},{8,16},{16,24},{1,9},{9,17},{17,25},{2,10},{10,18},{18,26},{... | collective-permute-start | bytes 393224 | tf_op jit(solution)/shard_map/ppermute | solution.py:20
  7.9 1.9 %collective-permute-start.1 = (bf16[4,4,32,128]{3,2,1,0:T(8,128)(2,1)S(1)}, bf16[4,4,32,128]{3,2,1,0:T(8,128)(2,1)S(1)}, u32[]{:S(2)}, u32[]{:S(2)}) collective-permute-start(bf16[4,4,32,128]{3,2,1,0:T(8,128)(2,1)S(1)} %reshape_squeeze.23), channel_id=1, source_target_pairs={{8,0},{16,8},{24,16},{9,1},{17,9},{25,17},{10,2},{18,10},{26,18},{... | collective-permute-start | bytes 393224 | tf_op jit(solution)/shard_map/ppermute | solution.py:20
  10.7 0.6 and_select_fusion.slot_ref
  12.6 0.6 reshape.677.near_ref
  13.3 0.9 collective-permute-done.1
  14.2 3.1 %collective-permute-start.2 = (bf16[6,4,32,128]{3,2,1,0:T(8,128)(2,1)S(1)}, bf16[6,4,32,128]{3,2,1,0:T(8,128)(2,1)S(1)}, u32[]{:S(2)}, u32[]{:S(2)}) collective-permute-start(bf16[6,4,32,128]{3,2,1,0:T(8,128)(2,1)S(1)} %pad_maximum_fusion.3), channel_id=1, source_target_pairs={{0,1},{1,2},{2,3},{3,4},{4,5},{5,6},{6,7},{8,9},{9,10},{10,11},{11... | collective-permute-start | bytes 589832 | tf_op jit(solution)/shard_map/ppermute | solution.py:23
  17.4 3.0 %collective-permute-start.3 = (bf16[6,4,32,128]{3,2,1,0:T(8,128)(2,1)S(1)}, bf16[6,4,32,128]{3,2,1,0:T(8,128)(2,1)S(1)}, u32[]{:S(2)}, u32[]{:S(2)}) collective-permute-start(bf16[6,4,32,128]{3,2,1,0:T(8,128)(2,1)S(1)} %pad_maximum_fusion.4), channel_id=1, source_target_pairs={{1,0},{2,1},{3,2},{4,3},{5,4},{6,5},{7,6},{9,8},{10,9},{11,10},{12... | collective-permute-start | bytes 589832 | tf_op jit(solution)/shard_map/ppermute | solution.py:23
  20.8 0.8 collective-permute-done.2
  21.8 4.0 %collective-permute-done.3 = bf16[6,4,32,128]{3,2,1,0:T(8,128)(2,1)S(1)} collective-permute-done((bf16[6,4,32,128]{3,2,1,0:T(8,128)(2,1)S(1)}, bf16[6,4,32,128]{3,2,1,0:T(8,128)(2,1)S(1)}, u32[]{:S(2)}, u32[]{:S(2)}) %collective-permute-start.3) | collective-permute-done | bytes 196640 | tf_op jit(solution)/shard_map/ppermute | solution.py:23
  26.0 1.8 %pad_maximum_fusion = bf16[6,6,4,64,64]{4,3,2,1,0:T(8,128)(2,1)} fusion(bf16[6,1,4,64,64]{4,3,2,1,0:T(8,128)(2,1)S(1)} %broadcast_in_dim_reshape.16, bf16[1,4,4,64,64]{4,3,2,1,0:T(8,128)(2,1)S(1)} %broadcast_in_dim_reshape.15, bf16[4,4,4,64,64]{4,3,2,1,0:T(8,128)(2,1)S(1)} %select_reduce_fusion, bf16[1,4,4,64,64]{4,3,2,1,0:T(8,128)(2,1)S(1)} %broadcast_in_dim_reshape.14, ...), kind=kLoop, calls=%fused_computation.1 | loop fusion | flops 2359296 | bytes 2359296 | tf_op jit(solution)/shard_map/concatenate | solution.py:51
  27.9 15.1 %shard_map.55 = (bf16[16,9,64,64]{3,2,1,0:T(8,128)(2,1)}, bf16[16,9,32,128]{3,2,1,0:T(8,128)(2,1)}) custom-call(s32[144]{0:T(256)} %reshape.677.near_ref, s32[576]{0:T(1024)} %and_select_fusion.slot_ref, bf16[16,9,64,64]{3,2,1,0:T(8,128)(2,1)} %bitcast.50, bf16[36,4,64,64]{3,2,1,0:T(8,128)(2,1)} %bitcast.47), custom_call_target="tpu_custom_call" | custom-call | tf_op jit(solution)/shard_map/pallas_call | solution.py:172
  43.0 1.1 %fusion.15 = (bf16[4,9,32,128]{3,2,1,0:T(8,128)(2,1)S(1)}, bf16[4,9,32,128]{3,2,1,0:T(8,128)(2,1)S(1)}) fusion(bf16[16,9,32,128]{3,2,1,0:T(8,128)(2,1)} %get-tuple-element.7), kind=kLoop, calls=%fused_computation.117 | loop fusion | bytes 1179648 | tf_op jit(solution)/shard_map/slice | solution.py:42
  44.1 3.8 %collective-permute-start.4 = (bf16[4,9,32,128]{3,2,1,0:T(8,128)(2,1)S(1)}, bf16[4,9,32,128]{3,2,1,0:T(8,128)(2,1)S(1)}, u32[]{:S(2)}, u32[]{:S(2)}) collective-permute-start(bf16[4,9,32,128]{3,2,1,0:T(8,128)(2,1)S(1)} %get-tuple-element.16), channel_id=1, source_target_pairs={{0,8},{8,16},{16,24},{1,9},{9,17},{17,25},{2,10},{10,18},{18,26},{... | collective-permute-start | bytes 884744 | tf_op jit(solution)/shard_map/ppermute | solution.py:20
  47.9 0.7 reshape.683.target_ref
  48.7 0.6 reshape.682.where_ref
  49.2 0.6 reshape.676.refs_8_
  49.8 1.9 %collective-permute-start.5 = (bf16[4,9,32,128]{3,2,1,0:T(8,128)(2,1)S(1)}, bf16[4,9,32,128]{3,2,1,0:T(8,128)(2,1)S(1)}, u32[]{:S(2)}, u32[]{:S(2)}) collective-permute-start(bf16[4,9,32,128]{3,2,1,0:T(8,128)(2,1)S(1)} %get-tuple-element.15), channel_id=1, source_target_pairs={{8,0},{16,8},{24,16},{9,1},{17,9},{25,17},{10,2},{18,10},{26,18},{... | collective-permute-start | bytes 884744 | tf_op jit(solution)/shard_map/ppermute | solution.py:20
  51.7 1.1 %slice_bitcast_fusion = (bf16[4,9,32,128]{3,2,1,0:T(8,128)(2,1)S(1)}, bf16[4,9,32,128]{3,2,1,0:T(8,128)(2,1)S(1)}) fusion(bf16[4,4,9,32,128]{4,3,2,1,0:T(8,128)(2,1)} %bitcast.51), kind=kLoop, calls=%fused_computation.8 | loop fusion | bytes 1179648 | tf_op jit(solution)/shard_map/squeeze | solution.py:44
  52.9 5.0 %collective-permute-done.5.refs_10_ = bf16[4,9,32,128]{3,2,1,0:T(8,128)(2,1)S(1)} collective-permute-done((bf16[4,9,32,128]{3,2,1,0:T(8,128)(2,1)S(1)}, bf16[4,9,32,128]{3,2,1,0:T(8,128)(2,1)S(1)}, u32[]{:S(2)}, u32[]{:S(2)}) %collective-permute-start.5) | collective-permute-done | bytes 294944 | tf_op jit(solution)/shard_map/ppermute | solution.py:20
  57.9 2.3 %collective-permute-start.7 = (bf16[6,9,32,128]{3,2,1,0:T(8,128)(2,1)S(1)}, bf16[6,9,32,128]{3,2,1,0:T(8,128)(2,1)S(1)}, u32[]{:S(2)}, u32[]{:S(2)}) collective-permute-start(bf16[6,9,32,128]{3,2,1,0:T(8,128)(2,1)S(1)} %pad_maximum_fusion.2), channel_id=1, source_target_pairs={{1,0},{2,1},{3,2},{4,3},{5,4},{6,5},{7,6},{9,8},{10,9},{11,10},{12... | collective-permute-start | bytes 1327112 | tf_op jit(solution)/shard_map/ppermute | solution.py:23
  60.3 3.0 %collective-permute-start.6 = (bf16[6,9,32,128]{3,2,1,0:T(8,128)(2,1)S(1)}, bf16[6,9,32,128]{3,2,1,0:T(8,128)(2,1)S(1)}, u32[]{:S(2)}, u32[]{:S(2)}) collective-permute-start(bf16[6,9,32,128]{3,2,1,0:T(8,128)(2,1)S(1)} %pad_maximum_fusion.1), channel_id=1, source_target_pairs={{0,1},{1,2},{2,3},{3,4},{4,5},{5,6},{6,7},{8,9},{9,10},{10,11},{11... | collective-permute-start | bytes 1327112 | tf_op jit(solution)/shard_map/ppermute | solution.py:23
  63.3 0.6 reshape_squeeze.20.refs_5_
  63.9 0.7 reshape_squeeze.21.refs_7_
  64.6 0.6 reshape_squeeze.18.refs_1_
  65.2 0.6 reshape_squeeze.19.refs_3_
  65.8 0.7 slice_reduce_fusion
  66.5 0.6 slice_bitcast_fusion.2
  67.2 12.6 %shard_map.56.refs_14_ = f32[100,64,64]{2,1,0:T(8,128)} custom-call(s32[16]{0:T(128)} %reshape.682.where_ref, s32[64]{0:T(128)} %reshape.683.target_ref, bf16[16,9,64,64]{3,2,1,0:T(8,128)(2,1)} %get-tuple-element.8.ap_ref, bf16[144,64,64]{2,1,0:T(8,128)(2,1)} %bitcast.48), custom_call_target="tpu_custom_call" | custom-call | flops 301989888 | bytes 6291456 | tf_op jit(solution)/shard_map/pallas_call | solution.py:222
  79.8 0.7 copy-done.2
  80.6 20.1 %shard_map.57 = bf16[4,25,64,64]{3,2,1,0:T(8,128)(2,1)} custom-call(s32[4]{0:T(128)} %get-tuple-element.35.refs_0_, s32[16]{0:T(128)} %reshape_squeeze.18.refs_1_, s32[4]{0:T(128)} %get-tuple-element.34.refs_2_, s32[16]{0:T(128)} %reshape_squeeze.19.refs_3_, s32[6]{0:T(128)} %get-tuple-element.12.refs_4_, s32[24]{0:T(128)} %reshape_squeeze.20.refs_5_, ...), custom_call_target="tpu_custom_call" | custom-call | tf_op jit(solution)/shard_map/pallas_call | solution.py:238
  (79 shorter events, 3.5 us)
Async XLA Ops:
  1.1 8.9 %copy-start.4 = (s32[4,4,9]{2,1,0:T(4,128)S(1)}, s32[4,4,9]{2,1,0:T(4,128)}, u32[]{:S(2)}) copy-start(s32[4,4,9]{2,1,0:T(4,128)} %param.6) | copy-start | bytes 1732
  3.9 16.6 %copy-start.5 = (s32[2,2,25]{2,1,0:T(2,128)S(1)}, s32[2,2,25]{2,1,0:T(2,128)}, u32[]{:S(2)}) copy-start(s32[2,2,25]{2,1,0:T(2,128)} %param.9) | copy-start | bytes 1204
  4.1 9.2 %collective-permute-start = (bf16[4,4,32,128]{3,2,1,0:T(8,128)(2,1)S(1)}, bf16[4,4,32,128]{3,2,1,0:T(8,128)(2,1)S(1)}, u32[]{:S(2)}, u32[]{:S(2)}) collective-permute-start(bf16[4,4,32,128]{3,2,1,0:T(8,128)(2,1)S(1)} %reshape_squeeze.22), channel_id=1, source_target_pairs={{0,8},{8,16},{16,24},{1,9},{9,17},{17,25},{2,10},{10,18},{18,26},{... | collective-permute-start | bytes 393224 | tf_op jit(solution)/shard_map/ppermute | solution.py:20
  7.9 6.3 %collective-permute-start.1 = (bf16[4,4,32,128]{3,2,1,0:T(8,128)(2,1)S(1)}, bf16[4,4,32,128]{3,2,1,0:T(8,128)(2,1)S(1)}, u32[]{:S(2)}, u32[]{:S(2)}) collective-permute-start(bf16[4,4,32,128]{3,2,1,0:T(8,128)(2,1)S(1)} %reshape_squeeze.23), channel_id=1, source_target_pairs={{8,0},{16,8},{24,16},{9,1},{17,9},{25,17},{10,2},{18,10},{26,18},{... | collective-permute-start | bytes 393224 | tf_op jit(solution)/shard_map/ppermute | solution.py:20
  14.2 7.4 %collective-permute-start.2 = (bf16[6,4,32,128]{3,2,1,0:T(8,128)(2,1)S(1)}, bf16[6,4,32,128]{3,2,1,0:T(8,128)(2,1)S(1)}, u32[]{:S(2)}, u32[]{:S(2)}) collective-permute-start(bf16[6,4,32,128]{3,2,1,0:T(8,128)(2,1)S(1)} %pad_maximum_fusion.3), channel_id=1, source_target_pairs={{0,1},{1,2},{2,3},{3,4},{4,5},{5,6},{6,7},{8,9},{9,10},{10,11},{11... | collective-permute-start | bytes 589832 | tf_op jit(solution)/shard_map/ppermute | solution.py:23
  17.4 8.4 %collective-permute-start.3 = (bf16[6,4,32,128]{3,2,1,0:T(8,128)(2,1)S(1)}, bf16[6,4,32,128]{3,2,1,0:T(8,128)(2,1)S(1)}, u32[]{:S(2)}, u32[]{:S(2)}) collective-permute-start(bf16[6,4,32,128]{3,2,1,0:T(8,128)(2,1)S(1)} %pad_maximum_fusion.4), channel_id=1, source_target_pairs={{1,0},{2,1},{3,2},{4,3},{5,4},{6,5},{7,6},{9,8},{10,9},{11,10},{12... | collective-permute-start | bytes 589832 | tf_op jit(solution)/shard_map/ppermute | solution.py:23
  44.1 8.7 %collective-permute-start.4 = (bf16[4,9,32,128]{3,2,1,0:T(8,128)(2,1)S(1)}, bf16[4,9,32,128]{3,2,1,0:T(8,128)(2,1)S(1)}, u32[]{:S(2)}, u32[]{:S(2)}) collective-permute-start(bf16[4,9,32,128]{3,2,1,0:T(8,128)(2,1)S(1)} %get-tuple-element.16), channel_id=1, source_target_pairs={{0,8},{8,16},{16,24},{1,9},{9,17},{17,25},{2,10},{10,18},{18,26},{... | collective-permute-start | bytes 884744 | tf_op jit(solution)/shard_map/ppermute | solution.py:20
  49.8 8.0 %collective-permute-start.5 = (bf16[4,9,32,128]{3,2,1,0:T(8,128)(2,1)S(1)}, bf16[4,9,32,128]{3,2,1,0:T(8,128)(2,1)S(1)}, u32[]{:S(2)}, u32[]{:S(2)}) collective-permute-start(bf16[4,9,32,128]{3,2,1,0:T(8,128)(2,1)S(1)} %get-tuple-element.15), channel_id=1, source_target_pairs={{8,0},{16,8},{24,16},{9,1},{17,9},{25,17},{10,2},{18,10},{26,18},{... | collective-permute-start | bytes 884744 | tf_op jit(solution)/shard_map/ppermute | solution.py:20
  52.8 26.9 %copy-start = (bf16[4,9,32,128]{3,2,1,0:T(8,128)(2,1)}, bf16[4,9,32,128]{3,2,1,0:T(8,128)(2,1)S(1)}, u32[]{:S(2)}) copy-start(bf16[4,9,32,128]{3,2,1,0:T(8,128)(2,1)S(1)} %collective-permute-done.4.refs_9_) | copy-start | bytes 884740
  57.8 21.9 %copy-start.1 = (bf16[4,9,32,128]{3,2,1,0:T(8,128)(2,1)}, bf16[4,9,32,128]{3,2,1,0:T(8,128)(2,1)S(1)}, u32[]{:S(2)}) copy-start(bf16[4,9,32,128]{3,2,1,0:T(8,128)(2,1)S(1)} %collective-permute-done.5.refs_10_) | copy-start | bytes 884740
  57.9 21.8 %collective-permute-start.7 = (bf16[6,9,32,128]{3,2,1,0:T(8,128)(2,1)S(1)}, bf16[6,9,32,128]{3,2,1,0:T(8,128)(2,1)S(1)}, u32[]{:S(2)}, u32[]{:S(2)}) collective-permute-start(bf16[6,9,32,128]{3,2,1,0:T(8,128)(2,1)S(1)} %pad_maximum_fusion.2), channel_id=1, source_target_pairs={{1,0},{2,1},{3,2},{4,3},{5,4},{6,5},{7,6},{9,8},{10,9},{11,10},{12... | collective-permute-start | bytes 1327112 | tf_op jit(solution)/shard_map/ppermute | solution.py:23
  60.3 19.5 %collective-permute-start.6 = (bf16[6,9,32,128]{3,2,1,0:T(8,128)(2,1)S(1)}, bf16[6,9,32,128]{3,2,1,0:T(8,128)(2,1)S(1)}, u32[]{:S(2)}, u32[]{:S(2)}) collective-permute-start(bf16[6,9,32,128]{3,2,1,0:T(8,128)(2,1)S(1)} %pad_maximum_fusion.1), channel_id=1, source_target_pairs={{0,1},{1,2},{2,3},{3,4},{4,5},{5,6},{6,7},{8,9},{9,10},{10,11},{11... | collective-permute-start | bytes 1327112 | tf_op jit(solution)/shard_map/ppermute | solution.py:23
  79.7 0.8 copy-start.2
  79.7 0.9 copy-start.3

commit v17 on v16

--- a/solution.py
+++ b/solution.py
@@ -88,8 +88,6 @@
 def add_terms(where_ref, target_ref, ap_ref, pt_ref, acc_ref):
     def one_tile(t, carry):
         w = where_ref[t]
-        dense = ap_ref.shape[-2:] != pt_ref.shape[1:]
-        blocks = [ap_ref[t, e].reshape(pt_ref.shape[1:]) for e in range(9)] if dense else None
         for q in range(4):
             g = target_ref[t * 4 + q]
 
@@ -97,7 +95,7 @@
             def _():
                 p = pt_ref[w * 4 + q]
                 for e in range(9):
-                    block = blocks[e] if dense else ap_ref[t, e]
+                    block = ap_ref[t, e].reshape(p.shape)
                     acc_ref[g + (e // 3) * 5 + e % 3] += lax.dot_general(
                         p, block, (((0,), (0,)), ((), ())), preferred_element_type=jnp.float32
                     )

time: 101 us -> 102 us (level)
  transfers between devices with their start and end apart: 8 -> 8, of which waited for: 4 -> 4; matrix products, arithmetic and copies ran while one was open for 11% -> 10% of each run, Pallas kernels for 12% -> 12%
where the time goes in v17:
time: 102 us
  Pallas kernels  48.7 us (48%)
  starting transfers between devices  23 us (23%)
  local copies, waits for them, and re-layouts  11.9 us (12%)
  waiting for transfers between devices  10.7 us (10%)
  other arithmetic  6.86 us (7%)
    pallas_call x1, Pallas kernels, body(): pl.pallas_call(coarse_kernel, out_shape=jax.ShapeDtypeStruct((o_r * o_c,...  21 us
    pallas_call x1, Pallas kernels, body(): pl.pallas_call(functools.partial(ap_kernel, n_r=n_r, n_c=n_c), out_shape=...  15.1 us
    pallas_call x1, Pallas kernels, body(): pl.pallas_call(own_kernel, out_shape=jax.ShapeDtypeStruct(acc_shape, jnp....  12.6 us
    ppermute x4, starting transfers between devices, shifted(): return lax.ppermute(piece, 'col', pairs)  11.6 us
    ppermute x4, starting transfers between devices, shifted(): return lax.ppermute(piece, 'row', pairs)  11.3 us
    ppermute x4, waiting for transfers between devices, shifted(): return lax.ppermute(piece, 'row', pairs)  5.87 us
    ppermute x4, waiting for transfers between devices, shifted(): return lax.ppermute(piece, 'col', pairs)  4.85 us
    reduce_sum x1, other arithmetic, body(): jnp.sum(jnp.where(match[..., None, None], p_blocks[:, :, None], jnp.zeros...  2.77 us
  transfers between devices with their start and end apart: 8, of which 4 were waited for; matrix products, arithmetic and copies ran while one was open for 10% of the time, Pallas kernels for 12%

profile of v17, /device:TPU:9, one launch (start us, length us, event | category | flops | bytes accessed | tf_op | source)
XLA Modules:
  0.0 101.8 jit_solution(7487739057399479595)
XLA Ops:
  0.3 0.8 broadcast_compare_fusion
  1.1 2.8 %select_reduce_fusion = bf16[4,4,4,64,64]{4,3,2,1,0:T(8,128)(2,1)S(1)} fusion(pred[4,4,4,4]{3,2,1,0:T(4,128)(4,1)S(1)} %broadcast_compare_fusion, bf16[4,4,4,64,64]{4,3,2,1,0:T(8,128)(2,1)} %param.7), kind=kLoop, calls=%fused_computation | loop fusion | flops 1835008 | bytes 1048832 | tf_op jit(solution)/shard_map/reduce_sum | solution.py:152
  4.1 3.7 %collective-permute-start = (bf16[4,4,32,128]{3,2,1,0:T(8,128)(2,1)S(1)}, bf16[4,4,32,128]{3,2,1,0:T(8,128)(2,1)S(1)}, u32[]{:S(2)}, u32[]{:S(2)}) collective-permute-start(bf16[4,4,32,128]{3,2,1,0:T(8,128)(2,1)S(1)} %reshape_squeeze.22), channel_id=1, source_target_pairs={{0,8},{8,16},{16,24},{1,9},{9,17},{17,25},{2,10},{10,18},{18,26},{... | collective-permute-start | bytes 393224 | tf_op jit(solution)/shard_map/ppermute | solution.py:20
  7.9 1.9 %collective-permute-start.1 = (bf16[4,4,32,128]{3,2,1,0:T(8,128)(2,1)S(1)}, bf16[4,4,32,128]{3,2,1,0:T(8,128)(2,1)S(1)}, u32[]{:S(2)}, u32[]{:S(2)}) collective-permute-start(bf16[4,4,32,128]{3,2,1,0:T(8,128)(2,1)S(1)} %reshape_squeeze.23), channel_id=1, source_target_pairs={{8,0},{16,8},{24,16},{9,1},{17,9},{25,17},{10,2},{18,10},{26,18},{... | collective-permute-start | bytes 393224 | tf_op jit(solution)/shard_map/ppermute | solution.py:20
  10.7 0.6 and_select_fusion.slot_ref
  12.6 0.6 reshape.677.near_ref
  13.3 0.9 collective-permute-done.1
  14.2 3.1 %collective-permute-start.2 = (bf16[6,4,32,128]{3,2,1,0:T(8,128)(2,1)S(1)}, bf16[6,4,32,128]{3,2,1,0:T(8,128)(2,1)S(1)}, u32[]{:S(2)}, u32[]{:S(2)}) collective-permute-start(bf16[6,4,32,128]{3,2,1,0:T(8,128)(2,1)S(1)} %pad_maximum_fusion.3), channel_id=1, source_target_pairs={{0,1},{1,2},{2,3},{3,4},{4,5},{5,6},{6,7},{8,9},{9,10},{10,11},{11... | collective-permute-start | bytes 589832 | tf_op jit(solution)/shard_map/ppermute | solution.py:23
  17.4 3.0 %collective-permute-start.3 = (bf16[6,4,32,128]{3,2,1,0:T(8,128)(2,1)S(1)}, bf16[6,4,32,128]{3,2,1,0:T(8,128)(2,1)S(1)}, u32[]{:S(2)}, u32[]{:S(2)}) collective-permute-start(bf16[6,4,32,128]{3,2,1,0:T(8,128)(2,1)S(1)} %pad_maximum_fusion.4), channel_id=1, source_target_pairs={{1,0},{2,1},{3,2},{4,3},{5,4},{6,5},{7,6},{9,8},{10,9},{11,10},{12... | collective-permute-start | bytes 589832 | tf_op jit(solution)/shard_map/ppermute | solution.py:23
  20.8 0.8 collective-permute-done.2
  21.8 4.0 %collective-permute-done.3 = bf16[6,4,32,128]{3,2,1,0:T(8,128)(2,1)S(1)} collective-permute-done((bf16[6,4,32,128]{3,2,1,0:T(8,128)(2,1)S(1)}, bf16[6,4,32,128]{3,2,1,0:T(8,128)(2,1)S(1)}, u32[]{:S(2)}, u32[]{:S(2)}) %collective-permute-start.3) | collective-permute-done | bytes 196640 | tf_op jit(solution)/shard_map/ppermute | solution.py:23
  26.0 1.8 %pad_maximum_fusion = bf16[6,6,4,64,64]{4,3,2,1,0:T(8,128)(2,1)} fusion(bf16[6,1,4,64,64]{4,3,2,1,0:T(8,128)(2,1)S(1)} %broadcast_in_dim_reshape.16, bf16[1,4,4,64,64]{4,3,2,1,0:T(8,128)(2,1)S(1)} %broadcast_in_dim_reshape.15, bf16[4,4,4,64,64]{4,3,2,1,0:T(8,128)(2,1)S(1)} %select_reduce_fusion, bf16[1,4,4,64,64]{4,3,2,1,0:T(8,128)(2,1)S(1)} %broadcast_in_dim_reshape.14, ...), kind=kLoop, calls=%fused_computation.1 | loop fusion | flops 2359296 | bytes 2359296 | tf_op jit(solution)/shard_map/concatenate | solution.py:51
  27.9 15.1 %shard_map.55 = (bf16[16,9,64,64]{3,2,1,0:T(8,128)(2,1)}, bf16[16,9,32,128]{3,2,1,0:T(8,128)(2,1)}) custom-call(s32[144]{0:T(256)} %reshape.677.near_ref, s32[576]{0:T(1024)} %and_select_fusion.slot_ref, bf16[16,9,64,64]{3,2,1,0:T(8,128)(2,1)} %bitcast.50, bf16[36,4,64,64]{3,2,1,0:T(8,128)(2,1)} %bitcast.47), custom_call_target="tpu_custom_call" | custom-call | tf_op jit(solution)/shard_map/pallas_call | solution.py:170
  43.0 1.1 %fusion.15 = (bf16[4,9,32,128]{3,2,1,0:T(8,128)(2,1)S(1)}, bf16[4,9,32,128]{3,2,1,0:T(8,128)(2,1)S(1)}) fusion(bf16[16,9,32,128]{3,2,1,0:T(8,128)(2,1)} %get-tuple-element.7), kind=kLoop, calls=%fused_computation.117 | loop fusion | bytes 1179648 | tf_op jit(solution)/shard_map/slice | solution.py:42
  44.1 3.8 %collective-permute-start.4 = (bf16[4,9,32,128]{3,2,1,0:T(8,128)(2,1)S(1)}, bf16[4,9,32,128]{3,2,1,0:T(8,128)(2,1)S(1)}, u32[]{:S(2)}, u32[]{:S(2)}) collective-permute-start(bf16[4,9,32,128]{3,2,1,0:T(8,128)(2,1)S(1)} %get-tuple-element.16), channel_id=1, source_target_pairs={{0,8},{8,16},{16,24},{1,9},{9,17},{17,25},{2,10},{10,18},{18,26},{... | collective-permute-start | bytes 884744 | tf_op jit(solution)/shard_map/ppermute | solution.py:20
  47.9 0.7 reshape.683.target_ref
  48.7 0.6 reshape.682.where_ref
  49.2 0.6 reshape.676.refs_8_
  49.8 1.9 %collective-permute-start.5 = (bf16[4,9,32,128]{3,2,1,0:T(8,128)(2,1)S(1)}, bf16[4,9,32,128]{3,2,1,0:T(8,128)(2,1)S(1)}, u32[]{:S(2)}, u32[]{:S(2)}) collective-permute-start(bf16[4,9,32,128]{3,2,1,0:T(8,128)(2,1)S(1)} %get-tuple-element.15), channel_id=1, source_target_pairs={{8,0},{16,8},{24,16},{9,1},{17,9},{25,17},{10,2},{18,10},{26,18},{... | collective-permute-start | bytes 884744 | tf_op jit(solution)/shard_map/ppermute | solution.py:20
  51.7 1.1 %slice_bitcast_fusion = (bf16[4,9,32,128]{3,2,1,0:T(8,128)(2,1)S(1)}, bf16[4,9,32,128]{3,2,1,0:T(8,128)(2,1)S(1)}) fusion(bf16[4,4,9,32,128]{4,3,2,1,0:T(8,128)(2,1)} %bitcast.51), kind=kLoop, calls=%fused_computation.8 | loop fusion | bytes 1179648 | tf_op jit(solution)/shard_map/squeeze | solution.py:44
  52.9 5.0 %collective-permute-done.5.refs_10_ = bf16[4,9,32,128]{3,2,1,0:T(8,128)(2,1)S(1)} collective-permute-done((bf16[4,9,32,128]{3,2,1,0:T(8,128)(2,1)S(1)}, bf16[4,9,32,128]{3,2,1,0:T(8,128)(2,1)S(1)}, u32[]{:S(2)}, u32[]{:S(2)}) %collective-permute-start.5) | collective-permute-done | bytes 294944 | tf_op jit(solution)/shard_map/ppermute | solution.py:20
  57.9 2.3 %collective-permute-start.7 = (bf16[6,9,32,128]{3,2,1,0:T(8,128)(2,1)S(1)}, bf16[6,9,32,128]{3,2,1,0:T(8,128)(2,1)S(1)}, u32[]{:S(2)}, u32[]{:S(2)}) collective-permute-start(bf16[6,9,32,128]{3,2,1,0:T(8,128)(2,1)S(1)} %pad_maximum_fusion.2), channel_id=1, source_target_pairs={{1,0},{2,1},{3,2},{4,3},{5,4},{6,5},{7,6},{9,8},{10,9},{11,10},{12... | collective-permute-start | bytes 1327112 | tf_op jit(solution)/shard_map/ppermute | solution.py:23
  60.3 3.2 %collective-permute-start.6 = (bf16[6,9,32,128]{3,2,1,0:T(8,128)(2,1)S(1)}, bf16[6,9,32,128]{3,2,1,0:T(8,128)(2,1)S(1)}, u32[]{:S(2)}, u32[]{:S(2)}) collective-permute-start(bf16[6,9,32,128]{3,2,1,0:T(8,128)(2,1)S(1)} %pad_maximum_fusion.1), channel_id=1, source_target_pairs={{0,1},{1,2},{2,3},{3,4},{4,5},{5,6},{6,7},{8,9},{9,10},{10,11},{11... | collective-permute-start | bytes 1327112 | tf_op jit(solution)/shard_map/ppermute | solution.py:23
  63.5 0.6 reshape_squeeze.20.refs_5_
  64.1 0.7 reshape_squeeze.21.refs_7_
  64.8 0.6 reshape_squeeze.18.refs_1_
  65.4 0.6 reshape_squeeze.19.refs_3_
  66.0 0.7 slice_reduce_fusion
  66.7 0.6 slice_bitcast_fusion.2
  67.3 12.6 %shard_map.56.refs_14_ = f32[100,64,64]{2,1,0:T(8,128)} custom-call(s32[16]{0:T(128)} %reshape.682.where_ref, s32[64]{0:T(128)} %reshape.683.target_ref, bf16[16,9,64,64]{3,2,1,0:T(8,128)(2,1)} %get-tuple-element.8.ap_ref, bf16[144,64,64]{2,1,0:T(8,128)(2,1)} %bitcast.48), custom_call_target="tpu_custom_call" | custom-call | flops 301989888 | bytes 6291456 | tf_op jit(solution)/shard_map/pallas_call | solution.py:220
  79.9 0.7 copy-done.2
  80.8 21.0 %shard_map.57 = bf16[4,25,64,64]{3,2,1,0:T(8,128)(2,1)} custom-call(s32[4]{0:T(128)} %get-tuple-element.35.refs_0_, s32[16]{0:T(128)} %reshape_squeeze.18.refs_1_, s32[4]{0:T(128)} %get-tuple-element.34.refs_2_, s32[16]{0:T(128)} %reshape_squeeze.19.refs_3_, s32[6]{0:T(128)} %get-tuple-element.12.refs_4_, s32[24]{0:T(128)} %reshape_squeeze.20.refs_5_, ...), custom_call_target="tpu_custom_call" | custom-call | tf_op jit(solution)/shard_map/pallas_call | solution.py:236
  (79 shorter events, 3.5 us)
Async XLA Ops:
  1.1 8.9 %copy-start.4 = (s32[4,4,9]{2,1,0:T(4,128)S(1)}, s32[4,4,9]{2,1,0:T(4,128)}, u32[]{:S(2)}) copy-start(s32[4,4,9]{2,1,0:T(4,128)} %param.6) | copy-start | bytes 1732
  3.9 16.6 %copy-start.5 = (s32[2,2,25]{2,1,0:T(2,128)S(1)}, s32[2,2,25]{2,1,0:T(2,128)}, u32[]{:S(2)}) copy-start(s32[2,2,25]{2,1,0:T(2,128)} %param.9) | copy-start | bytes 1204
  4.1 9.2 %collective-permute-start = (bf16[4,4,32,128]{3,2,1,0:T(8,128)(2,1)S(1)}, bf16[4,4,32,128]{3,2,1,0:T(8,128)(2,1)S(1)}, u32[]{:S(2)}, u32[]{:S(2)}) collective-permute-start(bf16[4,4,32,128]{3,2,1,0:T(8,128)(2,1)S(1)} %reshape_squeeze.22), channel_id=1, source_target_pairs={{0,8},{8,16},{16,24},{1,9},{9,17},{17,25},{2,10},{10,18},{18,26},{... | collective-permute-start | bytes 393224 | tf_op jit(solution)/shard_map/ppermute | solution.py:20
  7.9 6.3 %collective-permute-start.1 = (bf16[4,4,32,128]{3,2,1,0:T(8,128)(2,1)S(1)}, bf16[4,4,32,128]{3,2,1,0:T(8,128)(2,1)S(1)}, u32[]{:S(2)}, u32[]{:S(2)}) collective-permute-start(bf16[4,4,32,128]{3,2,1,0:T(8,128)(2,1)S(1)} %reshape_squeeze.23), channel_id=1, source_target_pairs={{8,0},{16,8},{24,16},{9,1},{17,9},{25,17},{10,2},{18,10},{26,18},{... | collective-permute-start | bytes 393224 | tf_op jit(solution)/shard_map/ppermute | solution.py:20
  14.2 7.4 %collective-permute-start.2 = (bf16[6,4,32,128]{3,2,1,0:T(8,128)(2,1)S(1)}, bf16[6,4,32,128]{3,2,1,0:T(8,128)(2,1)S(1)}, u32[]{:S(2)}, u32[]{:S(2)}) collective-permute-start(bf16[6,4,32,128]{3,2,1,0:T(8,128)(2,1)S(1)} %pad_maximum_fusion.3), channel_id=1, source_target_pairs={{0,1},{1,2},{2,3},{3,4},{4,5},{5,6},{6,7},{8,9},{9,10},{10,11},{11... | collective-permute-start | bytes 589832 | tf_op jit(solution)/shard_map/ppermute | solution.py:23
  17.4 8.4 %collective-permute-start.3 = (bf16[6,4,32,128]{3,2,1,0:T(8,128)(2,1)S(1)}, bf16[6,4,32,128]{3,2,1,0:T(8,128)(2,1)S(1)}, u32[]{:S(2)}, u32[]{:S(2)}) collective-permute-start(bf16[6,4,32,128]{3,2,1,0:T(8,128)(2,1)S(1)} %pad_maximum_fusion.4), channel_id=1, source_target_pairs={{1,0},{2,1},{3,2},{4,3},{5,4},{6,5},{7,6},{9,8},{10,9},{11,10},{12... | collective-permute-start | bytes 589832 | tf_op jit(solution)/shard_map/ppermute | solution.py:23
  44.1 8.7 %collective-permute-start.4 = (bf16[4,9,32,128]{3,2,1,0:T(8,128)(2,1)S(1)}, bf16[4,9,32,128]{3,2,1,0:T(8,128)(2,1)S(1)}, u32[]{:S(2)}, u32[]{:S(2)}) collective-permute-start(bf16[4,9,32,128]{3,2,1,0:T(8,128)(2,1)S(1)} %get-tuple-element.16), channel_id=1, source_target_pairs={{0,8},{8,16},{16,24},{1,9},{9,17},{17,25},{2,10},{10,18},{18,26},{... | collective-permute-start | bytes 884744 | tf_op jit(solution)/shard_map/ppermute | solution.py:20
  49.8 8.0 %collective-permute-start.5 = (bf16[4,9,32,128]{3,2,1,0:T(8,128)(2,1)S(1)}, bf16[4,9,32,128]{3,2,1,0:T(8,128)(2,1)S(1)}, u32[]{:S(2)}, u32[]{:S(2)}) collective-permute-start(bf16[4,9,32,128]{3,2,1,0:T(8,128)(2,1)S(1)} %get-tuple-element.15), channel_id=1, source_target_pairs={{8,0},{16,8},{24,16},{9,1},{17,9},{25,17},{10,2},{18,10},{26,18},{... | collective-permute-start | bytes 884744 | tf_op jit(solution)/shard_map/ppermute | solution.py:20
  52.8 27.1 %copy-start = (bf16[4,9,32,128]{3,2,1,0:T(8,128)(2,1)}, bf16[4,9,32,128]{3,2,1,0:T(8,128)(2,1)S(1)}, u32[]{:S(2)}) copy-start(bf16[4,9,32,128]{3,2,1,0:T(8,128)(2,1)S(1)} %collective-permute-done.4.refs_9_) | copy-start | bytes 884740
  57.8 22.1 %copy-start.1 = (bf16[4,9,32,128]{3,2,1,0:T(8,128)(2,1)}, bf16[4,9,32,128]{3,2,1,0:T(8,128)(2,1)S(1)}, u32[]{:S(2)}) copy-start(bf16[4,9,32,128]{3,2,1,0:T(8,128)(2,1)S(1)} %collective-permute-done.5.refs_10_) | copy-start | bytes 884740
  57.9 22.0 %collective-permute-start.7 = (bf16[6,9,32,128]{3,2,1,0:T(8,128)(2,1)S(1)}, bf16[6,9,32,128]{3,2,1,0:T(8,128)(2,1)S(1)}, u32[]{:S(2)}, u32[]{:S(2)}) collective-permute-start(bf16[6,9,32,128]{3,2,1,0:T(8,128)(2,1)S(1)} %pad_maximum_fusion.2), channel_id=1, source_target_pairs={{1,0},{2,1},{3,2},{4,3},{5,4},{6,5},{7,6},{9,8},{10,9},{11,10},{12... | collective-permute-start | bytes 1327112 | tf_op jit(solution)/shard_map/ppermute | solution.py:23
  60.3 19.6 %collective-permute-start.6 = (bf16[6,9,32,128]{3,2,1,0:T(8,128)(2,1)S(1)}, bf16[6,9,32,128]{3,2,1,0:T(8,128)(2,1)S(1)}, u32[]{:S(2)}, u32[]{:S(2)}) collective-permute-start(bf16[6,9,32,128]{3,2,1,0:T(8,128)(2,1)S(1)} %pad_maximum_fusion.1), channel_id=1, source_target_pairs={{0,1},{1,2},{2,3},{3,4},{4,5},{5,6},{6,7},{8,9},{9,10},{10,11},{11... | collective-permute-start | bytes 1327112 | tf_op jit(solution)/shard_map/ppermute | solution.py:23
  79.9 0.8 copy-start.2
  79.9 0.9 copy-start.3

commit v18 on v16

--- a/solution.py
+++ b/solution.py
@@ -151,11 +151,8 @@
     agg_x = mirror((xs - 1)[:, None] // 2 + two, coarse_cols)
     wanted = (agg_y[:, None, :, None] * coarse_cols + agg_x[None, :, None, :]).reshape(n_r, n_c, 4)
     match = p_cols[:, :, None, :] == wanted[:, :, :, None]
-    canon = jnp.sum(
-        jnp.where(match[..., None, None], p_blocks[:, :, None], jnp.zeros((), p_blocks.dtype)),
-        axis=3,
-        dtype=p_blocks.dtype,
-    )
+    which = jnp.argmax(match, axis=-1).astype(jnp.int32)
+    canon = jnp.take_along_axis(p_blocks, which[..., None, None], axis=2)
     p_ext = with_halo(canon)
     ext_r, ext_c = n_r + 2, n_c + 2
 

time: 101 us -> 102 us (level)
  local copies, waits for them, and re-layouts: 11.9 us -> 14 us
  other arithmetic: 6.86 us -> 5.51 us
    reduce_sum x1 -> x0, other arithmetic: 2.77 us -> none  [body(): jnp.sum(jnp.where(match[..., None, None], p_blocks[:, :, None], jnp.zeros...]
    another operation x0 -> x1, other arithmetic: none -> 2.03 us  [body(): which = jnp.argmax(match, axis=-1).astype(jnp.int32)]
  transfers between devices with their start and end apart: 8 -> 8, of which waited for: 4 -> 4; matrix products, arithmetic and copies ran while one was open for 11% -> 10% of each run, Pallas kernels for 12% -> 12%
where the time goes in v18:
time: 102 us
  Pallas kernels  47.8 us (47%)
  starting transfers between devices  22.9 us (22%)
  local copies, waits for them, and re-layouts  14 us (14%)
  waiting for transfers between devices  10.7 us (10%)
  other arithmetic  5.51 us (5%)
    pallas_call x1, Pallas kernels, body(): pl.pallas_call(coarse_kernel, out_shape=jax.ShapeDtypeStruct((o_r * o_c,...  20.1 us
    pallas_call x1, Pallas kernels, body(): pl.pallas_call(functools.partial(ap_kernel, n_r=n_r, n_c=n_c), out_shape=...  15.1 us
    pallas_call x1, Pallas kernels, body(): pl.pallas_call(own_kernel, out_shape=jax.ShapeDtypeStruct(acc_shape, jnp....  12.6 us
    ppermute x4, starting transfers between devices, shifted(): return lax.ppermute(piece, 'col', pairs)  11.5 us
    ppermute x4, starting transfers between devices, shifted(): return lax.ppermute(piece, 'row', pairs)  11.4 us
    ppermute x4, waiting for transfers between devices, shifted(): return lax.ppermute(piece, 'row', pairs)  5.57 us
    ppermute x4, waiting for transfers between devices, shifted(): return lax.ppermute(piece, 'col', pairs)  5.15 us
    another operation x4, local copies, waits for them, and re-layouts, body(): g.reshape(-1)  2.44 us
  transfers between devices with their start and end apart: 8, of which 4 were waited for; matrix products, arithmetic and copies ran while one was open for 10% of the time, Pallas kernels for 12%

profile of v18, /device:TPU:9, one launch (start us, length us, event | category | flops | bytes accessed | tf_op | source)
XLA Modules:
  0.0 101.7 jit_solution(705292899687334460)
XLA Ops:
  0.3 2.0 %iota_reduce_fusion = (pred[4,4,4]{2,1,0:T(4,128)(4,1)}, s32[4,4,4]{2,1,0:T(4,128)S(1)}) fusion(s32[4,4,4]{2,1,0:T(4,128)S(1)} %broadcast_add_fusion.1, s32[4,4,4]{2,1,0:T(4,128)} %param.8), kind=kLoop, calls=%fused_computation.17 | loop fusion | flops 1600 | bytes 832 | tf_op jit(solution)/shard_map/body/reduce | solution.py:154
  2.4 0.9 gather_fusion
  3.7 3.7 %collective-permute-start = (bf16[4,4,32,128]{3,2,1,0:T(8,128)(2,1)S(1)}, bf16[4,4,32,128]{3,2,1,0:T(8,128)(2,1)S(1)}, u32[]{:S(2)}, u32[]{:S(2)}) collective-permute-start(bf16[4,4,32,128]{3,2,1,0:T(8,128)(2,1)S(1)} %reshape_squeeze.22), channel_id=1, source_target_pairs={{0,8},{8,16},{16,24},{1,9},{9,17},{17,25},{2,10},{10,18},{18,26},{... | collective-permute-start | bytes 393224 | tf_op jit(solution)/shard_map/ppermute | solution.py:20
  7.5 1.9 %collective-permute-start.1 = (bf16[4,4,32,128]{3,2,1,0:T(8,128)(2,1)S(1)}, bf16[4,4,32,128]{3,2,1,0:T(8,128)(2,1)S(1)}, u32[]{:S(2)}, u32[]{:S(2)}) collective-permute-start(bf16[4,4,32,128]{3,2,1,0:T(8,128)(2,1)S(1)} %reshape_squeeze.23), channel_id=1, source_target_pairs={{8,0},{16,8},{24,16},{9,1},{17,9},{25,17},{10,2},{18,10},{26,18},{... | collective-permute-start | bytes 393224 | tf_op jit(solution)/shard_map/ppermute | solution.py:20
  10.3 0.6 and_select_fusion.slot_ref
  12.6 0.6 reshape.695.near_ref
  13.2 0.6 collective-permute-done.1
  13.9 3.1 %collective-permute-start.2 = (bf16[6,4,32,128]{3,2,1,0:T(8,128)(2,1)S(1)}, bf16[6,4,32,128]{3,2,1,0:T(8,128)(2,1)S(1)}, u32[]{:S(2)}, u32[]{:S(2)}) collective-permute-start(bf16[6,4,32,128]{3,2,1,0:T(8,128)(2,1)S(1)} %pad_maximum_fusion.3), channel_id=1, source_target_pairs={{0,1},{1,2},{2,3},{3,4},{4,5},{5,6},{6,7},{8,9},{9,10},{10,11},{11... | collective-permute-start | bytes 589832 | tf_op jit(solution)/shard_map/ppermute | solution.py:23
  17.1 3.0 %collective-permute-start.3 = (bf16[6,4,32,128]{3,2,1,0:T(8,128)(2,1)S(1)}, bf16[6,4,32,128]{3,2,1,0:T(8,128)(2,1)}, u32[]{:S(2)}, u32[]{:S(2)}) collective-permute-start(bf16[6,4,32,128]{3,2,1,0:T(8,128)(2,1)S(1)} %pad_maximum_fusion.4), channel_id=1, source_target_pairs={{1,0},{2,1},{3,2},{4,3},{5,4},{6,5},{7,6},{9,8},{10,9},{11,10},{12... | collective-permute-start | bytes 589832 | tf_op jit(solution)/shard_map/ppermute | solution.py:23
  20.5 0.9 collective-permute-done.2
  21.6 4.2 %collective-permute-done.3 = bf16[6,4,32,128]{3,2,1,0:T(8,128)(2,1)} collective-permute-done((bf16[6,4,32,128]{3,2,1,0:T(8,128)(2,1)S(1)}, bf16[6,4,32,128]{3,2,1,0:T(8,128)(2,1)}, u32[]{:S(2)}, u32[]{:S(2)}) %collective-permute-start.3) | collective-permute-done | bytes 196640 | tf_op jit(solution)/shard_map/ppermute | solution.py:23
  25.8 1.1 %broadcast_in_dim_reshape.16 = bf16[6,1,4,64,64]{4,3,2,1,0:T(8,128)(2,1)S(1)} reshape(bf16[6,4,32,128]{3,2,1,0:T(8,128)(2,1)} %collective-permute-done.3) | data formatting | bytes 393216 | tf_op jit(solution)/shard_map/broadcast_in_dim;reshape | solution.py:51
  26.9 1.8 %pad_maximum_fusion = bf16[6,6,4,64,64]{4,3,2,1,0:T(8,128)(2,1)} fusion(bf16[6,1,4,64,64]{4,3,2,1,0:T(8,128)(2,1)S(1)} %broadcast_in_dim_reshape.16, bf16[1,4,4,64,64]{4,3,2,1,0:T(8,128)(2,1)S(1)} %broadcast_in_dim_reshape.15, bf16[4,4,4,64,64]{4,3,2,1,0:T(8,128)(2,1)S(1)} %broadcast_select_fusion, ...), kind=kLoop, calls=%fused_computation.1 | loop fusion | flops 2359296 | bytes 2359296 | tf_op jit(solution)/shard_map/concatenate | solution.py:51
  28.7 15.1 %shard_map.55 = (bf16[16,9,64,64]{3,2,1,0:T(8,128)(2,1)}, bf16[16,9,32,128]{3,2,1,0:T(8,128)(2,1)}) custom-call(s32[144]{0:T(256)} %reshape.695.near_ref, s32[576]{0:T(1024)} %and_select_fusion.slot_ref, bf16[16,9,64,64]{3,2,1,0:T(8,128)(2,1)} %bitcast.56, bf16[36,4,64,64]{3,2,1,0:T(8,128)(2,1)} %bitcast.52), custom_call_target="tpu_custom_call" | custom-call | tf_op jit(solution)/shard_map/pallas_call | solution.py:169
  43.8 1.1 %fusion.15 = (bf16[4,9,32,128]{3,2,1,0:T(8,128)(2,1)S(1)}, bf16[4,9,32,128]{3,2,1,0:T(8,128)(2,1)S(1)}) fusion(bf16[16,9,32,128]{3,2,1,0:T(8,128)(2,1)} %get-tuple-element.9), kind=kLoop, calls=%fused_computation.121 | loop fusion | bytes 1179648 | tf_op jit(solution)/shard_map/slice | solution.py:42
  44.9 3.9 %collective-permute-start.4 = (bf16[4,9,32,128]{3,2,1,0:T(8,128)(2,1)S(1)}, bf16[4,9,32,128]{3,2,1,0:T(8,128)(2,1)S(1)}, u32[]{:S(2)}, u32[]{:S(2)}) collective-permute-start(bf16[4,9,32,128]{3,2,1,0:T(8,128)(2,1)S(1)} %get-tuple-element.18), channel_id=1, source_target_pairs={{0,8},{8,16},{16,24},{1,9},{9,17},{17,25},{2,10},{10,18},{18,26},{... | collective-permute-start | bytes 884744 | tf_op jit(solution)/shard_map/ppermute | solution.py:20
  48.9 0.6 reshape.702.target_ref
  49.6 0.6 reshape.701.where_ref
  50.1 0.6 reshape.694.refs_8_
  50.8 1.9 %collective-permute-start.5 = (bf16[4,9,32,128]{3,2,1,0:T(8,128)(2,1)S(1)}, bf16[4,9,32,128]{3,2,1,0:T(8,128)(2,1)S(1)}, u32[]{:S(2)}, u32[]{:S(2)}) collective-permute-start(bf16[4,9,32,128]{3,2,1,0:T(8,128)(2,1)S(1)} %get-tuple-element.17), channel_id=1, source_target_pairs={{8,0},{16,8},{24,16},{9,1},{17,9},{25,17},{10,2},{18,10},{26,18},{... | collective-permute-start | bytes 884744 | tf_op jit(solution)/shard_map/ppermute | solution.py:20
  52.7 1.1 %slice_bitcast_fusion = (bf16[4,9,32,128]{3,2,1,0:T(8,128)(2,1)S(1)}, bf16[4,9,32,128]{3,2,1,0:T(8,128)(2,1)S(1)}) fusion(bf16[4,4,9,32,128]{4,3,2,1,0:T(8,128)(2,1)} %bitcast.57), kind=kLoop, calls=%fused_computation.9 | loop fusion | bytes 1179648 | tf_op jit(solution)/shard_map/squeeze | solution.py:44
  53.8 5.0 %collective-permute-done.5.refs_10_ = bf16[4,9,32,128]{3,2,1,0:T(8,128)(2,1)S(1)} collective-permute-done((bf16[4,9,32,128]{3,2,1,0:T(8,128)(2,1)S(1)}, bf16[4,9,32,128]{3,2,1,0:T(8,128)(2,1)S(1)}, u32[]{:S(2)}, u32[]{:S(2)}) %collective-permute-start.5) | collective-permute-done | bytes 294944 | tf_op jit(solution)/shard_map/ppermute | solution.py:20
  58.9 2.3 %collective-permute-start.7 = (bf16[6,9,32,128]{3,2,1,0:T(8,128)(2,1)S(1)}, bf16[6,9,32,128]{3,2,1,0:T(8,128)(2,1)S(1)}, u32[]{:S(2)}, u32[]{:S(2)}) collective-permute-start(bf16[6,9,32,128]{3,2,1,0:T(8,128)(2,1)S(1)} %pad_maximum_fusion.2), channel_id=1, source_target_pairs={{1,0},{2,1},{3,2},{4,3},{5,4},{6,5},{7,6},{9,8},{10,9},{11,10},{12... | collective-permute-start | bytes 1327112 | tf_op jit(solution)/shard_map/ppermute | solution.py:23
  61.2 3.0 %collective-permute-start.6 = (bf16[6,9,32,128]{3,2,1,0:T(8,128)(2,1)S(1)}, bf16[6,9,32,128]{3,2,1,0:T(8,128)(2,1)S(1)}, u32[]{:S(2)}, u32[]{:S(2)}) collective-permute-start(bf16[6,9,32,128]{3,2,1,0:T(8,128)(2,1)S(1)} %pad_maximum_fusion.1), channel_id=1, source_target_pairs={{0,1},{1,2},{2,3},{3,4},{4,5},{5,6},{6,7},{8,9},{9,10},{10,11},{11... | collective-permute-start | bytes 1327112 | tf_op jit(solution)/shard_map/ppermute | solution.py:23
  64.3 0.6 reshape_squeeze.20.refs_5_
  64.9 0.6 reshape_squeeze.21.refs_7_
  65.5 0.7 reshape_squeeze.18.refs_1_
  66.7 0.7 slice_reduce_fusion
  67.4 0.6 slice_bitcast_fusion.2
  68.1 12.6 %shard_map.56.refs_14_ = f32[100,64,64]{2,1,0:T(8,128)} custom-call(s32[16]{0:T(128)} %reshape.701.where_ref, s32[64]{0:T(128)} %reshape.702.target_ref, bf16[16,9,64,64]{3,2,1,0:T(8,128)(2,1)} %get-tuple-element.10.ap_ref, bf16[144,64,64]{2,1,0:T(8,128)(2,1)} %bitcast.53), custom_call_target="tpu_custom_call" | custom-call | flops 301989888 | bytes 6291456 | tf_op jit(solution)/shard_map/pallas_call | solution.py:219
  80.7 0.7 copy-done.3
  81.6 20.1 %shard_map.57 = bf16[4,25,64,64]{3,2,1,0:T(8,128)(2,1)} custom-call(s32[4]{0:T(128)} %get-tuple-element.37.refs_0_, s32[16]{0:T(128)} %reshape_squeeze.18.refs_1_, s32[4]{0:T(128)} %get-tuple-element.36.refs_2_, s32[16]{0:T(128)} %reshape_squeeze.19.refs_3_, s32[6]{0:T(128)} %get-tuple-element.14.refs_4_, s32[24]{0:T(128)} %reshape_squeeze.20.refs_5_, ...), custom_call_target="tpu_custom_call" | custom-call | tf_op jit(solution)/shard_map/pallas_call | solution.py:235
  (89 shorter events, 4.5 us)
Async XLA Ops:
  0.0 2.4 %copy-start = (bf16[4,4,4,64,64]{4,3,2,1,0:T(8,128)(2,1)S(1)}, bf16[4,4,4,64,64]{4,3,2,1,0:T(8,128)(2,1)}, u32[]{:S(2)}) copy-start(bf16[4,4,4,64,64]{4,3,2,1,0:T(8,128)(2,1)} %param.7) | copy-start | bytes 1572868
  3.3 6.3 %copy-start.7 = (s32[4,4,9]{2,1,0:T(4,128)S(1)}, s32[4,4,9]{2,1,0:T(4,128)}, u32[]{:S(2)}) copy-start(s32[4,4,9]{2,1,0:T(4,128)} %param.6) | copy-start | bytes 1732
  3.5 16.6 %copy-start.8 = (s32[2,2,25]{2,1,0:T(2,128)S(1)}, s32[2,2,25]{2,1,0:T(2,128)}, u32[]{:S(2)}) copy-start(s32[2,2,25]{2,1,0:T(2,128)} %param.9) | copy-start | bytes 1204
  3.7 9.5 %collective-permute-start = (bf16[4,4,32,128]{3,2,1,0:T(8,128)(2,1)S(1)}, bf16[4,4,32,128]{3,2,1,0:T(8,128)(2,1)S(1)}, u32[]{:S(2)}, u32[]{:S(2)}) collective-permute-start(bf16[4,4,32,128]{3,2,1,0:T(8,128)(2,1)S(1)} %reshape_squeeze.22), channel_id=1, source_target_pairs={{0,8},{8,16},{16,24},{1,9},{9,17},{17,25},{2,10},{10,18},{18,26},{... | collective-permute-start | bytes 393224 | tf_op jit(solution)/shard_map/ppermute | solution.py:20
  7.5 6.3 %collective-permute-start.1 = (bf16[4,4,32,128]{3,2,1,0:T(8,128)(2,1)S(1)}, bf16[4,4,32,128]{3,2,1,0:T(8,128)(2,1)S(1)}, u32[]{:S(2)}, u32[]{:S(2)}) collective-permute-start(bf16[4,4,32,128]{3,2,1,0:T(8,128)(2,1)S(1)} %reshape_squeeze.23), channel_id=1, source_target_pairs={{8,0},{16,8},{24,16},{9,1},{17,9},{25,17},{10,2},{18,10},{26,18},{... | collective-permute-start | bytes 393224 | tf_op jit(solution)/shard_map/ppermute | solution.py:20
  11.7 0.6 copy-start.5
  13.9 7.5 %collective-permute-start.2 = (bf16[6,4,32,128]{3,2,1,0:T(8,128)(2,1)S(1)}, bf16[6,4,32,128]{3,2,1,0:T(8,128)(2,1)S(1)}, u32[]{:S(2)}, u32[]{:S(2)}) collective-permute-start(bf16[6,4,32,128]{3,2,1,0:T(8,128)(2,1)S(1)} %pad_maximum_fusion.3), channel_id=1, source_target_pairs={{0,1},{1,2},{2,3},{3,4},{4,5},{5,6},{6,7},{8,9},{9,10},{10,11},{11... | collective-permute-start | bytes 589832 | tf_op jit(solution)/shard_map/ppermute | solution.py:23
  17.1 8.7 %collective-permute-start.3 = (bf16[6,4,32,128]{3,2,1,0:T(8,128)(2,1)S(1)}, bf16[6,4,32,128]{3,2,1,0:T(8,128)(2,1)}, u32[]{:S(2)}, u32[]{:S(2)}) collective-permute-start(bf16[6,4,32,128]{3,2,1,0:T(8,128)(2,1)S(1)} %pad_maximum_fusion.4), channel_id=1, source_target_pairs={{1,0},{2,1},{3,2},{4,3},{5,4},{6,5},{7,6},{9,8},{10,9},{11,10},{12... | collective-permute-start | bytes 589832 | tf_op jit(solution)/shard_map/ppermute | solution.py:23
  28.7 20.2 %copy-start.6 = (s32[6,6,4]{2,1,0:T(8,128)S(1)}, s32[6,6,4]{2,1,0:T(8,128)}, u32[]{:S(2)}) copy-start(s32[6,6,4]{2,1,0:T(8,128)} %copy-done.5) | copy-start | bytes 1732
  44.9 8.8 %collective-permute-start.4 = (bf16[4,9,32,128]{3,2,1,0:T(8,128)(2,1)S(1)}, bf16[4,9,32,128]{3,2,1,0:T(8,128)(2,1)S(1)}, u32[]{:S(2)}, u32[]{:S(2)}) collective-permute-start(bf16[4,9,32,128]{3,2,1,0:T(8,128)(2,1)S(1)} %get-tuple-element.18), channel_id=1, source_target_pairs={{0,8},{8,16},{16,24},{1,9},{9,17},{17,25},{2,10},{10,18},{18,26},{... | collective-permute-start | bytes 884744 | tf_op jit(solution)/shard_map/ppermute | solution.py:20
  50.8 8.0 %collective-permute-start.5 = (bf16[4,9,32,128]{3,2,1,0:T(8,128)(2,1)S(1)}, bf16[4,9,32,128]{3,2,1,0:T(8,128)(2,1)S(1)}, u32[]{:S(2)}, u32[]{:S(2)}) collective-permute-start(bf16[4,9,32,128]{3,2,1,0:T(8,128)(2,1)S(1)} %get-tuple-element.17), channel_id=1, source_target_pairs={{8,0},{16,8},{24,16},{9,1},{17,9},{25,17},{10,2},{18,10},{26,18},{... | collective-permute-start | bytes 884744 | tf_op jit(solution)/shard_map/ppermute | solution.py:20
  53.8 26.9 %copy-start.1 = (bf16[4,9,32,128]{3,2,1,0:T(8,128)(2,1)}, bf16[4,9,32,128]{3,2,1,0:T(8,128)(2,1)S(1)}, u32[]{:S(2)}) copy-start(bf16[4,9,32,128]{3,2,1,0:T(8,128)(2,1)S(1)} %collective-permute-done.4.refs_9_) | copy-start | bytes 884740
  58.8 21.9 %copy-start.2 = (bf16[4,9,32,128]{3,2,1,0:T(8,128)(2,1)}, bf16[4,9,32,128]{3,2,1,0:T(8,128)(2,1)S(1)}, u32[]{:S(2)}) copy-start(bf16[4,9,32,128]{3,2,1,0:T(8,128)(2,1)S(1)} %collective-permute-done.5.refs_10_) | copy-start | bytes 884740
  58.9 21.8 %collective-permute-start.7 = (bf16[6,9,32,128]{3,2,1,0:T(8,128)(2,1)S(1)}, bf16[6,9,32,128]{3,2,1,0:T(8,128)(2,1)S(1)}, u32[]{:S(2)}, u32[]{:S(2)}) collective-permute-start(bf16[6,9,32,128]{3,2,1,0:T(8,128)(2,1)S(1)} %pad_maximum_fusion.2), channel_id=1, source_target_pairs={{1,0},{2,1},{3,2},{4,3},{5,4},{6,5},{7,6},{9,8},{10,9},{11,10},{12... | collective-permute-start | bytes 1327112 | tf_op jit(solution)/shard_map/ppermute | solution.py:23
  61.2 19.5 %collective-permute-start.6 = (bf16[6,9,32,128]{3,2,1,0:T(8,128)(2,1)S(1)}, bf16[6,9,32,128]{3,2,1,0:T(8,128)(2,1)S(1)}, u32[]{:S(2)}, u32[]{:S(2)}) collective-permute-start(bf16[6,9,32,128]{3,2,1,0:T(8,128)(2,1)S(1)} %pad_maximum_fusion.1), channel_id=1, source_target_pairs={{0,1},{1,2},{2,3},{3,4},{4,5},{5,6},{6,7},{8,9},{9,10},{10,11},{11... | collective-permute-start | bytes 1327112 | tf_op jit(solution)/shard_map/ppermute | solution.py:23
  80.7 0.8 copy-start.3
  80.7 0.9 copy-start.4

commit v19 on v16

--- a/solution.py
+++ b/solution.py
@@ -117,14 +117,15 @@
     tables, pick_ref = refs[: 2 * groups], refs[2 * groups]
     blocks = refs[2 * groups + 1 : 3 * groups + 1]
     pt_ref, part_ref, out_ref, acc_ref = refs[-4], refs[-3], refs[-2], refs[-1]
-    acc_ref[...] = part_ref[...]
+    acc_ref[...] = jnp.zeros(acc_ref.shape, jnp.float32)
     for i in range(groups):
         add_terms(tables[2 * i], tables[2 * i + 1], blocks[i], pt_ref, acc_ref)
     owned, stencil = out_ref.shape[0], out_ref.shape[1]
 
     def one_pick(i, carry):
         a = i // stencil
-        out_ref[a, i % stencil] = acc_ref[a * stencil + pick_ref[i]].astype(out_ref.dtype)
+        at = a * stencil + pick_ref[i]
+        out_ref[a, i % stencil] = (part_ref[at] + acc_ref[at]).astype(out_ref.dtype)
         return carry
 
     lax.fori_loop(0, owned * stencil, one_pick, 0)

time: 101 us -> 102 us (level)
  no operation moved by 1% of the time
where the time goes in v19:
time: 102 us; the launch traced here: 101 us
  Pallas kernels  48 us (47%)
  starting transfers between devices  22.8 us (22%)
  local copies, waits for them, and re-layouts  11.9 us (12%)
  waiting for transfers between devices  10.7 us (10%)
  other arithmetic  6.86 us (7%)
    pallas_call x1, Pallas kernels, body(): pl.pallas_call(coarse_kernel, out_shape=jax.ShapeDtypeStruct((o_r * o_c,...  20.3 us
    pallas_call x1, Pallas kernels, body(): pl.pallas_call(functools.partial(ap_kernel, n_r=n_r, n_c=n_c), out_shape=...  15.1 us
    pallas_call x1, Pallas kernels, body(): pl.pallas_call(own_kernel, out_shape=jax.ShapeDtypeStruct(acc_shape, jnp....  12.6 us
    ppermute x4, starting transfers between devices, shifted(): return lax.ppermute(piece, 'col', pairs)  11.5 us
    ppermute x4, starting transfers between devices, shifted(): return lax.ppermute(piece, 'row', pairs)  11.3 us
    ppermute x4, waiting for transfers between devices, shifted(): return lax.ppermute(piece, 'row', pairs)  5.87 us
    ppermute x4, waiting for transfers between devices, shifted(): return lax.ppermute(piece, 'col', pairs)  4.85 us
    reduce_sum x1, other arithmetic, body(): jnp.sum(jnp.where(match[..., None, None], p_blocks[:, :, None], jnp.zeros...  2.77 us
  transfers between devices with their start and end apart: 8, of which 4 were waited for; matrix products, arithmetic and copies ran while one was open for 11% of the time, Pallas kernels for 12%

profile of v19, /device:TPU:9, one launch (start us, length us, event | category | flops | bytes accessed | tf_op | source)
XLA Modules:
  0.0 101.0 jit_solution(1358265408191213548)
XLA Ops:
  0.3 0.8 broadcast_compare_fusion
  1.1 2.8 %select_reduce_fusion = bf16[4,4,4,64,64]{4,3,2,1,0:T(8,128)(2,1)S(1)} fusion(pred[4,4,4,4]{3,2,1,0:T(4,128)(4,1)S(1)} %broadcast_compare_fusion, bf16[4,4,4,64,64]{4,3,2,1,0:T(8,128)(2,1)} %param.7), kind=kLoop, calls=%fused_computation | loop fusion | flops 1835008 | bytes 1048832 | tf_op jit(solution)/shard_map/reduce_sum | solution.py:155
  4.1 3.7 %collective-permute-start = (bf16[4,4,32,128]{3,2,1,0:T(8,128)(2,1)S(1)}, bf16[4,4,32,128]{3,2,1,0:T(8,128)(2,1)S(1)}, u32[]{:S(2)}, u32[]{:S(2)}) collective-permute-start(bf16[4,4,32,128]{3,2,1,0:T(8,128)(2,1)S(1)} %reshape_squeeze.22), channel_id=1, source_target_pairs={{0,8},{8,16},{16,24},{1,9},{9,17},{17,25},{2,10},{10,18},{18,26},{... | collective-permute-start | bytes 393224 | tf_op jit(solution)/shard_map/ppermute | solution.py:20
  7.9 1.9 %collective-permute-start.1 = (bf16[4,4,32,128]{3,2,1,0:T(8,128)(2,1)S(1)}, bf16[4,4,32,128]{3,2,1,0:T(8,128)(2,1)S(1)}, u32[]{:S(2)}, u32[]{:S(2)}) collective-permute-start(bf16[4,4,32,128]{3,2,1,0:T(8,128)(2,1)S(1)} %reshape_squeeze.23), channel_id=1, source_target_pairs={{8,0},{16,8},{24,16},{9,1},{17,9},{25,17},{10,2},{18,10},{26,18},{... | collective-permute-start | bytes 393224 | tf_op jit(solution)/shard_map/ppermute | solution.py:20
  10.7 0.6 and_select_fusion.slot_ref
  12.6 0.6 reshape.677.near_ref
  13.3 0.9 collective-permute-done.1
  14.2 3.1 %collective-permute-start.2 = (bf16[6,4,32,128]{3,2,1,0:T(8,128)(2,1)S(1)}, bf16[6,4,32,128]{3,2,1,0:T(8,128)(2,1)S(1)}, u32[]{:S(2)}, u32[]{:S(2)}) collective-permute-start(bf16[6,4,32,128]{3,2,1,0:T(8,128)(2,1)S(1)} %pad_maximum_fusion.3), channel_id=1, source_target_pairs={{0,1},{1,2},{2,3},{3,4},{4,5},{5,6},{6,7},{8,9},{9,10},{10,11},{11... | collective-permute-start | bytes 589832 | tf_op jit(solution)/shard_map/ppermute | solution.py:23
  17.4 3.0 %collective-permute-start.3 = (bf16[6,4,32,128]{3,2,1,0:T(8,128)(2,1)S(1)}, bf16[6,4,32,128]{3,2,1,0:T(8,128)(2,1)S(1)}, u32[]{:S(2)}, u32[]{:S(2)}) collective-permute-start(bf16[6,4,32,128]{3,2,1,0:T(8,128)(2,1)S(1)} %pad_maximum_fusion.4), channel_id=1, source_target_pairs={{1,0},{2,1},{3,2},{4,3},{5,4},{6,5},{7,6},{9,8},{10,9},{11,10},{12... | collective-permute-start | bytes 589832 | tf_op jit(solution)/shard_map/ppermute | solution.py:23
  20.8 0.8 collective-permute-done.2
  21.8 4.0 %collective-permute-done.3 = bf16[6,4,32,128]{3,2,1,0:T(8,128)(2,1)S(1)} collective-permute-done((bf16[6,4,32,128]{3,2,1,0:T(8,128)(2,1)S(1)}, bf16[6,4,32,128]{3,2,1,0:T(8,128)(2,1)S(1)}, u32[]{:S(2)}, u32[]{:S(2)}) %collective-permute-start.3) | collective-permute-done | bytes 196640 | tf_op jit(solution)/shard_map/ppermute | solution.py:23
  26.0 1.8 %pad_maximum_fusion = bf16[6,6,4,64,64]{4,3,2,1,0:T(8,128)(2,1)} fusion(bf16[6,1,4,64,64]{4,3,2,1,0:T(8,128)(2,1)S(1)} %broadcast_in_dim_reshape.16, bf16[1,4,4,64,64]{4,3,2,1,0:T(8,128)(2,1)S(1)} %broadcast_in_dim_reshape.15, bf16[4,4,4,64,64]{4,3,2,1,0:T(8,128)(2,1)S(1)} %select_reduce_fusion, bf16[1,4,4,64,64]{4,3,2,1,0:T(8,128)(2,1)S(1)} %broadcast_in_dim_reshape.14, ...), kind=kLoop, calls=%fused_computation.1 | loop fusion | flops 2359296 | bytes 2359296 | tf_op jit(solution)/shard_map/concatenate | solution.py:51
  27.9 15.1 %shard_map.55 = (bf16[16,9,64,64]{3,2,1,0:T(8,128)(2,1)}, bf16[16,9,32,128]{3,2,1,0:T(8,128)(2,1)}) custom-call(s32[144]{0:T(256)} %reshape.677.near_ref, s32[576]{0:T(1024)} %and_select_fusion.slot_ref, bf16[16,9,64,64]{3,2,1,0:T(8,128)(2,1)} %bitcast.50, bf16[36,4,64,64]{3,2,1,0:T(8,128)(2,1)} %bitcast.47), custom_call_target="tpu_custom_call" | custom-call | tf_op jit(solution)/shard_map/pallas_call | solution.py:173
  43.0 1.1 %fusion.15 = (bf16[4,9,32,128]{3,2,1,0:T(8,128)(2,1)S(1)}, bf16[4,9,32,128]{3,2,1,0:T(8,128)(2,1)S(1)}) fusion(bf16[16,9,32,128]{3,2,1,0:T(8,128)(2,1)} %get-tuple-element.7), kind=kLoop, calls=%fused_computation.117 | loop fusion | bytes 1179648 | tf_op jit(solution)/shard_map/slice | solution.py:42
  44.1 3.8 %collective-permute-start.4 = (bf16[4,9,32,128]{3,2,1,0:T(8,128)(2,1)S(1)}, bf16[4,9,32,128]{3,2,1,0:T(8,128)(2,1)S(1)}, u32[]{:S(2)}, u32[]{:S(2)}) collective-permute-start(bf16[4,9,32,128]{3,2,1,0:T(8,128)(2,1)S(1)} %get-tuple-element.16), channel_id=1, source_target_pairs={{0,8},{8,16},{16,24},{1,9},{9,17},{17,25},{2,10},{10,18},{18,26},{... | collective-permute-start | bytes 884744 | tf_op jit(solution)/shard_map/ppermute | solution.py:20
  47.9 0.7 reshape.683.target_ref
  48.7 0.6 reshape.682.where_ref
  49.2 0.6 reshape.676.refs_8_
  49.8 1.9 %collective-permute-start.5 = (bf16[4,9,32,128]{3,2,1,0:T(8,128)(2,1)S(1)}, bf16[4,9,32,128]{3,2,1,0:T(8,128)(2,1)S(1)}, u32[]{:S(2)}, u32[]{:S(2)}) collective-permute-start(bf16[4,9,32,128]{3,2,1,0:T(8,128)(2,1)S(1)} %get-tuple-element.15), channel_id=1, source_target_pairs={{8,0},{16,8},{24,16},{9,1},{17,9},{25,17},{10,2},{18,10},{26,18},{... | collective-permute-start | bytes 884744 | tf_op jit(solution)/shard_map/ppermute | solution.py:20
  51.7 1.1 %slice_bitcast_fusion = (bf16[4,9,32,128]{3,2,1,0:T(8,128)(2,1)S(1)}, bf16[4,9,32,128]{3,2,1,0:T(8,128)(2,1)S(1)}) fusion(bf16[4,4,9,32,128]{4,3,2,1,0:T(8,128)(2,1)} %bitcast.51), kind=kLoop, calls=%fused_computation.8 | loop fusion | bytes 1179648 | tf_op jit(solution)/shard_map/squeeze | solution.py:44
  52.9 5.0 %collective-permute-done.5.refs_10_ = bf16[4,9,32,128]{3,2,1,0:T(8,128)(2,1)S(1)} collective-permute-done((bf16[4,9,32,128]{3,2,1,0:T(8,128)(2,1)S(1)}, bf16[4,9,32,128]{3,2,1,0:T(8,128)(2,1)S(1)}, u32[]{:S(2)}, u32[]{:S(2)}) %collective-permute-start.5) | collective-permute-done | bytes 294944 | tf_op jit(solution)/shard_map/ppermute | solution.py:20
  57.9 2.3 %collective-permute-start.7 = (bf16[6,9,32,128]{3,2,1,0:T(8,128)(2,1)S(1)}, bf16[6,9,32,128]{3,2,1,0:T(8,128)(2,1)S(1)}, u32[]{:S(2)}, u32[]{:S(2)}) collective-permute-start(bf16[6,9,32,128]{3,2,1,0:T(8,128)(2,1)S(1)} %pad_maximum_fusion.2), channel_id=1, source_target_pairs={{1,0},{2,1},{3,2},{4,3},{5,4},{6,5},{7,6},{9,8},{10,9},{11,10},{12... | collective-permute-start | bytes 1327112 | tf_op jit(solution)/shard_map/ppermute | solution.py:23
  60.3 3.0 %collective-permute-start.6 = (bf16[6,9,32,128]{3,2,1,0:T(8,128)(2,1)S(1)}, bf16[6,9,32,128]{3,2,1,0:T(8,128)(2,1)S(1)}, u32[]{:S(2)}, u32[]{:S(2)}) collective-permute-start(bf16[6,9,32,128]{3,2,1,0:T(8,128)(2,1)S(1)} %pad_maximum_fusion.1), channel_id=1, source_target_pairs={{0,1},{1,2},{2,3},{3,4},{4,5},{5,6},{6,7},{8,9},{9,10},{10,11},{11... | collective-permute-start | bytes 1327112 | tf_op jit(solution)/shard_map/ppermute | solution.py:23
  63.3 0.6 reshape_squeeze.20.refs_5_
  63.9 0.7 reshape_squeeze.21.refs_7_
  64.6 0.6 reshape_squeeze.18.refs_1_
  65.2 0.6 reshape_squeeze.19.refs_3_
  65.8 0.7 slice_reduce_fusion
  66.5 0.6 slice_bitcast_fusion.2
  67.2 12.6 %shard_map.56.refs_14_ = f32[100,64,64]{2,1,0:T(8,128)} custom-call(s32[16]{0:T(128)} %reshape.682.where_ref, s32[64]{0:T(128)} %reshape.683.target_ref, bf16[16,9,64,64]{3,2,1,0:T(8,128)(2,1)} %get-tuple-element.8.ap_ref, bf16[144,64,64]{2,1,0:T(8,128)(2,1)} %bitcast.48), custom_call_target="tpu_custom_call" | custom-call | flops 301989888 | bytes 6291456 | tf_op jit(solution)/shard_map/pallas_call | solution.py:223
  79.8 0.7 copy-done.2
  80.7 20.3 %shard_map.57 = bf16[4,25,64,64]{3,2,1,0:T(8,128)(2,1)} custom-call(s32[4]{0:T(128)} %get-tuple-element.35.refs_0_, s32[16]{0:T(128)} %reshape_squeeze.18.refs_1_, s32[4]{0:T(128)} %get-tuple-element.34.refs_2_, s32[16]{0:T(128)} %reshape_squeeze.19.refs_3_, s32[6]{0:T(128)} %get-tuple-element.12.refs_4_, s32[24]{0:T(128)} %reshape_squeeze.20.refs_5_, ...), custom_call_target="tpu_custom_call" | custom-call | tf_op jit(solution)/shard_map/pallas_call | solution.py:239
  (79 shorter events, 3.5 us)
Async XLA Ops:
  1.1 8.9 %copy-start.4 = (s32[4,4,9]{2,1,0:T(4,128)S(1)}, s32[4,4,9]{2,1,0:T(4,128)}, u32[]{:S(2)}) copy-start(s32[4,4,9]{2,1,0:T(4,128)} %param.6) | copy-start | bytes 1732
  3.9 16.6 %copy-start.5 = (s32[2,2,25]{2,1,0:T(2,128)S(1)}, s32[2,2,25]{2,1,0:T(2,128)}, u32[]{:S(2)}) copy-start(s32[2,2,25]{2,1,0:T(2,128)} %param.9) | copy-start | bytes 1204
  4.1 9.2 %collective-permute-start = (bf16[4,4,32,128]{3,2,1,0:T(8,128)(2,1)S(1)}, bf16[4,4,32,128]{3,2,1,0:T(8,128)(2,1)S(1)}, u32[]{:S(2)}, u32[]{:S(2)}) collective-permute-start(bf16[4,4,32,128]{3,2,1,0:T(8,128)(2,1)S(1)} %reshape_squeeze.22), channel_id=1, source_target_pairs={{0,8},{8,16},{16,24},{1,9},{9,17},{17,25},{2,10},{10,18},{18,26},{... | collective-permute-start | bytes 393224 | tf_op jit(solution)/shard_map/ppermute | solution.py:20
  7.9 6.3 %collective-permute-start.1 = (bf16[4,4,32,128]{3,2,1,0:T(8,128)(2,1)S(1)}, bf16[4,4,32,128]{3,2,1,0:T(8,128)(2,1)S(1)}, u32[]{:S(2)}, u32[]{:S(2)}) collective-permute-start(bf16[4,4,32,128]{3,2,1,0:T(8,128)(2,1)S(1)} %reshape_squeeze.23), channel_id=1, source_target_pairs={{8,0},{16,8},{24,16},{9,1},{17,9},{25,17},{10,2},{18,10},{26,18},{... | collective-permute-start | bytes 393224 | tf_op jit(solution)/shard_map/ppermute | solution.py:20
  14.2 7.4 %collective-permute-start.2 = (bf16[6,4,32,128]{3,2,1,0:T(8,128)(2,1)S(1)}, bf16[6,4,32,128]{3,2,1,0:T(8,128)(2,1)S(1)}, u32[]{:S(2)}, u32[]{:S(2)}) collective-permute-start(bf16[6,4,32,128]{3,2,1,0:T(8,128)(2,1)S(1)} %pad_maximum_fusion.3), channel_id=1, source_target_pairs={{0,1},{1,2},{2,3},{3,4},{4,5},{5,6},{6,7},{8,9},{9,10},{10,11},{11... | collective-permute-start | bytes 589832 | tf_op jit(solution)/shard_map/ppermute | solution.py:23
  17.4 8.4 %collective-permute-start.3 = (bf16[6,4,32,128]{3,2,1,0:T(8,128)(2,1)S(1)}, bf16[6,4,32,128]{3,2,1,0:T(8,128)(2,1)S(1)}, u32[]{:S(2)}, u32[]{:S(2)}) collective-permute-start(bf16[6,4,32,128]{3,2,1,0:T(8,128)(2,1)S(1)} %pad_maximum_fusion.4), channel_id=1, source_target_pairs={{1,0},{2,1},{3,2},{4,3},{5,4},{6,5},{7,6},{9,8},{10,9},{11,10},{12... | collective-permute-start | bytes 589832 | tf_op jit(solution)/shard_map/ppermute | solution.py:23
  44.1 8.8 %collective-permute-start.4 = (bf16[4,9,32,128]{3,2,1,0:T(8,128)(2,1)S(1)}, bf16[4,9,32,128]{3,2,1,0:T(8,128)(2,1)S(1)}, u32[]{:S(2)}, u32[]{:S(2)}) collective-permute-start(bf16[4,9,32,128]{3,2,1,0:T(8,128)(2,1)S(1)} %get-tuple-element.16), channel_id=1, source_target_pairs={{0,8},{8,16},{16,24},{1,9},{9,17},{17,25},{2,10},{10,18},{18,26},{... | collective-permute-start | bytes 884744 | tf_op jit(solution)/shard_map/ppermute | solution.py:20
  49.8 8.0 %collective-permute-start.5 = (bf16[4,9,32,128]{3,2,1,0:T(8,128)(2,1)S(1)}, bf16[4,9,32,128]{3,2,1,0:T(8,128)(2,1)S(1)}, u32[]{:S(2)}, u32[]{:S(2)}) collective-permute-start(bf16[4,9,32,128]{3,2,1,0:T(8,128)(2,1)S(1)} %get-tuple-element.15), channel_id=1, source_target_pairs={{8,0},{16,8},{24,16},{9,1},{17,9},{25,17},{10,2},{18,10},{26,18},{... | collective-permute-start | bytes 884744 | tf_op jit(solution)/shard_map/ppermute | solution.py:20
  52.8 26.9 %copy-start = (bf16[4,9,32,128]{3,2,1,0:T(8,128)(2,1)}, bf16[4,9,32,128]{3,2,1,0:T(8,128)(2,1)S(1)}, u32[]{:S(2)}) copy-start(bf16[4,9,32,128]{3,2,1,0:T(8,128)(2,1)S(1)} %collective-permute-done.4.refs_9_) | copy-start | bytes 884740
  57.9 21.9 %copy-start.1 = (bf16[4,9,32,128]{3,2,1,0:T(8,128)(2,1)}, bf16[4,9,32,128]{3,2,1,0:T(8,128)(2,1)S(1)}, u32[]{:S(2)}) copy-start(bf16[4,9,32,128]{3,2,1,0:T(8,128)(2,1)S(1)} %collective-permute-done.5.refs_10_) | copy-start | bytes 884740
  57.9 21.8 %collective-permute-start.7 = (bf16[6,9,32,128]{3,2,1,0:T(8,128)(2,1)S(1)}, bf16[6,9,32,128]{3,2,1,0:T(8,128)(2,1)S(1)}, u32[]{:S(2)}, u32[]{:S(2)}) collective-permute-start(bf16[6,9,32,128]{3,2,1,0:T(8,128)(2,1)S(1)} %pad_maximum_fusion.2), channel_id=1, source_target_pairs={{1,0},{2,1},{3,2},{4,3},{5,4},{6,5},{7,6},{9,8},{10,9},{11,10},{12... | collective-permute-start | bytes 1327112 | tf_op jit(solution)/shard_map/ppermute | solution.py:23
  60.3 19.5 %collective-permute-start.6 = (bf16[6,9,32,128]{3,2,1,0:T(8,128)(2,1)S(1)}, bf16[6,9,32,128]{3,2,1,0:T(8,128)(2,1)S(1)}, u32[]{:S(2)}, u32[]{:S(2)}) collective-permute-start(bf16[6,9,32,128]{3,2,1,0:T(8,128)(2,1)S(1)} %pad_maximum_fusion.1), channel_id=1, source_target_pairs={{0,1},{1,2},{2,3},{3,4},{4,5},{5,6},{6,7},{8,9},{9,10},{10,11},{11... | collective-permute-start | bytes 1327112 | tf_op jit(solution)/shard_map/ppermute | solution.py:23
  79.7 0.8 copy-start.2
  79.8 0.9 copy-start.3
